TPU v7x, 32 devices: a whole 2x2x4 slice. The times are simulated.
32 devices in a mesh: groups: 2 (over y), pts: 4 (over z), cam: 4 (over x, core).
Axes of the slice: x: 2, y: 2, z: 4, core: 2. Of those that a mesh axis runs over, the one named last changes fastest.
Arguments:
- cam_jac: float32 [2, 9, 131072], P(None, None, ('groups', 'pts', 'cam')), parts along dimension 2, may hold values from -0.4 to 0.4
- point_jac: float32 [2, 3, 131072], P(None, None, ('groups', 'pts', 'cam')), parts along dimension 2, may hold values from -3 to 3
- obs_cam: int32 [131072], P(('groups', 'pts', 'cam')), parts along dimension 0, may hold values from 0 to 511
- obs_point: int32 [131072], P(('groups', 'pts', 'cam')), parts along dimension 0, may hold values from 0 to 4095
- point_damp: float32 [32768], P(('groups', 'pts')), parts along dimension 0, may hold values from 0.5 to 4
- cam_damp: float32 [4096], P(('groups', 'cam')), parts along dimension 0, may hold values from 0.5 to 4
- reduced_rhs: float32 [9, 4096], P(None, ('groups', 'cam')), parts along dimension 1, may hold values from -6 to 6
Outputs:
- solution: float32 [9, 4096], P(None, ('groups', 'cam')), parts along dimension 1
- residual: float32 [9, 4096], P(None, ('groups', 'cam')), parts along dimension 1
There are 2 independent parts, one for each index of `groups`. A program takes and returns all parts, laid end to end along the dimension named above; each array names one. Nothing has to cross between parts.
All inputs are finite; a program needn't handle non-finite values.
Results may differ from a plain program's by a relative error of at most 0.0003.
Values sent between devices are 32-bit elements; how exact they have to be, the bound alone decides.
No kernel may reach another device: no remote copies, remote signals or barrier semaphores. Data moves between devices by JAX's collectives and lax.ppermute only.
A program may use at most 64 MiB of HBM per device.

v0:
```python
import jax
import jax.numpy as jnp
from jax import lax
from jax.sharding import PartitionSpec as P

ITERS = 3


HI = lax.Precision.HIGHEST


def segsum(terms, index, count):
    return jax.ops.segment_sum(terms.T, index, num_segments=count).T


def invert3(mat):
    c00 = mat[1, 1] * mat[2, 2] - mat[1, 2] * mat[2, 1]
    c01 = mat[0, 2] * mat[2, 1] - mat[0, 1] * mat[2, 2]
    c02 = mat[0, 1] * mat[1, 2] - mat[0, 2] * mat[1, 1]
    c10 = mat[1, 2] * mat[2, 0] - mat[1, 0] * mat[2, 2]
    c11 = mat[0, 0] * mat[2, 2] - mat[0, 2] * mat[2, 0]
    c12 = mat[0, 2] * mat[1, 0] - mat[0, 0] * mat[1, 2]
    c20 = mat[1, 0] * mat[2, 1] - mat[1, 1] * mat[2, 0]
    c21 = mat[0, 1] * mat[2, 0] - mat[0, 0] * mat[2, 1]
    c22 = mat[0, 0] * mat[1, 1] - mat[0, 1] * mat[1, 0]
    det = mat[0, 0] * c00 + mat[0, 1] * c10 + mat[0, 2] * c20
    adj = jnp.stack(
        [jnp.stack([c00, c01, c02]), jnp.stack([c10, c11, c12]), jnp.stack([c20, c21, c22])]
    )
    return adj / det


def normal_six(point_jac):
    pairs = [(0, 0), (0, 1), (0, 2), (1, 1), (1, 2), (2, 2)]
    return jnp.stack(
        [jnp.sum(point_jac[:, first] * point_jac[:, second], axis=0) for first, second in pairs]
    )


def expand_six(six):
    return jnp.stack(
        [
            jnp.stack([six[0], six[1], six[2]]),
            jnp.stack([six[1], six[3], six[4]]),
            jnp.stack([six[2], six[4], six[5]]),
        ]
    )


def point_inverse(six, damp):
    mat = expand_six(six) + damp[None, None, :] * jnp.eye(3, dtype=jnp.float32)[:, :, None]
    return invert3(mat)


def norm_sum(value):
    return lax.psum(value, "cam")


def on_device(cam_jac, point_jac, obs_cam, obs_point, point_damp, cam_damp, reduced_rhs):
    npts = point_damp.shape[0]
    ncam = reduced_rhs.shape[1]
    six_terms = segsum(normal_six(point_jac), obs_point, npts)
    pshare = npts // lax.axis_size("cam")
    pstart = lax.axis_index("cam") * pshare
    six_share = lax.psum_scatter(six_terms, "cam", scatter_dimension=1, tiled=True)
    damp_pts = lax.dynamic_slice_in_dim(point_damp, pstart, pshare, 0)
    inv_share = point_inverse(six_share, damp_pts)
    diag_terms = segsum(jnp.sum(cam_jac * cam_jac, axis=0), obs_cam, ncam)
    cam_diag = lax.psum(diag_terms, "pts") + cam_damp[None, :]
    solution = jnp.zeros_like(reduced_rhs)
    residual = reduced_rhs
    pre = residual / cam_diag
    direction = pre
    rz = norm_sum(jnp.sum(residual * pre))
    for step in range(ITERS):
        y = jnp.einsum("rko,ko->ro", cam_jac, direction[:, obs_cam], precision=HI)
        reduced_u_part = segsum(
            jnp.einsum("rao,ro->ao", point_jac, y, precision=HI), obs_point, npts
        )
        u_share = lax.psum_scatter(reduced_u_part, "cam", scatter_dimension=1, tiled=True)
        w_share = jnp.sum(inv_share * u_share[None, :, :], axis=1)
        w = lax.all_gather(w_share, "cam", axis=1, tiled=True)
        z = y - jnp.einsum("rao,ao->ro", point_jac, w[:, obs_point], precision=HI)
        image = cam_damp[None, :] * direction + lax.psum(
            segsum(jnp.einsum("rko,ro->ko", cam_jac, z, precision=HI), obs_cam, ncam), "pts"
        )
        alpha = rz / lax.psum(jnp.sum(direction * image), "cam")
        solution = solution + alpha * direction
        residual = residual - alpha * image
        pre = residual / cam_diag
        new_rz = norm_sum(jnp.sum(residual * pre))
        direction = pre + new_rz / rz * direction
        rz = new_rz
    return (solution, residual)


def solution(mesh):
    return jax.shard_map(
        on_device,
        mesh=mesh,
        in_specs=(
            P(None, None, ("groups", "pts", "cam")),
            P(None, None, ("groups", "pts", "cam")),
            P(("groups", "pts", "cam")),
            P(("groups", "pts", "cam")),
            P(("groups", "pts")),
            P(("groups", "cam")),
            P(None, ("groups", "cam")),
        ),
        out_specs=(P(None, ("groups", "cam")), P(None, ("groups", "cam"))),
        check_vma=False,
    )
```

profile of v0, /device:TPU:0, one launch (start us, length us, event | category | flops | bytes accessed | tf_op | source)
XLA Modules:
  0.0 563.1 jit_solution(943922802294246688)
XLA Ops:
  7.2 0.7 fusion.19
  8.0 1.3 multiply_reduce_fusion.6
  9.3 0.6 copy.113
  10.0 22.5 %scatter_custom_fusion = f32[512,9]{1,0:T(8,128)S(1)} fusion(s32[4096]{0:T(1024)} %param.9, f32[4096,9]{1,0:T(8,128)S(1)} %copy.113, f32[]{:T(128)} %constant.6.clone.1), kind=kCustom, calls=%fused_computation.36 | custom fusion | flops 36864 | bytes 18944 | tf_op jit(solution)/shard_map/scatter-add | solution.py:13
  32.6 20.8 %psum.70 = f32[9,512]{1,0:T(8,128)S(1)} all-reduce(f32[9,512]{1,0:T(8,128)S(1)} %bitcast.122), channel_id=1, replica_groups=mesh['groups'=2,'pts'=4,'cam'=4] {'pts'}, use_global_device_ids=true, to_apply=%region_2.0 | all-reduce | flops 4608 | bytes 36864 | tf_op jit(solution)/shard_map/psum | solution.py:69
  53.6 10.8 %gather_fusion = f32[4096,9]{1,0:T(8,128)S(1)} fusion(f32[9,512]{0,1:T(8,128)S(1)} %copy.115, s32[4096]{0:T(1024)S(1)} %fusion.19), kind=kCustom, calls=%fused_computation | custom fusion | bytes 311296 | tf_op jit(solution)/shard_map/gather | solution.py:76
  64.4 0.6 copy.217
  65.4 0.6 copy.146
  66.0 23.8 %scatter_custom_fusion.2 = f32[4096,3]{1,0:T(8,128)} fusion(s32[4096]{0:T(1024)S(1)} %copy-done.5, f32[4096,3]{1,0:T(8,128)S(1)} %copy.146, f32[]{:T(128)} %constant.6.clone.1), kind=kCustom, calls=%fused_computation.18 | custom fusion | flops 12288 | bytes 49156 | tf_op jit(solution)/shard_map/scatter-add | solution.py:13
  89.9 0.2 multiply_reduce_fusion.21
  90.3 0.6 copy.116
  91.0 23.7 %scatter_custom_fusion.1 = f32[4096,6]{1,0:T(8,128)} fusion(s32[4096]{0:T(1024)S(1)} %copy-done.5, f32[4096,6]{1,0:T(8,128)S(1)} %copy.116, f32[]{:T(128)} %constant.6.clone.1), kind=kCustom, calls=%fused_computation.20 | custom fusion | flops 24576 | bytes 98308 | tf_op jit(solution)/shard_map/scatter-add | solution.py:13
  114.8 4.6 reduce-scatter.7.cloned.1.call-done
  119.4 1.2 copy.122
  120.6 32.5 %reduce-scatter.5.cloned.1.call-done = f32[6,1024]{0,1:T(8,128)} async-done(((f32[6,4096]{0,1:T(8,128)}), f32[6,1024]{0,1:T(8,128)}) %reduce-scatter.5.cloned.1.call-update) | async-done | bytes 24592 | tf_op jit(solution)/shard_map/reduce_scatter | solution.py:65
  153.1 1.1 slice_bitcast_fusion
  154.5 0.3 fusion.23
  155.2 0.3 fusion.22
  156.5 15.3 %all_gather.9 = f32[3,4096]{0,1:T(8,128)S(1)} all-gather(f32[3,1024]{0,1:T(8,128)S(1)} %copy.123), channel_id=1, replica_groups=mesh['groups'=2,'pts'=4,'cam'=4] {'cam'}, dimensions={1}, use_global_device_ids=true | all-gather | bytes 61440 | tf_op jit(solution)/shard_map/all_gather | solution.py:82
  171.9 14.1 %gather_fusion.1 = f32[4096,3]{1,0:T(8,128)} fusion(f32[3,4096]{0,1:T(8,128)S(1)} %all_gather.9, s32[4096]{0:T(1024)S(1)} %fusion.20), kind=kCustom, calls=%fused_computation.1 | custom fusion | bytes 114688 | tf_op jit(solution)/shard_map/gather | solution.py:83
  185.9 2.2 copy.220
  188.2 0.4 multiply_reduce_fusion.4
  188.6 0.6 copy.160
  189.3 22.5 %scatter_custom_fusion.3 = f32[512,9]{1,0:T(8,128)S(1)} fusion(s32[4096]{0:T(1024)} %param.9, f32[4096,9]{1,0:T(8,128)S(1)} %copy.160, f32[]{:T(128)} %constant.6.clone.1), kind=kCustom, calls=%fused_computation.34 | custom fusion | flops 36864 | bytes 18944 | tf_op jit(solution)/shard_map/scatter-add | solution.py:13
  211.9 19.0 %psum.72 = f32[9,512]{1,0:T(8,128)S(1)} all-reduce(f32[9,512]{1,0:T(8,128)S(1)} %bitcast.123), channel_id=1, replica_groups=mesh['groups'=2,'pts'=4,'cam'=4] {'pts'}, use_global_device_ids=true, to_apply=%region_17.0 | all-reduce | flops 4608 | bytes 36864 | tf_op jit(solution)/shard_map/psum | solution.py:84
  231.0 0.6 multiply_reduce_fusion.20
  231.6 6.3 %all-reduce = (f32[]{:T(128)}, f32[]{:T(128)}) all-reduce(f32[]{:T(128)} %get-tuple-element.21, f32[]{:T(128)} %get-tuple-element.20), channel_id=1, replica_groups=mesh['groups'=2,'pts'=4,'cam'=4] {'cam'}, use_global_device_ids=true, to_apply=%region_4.0 | all-reduce | flops 2 | bytes 16 | tf_op jit(solution)/shard_map/psum | solution.py:56
  239.2 0.6 multiply_reduce_fusion.19
  239.8 7.1 %psum.74 = f32[]{:T(128)} all-reduce(f32[]{:T(128)} %get-tuple-element.26), channel_id=1, replica_groups=mesh['groups'=2,'pts'=4,'cam'=4] {'cam'}, use_global_device_ids=true, to_apply=%region_21.0 | all-reduce | flops 1 | bytes 8 | tf_op jit(solution)/shard_map/psum | solution.py:56
  248.4 10.8 %gather_fusion.2 = f32[4096,9]{1,0:T(8,128)S(1)} fusion(f32[9,512]{0,1:T(8,128)S(1)} %copy.125, s32[4096]{0:T(1024)S(1)} %fusion.19), kind=kCustom, calls=%fused_computation.2 | custom fusion | bytes 311296 | tf_op jit(solution)/shard_map/gather | solution.py:76
  259.2 0.6 copy.222
  260.1 0.6 copy.174
  260.8 23.8 %scatter_custom_fusion.4 = f32[4096,3]{1,0:T(8,128)} fusion(s32[4096]{0:T(1024)S(1)} %copy-done.5, f32[4096,3]{1,0:T(8,128)S(1)} %copy.174, f32[]{:T(128)} %constant.6.clone.1), kind=kCustom, calls=%fused_computation.16 | custom fusion | flops 12288 | bytes 49156 | tf_op jit(solution)/shard_map/scatter-add | solution.py:13
  284.6 28.9 %reduce-scatter.9.cloned.1.call-done = f32[3,1024]{0,1:T(8,128)} async-done(((f32[3,4096]{0,1:T(8,128)}), f32[3,1024]{0,1:T(8,128)}) %reduce-scatter.9.cloned.1.call-update) | async-done | bytes 12304 | tf_op jit(solution)/shard_map/reduce_scatter | solution.py:80
  313.5 1.2 copy.126
  314.8 0.2 copy.127
  315.0 15.1 %all_gather.10 = f32[3,4096]{0,1:T(8,128)S(1)} all-gather(f32[3,1024]{0,1:T(8,128)S(1)} %copy.127), channel_id=1, replica_groups=mesh['groups'=2,'pts'=4,'cam'=4] {'cam'}, dimensions={1}, use_global_device_ids=true | all-gather | bytes 61440 | tf_op jit(solution)/shard_map/all_gather | solution.py:82
  330.1 14.1 %gather_fusion.3 = f32[4096,3]{1,0:T(8,128)} fusion(f32[3,4096]{0,1:T(8,128)S(1)} %all_gather.10, s32[4096]{0:T(1024)S(1)} %fusion.20), kind=kCustom, calls=%fused_computation.3 | custom fusion | bytes 114688 | tf_op jit(solution)/shard_map/gather | solution.py:83
  344.2 2.2 copy.225
  346.5 0.4 multiply_reduce_fusion.2
  346.9 0.6 copy.188
  347.6 22.5 %scatter_custom_fusion.5 = f32[512,9]{1,0:T(8,128)S(1)} fusion(s32[4096]{0:T(1024)} %param.9, f32[4096,9]{1,0:T(8,128)S(1)} %copy.188, f32[]{:T(128)} %constant.6.clone.1), kind=kCustom, calls=%fused_computation.32 | custom fusion | flops 36864 | bytes 18944 | tf_op jit(solution)/shard_map/scatter-add | solution.py:13
  370.2 19.0 %psum.75 = f32[9,512]{1,0:T(8,128)S(1)} all-reduce(f32[9,512]{1,0:T(8,128)S(1)} %bitcast.124), channel_id=1, replica_groups=mesh['groups'=2,'pts'=4,'cam'=4] {'pts'}, use_global_device_ids=true, to_apply=%region_26.0 | all-reduce | flops 4608 | bytes 36864 | tf_op jit(solution)/shard_map/psum | solution.py:84
  389.2 0.6 multiply_reduce_fusion.18
  389.8 6.3 %psum.76 = f32[]{:T(128)} all-reduce(f32[]{:T(128)} %multiply_reduce_fusion.18), channel_id=1, replica_groups=mesh['groups'=2,'pts'=4,'cam'=4] {'cam'}, use_global_device_ids=true, to_apply=%region_28.0 | all-reduce | flops 1 | bytes 8 | tf_op jit(solution)/shard_map/psum | solution.py:87
  397.4 0.6 multiply_reduce_fusion.17
  398.1 7.3 %psum.77 = f32[]{:T(128)} all-reduce(f32[]{:T(128)} %get-tuple-element.24), channel_id=1, replica_groups=mesh['groups'=2,'pts'=4,'cam'=4] {'cam'}, use_global_device_ids=true, to_apply=%region_30.0 | all-reduce | flops 1 | bytes 8 | tf_op jit(solution)/shard_map/psum | solution.py:56
  406.9 10.8 %gather_fusion.4 = f32[4096,9]{1,0:T(8,128)S(1)} fusion(f32[9,512]{0,1:T(8,128)S(1)} %copy.129, s32[4096]{0:T(1024)S(1)} %fusion.19), kind=kCustom, calls=%fused_computation.4 | custom fusion | bytes 311296 | tf_op jit(solution)/shard_map/gather | solution.py:76
  417.7 0.6 copy.227
  418.6 0.6 copy.202
  419.3 23.8 %scatter_custom_fusion.6 = f32[4096,3]{1,0:T(8,128)} fusion(s32[4096]{0:T(1024)S(1)} %copy-done.5, f32[4096,3]{1,0:T(8,128)S(1)} %copy.202, f32[]{:T(128)} %constant.6.clone.1), kind=kCustom, calls=%fused_computation.14 | custom fusion | flops 12288 | bytes 49156 | tf_op jit(solution)/shard_map/scatter-add | solution.py:13
  443.1 28.9 %reduce-scatter.11.cloned.1.call-done = f32[3,1024]{0,1:T(8,128)} async-done(((f32[3,4096]{0,1:T(8,128)}), f32[3,1024]{0,1:T(8,128)}) %reduce-scatter.11.cloned.1.call-update) | async-done | bytes 12304 | tf_op jit(solution)/shard_map/reduce_scatter | solution.py:80
  472.0 1.2 copy.130
  473.3 0.2 copy.131
  473.5 15.2 %all_gather.11 = f32[3,4096]{0,1:T(8,128)S(1)} all-gather(f32[3,1024]{0,1:T(8,128)S(1)} %copy.131), channel_id=1, replica_groups=mesh['groups'=2,'pts'=4,'cam'=4] {'cam'}, dimensions={1}, use_global_device_ids=true | all-gather | bytes 61440 | tf_op jit(solution)/shard_map/all_gather | solution.py:82
  488.7 14.1 %gather_fusion.5 = f32[4096,3]{1,0:T(8,128)} fusion(f32[3,4096]{0,1:T(8,128)S(1)} %all_gather.11, s32[4096]{0:T(1024)S(1)} %fusion.20), kind=kCustom, calls=%fused_computation.5 | custom fusion | bytes 114688 | tf_op jit(solution)/shard_map/gather | solution.py:83
  502.7 2.2 copy.230
  505.1 0.4 multiply_reduce_fusion
  505.5 0.6 copy.216
  506.1 22.5 %scatter_custom_fusion.7 = f32[512,9]{1,0:T(8,128)S(1)} fusion(s32[4096]{0:T(1024)} %param.9, f32[4096,9]{1,0:T(8,128)S(1)} %copy.216, f32[]{:T(128)} %constant.6.clone.1), kind=kCustom, calls=%fused_computation.30 | custom fusion | flops 36864 | bytes 18944 | tf_op jit(solution)/shard_map/scatter-add | solution.py:13
  528.8 19.0 %psum.78 = f32[9,512]{1,0:T(8,128)S(1)} all-reduce(f32[9,512]{1,0:T(8,128)S(1)} %bitcast.125), channel_id=1, replica_groups=mesh['groups'=2,'pts'=4,'cam'=4] {'pts'}, use_global_device_ids=true, to_apply=%region_35.0 | all-reduce | flops 4608 | bytes 36864 | tf_op jit(solution)/shard_map/psum | solution.py:84
  547.8 0.6 multiply_reduce_fusion.16
  548.4 6.3 %psum.79 = f32[]{:T(128)} all-reduce(f32[]{:T(128)} %multiply_reduce_fusion.16), channel_id=1, replica_groups=mesh['groups'=2,'pts'=4,'cam'=4] {'cam'}, use_global_device_ids=true, to_apply=%region_37.0 | all-reduce | flops 1 | bytes 8 | tf_op jit(solution)/shard_map/psum | solution.py:87
  556.0 0.6 multiply_subtract_fusion
  (63 shorter events, 4.1 us)
Async XLA Ops:
  7.2 46.3 %copy-start.4 = (f32[512]{0:T(512)S(1)}, f32[512]{0:T(512)}, u32[]{:S(2)}) copy-start(f32[512]{0:T(512)} %param.12) | copy-start | bytes 6148
  7.2 46.3 %copy-start.3 = (f32[9,512]{1,0:T(8,128)S(1)}, f32[9,512]{1,0:T(8,128)}, u32[]{:S(2)}) copy-start(f32[9,512]{1,0:T(8,128)} %param.13) | copy-start | bytes 55300
  7.2 112.2 %reduce-scatter.7.cloned.1.call-start = ((), (), s32[]{:S(2)}) async-start(), calls=%async_computation.5 | async-start | bytes 2621440 | tf_op jit(solution)/shard_map/reduce_scatter | solution.py:80
  53.6 11.4 %copy-start = (f32[2,9,4096]{2,0,1:T(2,128)S(1)}, f32[2,9,4096]{2,0,1:T(2,128)}, u32[]{:S(2)}) copy-start(f32[2,9,4096]{2,0,1:T(2,128)} %param.7) | copy-start | bytes 884740
  53.6 11.6 %copy-start.2 = (f32[2,3,4096]{2,0,1:T(2,128)S(1)}, f32[2,3,4096]{2,0,1:T(2,128)}, u32[]{:S(2)}) copy-start(f32[2,3,4096]{2,0,1:T(2,128)} %param.8) | copy-start | bytes 294916
  64.4 1.6 copy-start.5
  89.9 63.3 %reduce-scatter.5.cloned.1.call-start = ((), (), s32[]{:S(2)}) async-start(), calls=%async_computation.4 | async-start | bytes 2621440 | tf_op jit(solution)/shard_map/reduce_scatter | solution.py:65
  114.7 198.8 %reduce-scatter.9.cloned.1.call-start = ((), (), s32[]{:S(2)}) async-start(), calls=%async_computation.6 | async-start | bytes 2621440 | tf_op jit(solution)/shard_map/reduce_scatter | solution.py:80
  153.1 1.3 copy-start.1
  154.8 1.2 dynamic-slice-start
  284.6 187.4 %reduce-scatter.11.cloned.1.call-start = ((), (), s32[]{:S(2)}) async-start(), calls=%async_computation.7 | async-start | bytes 2621440 | tf_op jit(solution)/shard_map/reduce_scatter | solution.py:80
Sparse Core Ops, SparseCore 0:
  90.0 29.3 reduce-scatter.6
  121.9 31.1 reduce-scatter.4
  284.7 28.7 reduce-scatter.8
  443.2 28.7 reduce-scatter.10
where the time goes:
time: 564 us; the launch traced here: 563 us
  other arithmetic  194 us (34%)
  blocking collectives  157 us (28%)
  local copies, waits for them, and re-layouts  96.3 us (17%)
  waiting for transfers between devices  95 us (17%)
  between operations  21 us (4%)
    scatter-add x8, other arithmetic, segsum(): return jax.ops.segment_sum(terms.T, index, num_segments=count).T  185 us
    reduce_scatter x3, waiting for transfers between devices, on_device(): lax.psum_scatter(reduced_u_part, 'cam', scatter_dimension=1, tiled=True)  62.4 us
    psum x3, blocking collectives, on_device(): lax.psum(segsum(jnp.einsum('rko,ro->ko', cam_jac, z, precision=HI), obs_c...  57 us
    all_gather x3, blocking collectives, on_device(): w = lax.all_gather(w_share, 'cam', axis=1, tiled=True)  45.6 us
    gather x3, local copies, waits for them, and re-layouts, on_device(): z = y - jnp.einsum('rao,ao->ro', point_jac, w[:, obs_point], precision=HI)  42.2 us
    reduce_scatter x1, waiting for transfers between devices, on_device(): lax.psum_scatter(six_terms, 'cam', scatter_dimension=1, tiled=True)  32.5 us
    gather x3, local copies, waits for them, and re-layouts, on_device(): y = jnp.einsum('rko,ko->ro', cam_jac, direction[:, obs_cam], precision=HI)  32.3 us
    psum x1, blocking collectives, on_device(): cam_diag = lax.psum(diag_terms, 'pts') + cam_damp[None, :]  20.8 us
  transfers between devices with their start and end apart: 4, of which 4 were waited for; matrix products, arithmetic and copies ran while one was open for 5% of the time, Pallas kernels for 0%

commit v1 on v0

--- a/solution.py
+++ b/solution.py
@@ -5,12 +5,57 @@
 
 ITERS = 3
 
-
-HI = lax.Precision.HIGHEST
+BF = jnp.bfloat16
+F32 = jnp.float32
 
 
-def segsum(terms, index, count):
-    return jax.ops.segment_sum(terms.T, index, num_segments=count).T
+def split_of(count):
+    lo = 1 << (max(count.bit_length() - 1, 0) // 2)
+    while count % lo:
+        lo //= 2
+    return count // lo, lo
+
+
+def pieces(value):
+    first = lax.reduce_precision(value, exponent_bits=8, mantissa_bits=7)
+    rest = value - first
+    second = lax.reduce_precision(rest, exponent_bits=8, mantissa_bits=7)
+    third = rest - second
+    return first.astype(BF), second.astype(BF), third.astype(BF)
+
+
+class Index:
+    def __init__(self, index, count):
+        self.count = count
+        self.hi, self.lo = split_of(count)
+        high = index // self.lo
+        low = index % self.lo
+        hot = (lax.broadcasted_iota(jnp.int32, (self.hi, index.shape[0]), 0) == high[None, :])
+        self.hot = hot.astype(BF)
+        self.hot3 = jnp.concatenate([self.hot] * 3, axis=1)
+        self.hot3t = jnp.concatenate([self.hot] * 3, axis=0)
+        self.low = lax.broadcasted_iota(jnp.int32, (self.lo, index.shape[0]), 0) == low[None, :]
+
+    def segsum(self, terms):
+        ncol = terms.shape[0]
+        parts = [
+            jnp.where(self.low[None], part[:, None, :], jnp.zeros((), BF)).reshape(ncol * self.lo, -1)
+            for part in pieces(terms)
+        ]
+        spread = jnp.concatenate(parts, axis=1)
+        out = lax.dot_general(
+            self.hot3, spread, (((1,), (1,)), ((), ())), preferred_element_type=F32
+        )
+        return out.reshape(self.hi, ncol, self.lo).transpose(1, 0, 2).reshape(ncol, self.count)
+
+    def gather(self, table):
+        ncol = table.shape[0]
+        mat = table.reshape(ncol, self.hi, self.lo).transpose(0, 2, 1).reshape(ncol * self.lo, self.hi)
+        stacked = jnp.concatenate(pieces(mat), axis=1)
+        spread = lax.dot_general(
+            stacked, self.hot3t, (((1,), (0,)), ((), ())), preferred_element_type=F32
+        ).reshape(ncol, self.lo, -1)
+        return jnp.sum(jnp.where(self.low[None], spread, 0.0), axis=1)
 
 
 def invert3(mat):
@@ -59,13 +104,15 @@
 def on_device(cam_jac, point_jac, obs_cam, obs_point, point_damp, cam_damp, reduced_rhs):
     npts = point_damp.shape[0]
     ncam = reduced_rhs.shape[1]
-    six_terms = segsum(normal_six(point_jac), obs_point, npts)
+    by_point = Index(obs_point, npts)
+    by_cam = Index(obs_cam, ncam)
+    six_terms = by_point.segsum(normal_six(point_jac))
     pshare = npts // lax.axis_size("cam")
     pstart = lax.axis_index("cam") * pshare
     six_share = lax.psum_scatter(six_terms, "cam", scatter_dimension=1, tiled=True)
     damp_pts = lax.dynamic_slice_in_dim(point_damp, pstart, pshare, 0)
     inv_share = point_inverse(six_share, damp_pts)
-    diag_terms = segsum(jnp.sum(cam_jac * cam_jac, axis=0), obs_cam, ncam)
+    diag_terms = by_cam.segsum(jnp.sum(cam_jac * cam_jac, axis=0))
     cam_diag = lax.psum(diag_terms, "pts") + cam_damp[None, :]
     solution = jnp.zeros_like(reduced_rhs)
     residual = reduced_rhs
@@ -73,16 +120,15 @@
     direction = pre
     rz = norm_sum(jnp.sum(residual * pre))
     for step in range(ITERS):
-        y = jnp.einsum("rko,ko->ro", cam_jac, direction[:, obs_cam], precision=HI)
-        reduced_u_part = segsum(
-            jnp.einsum("rao,ro->ao", point_jac, y, precision=HI), obs_point, npts
-        )
+        dir_obs = by_cam.gather(direction)
+        y = jnp.sum(cam_jac * dir_obs[None], axis=1)
+        reduced_u_part = by_point.segsum(jnp.sum(point_jac * y[:, None, :], axis=0))
         u_share = lax.psum_scatter(reduced_u_part, "cam", scatter_dimension=1, tiled=True)
         w_share = jnp.sum(inv_share * u_share[None, :, :], axis=1)
         w = lax.all_gather(w_share, "cam", axis=1, tiled=True)
-        z = y - jnp.einsum("rao,ao->ro", point_jac, w[:, obs_point], precision=HI)
+        z = y - jnp.sum(point_jac * by_point.gather(w)[None], axis=1)
         image = cam_damp[None, :] * direction + lax.psum(
-            segsum(jnp.einsum("rko,ro->ko", cam_jac, z, precision=HI), obs_cam, ncam), "pts"
+            by_cam.segsum(jnp.sum(cam_jac * z[:, None, :], axis=0)), "pts"
         )
         alpha = rz / lax.psum(jnp.sum(direction * image), "cam")
         solution = solution + alpha * direction

time: 564 us -> 302 us (0.54)
  other arithmetic: 194 us -> 16.9 us
  local copies, waits for them, and re-layouts: 96.3 us -> 19.2 us
  blocking collectives: 157 us -> 126 us
  matrix products: 0 us -> 15 us
  waiting for transfers between devices: 95 us -> 102 us
    scatter-add x8 -> x0, other arithmetic: 185 us -> none  [segsum(): return jax.ops.segment_sum(terms.T, index, num_segments=count).T]
    unnamed x4 -> x7, waiting for transfers between devices: 0.07 us -> 81.6 us
    gather x6 -> x0, local copies, waits for them, and re-layouts: 74.6 us -> none  [the longest x3 42.2 us: on_device(): z = y - jnp.einsum('rao,ao->ro', point_jac, w[:, obs_point], precision=HI)]
    reduce_scatter x3 -> x0, waiting for transfers between devices: 62.4 us -> none  [on_device(): lax.psum_scatter(reduced_u_part, 'cam', scatter_dimension=1, tiled=True)]
    all_gather x3, blocking collectives: 45.6 us -> 15.9 us  [on_device(): w = lax.all_gather(w_share, 'cam', axis=1, tiled=True)]
    dot_general x0 -> x14, matrix products: none -> 15 us  [the longest x8 11.6 us: segsum(): lax.dot_general(self.hot3, spread, (((1,), (1,)), ((), ())), preferred_el...]
    reduce_scatter x1, waiting for transfers between devices: 32.5 us -> 20.9 us  [on_device(): lax.psum_scatter(six_terms, 'cam', scatter_dimension=1, tiled=True)]
    unnamed x18 -> x14, local copies, waits for them, and re-layouts: 8.52 us -> 13 us
  transfers between devices with their start and end apart: 4 -> 4, of which waited for: 4 -> 4; matrix products, arithmetic and copies ran while one was open for 5% -> 2% of each run, Pallas kernels for 0% -> 0%
where the time goes in v1:
time: 302 us; the launch traced here: 301 us
  blocking collectives  126 us (42%)
  waiting for transfers between devices  102 us (34%)
  between operations  21.1 us (7%)
  local copies, waits for them, and re-layouts  19.2 us (6%)
  other arithmetic  16.9 us (6%)
  matrix products  15 us (5%)
    unnamed x7, waiting for transfers between devices  81.6 us
    psum x3, blocking collectives, on_device(): lax.psum(by_cam.segsum(jnp.sum(cam_jac * z[:, None, :], axis=0)), 'pts')  56.9 us
    reduce_scatter x1, waiting for transfers between devices, on_device(): lax.psum_scatter(six_terms, 'cam', scatter_dimension=1, tiled=True)  20.9 us
    psum x1, blocking collectives, on_device(): cam_diag = lax.psum(diag_terms, 'pts') + cam_damp[None, :]  20.9 us
    psum x3, blocking collectives, norm_sum(): return lax.psum(value, 'cam')  19.5 us
    all_gather x3, blocking collectives, on_device(): w = lax.all_gather(w_share, 'cam', axis=1, tiled=True)  15.9 us
    psum x2, blocking collectives, on_device(): alpha = rz / lax.psum(jnp.sum(direction * image), 'cam')  13.1 us
    unnamed x14, local copies, waits for them, and re-layouts  13 us
  transfers between devices with their start and end apart: 4, of which 4 were waited for; matrix products, arithmetic and copies ran while one was open for 2% of the time, Pallas kernels for 0%

profile of v1, /device:TPU:0, one launch (start us, length us, event | category | flops | bytes accessed | tf_op | source)
XLA Modules:
  0.0 301.3 jit_solution(13803809787770061255)
XLA Ops:
  7.2 0.7 add_select_fusion.1
  7.9 0.7 add_select_fusion.3
  8.7 1.4 multiply_reduce_fusion.6
  10.2 0.4 broadcast_select_fusion.23
  10.6 1.1 fusion.24
  12.0 20.9 %psum.70 = f32[9,512]{1,0:T(8,128)S(1)} all-reduce(f32[9,512]{1,0:T(8,128)S(1)} %reshape.948), channel_id=1, replica_groups=mesh['groups'=2,'pts'=4,'cam'=4] {'pts'}, use_global_device_ids=true, to_apply=%region_1.2 | all-reduce | flops 4608 | bytes 36864 | tf_op jit(solution)/shard_map/psum | solution.py:116
  33.1 0.5 fusion.55
  33.7 0.5 select_reduce_fusion.5
  34.1 0.5 copy-done
  35.2 0.4 broadcast_select_fusion.11
  35.6 1.4 fusion.6
  37.1 2.9 copy.107
  40.5 0.9 broadcast_select_fusion.2
  41.4 3.0 %fusion = f32[64,384]{1,0:T(8,128)S(1)} fusion(bf16[384,4096]{1,0:T(8,128)(2,1)S(1)} %bitcast.157, bf16[384,4096]{1,0:T(8,128)(2,1)S(1)} %bitcast.156, bf16[384,4096]{1,0:T(8,128)(2,1)S(1)} %bitcast.155, bf16[64,4096]{1,0:T(8,128)(2,1)S(1)} %get-tuple-element.105), kind=kOutput, calls=%fused_computation | convolution fusion | flops 637009920 | bytes 10059776 | tf_op jit(solution)/shard_map/dot_general | solution.py:46
  44.6 0.7 reshape.953
  45.4 0.7 dynamic_slice.3
  46.2 23.4 %reduce-scatter.13.cloned.1.call-done = f32[1024,3]{1,0:T(8,128)} async-done(((f32[4096,3]{1,0:T(8,128)}), f32[1024,3]{1,0:T(8,128)}) %reduce-scatter.13.cloned.1.call-update) | async-done | bytes 12304
  69.5 1.2 copy.102
  70.8 20.9 %reduce-scatter.11.cloned.1.call-done = f32[6,1024]{1,0:T(8,128)} async-done(((f32[6,4096]{1,0:T(8,128)}), f32[6,1024]{1,0:T(8,128)}) %reduce-scatter.11.cloned.1.call-update) | async-done | bytes 24592 | tf_op jit(solution)/shard_map/reduce_scatter | solution.py:112
  91.6 0.8 fusion.120
  92.5 0.8 fusion.119
  93.4 0.8 slice_bitcast_fusion
  94.4 5.4 %all_gather.9 = f32[3,4096]{1,0:T(4,128)S(1)} all-gather(f32[3,1024]{1,0:T(4,128)S(1)} %get-tuple-element.16), channel_id=1, replica_groups=mesh['groups'=2,'pts'=4,'cam'=4] {'cam'}, dimensions={1}, use_global_device_ids=true | all-gather | bytes 61440 | tf_op jit(solution)/shard_map/all_gather | solution.py:128
  100.1 0.6 fusion.51
  100.7 0.4 select_reduce_fusion.2
  101.7 0.4 broadcast_select_fusion.20
  102.1 1.1 fusion.30
  103.4 19.0 %psum.72 = f32[9,512]{1,0:T(8,128)S(1)} all-reduce(f32[9,512]{1,0:T(8,128)S(1)} %reshape.960), channel_id=1, replica_groups=mesh['groups'=2,'pts'=4,'cam'=4] {'pts'}, use_global_device_ids=true, to_apply=%region_19.20 | all-reduce | flops 4608 | bytes 36864 | tf_op jit(solution)/shard_map/psum | solution.py:130
  122.4 0.6 multiply_reduce_fusion.20
  123.0 6.6 %all-reduce = (f32[]{:T(128)}, f32[]{:T(128)}) all-reduce(f32[]{:T(128)} %get-tuple-element.9, f32[]{:T(128)} %get-tuple-element.8), channel_id=1, replica_groups=mesh['groups'=2,'pts'=4,'cam'=4] {'cam'}, use_global_device_ids=true, to_apply=%region_3.4 | all-reduce | flops 2 | bytes 16 | tf_op jit(solution)/shard_map/psum | solution.py:101
  131.0 0.6 multiply_reduce_fusion.19
  131.6 6.4 %psum.74 = f32[]{:T(128)} all-reduce(f32[]{:T(128)} %get-tuple-element.14), channel_id=1, replica_groups=mesh['groups'=2,'pts'=4,'cam'=4] {'cam'}, use_global_device_ids=true, to_apply=%region_23.24 | all-reduce | flops 1 | bytes 8 | tf_op jit(solution)/shard_map/psum | solution.py:101
  139.5 0.5 fusion.54
  140.1 0.4 select_reduce_fusion.4
  140.9 0.4 broadcast_select_fusion.8
  141.3 1.4 fusion.12
  142.8 2.9 copy.108
  145.8 29.0 %reduce-scatter.15.cloned.1.call-done = f32[1024,3]{1,0:T(8,128)} async-done(((f32[4096,3]{1,0:T(8,128)}), f32[1024,3]{1,0:T(8,128)}) %reduce-scatter.15.cloned.1.call-update) | async-done | bytes 12304
  174.8 1.2 copy.104
  176.1 5.2 %all_gather.10 = f32[3,4096]{1,0:T(4,128)S(1)} all-gather(f32[3,1024]{1,0:T(4,128)S(1)} %multiply_reduce_fusion.14), channel_id=1, replica_groups=mesh['groups'=2,'pts'=4,'cam'=4] {'cam'}, dimensions={1}, use_global_device_ids=true | all-gather | bytes 61440 | tf_op jit(solution)/shard_map/all_gather | solution.py:128
  181.6 0.6 fusion.50
  182.2 0.4 select_reduce_fusion.1
  183.1 0.4 broadcast_select_fusion.17
  183.6 1.1 fusion.36
  184.9 19.0 %psum.75 = f32[9,512]{1,0:T(8,128)S(1)} all-reduce(f32[9,512]{1,0:T(8,128)S(1)} %reshape.970), channel_id=1, replica_groups=mesh['groups'=2,'pts'=4,'cam'=4] {'pts'}, use_global_device_ids=true, to_apply=%region_32.33 | all-reduce | flops 4608 | bytes 36864 | tf_op jit(solution)/shard_map/psum | solution.py:130
  203.9 0.6 multiply_reduce_fusion.18
  204.5 6.6 %psum.76 = f32[]{:T(128)} all-reduce(f32[]{:T(128)} %multiply_reduce_fusion.18), channel_id=1, replica_groups=mesh['groups'=2,'pts'=4,'cam'=4] {'cam'}, use_global_device_ids=true, to_apply=%region_34.35 | all-reduce | flops 1 | bytes 8 | tf_op jit(solution)/shard_map/psum | solution.py:133
  212.4 0.6 multiply_reduce_fusion.17
  213.0 6.6 %psum.77 = f32[]{:T(128)} all-reduce(f32[]{:T(128)} %get-tuple-element.12), channel_id=1, replica_groups=mesh['groups'=2,'pts'=4,'cam'=4] {'cam'}, use_global_device_ids=true, to_apply=%region_36.37 | all-reduce | flops 1 | bytes 8 | tf_op jit(solution)/shard_map/psum | solution.py:101
  221.2 0.5 fusion.53
  221.7 0.4 select_reduce_fusion.3
  222.5 0.4 broadcast_select_fusion.5
  223.0 1.4 fusion.18
  224.4 2.9 copy.109
  227.4 29.1 %reduce-scatter.17.cloned.1.call-done = f32[1024,3]{1,0:T(8,128)} async-done(((f32[4096,3]{1,0:T(8,128)}), f32[1024,3]{1,0:T(8,128)}) %reduce-scatter.17.cloned.1.call-update) | async-done | bytes 12304
  256.5 1.2 copy.106
  257.8 5.2 %all_gather.11 = f32[3,4096]{1,0:T(4,128)S(1)} all-gather(f32[3,1024]{1,0:T(4,128)S(1)} %multiply_reduce_fusion.13), channel_id=1, replica_groups=mesh['groups'=2,'pts'=4,'cam'=4] {'cam'}, dimensions={1}, use_global_device_ids=true | all-gather | bytes 61440 | tf_op jit(solution)/shard_map/all_gather | solution.py:128
  263.3 0.6 fusion.49
  264.9 0.4 broadcast_select_fusion.14
  265.3 1.1 fusion.42
  266.6 19.0 %psum.78 = f32[9,512]{1,0:T(8,128)S(1)} all-reduce(f32[9,512]{1,0:T(8,128)S(1)} %reshape.980), channel_id=1, replica_groups=mesh['groups'=2,'pts'=4,'cam'=4] {'pts'}, use_global_device_ids=true, to_apply=%region_45.46 | all-reduce | flops 4608 | bytes 36864 | tf_op jit(solution)/shard_map/psum | solution.py:130
  285.6 0.6 multiply_reduce_fusion.16
  286.2 6.6 %psum.79 = f32[]{:T(128)} all-reduce(f32[]{:T(128)} %multiply_reduce_fusion.16), channel_id=1, replica_groups=mesh['groups'=2,'pts'=4,'cam'=4] {'cam'}, use_global_device_ids=true, to_apply=%region_47.48 | all-reduce | flops 1 | bytes 8 | tf_op jit(solution)/shard_map/psum | solution.py:133
  294.1 0.6 multiply_subtract_fusion
  (87 shorter events, 6.9 us)
Async XLA Ops:
  7.2 62.4 %reduce-scatter.13.cloned.1.call-start = ((), (), s32[]{:S(2)}) async-start(), calls=%async_computation.5 | async-start | bytes 2621440
  10.6 22.2 %copy-start.2 = (f32[9,512]{1,0:T(8,128)S(1)}, f32[9,512]{1,0:T(8,128)}, u32[]{:S(2)}) copy-start(f32[9,512]{1,0:T(8,128)} %param.13) | copy-start | bytes 55300
  10.6 22.2 %copy-start.3 = (f32[512]{0:T(512)S(1)}, f32[512]{0:T(512)}, u32[]{:S(2)}) copy-start(f32[512]{0:T(512)} %param.12) | copy-start | bytes 6148
  33.6 1.0 copy-start
  33.7 1.1 copy-start.1
  40.0 51.6 %reduce-scatter.11.cloned.1.call-start = ((), (), s32[]{:S(2)}) async-start(), calls=%async_computation.4 | async-start | bytes 163840 | tf_op jit(solution)/shard_map/reduce_scatter | solution.py:112
  45.4 129.4 %reduce-scatter.15.cloned.1.call-start = ((), (), s32[]{:S(2)}) async-start(), calls=%async_computation.6 | async-start | bytes 2621440
  145.7 110.8 %reduce-scatter.17.cloned.1.call-start = ((), (), s32[]{:S(2)}) async-start(), calls=%async_computation.7 | async-start | bytes 2621440
Sparse Core Ops, SparseCore 0:
  40.2 29.3 reduce-scatter.12
  72.0 19.6 reduce-scatter.10
  145.8 28.8 reduce-scatter.14
  227.5 28.9 reduce-scatter.16

commit v2 on v1

--- a/solution.py
+++ b/solution.py
@@ -97,8 +97,22 @@
     return invert3(mat)
 
 
+SIZES = {}
+
+
+def allsum(value, axis):
+    size = SIZES[axis]
+    if size & (size - 1):
+        return lax.psum(value, axis)
+    step = 1
+    while step < size:
+        value = value + lax.ppermute(value, axis, [(i, i ^ step) for i in range(size)])
+        step *= 2
+    return value
+
+
 def norm_sum(value):
-    return lax.psum(value, "cam")
+    return allsum(value, "cam")
 
 
 def on_device(cam_jac, point_jac, obs_cam, obs_point, point_damp, cam_damp, reduced_rhs):
@@ -106,14 +120,10 @@
     ncam = reduced_rhs.shape[1]
     by_point = Index(obs_point, npts)
     by_cam = Index(obs_cam, ncam)
-    six_terms = by_point.segsum(normal_six(point_jac))
-    pshare = npts // lax.axis_size("cam")
-    pstart = lax.axis_index("cam") * pshare
-    six_share = lax.psum_scatter(six_terms, "cam", scatter_dimension=1, tiled=True)
-    damp_pts = lax.dynamic_slice_in_dim(point_damp, pstart, pshare, 0)
-    inv_share = point_inverse(six_share, damp_pts)
+    six_terms = allsum(by_point.segsum(normal_six(point_jac)), "cam")
+    inv = point_inverse(six_terms, point_damp)
     diag_terms = by_cam.segsum(jnp.sum(cam_jac * cam_jac, axis=0))
-    cam_diag = lax.psum(diag_terms, "pts") + cam_damp[None, :]
+    cam_diag = allsum(diag_terms, "pts") + cam_damp[None, :]
     solution = jnp.zeros_like(reduced_rhs)
     residual = reduced_rhs
     pre = residual / cam_diag
@@ -122,15 +132,13 @@
     for step in range(ITERS):
         dir_obs = by_cam.gather(direction)
         y = jnp.sum(cam_jac * dir_obs[None], axis=1)
-        reduced_u_part = by_point.segsum(jnp.sum(point_jac * y[:, None, :], axis=0))
-        u_share = lax.psum_scatter(reduced_u_part, "cam", scatter_dimension=1, tiled=True)
-        w_share = jnp.sum(inv_share * u_share[None, :, :], axis=1)
-        w = lax.all_gather(w_share, "cam", axis=1, tiled=True)
+        u = allsum(by_point.segsum(jnp.sum(point_jac * y[:, None, :], axis=0)), "cam")
+        w = jnp.sum(inv * u[None, :, :], axis=1)
         z = y - jnp.sum(point_jac * by_point.gather(w)[None], axis=1)
-        image = cam_damp[None, :] * direction + lax.psum(
+        image = cam_damp[None, :] * direction + allsum(
             by_cam.segsum(jnp.sum(cam_jac * z[:, None, :], axis=0)), "pts"
         )
-        alpha = rz / lax.psum(jnp.sum(direction * image), "cam")
+        alpha = rz / allsum(jnp.sum(direction * image), "cam")
         solution = solution + alpha * direction
         residual = residual - alpha * image
         pre = residual / cam_diag
@@ -141,6 +149,7 @@
 
 
 def solution(mesh):
+    SIZES.update(mesh.shape)
     return jax.shard_map(
         on_device,
         mesh=mesh,

time: 302 us -> 130 us (0.43)
  blocking collectives: 126 us -> 0 us
  waiting for transfers between devices: 102 us -> 48 us
  starting transfers between devices: 0.16 us -> 31.8 us
  local copies, waits for them, and re-layouts: 19.2 us -> 3.64 us
  between operations: 21.1 us -> 13.6 us
    psum x9 -> x0, blocking collectives: 110 us -> none  [the longest x3 56.9 us: on_device(): lax.psum(by_cam.segsum(jnp.sum(cam_jac * z[:, None, :], axis=0)), 'pts')]
    unnamed x7 -> x0, waiting for transfers between devices: 81.6 us -> none
    ppermute x0 -> x28, waiting for transfers between devices: none -> 48 us  [allsum(): lax.ppermute(value, axis, [(i, i ^ step) for i in range(size)])]
    ppermute x0 -> x28, starting transfers between devices: none -> 31.8 us  [allsum(): lax.ppermute(value, axis, [(i, i ^ step) for i in range(size)])]
    reduce_scatter x1 -> x0, waiting for transfers between devices: 20.9 us -> none  [on_device(): lax.psum_scatter(six_terms, 'cam', scatter_dimension=1, tiled=True)]
    all_gather x3 -> x0, blocking collectives: 15.9 us -> none  [on_device(): w = lax.all_gather(w_share, 'cam', axis=1, tiled=True)]
    unnamed x14 -> x12, local copies, waits for them, and re-layouts: 13 us -> 0.52 us
  transfers between devices with their start and end apart: 4 -> 28, of which waited for: 4 -> 24; matrix products, arithmetic and copies ran while one was open for 2% -> 7% of each run, Pallas kernels for 0% -> 0%
where the time goes in v2:
time: 130 us; the launch traced here: 129 us
  waiting for transfers between devices  48 us (37%)
  starting transfers between devices  31.8 us (24%)
  other arithmetic  17.2 us (13%)
  matrix products  14.9 us (11%)
  between operations  13.6 us (10%)
  local copies, waits for them, and re-layouts  3.64 us (3%)
    ppermute x28, waiting for transfers between devices, allsum(): lax.ppermute(value, axis, [(i, i ^ step) for i in range(size)])  48 us
    ppermute x28, starting transfers between devices, allsum(): lax.ppermute(value, axis, [(i, i ^ step) for i in range(size)])  31.8 us
    dot_general x8, matrix products, segsum(): lax.dot_general(self.hot3, spread, (((1,), (1,)), ((), ())), preferred_el...  11.5 us
    select_n x8, other arithmetic, segsum(): jnp.where(self.low[None], part[:, None, :], jnp.zeros((), BF))  4.05 us
    dot_general x6, matrix products, gather(): lax.dot_general(stacked, self.hot3t, (((1,), (0,)), ((), ())), preferred_...  3.4 us
    reduce_sum x6, other arithmetic, gather(): return jnp.sum(jnp.where(self.low[None], spread, 0.0), axis=1)  2.61 us
  transfers between devices with their start and end apart: 28, of which 24 were waited for; matrix products, arithmetic and copies ran while one was open for 7% of the time, Pallas kernels for 0%

profile of v2, /device:TPU:0, one launch (start us, length us, event | category | flops | bytes accessed | tf_op | source)
XLA Modules:
  0.0 129.1 jit_solution(977254847377583238)
XLA Ops:
  0.6 0.7 add_select_fusion.3
  1.4 1.4 %multiply_reduce_fusion.6 = f32[9,4096]{1,0:T(8,128)S(1)} fusion(f32[2,9,4096]{2,0,1:T(2,128)} %param.7), kind=kLoop, calls=%fused_computation.115 | loop fusion | flops 110592 | bytes 442368 | tf_op jit(solution)/shard_map/reduce_sum | solution.py:125
  3.3 1.1 fusion.24
  4.6 3.1 %collective-permute-start = (f32[9,512]{1,0:T(8,128)S(1)}, f32[9,512]{1,0:T(8,128)S(1)}, u32[]{:S(2)}, u32[]{:S(2)}) collective-permute-start(f32[9,512]{1,0:T(8,128)S(1)} %reshape.948), channel_id=1, source_target_pairs={{0,4},{4,0},{8,12},{12,8},{1,5},{5,1},{9,13},{13,9},{2,6},{6,2},{1... | collective-permute-start | bytes 55304 | tf_op jit(solution)/shard_map/ppermute | solution.py:109
  8.5 0.9 broadcast_select_fusion.2
  9.6 3.0 %collective-permute-start.1 = (f32[9,512]{1,0:T(8,128)S(1)}, f32[9,512]{1,0:T(8,128)S(1)}, u32[]{:S(2)}, u32[]{:S(2)}) collective-permute-start(f32[9,512]{1,0:T(8,128)S(1)} %add.137), channel_id=1, source_target_pairs={{0,8},{4,12},{8,0},{12,4},{1,9},{5,13},{9,1},{13,5},{2,10},{6,14},... | collective-permute-start | bytes 55304 | tf_op jit(solution)/shard_map/ppermute | solution.py:109
  12.7 3.0 %fusion = f32[64,384]{1,0:T(8,128)S(1)} fusion(bf16[384,4096]{1,0:T(8,128)(2,1)S(1)} %bitcast.142, bf16[384,4096]{1,0:T(8,128)(2,1)S(1)} %bitcast.141, bf16[384,4096]{1,0:T(8,128)(2,1)S(1)} %bitcast.140, bf16[64,4096]{1,0:T(8,128)(2,1)S(1)} %get-tuple-element.107), kind=kOutput, calls=%fused_computation | convolution fusion | flops 637009920 | bytes 10059776 | tf_op jit(solution)/shard_map/dot_general | solution.py:46
  16.3 0.5 fusion.55
  18.6 1.4 %fusion.6 = f32[64,192]{0,1:T(8,128)S(1)} fusion(bf16[192,4096]{1,0:T(8,128)(2,1)S(1)} %bitcast.145, bf16[192,4096]{1,0:T(8,128)(2,1)S(1)} %bitcast.144, bf16[192,4096]{1,0:T(8,128)(2,1)S(1)} %bitcast.143, bf16[64,4096]{1,0:T(8,128)(2,1)S(1)} %get-tuple-element.107), kind=kOutput, calls=%fused_computation.6 | convolution fusion | flops 320864256 | bytes 5292032 | tf_op jit(solution)/shard_map/dot_general | solution.py:46
  20.3 0.5 collective-permute-start.6
  20.8 0.9 collective-permute-done.6
  21.7 1.6 %collective-permute-start.7 = (f32[3,4096]{1,0:T(4,128)S(1)}, f32[3,4096]{1,0:T(4,128)S(1)}, u32[]{:S(2)}, u32[]{:S(2)}) collective-permute-start(f32[3,4096]{1,0:T(4,128)S(1)} %add.149), channel_id=1, source_target_pairs={{0,2},{1,3},{2,0},{3,1},{4,6},{5,7},{6,4},{7,5},{8,10},{9,11},{10,... | collective-permute-start | bytes 147464 | tf_op jit(solution)/shard_map/ppermute | solution.py:109
  23.3 0.6 collective-permute-start.5
  23.9 2.3 %collective-permute-done.7 = f32[3,4096]{1,0:T(4,128)S(1)} collective-permute-done((f32[3,4096]{1,0:T(4,128)S(1)}, f32[3,4096]{1,0:T(4,128)S(1)}, u32[]{:S(2)}, u32[]{:S(2)}) %collective-permute-start.7) | collective-permute-done | bytes 49184 | tf_op jit(solution)/shard_map/ppermute | solution.py:109
  26.3 2.7 %collective-permute-done.5 = f32[6,4096]{1,0:T(8,128)S(1)} collective-permute-done((f32[6,4096]{1,0:T(8,128)S(1)}, f32[6,4096]{1,0:T(8,128)S(1)}, u32[]{:S(2)}, u32[]{:S(2)}) %collective-permute-start.5) | collective-permute-done | bytes 98336 | tf_op jit(solution)/shard_map/ppermute | solution.py:109
  30.2 0.6 fusion.51
  31.8 0.6 broadcast_select_fusion.20
  32.3 1.1 fusion.30
  33.6 1.6 %collective-permute-start.8 = (f32[9,512]{1,0:T(8,128)S(1)}, f32[9,512]{1,0:T(8,128)S(1)}, u32[]{:S(2)}, u32[]{:S(2)}) collective-permute-start(f32[9,512]{1,0:T(8,128)S(1)} %reshape.960), channel_id=1, source_target_pairs={{0,4},{4,0},{8,12},{12,8},{1,5},{5,1},{9,13},{13,9},{2,6},{6,2},{1... | collective-permute-start | bytes 55304 | tf_op jit(solution)/shard_map/ppermute | solution.py:109
  35.3 2.3 %collective-permute-done.8 = f32[9,512]{1,0:T(8,128)S(1)} collective-permute-done((f32[9,512]{1,0:T(8,128)S(1)}, f32[9,512]{1,0:T(8,128)S(1)}, u32[]{:S(2)}, u32[]{:S(2)}) %collective-permute-start.8) | collective-permute-done | bytes 18464 | tf_op jit(solution)/shard_map/ppermute | solution.py:109
  37.6 1.3 collective-permute-start.9
  38.9 3.6 %collective-permute-done.9 = f32[9,512]{1,0:T(8,128)S(1)} collective-permute-done((f32[9,512]{1,0:T(8,128)S(1)}, f32[9,512]{1,0:T(8,128)S(1)}, u32[]{:S(2)}, u32[]{:S(2)}) %collective-permute-start.9) | collective-permute-done | bytes 18464 | tf_op jit(solution)/shard_map/ppermute | solution.py:109
  42.4 0.6 multiply_reduce_fusion.20
  43.6 0.9 collective-permute-done.10
  45.7 2.9 %collective-permute-start.11 = (f32[]{:T(128)}, f32[]{:T(128)}, u32[]{:S(2)}, u32[]{:S(2)}) collective-permute-start(f32[]{:T(128)} %add.154), channel_id=1, source_target_pairs={{0,2},{1,3},{2,0},{3,1},{4,6},{5,7},{6,4},{7,5},{8,10},{9,11},{10,... | collective-permute-start | bytes 20 | tf_op jit(solution)/shard_map/ppermute | solution.py:109
  49.9 1.9 %collective-permute-start.3 = (f32[]{:T(128)}, f32[]{:T(128)}, u32[]{:S(2)}, u32[]{:S(2)}) collective-permute-start(f32[]{:T(128)} %add.141), channel_id=1, source_target_pairs={{0,2},{1,3},{2,0},{3,1},{4,6},{5,7},{6,4},{7,5},{8,10},{9,11},{10,... | collective-permute-start | bytes 20 | tf_op jit(solution)/shard_map/ppermute | solution.py:109
  52.4 1.1 collective-permute-done.3
  54.2 0.6 multiply_reduce_fusion.19
  54.8 1.3 collective-permute-done.12
  57.5 1.9 %collective-permute-start.13 = (f32[]{:T(128)}, f32[]{:T(128)}, u32[]{:S(2)}, u32[]{:S(2)}) collective-permute-start(f32[]{:T(128)} %add.156), channel_id=1, source_target_pairs={{0,2},{1,3},{2,0},{3,1},{4,6},{5,7},{6,4},{7,5},{8,10},{9,11},{10,... | collective-permute-start | bytes 20 | tf_op jit(solution)/shard_map/ppermute | solution.py:109
  59.3 1.7 %collective-permute-done.13 = f32[]{:T(128)} collective-permute-done((f32[]{:T(128)}, f32[]{:T(128)}, u32[]{:S(2)}, u32[]{:S(2)}) %collective-permute-start.13) | collective-permute-done | bytes 36 | tf_op jit(solution)/shard_map/ppermute | solution.py:109
  63.8 1.4 %fusion.12 = f32[64,192]{0,1:T(8,128)S(1)} fusion(bf16[192,4096]{1,0:T(8,128)(2,1)S(1)} %bitcast.148, bf16[192,4096]{1,0:T(8,128)(2,1)S(1)} %bitcast.147, bf16[192,4096]{1,0:T(8,128)(2,1)S(1)} %bitcast.146, bf16[64,4096]{1,0:T(8,128)(2,1)S(1)} %get-tuple-element.107), kind=kOutput, calls=%fused_computation.12 | convolution fusion | flops 320864256 | bytes 5292032 | tf_op jit(solution)/shard_map/dot_general | solution.py:46
  65.5 1.2 collective-permute-done.14
  66.8 0.6 collective-permute-start.15
  67.4 3.7 %collective-permute-done.15 = f32[3,4096]{1,0:T(4,128)S(1)} collective-permute-done((f32[3,4096]{1,0:T(4,128)S(1)}, f32[3,4096]{1,0:T(4,128)S(1)}, u32[]{:S(2)}, u32[]{:S(2)}) %collective-permute-start.15) | collective-permute-done | bytes 49184 | tf_op jit(solution)/shard_map/ppermute | solution.py:109
  71.6 0.6 fusion.50
  73.6 1.1 fusion.36
  74.9 1.6 %collective-permute-start.16 = (f32[9,512]{1,0:T(8,128)S(1)}, f32[9,512]{1,0:T(8,128)S(1)}, u32[]{:S(2)}, u32[]{:S(2)}) collective-permute-start(f32[9,512]{1,0:T(8,128)S(1)} %reshape.970), channel_id=1, source_target_pairs={{0,4},{4,0},{8,12},{12,8},{1,5},{5,1},{9,13},{13,9},{2,6},{6,2},{1... | collective-permute-start | bytes 55304 | tf_op jit(solution)/shard_map/ppermute | solution.py:109
  76.5 2.3 %collective-permute-done.16 = f32[9,512]{1,0:T(8,128)S(1)} collective-permute-done((f32[9,512]{1,0:T(8,128)S(1)}, f32[9,512]{1,0:T(8,128)S(1)}, u32[]{:S(2)}, u32[]{:S(2)}) %collective-permute-start.16) | collective-permute-done | bytes 18464 | tf_op jit(solution)/shard_map/ppermute | solution.py:109
  78.9 1.1 collective-permute-start.17
  80.0 3.7 %collective-permute-done.17 = f32[9,512]{1,0:T(8,128)S(1)} collective-permute-done((f32[9,512]{1,0:T(8,128)S(1)}, f32[9,512]{1,0:T(8,128)S(1)}, u32[]{:S(2)}, u32[]{:S(2)}) %collective-permute-start.17) | collective-permute-done | bytes 18464 | tf_op jit(solution)/shard_map/ppermute | solution.py:109
  83.7 0.6 multiply_reduce_fusion.18
  84.3 1.3 collective-permute-done.18
  86.9 1.9 %collective-permute-start.19 = (f32[]{:T(128)}, f32[]{:T(128)}, u32[]{:S(2)}, u32[]{:S(2)}) collective-permute-start(f32[]{:T(128)} %add.164), channel_id=1, source_target_pairs={{0,2},{1,3},{2,0},{3,1},{4,6},{5,7},{6,4},{7,5},{8,10},{9,11},{10,... | collective-permute-start | bytes 20 | tf_op jit(solution)/shard_map/ppermute | solution.py:109
  88.8 1.7 %collective-permute-done.19 = f32[]{:T(128)} collective-permute-done((f32[]{:T(128)}, f32[]{:T(128)}, u32[]{:S(2)}, u32[]{:S(2)}) %collective-permute-start.19) | collective-permute-done | bytes 36 | tf_op jit(solution)/shard_map/ppermute | solution.py:109
  91.2 0.6 multiply_reduce_fusion.17
  91.8 1.3 collective-permute-done.20
  94.5 1.9 %collective-permute-start.21 = (f32[]{:T(128)}, f32[]{:T(128)}, u32[]{:S(2)}, u32[]{:S(2)}) collective-permute-start(f32[]{:T(128)} %add.167), channel_id=1, source_target_pairs={{0,2},{1,3},{2,0},{3,1},{4,6},{5,7},{6,4},{7,5},{8,10},{9,11},{10,... | collective-permute-start | bytes 20 | tf_op jit(solution)/shard_map/ppermute | solution.py:109
  96.3 1.7 %collective-permute-done.21 = f32[]{:T(128)} collective-permute-done((f32[]{:T(128)}, f32[]{:T(128)}, u32[]{:S(2)}, u32[]{:S(2)}) %collective-permute-start.21) | collective-permute-done | bytes 36 | tf_op jit(solution)/shard_map/ppermute | solution.py:109
  100.8 1.4 %fusion.18 = f32[64,192]{0,1:T(8,128)S(1)} fusion(bf16[192,4096]{1,0:T(8,128)(2,1)S(1)} %bitcast.151, bf16[192,4096]{1,0:T(8,128)(2,1)S(1)} %bitcast.150, bf16[192,4096]{1,0:T(8,128)(2,1)S(1)} %bitcast.149, bf16[64,4096]{1,0:T(8,128)(2,1)S(1)} %get-tuple-element.107), kind=kOutput, calls=%fused_computation.18 | convolution fusion | flops 320864256 | bytes 5292032 | tf_op jit(solution)/shard_map/dot_general | solution.py:46
  102.8 1.2 collective-permute-done.22
  104.0 0.6 collective-permute-start.23
  104.6 3.7 %collective-permute-done.23 = f32[3,4096]{1,0:T(4,128)S(1)} collective-permute-done((f32[3,4096]{1,0:T(4,128)S(1)}, f32[3,4096]{1,0:T(4,128)S(1)}, u32[]{:S(2)}, u32[]{:S(2)}) %collective-permute-start.23) | collective-permute-done | bytes 49184 | tf_op jit(solution)/shard_map/ppermute | solution.py:109
  108.8 0.6 fusion.49
  110.8 1.1 fusion.42
  112.1 1.6 %collective-permute-start.24 = (f32[9,512]{1,0:T(8,128)S(1)}, f32[9,512]{1,0:T(8,128)S(1)}, u32[]{:S(2)}, u32[]{:S(2)}) collective-permute-start(f32[9,512]{1,0:T(8,128)S(1)} %reshape.980), channel_id=1, source_target_pairs={{0,4},{4,0},{8,12},{12,8},{1,5},{5,1},{9,13},{13,9},{2,6},{6,2},{1... | collective-permute-start | bytes 55304 | tf_op jit(solution)/shard_map/ppermute | solution.py:109
  113.8 2.3 %collective-permute-done.24 = f32[9,512]{1,0:T(8,128)S(1)} collective-permute-done((f32[9,512]{1,0:T(8,128)S(1)}, f32[9,512]{1,0:T(8,128)S(1)}, u32[]{:S(2)}, u32[]{:S(2)}) %collective-permute-start.24) | collective-permute-done | bytes 18464 | tf_op jit(solution)/shard_map/ppermute | solution.py:109
  116.1 1.1 collective-permute-start.25
  117.2 3.7 %collective-permute-done.25 = f32[9,512]{1,0:T(8,128)S(1)} collective-permute-done((f32[9,512]{1,0:T(8,128)S(1)}, f32[9,512]{1,0:T(8,128)S(1)}, u32[]{:S(2)}, u32[]{:S(2)}) %collective-permute-start.25) | collective-permute-done | bytes 18464 | tf_op jit(solution)/shard_map/ppermute | solution.py:109
  120.9 0.6 multiply_reduce_fusion.16
  121.5 1.3 collective-permute-done.26
  124.1 1.9 %collective-permute-start.27 = (f32[]{:T(128)}, f32[]{:T(128)}, u32[]{:S(2)}, u32[]{:S(2)}) collective-permute-start(f32[]{:T(128)} %add.175), channel_id=1, source_target_pairs={{0,2},{1,3},{2,0},{3,1},{4,6},{5,7},{6,4},{7,5},{8,10},{9,11},{10,... | collective-permute-start | bytes 20 | tf_op jit(solution)/shard_map/ppermute | solution.py:109
  126.0 1.7 %collective-permute-done.27 = f32[]{:T(128)} collective-permute-done((f32[]{:T(128)}, f32[]{:T(128)}, u32[]{:S(2)}, u32[]{:S(2)}) %collective-permute-start.27) | collective-permute-done | bytes 36 | tf_op jit(solution)/shard_map/ppermute | solution.py:109
  128.5 0.6 multiply_subtract_fusion
  (134 shorter events, 15.8 us)
Async XLA Ops:
  3.3 4.4 %copy-start.1 = (f32[2,3,4096]{2,0,1:T(2,128)S(1)}, f32[2,3,4096]{2,0,1:T(2,128)}, u32[]{:S(2)}) copy-start(f32[2,3,4096]{2,0,1:T(2,128)} %param.8) | copy-start | bytes 294916
  3.3 4.9 %copy-start.4 = (s32[4096]{0:T(1024)S(1)}, s32[4096]{0:T(1024)}, u32[]{:S(2)}) copy-start(s32[4096]{0:T(1024)} %param.10) | copy-start | bytes 49156
  4.6 5.0 %collective-permute-start = (f32[9,512]{1,0:T(8,128)S(1)}, f32[9,512]{1,0:T(8,128)S(1)}, u32[]{:S(2)}, u32[]{:S(2)}) collective-permute-start(f32[9,512]{1,0:T(8,128)S(1)} %reshape.948), channel_id=1, source_target_pairs={{0,4},{4,0},{8,12},{12,8},{1,5},{5,1},{9,13},{13,9},{2,6},{6,2},{1... | collective-permute-start | bytes 55304 | tf_op jit(solution)/shard_map/ppermute | solution.py:109
  9.6 6.4 %collective-permute-start.1 = (f32[9,512]{1,0:T(8,128)S(1)}, f32[9,512]{1,0:T(8,128)S(1)}, u32[]{:S(2)}, u32[]{:S(2)}) collective-permute-start(f32[9,512]{1,0:T(8,128)S(1)} %add.137), channel_id=1, source_target_pairs={{0,8},{4,12},{8,0},{12,4},{1,9},{5,13},{9,1},{13,5},{2,10},{6,14},... | collective-permute-start | bytes 55304 | tf_op jit(solution)/shard_map/ppermute | solution.py:109
  12.7 3.4 %copy-start.2 = (f32[9,512]{1,0:T(8,128)S(1)}, f32[9,512]{1,0:T(8,128)}, u32[]{:S(2)}) copy-start(f32[9,512]{1,0:T(8,128)} %param.13) | copy-start | bytes 55300
  12.7 3.4 %copy-start.3 = (f32[512]{0:T(512)S(1)}, f32[512]{0:T(512)}, u32[]{:S(2)}) copy-start(f32[512]{0:T(512)} %param.12) | copy-start | bytes 6148
  16.0 7.3 %collective-permute-start.4 = (f32[6,4096]{1,0:T(8,128)S(1)}, f32[6,4096]{1,0:T(8,128)S(1)}, u32[]{:S(2)}, u32[]{:S(2)}) collective-permute-start(f32[6,4096]{1,0:T(8,128)S(1)} %reshape.953), channel_id=1, source_target_pairs={{0,1},{1,0},{2,3},{3,2},{4,5},{5,4},{6,7},{7,6},{8,9},{9,8},{10,11... | collective-permute-start | bytes 294920 | tf_op jit(solution)/shard_map/ppermute | solution.py:109
  16.8 1.0 copy-start
  20.1 9.1 %copy-start.5 = (f32[4096]{0:T(1024)S(1)}, f32[4096]{0:T(1024)}, u32[]{:S(2)}) copy-start(f32[4096]{0:T(1024)} %param.11) | copy-start | bytes 49156
  20.3 1.4 %collective-permute-start.6 = (f32[3,4096]{1,0:T(4,128)S(1)}, f32[3,4096]{1,0:T(4,128)S(1)}, u32[]{:S(2)}, u32[]{:S(2)}) collective-permute-start(f32[3,4096]{1,0:T(4,128)S(1)} %reshape.955), channel_id=1, source_target_pairs={{0,1},{1,0},{2,3},{3,2},{4,5},{5,4},{6,7},{7,6},{8,9},{9,8},{10,11... | collective-permute-start | bytes 147464 | tf_op jit(solution)/shard_map/ppermute | solution.py:109
  21.7 4.5 %collective-permute-start.7 = (f32[3,4096]{1,0:T(4,128)S(1)}, f32[3,4096]{1,0:T(4,128)S(1)}, u32[]{:S(2)}, u32[]{:S(2)}) collective-permute-start(f32[3,4096]{1,0:T(4,128)S(1)} %add.149), channel_id=1, source_target_pairs={{0,2},{1,3},{2,0},{3,1},{4,6},{5,7},{6,4},{7,5},{8,10},{9,11},{10,... | collective-permute-start | bytes 147464 | tf_op jit(solution)/shard_map/ppermute | solution.py:109
  23.3 5.6 %collective-permute-start.5 = (f32[6,4096]{1,0:T(8,128)S(1)}, f32[6,4096]{1,0:T(8,128)S(1)}, u32[]{:S(2)}, u32[]{:S(2)}) collective-permute-start(f32[6,4096]{1,0:T(8,128)S(1)} %add.144), channel_id=1, source_target_pairs={{0,2},{1,3},{2,0},{3,1},{4,6},{5,7},{6,4},{7,5},{8,10},{9,11},{10,... | collective-permute-start | bytes 294920 | tf_op jit(solution)/shard_map/ppermute | solution.py:109
  33.6 4.0 %collective-permute-start.8 = (f32[9,512]{1,0:T(8,128)S(1)}, f32[9,512]{1,0:T(8,128)S(1)}, u32[]{:S(2)}, u32[]{:S(2)}) collective-permute-start(f32[9,512]{1,0:T(8,128)S(1)} %reshape.960), channel_id=1, source_target_pairs={{0,4},{4,0},{8,12},{12,8},{1,5},{5,1},{9,13},{13,9},{2,6},{6,2},{1... | collective-permute-start | bytes 55304 | tf_op jit(solution)/shard_map/ppermute | solution.py:109
  37.6 4.8 %collective-permute-start.9 = (f32[9,512]{1,0:T(8,128)S(1)}, f32[9,512]{1,0:T(8,128)S(1)}, u32[]{:S(2)}, u32[]{:S(2)}) collective-permute-start(f32[9,512]{1,0:T(8,128)S(1)} %add.151), channel_id=1, source_target_pairs={{0,8},{4,12},{8,0},{12,4},{1,9},{5,13},{9,1},{13,5},{2,10},{6,14},... | collective-permute-start | bytes 55304 | tf_op jit(solution)/shard_map/ppermute | solution.py:109
  43.1 1.4 %collective-permute-start.10 = (f32[]{:T(128)}, f32[]{:T(128)}, u32[]{:S(2)}, u32[]{:S(2)}) collective-permute-start(f32[]{:T(128)} %get-tuple-element.8), channel_id=1, source_target_pairs={{0,1},{1,0},{2,3},{3,2},{4,5},{5,4},{6,7},{7,6},{8,9},{9,8},{10,11... | collective-permute-start | bytes 20 | tf_op jit(solution)/shard_map/ppermute | solution.py:109
  43.1 5.5 %collective-permute-start.2 = (f32[]{:T(128)}, f32[]{:T(128)}, u32[]{:S(2)}, u32[]{:S(2)}) collective-permute-start(f32[]{:T(128)} %get-tuple-element.9), channel_id=1, source_target_pairs={{0,1},{1,0},{2,3},{3,2},{4,5},{5,4},{6,7},{7,6},{8,9},{9,8},{10,11... | collective-permute-start | bytes 20 | tf_op jit(solution)/shard_map/ppermute | solution.py:109
  45.7 6.1 %collective-permute-start.11 = (f32[]{:T(128)}, f32[]{:T(128)}, u32[]{:S(2)}, u32[]{:S(2)}) collective-permute-start(f32[]{:T(128)} %add.154), channel_id=1, source_target_pairs={{0,2},{1,3},{2,0},{3,1},{4,6},{5,7},{6,4},{7,5},{8,10},{9,11},{10,... | collective-permute-start | bytes 20 | tf_op jit(solution)/shard_map/ppermute | solution.py:109
  49.9 3.6 %collective-permute-start.3 = (f32[]{:T(128)}, f32[]{:T(128)}, u32[]{:S(2)}, u32[]{:S(2)}) collective-permute-start(f32[]{:T(128)} %add.141), channel_id=1, source_target_pairs={{0,2},{1,3},{2,0},{3,1},{4,6},{5,7},{6,4},{7,5},{8,10},{9,11},{10,... | collective-permute-start | bytes 20 | tf_op jit(solution)/shard_map/ppermute | solution.py:109
  54.8 1.3 collective-permute-start.12
  57.5 3.6 %collective-permute-start.13 = (f32[]{:T(128)}, f32[]{:T(128)}, u32[]{:S(2)}, u32[]{:S(2)}) collective-permute-start(f32[]{:T(128)} %add.156), channel_id=1, source_target_pairs={{0,2},{1,3},{2,0},{3,1},{4,6},{5,7},{6,4},{7,5},{8,10},{9,11},{10,... | collective-permute-start | bytes 20 | tf_op jit(solution)/shard_map/ppermute | solution.py:109
  65.5 1.3 %collective-permute-start.14 = (f32[3,4096]{1,0:T(4,128)S(1)}, f32[3,4096]{1,0:T(4,128)S(1)}, u32[]{:S(2)}, u32[]{:S(2)}) collective-permute-start(f32[3,4096]{1,0:T(4,128)S(1)} %reshape.965), channel_id=1, source_target_pairs={{0,1},{1,0},{2,3},{3,2},{4,5},{5,4},{6,7},{7,6},{8,9},{9,8},{10,11... | collective-permute-start | bytes 147464 | tf_op jit(solution)/shard_map/ppermute | solution.py:109
  66.8 4.3 %collective-permute-start.15 = (f32[3,4096]{1,0:T(4,128)S(1)}, f32[3,4096]{1,0:T(4,128)S(1)}, u32[]{:S(2)}, u32[]{:S(2)}) collective-permute-start(f32[3,4096]{1,0:T(4,128)S(1)} %add.159), channel_id=1, source_target_pairs={{0,2},{1,3},{2,0},{3,1},{4,6},{5,7},{6,4},{7,5},{8,10},{9,11},{10,... | collective-permute-start | bytes 147464 | tf_op jit(solution)/shard_map/ppermute | solution.py:109
  74.9 4.0 %collective-permute-start.16 = (f32[9,512]{1,0:T(8,128)S(1)}, f32[9,512]{1,0:T(8,128)S(1)}, u32[]{:S(2)}, u32[]{:S(2)}) collective-permute-start(f32[9,512]{1,0:T(8,128)S(1)} %reshape.970), channel_id=1, source_target_pairs={{0,4},{4,0},{8,12},{12,8},{1,5},{5,1},{9,13},{13,9},{2,6},{6,2},{1... | collective-permute-start | bytes 55304 | tf_op jit(solution)/shard_map/ppermute | solution.py:109
  78.9 4.8 %collective-permute-start.17 = (f32[9,512]{1,0:T(8,128)S(1)}, f32[9,512]{1,0:T(8,128)S(1)}, u32[]{:S(2)}, u32[]{:S(2)}) collective-permute-start(f32[9,512]{1,0:T(8,128)S(1)} %add.161), channel_id=1, source_target_pairs={{0,8},{4,12},{8,0},{12,4},{1,9},{5,13},{9,1},{13,5},{2,10},{6,14},... | collective-permute-start | bytes 55304 | tf_op jit(solution)/shard_map/ppermute | solution.py:109
  84.3 1.3 collective-permute-start.18
  86.9 3.6 %collective-permute-start.19 = (f32[]{:T(128)}, f32[]{:T(128)}, u32[]{:S(2)}, u32[]{:S(2)}) collective-permute-start(f32[]{:T(128)} %add.164), channel_id=1, source_target_pairs={{0,2},{1,3},{2,0},{3,1},{4,6},{5,7},{6,4},{7,5},{8,10},{9,11},{10,... | collective-permute-start | bytes 20 | tf_op jit(solution)/shard_map/ppermute | solution.py:109
  91.8 1.3 collective-permute-start.20
  94.5 3.6 %collective-permute-start.21 = (f32[]{:T(128)}, f32[]{:T(128)}, u32[]{:S(2)}, u32[]{:S(2)}) collective-permute-start(f32[]{:T(128)} %add.167), channel_id=1, source_target_pairs={{0,2},{1,3},{2,0},{3,1},{4,6},{5,7},{6,4},{7,5},{8,10},{9,11},{10,... | collective-permute-start | bytes 20 | tf_op jit(solution)/shard_map/ppermute | solution.py:109
  102.5 1.5 %collective-permute-start.22 = (f32[3,4096]{1,0:T(4,128)S(1)}, f32[3,4096]{1,0:T(4,128)S(1)}, u32[]{:S(2)}, u32[]{:S(2)}) collective-permute-start(f32[3,4096]{1,0:T(4,128)S(1)} %reshape.975), channel_id=1, source_target_pairs={{0,1},{1,0},{2,3},{3,2},{4,5},{5,4},{6,7},{7,6},{8,9},{9,8},{10,11... | collective-permute-start | bytes 147464 | tf_op jit(solution)/shard_map/ppermute | solution.py:109
  104.0 4.3 %collective-permute-start.23 = (f32[3,4096]{1,0:T(4,128)S(1)}, f32[3,4096]{1,0:T(4,128)S(1)}, u32[]{:S(2)}, u32[]{:S(2)}) collective-permute-start(f32[3,4096]{1,0:T(4,128)S(1)} %add.170), channel_id=1, source_target_pairs={{0,2},{1,3},{2,0},{3,1},{4,6},{5,7},{6,4},{7,5},{8,10},{9,11},{10,... | collective-permute-start | bytes 147464 | tf_op jit(solution)/shard_map/ppermute | solution.py:109
  112.1 4.0 %collective-permute-start.24 = (f32[9,512]{1,0:T(8,128)S(1)}, f32[9,512]{1,0:T(8,128)S(1)}, u32[]{:S(2)}, u32[]{:S(2)}) collective-permute-start(f32[9,512]{1,0:T(8,128)S(1)} %reshape.980), channel_id=1, source_target_pairs={{0,4},{4,0},{8,12},{12,8},{1,5},{5,1},{9,13},{13,9},{2,6},{6,2},{1... | collective-permute-start | bytes 55304 | tf_op jit(solution)/shard_map/ppermute | solution.py:109
  116.1 4.8 %collective-permute-start.25 = (f32[9,512]{1,0:T(8,128)S(1)}, f32[9,512]{1,0:T(8,128)S(1)}, u32[]{:S(2)}, u32[]{:S(2)}) collective-permute-start(f32[9,512]{1,0:T(8,128)S(1)} %add.172), channel_id=1, source_target_pairs={{0,8},{4,12},{8,0},{12,4},{1,9},{5,13},{9,1},{13,5},{2,10},{6,14},... | collective-permute-start | bytes 55304 | tf_op jit(solution)/shard_map/ppermute | solution.py:109
  121.5 1.3 collective-permute-start.26
  124.1 3.6 %collective-permute-start.27 = (f32[]{:T(128)}, f32[]{:T(128)}, u32[]{:S(2)}, u32[]{:S(2)}) collective-permute-start(f32[]{:T(128)} %add.175), channel_id=1, source_target_pairs={{0,2},{1,3},{2,0},{3,1},{4,6},{5,7},{6,4},{7,5},{8,10},{9,11},{10,... | collective-permute-start | bytes 20 | tf_op jit(solution)/shard_map/ppermute | solution.py:109

commit v3 on v2

--- a/solution.py
+++ b/solution.py
@@ -102,6 +102,18 @@
 
 def allsum(value, axis):
     size = SIZES[axis]
+    if size <= 4:
+        me = lax.axis_index(axis)
+        got = [value] + [
+            lax.ppermute(value, axis, [(i, (i + shift) % size) for i in range(size)])
+            for shift in range(1, size)
+        ]
+        stacked = jnp.stack(got)
+        ordered = [stacked[(me - source) % size] for source in range(size)]
+        while len(ordered) > 1:
+            ordered = [ordered[i] + ordered[i + 1] if i + 1 < len(ordered) else ordered[i]
+                       for i in range(0, len(ordered), 2)]
+        return ordered[0]
     if size & (size - 1):
         return lax.psum(value, axis)
     step = 1

time: 130 us -> 143 us (1.10)
  waiting for transfers between devices: 48 us -> 26.3 us
  other arithmetic: 17.2 us -> 33.5 us
  starting transfers between devices: 31.8 us -> 41.6 us
  local copies, waits for them, and re-layouts: 3.64 us -> 8.52 us
  between operations: 13.6 us -> 16.8 us
    ppermute x28 -> x42, waiting for transfers between devices: 48 us -> 26.3 us  [allsum(): lax.ppermute(value, axis, [(i, (i + shift) % size) for i in range(size)])]
    another operation x0 -> x14, other arithmetic: none -> 15.8 us  [allsum(): stacked = jnp.stack(got)]
    ppermute x28 -> x42, starting transfers between devices: 31.8 us -> 41.6 us  [allsum(): lax.ppermute(value, axis, [(i, (i + shift) % size) for i in range(size)])]
    dynamic_slice x0 -> x6, local copies, waits for them, and re-layouts: none -> 4 us  [allsum(): ordered = [stacked[(me - source) % size] for source in range(size)]]
  transfers between devices with their start and end apart: 28 -> 42, of which waited for: 24 -> 22; matrix products, arithmetic and copies ran while one was open for 7% -> 9% of each run, Pallas kernels for 0% -> 0%
where the time goes in v3:
time: 143 us; the launch traced here: 142 us
  starting transfers between devices  41.6 us (29%)
  other arithmetic  33.5 us (23%)
  waiting for transfers between devices  26.3 us (18%)
  between operations  16.8 us (12%)
  matrix products  14.9 us (10%)
  local copies, waits for them, and re-layouts  8.52 us (6%)
    ppermute x42, starting transfers between devices, allsum(): lax.ppermute(value, axis, [(i, (i + shift) % size) for i in range(size)])  41.6 us
    ppermute x42, waiting for transfers between devices, allsum(): lax.ppermute(value, axis, [(i, (i + shift) % size) for i in range(size)])  26.3 us
    another operation x14, other arithmetic, allsum(): stacked = jnp.stack(got)  15.8 us
    dot_general x8, matrix products, segsum(): lax.dot_general(self.hot3, spread, (((1,), (1,)), ((), ())), preferred_el...  11.5 us
    dynamic_slice x6, local copies, waits for them, and re-layouts, allsum(): ordered = [stacked[(me - source) % size] for source in range(size)]  4 us
    select_n x8, other arithmetic, segsum(): jnp.where(self.low[None], part[:, None, :], jnp.zeros((), BF))  3.88 us
    dot_general x6, matrix products, gather(): lax.dot_general(stacked, self.hot3t, (((1,), (0,)), ((), ())), preferred_...  3.4 us
  transfers between devices with their start and end apart: 42, of which 22 were waited for; matrix products, arithmetic and copies ran while one was open for 9% of the time, Pallas kernels for 0%

profile of v3, /device:TPU:0, one launch (start us, length us, event | category | flops | bytes accessed | tf_op | source)
XLA Modules:
  0.0 141.6 jit_solution(6631939716706328814)
XLA Ops:
  0.6 0.7 add_select_fusion.3
  1.4 1.4 multiply_reduce_fusion.6
  3.3 1.1 fusion.24
  4.6 3.1 %collective-permute-start = (f32[9,512]{1,0:T(8,128)S(1)}, f32[9,512]{1,0:T(8,128)S(1)}, u32[]{:S(2)}, u32[]{:S(2)}) collective-permute-start(f32[9,512]{1,0:T(8,128)S(1)} %reshape.989), channel_id=1, source_target_pairs={{0,4},{4,8},{8,12},{12,0},{1,5},{5,9},{9,13},{13,1},{2,6},{6,10},{... | collective-permute-start | bytes 55304 | tf_op jit(solution)/shard_map/ppermute | solution.py:108
  7.7 2.6 %collective-permute-start.1 = (f32[9,512]{1,0:T(8,128)S(1)}, f32[9,512]{1,0:T(8,128)S(1)}, u32[]{:S(2)}, u32[]{:S(2)}) collective-permute-start(f32[9,512]{1,0:T(8,128)S(1)} %reshape.989), channel_id=1, source_target_pairs={{0,8},{4,12},{8,0},{12,4},{1,9},{5,13},{9,1},{13,5},{2,10},{6,14},... | collective-permute-start | bytes 55304 | tf_op jit(solution)/shard_map/ppermute | solution.py:108
  10.3 1.4 collective-permute-start.2
  12.4 0.9 broadcast_select_fusion.2
  13.3 3.0 %fusion = f32[64,384]{1,0:T(8,128)S(1)} fusion(bf16[384,4096]{1,0:T(8,128)(2,1)S(1)} %bitcast.219, bf16[384,4096]{1,0:T(8,128)(2,1)S(1)} %bitcast.218, bf16[384,4096]{1,0:T(8,128)(2,1)S(1)} %bitcast.217, bf16[64,4096]{1,0:T(8,128)(2,1)S(1)} %get-tuple-element.134), kind=kOutput, calls=%fused_computation | convolution fusion | flops 637009920 | bytes 10059776 | tf_op jit(solution)/shard_map/dot_general | solution.py:46
  16.6 1.6 %collective-permute-start.7 = (f32[6,4096]{1,0:T(8,128)S(1)}, f32[6,4096]{1,0:T(8,128)S(1)}, u32[]{:S(2)}, u32[]{:S(2)}) collective-permute-start(f32[6,4096]{1,0:T(8,128)S(1)} %reshape.994), channel_id=1, source_target_pairs={{0,2},{1,3},{2,0},{3,1},{4,6},{5,7},{6,4},{7,5},{8,10},{9,11},{10,... | collective-permute-start | bytes 294920 | tf_op jit(solution)/shard_map/ppermute | solution.py:108
  21.0 1.4 %fusion.6 = f32[64,192]{0,1:T(8,128)S(1)} fusion(bf16[192,4096]{1,0:T(8,128)(2,1)S(1)} %bitcast.222, bf16[192,4096]{1,0:T(8,128)(2,1)S(1)} %bitcast.221, bf16[192,4096]{1,0:T(8,128)(2,1)S(1)} %bitcast.220, bf16[64,4096]{1,0:T(8,128)(2,1)S(1)} %get-tuple-element.134), kind=kOutput, calls=%fused_computation.6 | convolution fusion | flops 320864256 | bytes 5292032 | tf_op jit(solution)/shard_map/dot_general | solution.py:46
  23.0 1.5 %collective-permute-start.10 = (f32[3,4096]{1,0:T(4,128)S(1)}, f32[3,4096]{1,0:T(4,128)S(1)}, u32[]{:S(2)}, u32[]{:S(2)}) collective-permute-start(f32[3,4096]{1,0:T(4,128)S(1)} %reshape.996), channel_id=1, source_target_pairs={{0,2},{1,3},{2,0},{3,1},{4,6},{5,7},{6,4},{7,5},{8,10},{9,11},{10,... | collective-permute-start | bytes 147464 | tf_op jit(solution)/shard_map/ppermute | solution.py:108
  25.0 1.4 collective-permute-done.9
  26.4 1.4 collective-permute-done.10
  27.9 1.0 collective-permute-done.8
  32.2 1.1 fusion.30
  33.5 0.7 collective-permute-start.12
  34.5 2.8 %collective-permute-start.14 = (f32[9,512]{1,0:T(8,128)S(1)}, f32[9,512]{1,0:T(8,128)S(1)}, u32[]{:S(2)}, u32[]{:S(2)}) collective-permute-start(f32[9,512]{1,0:T(8,128)S(1)} %reshape.1001), channel_id=1, source_target_pairs={{0,12},{4,0},{8,4},{12,8},{1,13},{5,1},{9,5},{13,9},{2,14},{6,2},{... | collective-permute-start | bytes 55304 | tf_op jit(solution)/shard_map/ppermute | solution.py:108
  37.5 2.2 %collective-permute-done.12 = f32[9,512]{1,0:T(8,128)S(1)} collective-permute-done((f32[9,512]{1,0:T(8,128)S(1)}, f32[9,512]{1,0:T(8,128)S(1)}, u32[]{:S(2)}, u32[]{:S(2)}) %collective-permute-start.12) | collective-permute-done | bytes 18464 | tf_op jit(solution)/shard_map/ppermute | solution.py:108
  39.7 1.0 collective-permute-done.13
  41.3 0.8 collective-permute-start.16
  42.1 1.3 collective-permute-start.17
  43.4 1.4 collective-permute-start.4
  44.8 1.5 %collective-permute-start.5 = (f32[]{:T(128)}, f32[]{:T(128)}, u32[]{:S(2)}, u32[]{:S(2)}) collective-permute-start(f32[]{:T(128)} %get-tuple-element.9), channel_id=1, source_target_pairs={{0,3},{1,0},{2,1},{3,2},{4,7},{5,4},{6,5},{7,6},{8,11},{9,8},{10,9... | collective-permute-start | bytes 20 | tf_op jit(solution)/shard_map/ppermute | solution.py:108
  46.3 2.6 %pad_maximum_fusion.27 = f32[4]{0:T(128)S(1)} fusion(f32[1]{0:T(128)} %bitcast.75, f32[1]{0:T(128)} %bitcast.74, f32[1]{0:T(128)} %bitcast.73, f32[1]{0:T(128)} %bitcast.72), kind=kLoop, calls=%fused_computation.284 | loop fusion | flops 12 | bytes 32 | tf_op jit(solution)/shard_map/stack | solution.py:111
  49.6 2.6 %pad_maximum_fusion.26 = f32[4]{0:T(128)S(1)} fusion(f32[1]{0:T(128)} %bitcast.13, f32[1]{0:T(128)} %bitcast.12, f32[1]{0:T(128)} %bitcast.11, f32[1]{0:T(128)} %bitcast.10), kind=kLoop, calls=%fused_computation.283 | loop fusion | flops 12 | bytes 32 | tf_op jit(solution)/shard_map/stack | solution.py:111
  52.2 0.7 fusion.125
  59.2 1.3 collective-permute-start.20
  60.6 1.1 collective-permute-done.18
  61.7 0.7 collective-permute-done.19
  62.4 2.6 %pad_maximum_fusion.28 = f32[4]{0:T(128)S(1)} fusion(f32[1]{0:T(128)} %bitcast.80, f32[1]{0:T(128)} %bitcast.79, f32[1]{0:T(128)} %bitcast.78, f32[1]{0:T(128)} %bitcast.77), kind=kLoop, calls=%fused_computation.285 | loop fusion | flops 12 | bytes 32 | tf_op jit(solution)/shard_map/stack | solution.py:111
  70.3 1.4 %fusion.12 = f32[64,192]{0,1:T(8,128)S(1)} fusion(bf16[192,4096]{1,0:T(8,128)(2,1)S(1)} %bitcast.225, bf16[192,4096]{1,0:T(8,128)(2,1)S(1)} %bitcast.224, bf16[192,4096]{1,0:T(8,128)(2,1)S(1)} %bitcast.223, bf16[64,4096]{1,0:T(8,128)(2,1)S(1)} %get-tuple-element.134), kind=kOutput, calls=%fused_computation.12 | convolution fusion | flops 320864256 | bytes 5292032 | tf_op jit(solution)/shard_map/dot_general | solution.py:46
  71.9 1.2 collective-permute-start.21
  73.8 0.8 collective-permute-start.23
  74.7 1.0 collective-permute-done.21
  75.7 1.7 %collective-permute-done.22 = f32[3,4096]{1,0:T(4,128)S(1)} collective-permute-done((f32[3,4096]{1,0:T(4,128)S(1)}, f32[3,4096]{1,0:T(4,128)S(1)}, u32[]{:S(2)}, u32[]{:S(2)}) %collective-permute-start.22) | collective-permute-done | bytes 49184 | tf_op jit(solution)/shard_map/ppermute | solution.py:108
  80.0 1.1 fusion.36
  81.2 1.2 collective-permute-start.24
  82.5 1.9 %collective-permute-start.25 = (f32[9,512]{1,0:T(8,128)S(1)}, f32[9,512]{1,0:T(8,128)S(1)}, u32[]{:S(2)}, u32[]{:S(2)}) collective-permute-start(f32[9,512]{1,0:T(8,128)S(1)} %reshape.1011), channel_id=1, source_target_pairs={{0,8},{4,12},{8,0},{12,4},{1,9},{5,13},{9,1},{13,5},{2,10},{6,14},... | collective-permute-start | bytes 55304 | tf_op jit(solution)/shard_map/ppermute | solution.py:108
  84.4 0.7 collective-permute-start.26
  85.2 2.2 %collective-permute-done.24 = f32[9,512]{1,0:T(8,128)S(1)} collective-permute-done((f32[9,512]{1,0:T(8,128)S(1)}, f32[9,512]{1,0:T(8,128)S(1)}, u32[]{:S(2)}, u32[]{:S(2)}) %collective-permute-start.24) | collective-permute-done | bytes 18464 | tf_op jit(solution)/shard_map/ppermute | solution.py:108
  87.5 1.0 collective-permute-done.25
  89.3 0.7 collective-permute-start.28
  90.0 1.5 %collective-permute-start.29 = (f32[]{:T(128)}, f32[]{:T(128)}, u32[]{:S(2)}, u32[]{:S(2)}) collective-permute-start(f32[]{:T(128)} %get-tuple-element.15), channel_id=1, source_target_pairs={{0,3},{1,0},{2,1},{3,2},{4,7},{5,4},{6,5},{7,6},{8,11},{9,8},{10,9... | collective-permute-start | bytes 20 | tf_op jit(solution)/shard_map/ppermute | solution.py:108
  91.5 1.0 collective-permute-done.27
  93.1 2.6 %pad_maximum_fusion.29 = f32[4]{0:T(128)S(1)} fusion(f32[1]{0:T(128)} %bitcast.111, f32[1]{0:T(128)} %bitcast.110, f32[1]{0:T(128)} %bitcast.109, f32[1]{0:T(128)} %bitcast.108), kind=kLoop, calls=%fused_computation.286 | loop fusion | flops 12 | bytes 32 | tf_op jit(solution)/shard_map/stack | solution.py:111
  99.6 1.3 collective-permute-start.30
  100.9 0.7 collective-permute-start.31
  102.7 2.0 %collective-permute-done.31 = f32[]{:T(128)} collective-permute-done((f32[]{:T(128)}, f32[]{:T(128)}, u32[]{:S(2)}, u32[]{:S(2)}) %collective-permute-start.31) | collective-permute-done | bytes 36 | tf_op jit(solution)/shard_map/ppermute | solution.py:108
  104.7 2.5 %pad_maximum_fusion.30 = f32[4]{0:T(128)S(1)} fusion(f32[1]{0:T(128)} %bitcast.116, f32[1]{0:T(128)} %bitcast.115, f32[1]{0:T(128)} %bitcast.114, f32[1]{0:T(128)} %bitcast.113), kind=kLoop, calls=%fused_computation.287 | loop fusion | flops 12 | bytes 32 | tf_op jit(solution)/shard_map/stack | solution.py:111
  112.4 1.4 %fusion.18 = f32[64,192]{0,1:T(8,128)S(1)} fusion(bf16[192,4096]{1,0:T(8,128)(2,1)S(1)} %bitcast.228, bf16[192,4096]{1,0:T(8,128)(2,1)S(1)} %bitcast.227, bf16[192,4096]{1,0:T(8,128)(2,1)S(1)} %bitcast.226, bf16[64,4096]{1,0:T(8,128)(2,1)S(1)} %get-tuple-element.134), kind=kOutput, calls=%fused_computation.18 | convolution fusion | flops 320864256 | bytes 5292032 | tf_op jit(solution)/shard_map/dot_general | solution.py:46
  114.2 1.0 collective-permute-start.34
  115.2 1.2 collective-permute-start.35
  116.5 1.4 %collective-permute-done.33 = f32[3,4096]{1,0:T(4,128)S(1)} collective-permute-done((f32[3,4096]{1,0:T(4,128)S(1)}, f32[3,4096]{1,0:T(4,128)S(1)}, u32[]{:S(2)}, u32[]{:S(2)}) %collective-permute-start.33) | collective-permute-done | bytes 49184 | tf_op jit(solution)/shard_map/ppermute | solution.py:108
  117.9 1.3 collective-permute-done.34
  121.7 1.1 fusion.42
  123.0 1.0 collective-permute-start.36
  124.0 2.0 %collective-permute-start.37 = (f32[9,512]{1,0:T(8,128)S(1)}, f32[9,512]{1,0:T(8,128)S(1)}, u32[]{:S(2)}, u32[]{:S(2)}) collective-permute-start(f32[9,512]{1,0:T(8,128)S(1)} %reshape.1021), channel_id=1, source_target_pairs={{0,8},{4,12},{8,0},{12,4},{1,9},{5,13},{9,1},{13,5},{2,10},{6,14},... | collective-permute-start | bytes 55304 | tf_op jit(solution)/shard_map/ppermute | solution.py:108
  126.0 0.9 collective-permute-start.38
  127.0 2.2 %collective-permute-done.36 = f32[9,512]{1,0:T(8,128)S(1)} collective-permute-done((f32[9,512]{1,0:T(8,128)S(1)}, f32[9,512]{1,0:T(8,128)S(1)}, u32[]{:S(2)}, u32[]{:S(2)}) %collective-permute-start.36) | collective-permute-done | bytes 18464 | tf_op jit(solution)/shard_map/ppermute | solution.py:108
  129.3 0.9 collective-permute-done.37
  130.8 1.0 collective-permute-start.40
  131.7 1.5 %collective-permute-start.41 = (f32[]{:T(128)}, f32[]{:T(128)}, u32[]{:S(2)}, u32[]{:S(2)}) collective-permute-start(f32[]{:T(128)} %get-tuple-element.10), channel_id=1, source_target_pairs={{0,3},{1,0},{2,1},{3,2},{4,7},{5,4},{6,5},{7,6},{8,11},{9,8},{10,9... | collective-permute-start | bytes 20 | tf_op jit(solution)/shard_map/ppermute | solution.py:108
  133.8 0.7 collective-permute-done.40
  134.6 2.5 %pad_maximum_fusion.31 = f32[4]{0:T(128)S(1)} fusion(f32[1]{0:T(128)} %bitcast.147, f32[1]{0:T(128)} %bitcast.146, f32[1]{0:T(128)} %bitcast.145, f32[1]{0:T(128)} %bitcast.144), kind=kLoop, calls=%fused_computation.288 | loop fusion | flops 12 | bytes 32 | tf_op jit(solution)/shard_map/stack | solution.py:111
  (183 shorter events, 31.3 us)
Async XLA Ops:
  3.3 8.4 %copy-start.1 = (f32[2,3,4096]{2,0,1:T(2,128)S(1)}, f32[2,3,4096]{2,0,1:T(2,128)}, u32[]{:S(2)}) copy-start(f32[2,3,4096]{2,0,1:T(2,128)} %param.8) | copy-start | bytes 294916
  3.3 8.8 %copy-start.4 = (s32[4096]{0:T(1024)S(1)}, s32[4096]{0:T(1024)}, u32[]{:S(2)}) copy-start(s32[4096]{0:T(1024)} %param.10) | copy-start | bytes 49156
  4.6 13.7 %collective-permute-start = (f32[9,512]{1,0:T(8,128)S(1)}, f32[9,512]{1,0:T(8,128)S(1)}, u32[]{:S(2)}, u32[]{:S(2)}) collective-permute-start(f32[9,512]{1,0:T(8,128)S(1)} %reshape.989), channel_id=1, source_target_pairs={{0,4},{4,8},{8,12},{12,0},{1,5},{5,9},{9,13},{13,1},{2,6},{6,10},{... | collective-permute-start | bytes 55304 | tf_op jit(solution)/shard_map/ppermute | solution.py:108
  7.7 10.6 %collective-permute-start.1 = (f32[9,512]{1,0:T(8,128)S(1)}, f32[9,512]{1,0:T(8,128)S(1)}, u32[]{:S(2)}, u32[]{:S(2)}) collective-permute-start(f32[9,512]{1,0:T(8,128)S(1)} %reshape.989), channel_id=1, source_target_pairs={{0,8},{4,12},{8,0},{12,4},{1,9},{5,13},{9,1},{13,5},{2,10},{6,14},... | collective-permute-start | bytes 55304 | tf_op jit(solution)/shard_map/ppermute | solution.py:108
  10.3 8.0 %collective-permute-start.2 = (f32[9,512]{1,0:T(8,128)S(1)}, f32[9,512]{1,0:T(8,128)S(1)}, u32[]{:S(2)}, u32[]{:S(2)}) collective-permute-start(f32[9,512]{1,0:T(8,128)S(1)} %reshape.989), channel_id=1, source_target_pairs={{0,12},{4,0},{8,4},{12,8},{1,13},{5,1},{9,5},{13,9},{2,14},{6,2},{... | collective-permute-start | bytes 55304 | tf_op jit(solution)/shard_map/ppermute | solution.py:108
  16.3 2.1 %copy-start.2 = (f32[9,512]{1,0:T(8,128)S(1)}, f32[9,512]{1,0:T(8,128)}, u32[]{:S(2)}) copy-start(f32[9,512]{1,0:T(8,128)} %param.13) | copy-start | bytes 55300
  16.3 2.1 %copy-start.3 = (f32[512]{0:T(512)S(1)}, f32[512]{0:T(512)}, u32[]{:S(2)}) copy-start(f32[512]{0:T(512)} %param.12) | copy-start | bytes 6148
  16.6 11.3 %collective-permute-start.6 = (f32[6,4096]{1,0:T(8,128)S(1)}, f32[6,4096]{1,0:T(8,128)S(1)}, u32[]{:S(2)}, u32[]{:S(2)}) collective-permute-start(f32[6,4096]{1,0:T(8,128)S(1)} %reshape.994), channel_id=1, source_target_pairs={{0,1},{1,2},{2,3},{3,0},{4,5},{5,6},{6,7},{7,4},{8,9},{9,10},{10,1... | collective-permute-start | bytes 294920 | tf_op jit(solution)/shard_map/ppermute | solution.py:108
  16.6 11.3 %collective-permute-start.7 = (f32[6,4096]{1,0:T(8,128)S(1)}, f32[6,4096]{1,0:T(8,128)S(1)}, u32[]{:S(2)}, u32[]{:S(2)}) collective-permute-start(f32[6,4096]{1,0:T(8,128)S(1)} %reshape.994), channel_id=1, source_target_pairs={{0,2},{1,3},{2,0},{3,1},{4,6},{5,7},{6,4},{7,5},{8,10},{9,11},{10,... | collective-permute-start | bytes 294920 | tf_op jit(solution)/shard_map/ppermute | solution.py:108
  19.2 1.0 copy-start
  22.6 3.7 %collective-permute-start.9 = (f32[3,4096]{1,0:T(4,128)S(1)}, f32[3,4096]{1,0:T(4,128)S(1)}, u32[]{:S(2)}, u32[]{:S(2)}) collective-permute-start(f32[3,4096]{1,0:T(4,128)S(1)} %reshape.996), channel_id=1, source_target_pairs={{0,1},{1,2},{2,3},{3,0},{4,5},{5,6},{6,7},{7,4},{8,9},{9,10},{10,1... | collective-permute-start | bytes 147464 | tf_op jit(solution)/shard_map/ppermute | solution.py:108
  23.0 4.8 %collective-permute-start.10 = (f32[3,4096]{1,0:T(4,128)S(1)}, f32[3,4096]{1,0:T(4,128)S(1)}, u32[]{:S(2)}, u32[]{:S(2)}) collective-permute-start(f32[3,4096]{1,0:T(4,128)S(1)} %reshape.996), channel_id=1, source_target_pairs={{0,2},{1,3},{2,0},{3,1},{4,6},{5,7},{6,4},{7,5},{8,10},{9,11},{10,... | collective-permute-start | bytes 147464 | tf_op jit(solution)/shard_map/ppermute | solution.py:108
  24.5 3.3 %collective-permute-start.11 = (f32[3,4096]{1,0:T(4,128)S(1)}, f32[3,4096]{1,0:T(4,128)S(1)}, u32[]{:S(2)}, u32[]{:S(2)}) collective-permute-start(f32[3,4096]{1,0:T(4,128)S(1)} %reshape.996), channel_id=1, source_target_pairs={{0,3},{1,0},{2,1},{3,2},{4,7},{5,4},{6,5},{7,6},{8,11},{9,8},{10,9... | collective-permute-start | bytes 147464 | tf_op jit(solution)/shard_map/ppermute | solution.py:108
  25.0 4.2 %copy-start.5 = (f32[4096]{0:T(1024)S(1)}, f32[4096]{0:T(1024)}, u32[]{:S(2)}) copy-start(f32[4096]{0:T(1024)} %param.11) | copy-start | bytes 49156
  26.4 2.5 %collective-permute-start.8 = (f32[6,4096]{1,0:T(8,128)S(1)}, f32[6,4096]{1,0:T(8,128)S(1)}, u32[]{:S(2)}, u32[]{:S(2)}) collective-permute-start(f32[6,4096]{1,0:T(8,128)S(1)} %reshape.994), channel_id=1, source_target_pairs={{0,3},{1,0},{2,1},{3,2},{4,7},{5,4},{6,5},{7,6},{8,11},{9,8},{10,9... | collective-permute-start | bytes 294920 | tf_op jit(solution)/shard_map/ppermute | solution.py:108
  33.5 6.2 %collective-permute-start.12 = (f32[9,512]{1,0:T(8,128)S(1)}, f32[9,512]{1,0:T(8,128)S(1)}, u32[]{:S(2)}, u32[]{:S(2)}) collective-permute-start(f32[9,512]{1,0:T(8,128)S(1)} %reshape.1001), channel_id=1, source_target_pairs={{0,4},{4,8},{8,12},{12,0},{1,5},{5,9},{9,13},{13,1},{2,6},{6,10},{... | collective-permute-start | bytes 55304 | tf_op jit(solution)/shard_map/ppermute | solution.py:108
  34.2 6.5 %collective-permute-start.13 = (f32[9,512]{1,0:T(8,128)S(1)}, f32[9,512]{1,0:T(8,128)S(1)}, u32[]{:S(2)}, u32[]{:S(2)}) collective-permute-start(f32[9,512]{1,0:T(8,128)S(1)} %reshape.1001), channel_id=1, source_target_pairs={{0,8},{4,12},{8,0},{12,4},{1,9},{5,13},{9,1},{13,5},{2,10},{6,14},... | collective-permute-start | bytes 55304 | tf_op jit(solution)/shard_map/ppermute | solution.py:108
  34.5 6.1 %collective-permute-start.14 = (f32[9,512]{1,0:T(8,128)S(1)}, f32[9,512]{1,0:T(8,128)S(1)}, u32[]{:S(2)}, u32[]{:S(2)}) collective-permute-start(f32[9,512]{1,0:T(8,128)S(1)} %reshape.1001), channel_id=1, source_target_pairs={{0,12},{4,0},{8,4},{12,8},{1,13},{5,1},{9,5},{13,9},{2,14},{6,2},{... | collective-permute-start | bytes 55304 | tf_op jit(solution)/shard_map/ppermute | solution.py:108
  41.3 3.5 %collective-permute-start.15 = (f32[]{:T(128)}, f32[]{:T(128)}, u32[]{:S(2)}, u32[]{:S(2)}) collective-permute-start(f32[]{:T(128)} %get-tuple-element.8), channel_id=1, source_target_pairs={{0,1},{1,2},{2,3},{3,0},{4,5},{5,6},{6,7},{7,4},{8,9},{9,10},{10,1... | collective-permute-start | bytes 20 | tf_op jit(solution)/shard_map/ppermute | solution.py:108
  41.3 5.0 %collective-permute-start.16 = (f32[]{:T(128)}, f32[]{:T(128)}, u32[]{:S(2)}, u32[]{:S(2)}) collective-permute-start(f32[]{:T(128)} %get-tuple-element.8), channel_id=1, source_target_pairs={{0,2},{1,3},{2,0},{3,1},{4,6},{5,7},{6,4},{7,5},{8,10},{9,11},{10,... | collective-permute-start | bytes 20 | tf_op jit(solution)/shard_map/ppermute | solution.py:108
  42.1 4.2 %collective-permute-start.17 = (f32[]{:T(128)}, f32[]{:T(128)}, u32[]{:S(2)}, u32[]{:S(2)}) collective-permute-start(f32[]{:T(128)} %get-tuple-element.8), channel_id=1, source_target_pairs={{0,3},{1,0},{2,1},{3,2},{4,7},{5,4},{6,5},{7,6},{8,11},{9,8},{10,9... | collective-permute-start | bytes 20 | tf_op jit(solution)/shard_map/ppermute | solution.py:108
  43.4 6.1 %collective-permute-start.3 = (f32[]{:T(128)}, f32[]{:T(128)}, u32[]{:S(2)}, u32[]{:S(2)}) collective-permute-start(f32[]{:T(128)} %get-tuple-element.9), channel_id=1, source_target_pairs={{0,1},{1,2},{2,3},{3,0},{4,5},{5,6},{6,7},{7,4},{8,9},{9,10},{10,1... | collective-permute-start | bytes 20 | tf_op jit(solution)/shard_map/ppermute | solution.py:108
  43.4 6.1 %collective-permute-start.4 = (f32[]{:T(128)}, f32[]{:T(128)}, u32[]{:S(2)}, u32[]{:S(2)}) collective-permute-start(f32[]{:T(128)} %get-tuple-element.9), channel_id=1, source_target_pairs={{0,2},{1,3},{2,0},{3,1},{4,6},{5,7},{6,4},{7,5},{8,10},{9,11},{10,... | collective-permute-start | bytes 20 | tf_op jit(solution)/shard_map/ppermute | solution.py:108
  44.8 4.7 %collective-permute-start.5 = (f32[]{:T(128)}, f32[]{:T(128)}, u32[]{:S(2)}, u32[]{:S(2)}) collective-permute-start(f32[]{:T(128)} %get-tuple-element.9), channel_id=1, source_target_pairs={{0,3},{1,0},{2,1},{3,2},{4,7},{5,4},{6,5},{7,6},{8,11},{9,8},{10,9... | collective-permute-start | bytes 20 | tf_op jit(solution)/shard_map/ppermute | solution.py:108
  58.5 3.2 %collective-permute-start.18 = (f32[]{:T(128)}, f32[]{:T(128)}, u32[]{:S(2)}, u32[]{:S(2)}) collective-permute-start(f32[]{:T(128)} %get-tuple-element.17), channel_id=1, source_target_pairs={{0,1},{1,2},{2,3},{3,0},{4,5},{5,6},{6,7},{7,4},{8,9},{9,10},{10,1... | collective-permute-start | bytes 20 | tf_op jit(solution)/shard_map/ppermute | solution.py:108
  58.6 3.8 %collective-permute-start.19 = (f32[]{:T(128)}, f32[]{:T(128)}, u32[]{:S(2)}, u32[]{:S(2)}) collective-permute-start(f32[]{:T(128)} %get-tuple-element.17), channel_id=1, source_target_pairs={{0,2},{1,3},{2,0},{3,1},{4,6},{5,7},{6,4},{7,5},{8,10},{9,11},{10,... | collective-permute-start | bytes 20 | tf_op jit(solution)/shard_map/ppermute | solution.py:108
  59.2 3.2 %collective-permute-start.20 = (f32[]{:T(128)}, f32[]{:T(128)}, u32[]{:S(2)}, u32[]{:S(2)}) collective-permute-start(f32[]{:T(128)} %get-tuple-element.17), channel_id=1, source_target_pairs={{0,3},{1,0},{2,1},{3,2},{4,7},{5,4},{6,5},{7,6},{8,11},{9,8},{10,9... | collective-permute-start | bytes 20 | tf_op jit(solution)/shard_map/ppermute | solution.py:108
  71.9 3.7 %collective-permute-start.21 = (f32[3,4096]{1,0:T(4,128)S(1)}, f32[3,4096]{1,0:T(4,128)S(1)}, u32[]{:S(2)}, u32[]{:S(2)}) collective-permute-start(f32[3,4096]{1,0:T(4,128)S(1)} %reshape.1006), channel_id=1, source_target_pairs={{0,1},{1,2},{2,3},{3,0},{4,5},{5,6},{6,7},{7,4},{8,9},{9,10},{10,1... | collective-permute-start | bytes 147464 | tf_op jit(solution)/shard_map/ppermute | solution.py:108
  73.2 4.3 %collective-permute-start.22 = (f32[3,4096]{1,0:T(4,128)S(1)}, f32[3,4096]{1,0:T(4,128)S(1)}, u32[]{:S(2)}, u32[]{:S(2)}) collective-permute-start(f32[3,4096]{1,0:T(4,128)S(1)} %reshape.1006), channel_id=1, source_target_pairs={{0,2},{1,3},{2,0},{3,1},{4,6},{5,7},{6,4},{7,5},{8,10},{9,11},{10,... | collective-permute-start | bytes 147464 | tf_op jit(solution)/shard_map/ppermute | solution.py:108
  73.8 3.6 %collective-permute-start.23 = (f32[3,4096]{1,0:T(4,128)S(1)}, f32[3,4096]{1,0:T(4,128)S(1)}, u32[]{:S(2)}, u32[]{:S(2)}) collective-permute-start(f32[3,4096]{1,0:T(4,128)S(1)} %reshape.1006), channel_id=1, source_target_pairs={{0,3},{1,0},{2,1},{3,2},{4,7},{5,4},{6,5},{7,6},{8,11},{9,8},{10,9... | collective-permute-start | bytes 147464 | tf_op jit(solution)/shard_map/ppermute | solution.py:108
  81.2 6.2 %collective-permute-start.24 = (f32[9,512]{1,0:T(8,128)S(1)}, f32[9,512]{1,0:T(8,128)S(1)}, u32[]{:S(2)}, u32[]{:S(2)}) collective-permute-start(f32[9,512]{1,0:T(8,128)S(1)} %reshape.1011), channel_id=1, source_target_pairs={{0,4},{4,8},{8,12},{12,0},{1,5},{5,9},{9,13},{13,1},{2,6},{6,10},{... | collective-permute-start | bytes 55304 | tf_op jit(solution)/shard_map/ppermute | solution.py:108
  82.5 6.0 %collective-permute-start.25 = (f32[9,512]{1,0:T(8,128)S(1)}, f32[9,512]{1,0:T(8,128)S(1)}, u32[]{:S(2)}, u32[]{:S(2)}) collective-permute-start(f32[9,512]{1,0:T(8,128)S(1)} %reshape.1011), channel_id=1, source_target_pairs={{0,8},{4,12},{8,0},{12,4},{1,9},{5,13},{9,1},{13,5},{2,10},{6,14},... | collective-permute-start | bytes 55304 | tf_op jit(solution)/shard_map/ppermute | solution.py:108
  84.4 4.3 %collective-permute-start.26 = (f32[9,512]{1,0:T(8,128)S(1)}, f32[9,512]{1,0:T(8,128)S(1)}, u32[]{:S(2)}, u32[]{:S(2)}) collective-permute-start(f32[9,512]{1,0:T(8,128)S(1)} %reshape.1011), channel_id=1, source_target_pairs={{0,12},{4,0},{8,4},{12,8},{1,13},{5,1},{9,5},{13,9},{2,14},{6,2},{... | collective-permute-start | bytes 55304 | tf_op jit(solution)/shard_map/ppermute | solution.py:108
  89.3 3.2 %collective-permute-start.27 = (f32[]{:T(128)}, f32[]{:T(128)}, u32[]{:S(2)}, u32[]{:S(2)}) collective-permute-start(f32[]{:T(128)} %get-tuple-element.15), channel_id=1, source_target_pairs={{0,1},{1,2},{2,3},{3,0},{4,5},{5,6},{6,7},{7,4},{8,9},{9,10},{10,1... | collective-permute-start | bytes 20 | tf_op jit(solution)/shard_map/ppermute | solution.py:108
  89.3 3.8 %collective-permute-start.28 = (f32[]{:T(128)}, f32[]{:T(128)}, u32[]{:S(2)}, u32[]{:S(2)}) collective-permute-start(f32[]{:T(128)} %get-tuple-element.15), channel_id=1, source_target_pairs={{0,2},{1,3},{2,0},{3,1},{4,6},{5,7},{6,4},{7,5},{8,10},{9,11},{10,... | collective-permute-start | bytes 20 | tf_op jit(solution)/shard_map/ppermute | solution.py:108
  90.0 3.1 %collective-permute-start.29 = (f32[]{:T(128)}, f32[]{:T(128)}, u32[]{:S(2)}, u32[]{:S(2)}) collective-permute-start(f32[]{:T(128)} %get-tuple-element.15), channel_id=1, source_target_pairs={{0,3},{1,0},{2,1},{3,2},{4,7},{5,4},{6,5},{7,6},{8,11},{9,8},{10,9... | collective-permute-start | bytes 20 | tf_op jit(solution)/shard_map/ppermute | solution.py:108
  99.6 3.1 %collective-permute-start.30 = (f32[]{:T(128)}, f32[]{:T(128)}, u32[]{:S(2)}, u32[]{:S(2)}) collective-permute-start(f32[]{:T(128)} %get-tuple-element.12), channel_id=1, source_target_pairs={{0,1},{1,2},{2,3},{3,0},{4,5},{5,6},{6,7},{7,4},{8,9},{9,10},{10,1... | collective-permute-start | bytes 20 | tf_op jit(solution)/shard_map/ppermute | solution.py:108
  100.9 3.8 %collective-permute-start.31 = (f32[]{:T(128)}, f32[]{:T(128)}, u32[]{:S(2)}, u32[]{:S(2)}) collective-permute-start(f32[]{:T(128)} %get-tuple-element.12), channel_id=1, source_target_pairs={{0,2},{1,3},{2,0},{3,1},{4,6},{5,7},{6,4},{7,5},{8,10},{9,11},{10,... | collective-permute-start | bytes 20 | tf_op jit(solution)/shard_map/ppermute | solution.py:108
  101.6 3.1 %collective-permute-start.32 = (f32[]{:T(128)}, f32[]{:T(128)}, u32[]{:S(2)}, u32[]{:S(2)}) collective-permute-start(f32[]{:T(128)} %get-tuple-element.12), channel_id=1, source_target_pairs={{0,3},{1,0},{2,1},{3,2},{4,7},{5,4},{6,5},{7,6},{8,11},{9,8},{10,9... | collective-permute-start | bytes 20 | tf_op jit(solution)/shard_map/ppermute | solution.py:108
  114.1 3.8 %collective-permute-start.33 = (f32[3,4096]{1,0:T(4,128)S(1)}, f32[3,4096]{1,0:T(4,128)S(1)}, u32[]{:S(2)}, u32[]{:S(2)}) collective-permute-start(f32[3,4096]{1,0:T(4,128)S(1)} %reshape.1016), channel_id=1, source_target_pairs={{0,1},{1,2},{2,3},{3,0},{4,5},{5,6},{6,7},{7,4},{8,9},{9,10},{10,1... | collective-permute-start | bytes 147464 | tf_op jit(solution)/shard_map/ppermute | solution.py:108
  114.2 5.0 %collective-permute-start.34 = (f32[3,4096]{1,0:T(4,128)S(1)}, f32[3,4096]{1,0:T(4,128)S(1)}, u32[]{:S(2)}, u32[]{:S(2)}) collective-permute-start(f32[3,4096]{1,0:T(4,128)S(1)} %reshape.1016), channel_id=1, source_target_pairs={{0,2},{1,3},{2,0},{3,1},{4,6},{5,7},{6,4},{7,5},{8,10},{9,11},{10,... | collective-permute-start | bytes 147464 | tf_op jit(solution)/shard_map/ppermute | solution.py:108
  115.2 4.0 %collective-permute-start.35 = (f32[3,4096]{1,0:T(4,128)S(1)}, f32[3,4096]{1,0:T(4,128)S(1)}, u32[]{:S(2)}, u32[]{:S(2)}) collective-permute-start(f32[3,4096]{1,0:T(4,128)S(1)} %reshape.1016), channel_id=1, source_target_pairs={{0,3},{1,0},{2,1},{3,2},{4,7},{5,4},{6,5},{7,6},{8,11},{9,8},{10,9... | collective-permute-start | bytes 147464 | tf_op jit(solution)/shard_map/ppermute | solution.py:108
  123.0 6.2 %collective-permute-start.36 = (f32[9,512]{1,0:T(8,128)S(1)}, f32[9,512]{1,0:T(8,128)S(1)}, u32[]{:S(2)}, u32[]{:S(2)}) collective-permute-start(f32[9,512]{1,0:T(8,128)S(1)} %reshape.1021), channel_id=1, source_target_pairs={{0,4},{4,8},{8,12},{12,0},{1,5},{5,9},{9,13},{13,1},{2,6},{6,10},{... | collective-permute-start | bytes 55304 | tf_op jit(solution)/shard_map/ppermute | solution.py:108
  124.0 6.1 %collective-permute-start.37 = (f32[9,512]{1,0:T(8,128)S(1)}, f32[9,512]{1,0:T(8,128)S(1)}, u32[]{:S(2)}, u32[]{:S(2)}) collective-permute-start(f32[9,512]{1,0:T(8,128)S(1)} %reshape.1021), channel_id=1, source_target_pairs={{0,8},{4,12},{8,0},{12,4},{1,9},{5,13},{9,1},{13,5},{2,10},{6,14},... | collective-permute-start | bytes 55304 | tf_op jit(solution)/shard_map/ppermute | solution.py:108
  126.0 4.1 %collective-permute-start.38 = (f32[9,512]{1,0:T(8,128)S(1)}, f32[9,512]{1,0:T(8,128)S(1)}, u32[]{:S(2)}, u32[]{:S(2)}) collective-permute-start(f32[9,512]{1,0:T(8,128)S(1)} %reshape.1021), channel_id=1, source_target_pairs={{0,12},{4,0},{8,4},{12,8},{1,13},{5,1},{9,5},{13,9},{2,14},{6,2},{... | collective-permute-start | bytes 55304 | tf_op jit(solution)/shard_map/ppermute | solution.py:108
  130.8 3.1 %collective-permute-start.39 = (f32[]{:T(128)}, f32[]{:T(128)}, u32[]{:S(2)}, u32[]{:S(2)}) collective-permute-start(f32[]{:T(128)} %get-tuple-element.10), channel_id=1, source_target_pairs={{0,1},{1,2},{2,3},{3,0},{4,5},{5,6},{6,7},{7,4},{8,9},{9,10},{10,1... | collective-permute-start | bytes 20 | tf_op jit(solution)/shard_map/ppermute | solution.py:108
  130.8 3.8 %collective-permute-start.40 = (f32[]{:T(128)}, f32[]{:T(128)}, u32[]{:S(2)}, u32[]{:S(2)}) collective-permute-start(f32[]{:T(128)} %get-tuple-element.10), channel_id=1, source_target_pairs={{0,2},{1,3},{2,0},{3,1},{4,6},{5,7},{6,4},{7,5},{8,10},{9,11},{10,... | collective-permute-start | bytes 20 | tf_op jit(solution)/shard_map/ppermute | solution.py:108
  131.7 2.9 %collective-permute-start.41 = (f32[]{:T(128)}, f32[]{:T(128)}, u32[]{:S(2)}, u32[]{:S(2)}) collective-permute-start(f32[]{:T(128)} %get-tuple-element.10), channel_id=1, source_target_pairs={{0,3},{1,0},{2,1},{3,2},{4,7},{5,4},{6,5},{7,6},{8,11},{9,8},{10,9... | collective-permute-start | bytes 20 | tf_op jit(solution)/shard_map/ppermute | solution.py:108

commit v4 on v2

--- a/solution.py
+++ b/solution.py
@@ -102,6 +102,11 @@
 
 def allsum(value, axis):
     size = SIZES[axis]
+    if size == 4:
+        peers = [
+            lax.ppermute(value, axis, [(i, i ^ mask) for i in range(size)]) for mask in (1, 2, 3)
+        ]
+        return (value + peers[0]) + (peers[1] + peers[2])
     if size & (size - 1):
         return lax.psum(value, axis)
     step = 1

time: 130 us -> 126 us (0.969)
  waiting for transfers between devices: 48 us -> 32.2 us
  starting transfers between devices: 31.8 us -> 39.8 us
  between operations: 13.6 us -> 16.9 us
    ppermute x28 -> x42, waiting for transfers between devices: 48 us -> 32.2 us  [allsum(): lax.ppermute(value, axis, [(i, i ^ mask) for i in range(size)])]
    ppermute x28 -> x42, starting transfers between devices: 31.8 us -> 39.8 us  [allsum(): lax.ppermute(value, axis, [(i, i ^ mask) for i in range(size)])]
  transfers between devices with their start and end apart: 28 -> 42, of which waited for: 24 -> 15; matrix products, arithmetic and copies ran while one was open for 7% -> 7% of each run, Pallas kernels for 0% -> 0%
where the time goes in v4:
time: 126 us
  starting transfers between devices  39.8 us (32%)
  waiting for transfers between devices  32.2 us (26%)
  other arithmetic  17.8 us (14%)
  between operations  16.9 us (13%)
  matrix products  15.2 us (12%)
  local copies, waits for them, and re-layouts  3.65 us (3%)
    ppermute x42, starting transfers between devices, allsum(): lax.ppermute(value, axis, [(i, i ^ mask) for i in range(size)])  39.8 us
    ppermute x42, waiting for transfers between devices, allsum(): lax.ppermute(value, axis, [(i, i ^ mask) for i in range(size)])  32.2 us
    dot_general x8, matrix products, segsum(): lax.dot_general(self.hot3, spread, (((1,), (1,)), ((), ())), preferred_el...  11.8 us
    select_n x8, other arithmetic, segsum(): jnp.where(self.low[None], part[:, None, :], jnp.zeros((), BF))  3.87 us
    dot_general x6, matrix products, gather(): lax.dot_general(stacked, self.hot3t, (((1,), (0,)), ((), ())), preferred_...  3.41 us
    reduce_sum x6, other arithmetic, gather(): return jnp.sum(jnp.where(self.low[None], spread, 0.0), axis=1)  2.61 us
  transfers between devices with their start and end apart: 42, of which 15 were waited for; matrix products, arithmetic and copies ran while one was open for 7% of the time, Pallas kernels for 0%

profile of v4, /device:TPU:0, one launch (start us, length us, event | category | flops | bytes accessed | tf_op | source)
XLA Modules:
  0.0 125.6 jit_solution(13698412994482476285)
XLA Ops:
  0.6 0.7 add_select_fusion.3
  1.4 1.4 %multiply_reduce_fusion.6 = f32[9,4096]{1,0:T(8,128)S(1)} fusion(f32[2,9,4096]{2,0,1:T(2,128)} %param.7), kind=kLoop, calls=%fused_computation.115 | loop fusion | flops 110592 | bytes 442368 | tf_op jit(solution)/shard_map/reduce_sum | solution.py:130
  3.3 1.1 fusion.24
  4.6 3.1 %collective-permute-start = (f32[9,512]{1,0:T(8,128)S(1)}, f32[9,512]{1,0:T(8,128)S(1)}, u32[]{:S(2)}, u32[]{:S(2)}) collective-permute-start(f32[9,512]{1,0:T(8,128)S(1)} %reshape.948), channel_id=1, source_target_pairs={{0,4},{4,0},{8,12},{12,8},{1,5},{5,1},{9,13},{13,9},{2,6},{6,2},{1... | collective-permute-start | bytes 55304 | tf_op jit(solution)/shard_map/ppermute | solution.py:107
  7.7 2.6 %collective-permute-start.1 = (f32[9,512]{1,0:T(8,128)S(1)}, f32[9,512]{1,0:T(8,128)S(1)}, u32[]{:S(2)}, u32[]{:S(2)}) collective-permute-start(f32[9,512]{1,0:T(8,128)S(1)} %reshape.948), channel_id=1, source_target_pairs={{0,8},{4,12},{8,0},{12,4},{1,9},{5,13},{9,1},{13,5},{2,10},{6,14},... | collective-permute-start | bytes 55304 | tf_op jit(solution)/shard_map/ppermute | solution.py:107
  11.0 0.9 broadcast_select_fusion.2
  12.0 3.0 %fusion = f32[64,384]{1,0:T(8,128)S(1)} fusion(bf16[384,4096]{1,0:T(8,128)(2,1)S(1)} %bitcast.142, bf16[384,4096]{1,0:T(8,128)(2,1)S(1)} %bitcast.141, bf16[384,4096]{1,0:T(8,128)(2,1)S(1)} %bitcast.140, bf16[64,4096]{1,0:T(8,128)(2,1)S(1)} %get-tuple-element.110), kind=kOutput, calls=%fused_computation | convolution fusion | flops 637009920 | bytes 10059776 | tf_op jit(solution)/shard_map/dot_general | solution.py:46
  15.3 1.8 %collective-permute-start.7 = (f32[6,4096]{1,0:T(8,128)S(1)}, f32[6,4096]{1,0:T(8,128)S(1)}, u32[]{:S(2)}, u32[]{:S(2)}) collective-permute-start(f32[6,4096]{1,0:T(8,128)S(1)} %reshape.953), channel_id=1, source_target_pairs={{0,2},{1,3},{2,0},{3,1},{4,6},{5,7},{6,4},{7,5},{8,10},{9,11},{10,... | collective-permute-start | bytes 294920 | tf_op jit(solution)/shard_map/ppermute | solution.py:107
  19.7 1.4 %fusion.6 = f32[64,192]{0,1:T(8,128)S(1)} fusion(bf16[192,4096]{1,0:T(8,128)(2,1)S(1)} %bitcast.145, bf16[192,4096]{1,0:T(8,128)(2,1)S(1)} %bitcast.144, bf16[192,4096]{1,0:T(8,128)(2,1)S(1)} %bitcast.143, bf16[64,4096]{1,0:T(8,128)(2,1)S(1)} %get-tuple-element.110), kind=kOutput, calls=%fused_computation.6 | convolution fusion | flops 320864256 | bytes 5292032 | tf_op jit(solution)/shard_map/dot_general | solution.py:46
  21.8 1.1 collective-permute-start.11
  22.9 0.6 collective-permute-start.9
  23.5 2.7 %collective-permute-done.10 = f32[3,4096]{1,0:T(4,128)S(1)} collective-permute-done((f32[3,4096]{1,0:T(4,128)S(1)}, f32[3,4096]{1,0:T(4,128)S(1)}, u32[]{:S(2)}, u32[]{:S(2)}) %collective-permute-start.10) | collective-permute-done | bytes 49184 | tf_op jit(solution)/shard_map/ppermute | solution.py:107
  26.3 4.3 %collective-permute-done.8 = f32[6,4096]{1,0:T(8,128)S(1)} collective-permute-done((f32[6,4096]{1,0:T(8,128)S(1)}, f32[6,4096]{1,0:T(8,128)S(1)}, u32[]{:S(2)}, u32[]{:S(2)}) %collective-permute-start.8) | collective-permute-done | bytes 98336 | tf_op jit(solution)/shard_map/ppermute | solution.py:107
  31.9 0.6 fusion.51
  33.0 0.6 multiply_reduce_fusion.4
  34.1 1.1 fusion.30
  35.3 0.8 collective-permute-start.12
  36.2 3.5 %collective-permute-start.13 = (f32[9,512]{1,0:T(8,128)S(1)}, f32[9,512]{1,0:T(8,128)S(1)}, u32[]{:S(2)}, u32[]{:S(2)}) collective-permute-start(f32[9,512]{1,0:T(8,128)S(1)} %reshape.960), channel_id=1, source_target_pairs={{0,8},{4,12},{8,0},{12,4},{1,9},{5,13},{9,1},{13,5},{2,10},{6,14},... | collective-permute-start | bytes 55304 | tf_op jit(solution)/shard_map/ppermute | solution.py:107
  39.8 2.5 %collective-permute-done.13 = f32[9,512]{1,0:T(8,128)S(1)} collective-permute-done((f32[9,512]{1,0:T(8,128)S(1)}, f32[9,512]{1,0:T(8,128)S(1)}, u32[]{:S(2)}, u32[]{:S(2)}) %collective-permute-start.13) | collective-permute-done | bytes 18464 | tf_op jit(solution)/shard_map/ppermute | solution.py:107
  42.3 3.1 %collective-permute-done.14 = f32[9,512]{1,0:T(8,128)S(1)} collective-permute-done((f32[9,512]{1,0:T(8,128)S(1)}, f32[9,512]{1,0:T(8,128)S(1)}, u32[]{:S(2)}, u32[]{:S(2)}) %collective-permute-start.14) | collective-permute-done | bytes 18464 | tf_op jit(solution)/shard_map/ppermute | solution.py:107
  45.4 0.6 multiply_reduce_fusion.20
  46.0 0.6 collective-permute-start.16
  46.6 1.6 %collective-permute-start.15 = (f32[]{:T(128)}, f32[]{:T(128)}, u32[]{:S(2)}, u32[]{:S(2)}) collective-permute-start(f32[]{:T(128)} %get-tuple-element.8), channel_id=1, source_target_pairs={{0,1},{1,0},{2,3},{3,2},{4,5},{5,4},{6,7},{7,6},{8,9},{9,8},{10,11... | collective-permute-start | bytes 20 | tf_op jit(solution)/shard_map/ppermute | solution.py:107
  48.1 0.6 collective-permute-start.4
  48.7 0.8 collective-permute-start.5
  49.5 0.8 collective-permute-start.3
  55.4 0.6 multiply_reduce_fusion.19
  56.0 0.6 collective-permute-start.19
  56.6 0.8 collective-permute-start.20
  57.4 0.8 collective-permute-start.18
  58.2 1.1 collective-permute-done.18
  63.9 1.4 %fusion.12 = f32[64,192]{0,1:T(8,128)S(1)} fusion(bf16[192,4096]{1,0:T(8,128)(2,1)S(1)} %bitcast.148, bf16[192,4096]{1,0:T(8,128)(2,1)S(1)} %bitcast.147, bf16[192,4096]{1,0:T(8,128)(2,1)S(1)} %bitcast.146, bf16[64,4096]{1,0:T(8,128)(2,1)S(1)} %get-tuple-element.110), kind=kOutput, calls=%fused_computation.12 | convolution fusion | flops 320864256 | bytes 5292032 | tf_op jit(solution)/shard_map/dot_general | solution.py:46
  66.0 0.6 collective-permute-start.22
  66.5 0.9 collective-permute-start.23
  67.5 3.4 %collective-permute-done.22 = f32[3,4096]{1,0:T(4,128)S(1)} collective-permute-done((f32[3,4096]{1,0:T(4,128)S(1)}, f32[3,4096]{1,0:T(4,128)S(1)}, u32[]{:S(2)}, u32[]{:S(2)}) %collective-permute-start.22) | collective-permute-done | bytes 49184 | tf_op jit(solution)/shard_map/ppermute | solution.py:107
  71.4 0.6 fusion.50
  73.4 1.1 fusion.36
  74.8 1.0 collective-permute-start.25
  75.7 3.4 %collective-permute-start.26 = (f32[9,512]{1,0:T(8,128)S(1)}, f32[9,512]{1,0:T(8,128)S(1)}, u32[]{:S(2)}, u32[]{:S(2)}) collective-permute-start(f32[9,512]{1,0:T(8,128)S(1)} %reshape.970), channel_id=1, source_target_pairs={{0,12},{4,8},{8,4},{12,0},{1,13},{5,9},{9,5},{13,1},{2,14},{6,10},... | collective-permute-start | bytes 55304 | tf_op jit(solution)/shard_map/ppermute | solution.py:107
  79.1 0.8 collective-permute-done.25
  79.9 1.6 %collective-permute-done.26 = f32[9,512]{1,0:T(8,128)S(1)} collective-permute-done((f32[9,512]{1,0:T(8,128)S(1)}, f32[9,512]{1,0:T(8,128)S(1)}, u32[]{:S(2)}, u32[]{:S(2)}) %collective-permute-start.26) | collective-permute-done | bytes 18464 | tf_op jit(solution)/shard_map/ppermute | solution.py:107
  81.5 0.6 multiply_reduce_fusion.18
  82.1 1.3 %collective-permute-start.28 = (f32[]{:T(128)}, f32[]{:T(128)}, u32[]{:S(2)}, u32[]{:S(2)}) collective-permute-start(f32[]{:T(128)} %get-tuple-element.15), channel_id=1, source_target_pairs={{0,2},{1,3},{2,0},{3,1},{4,6},{5,7},{6,4},{7,5},{8,10},{9,11},{10,... | collective-permute-start | bytes 20 | tf_op jit(solution)/shard_map/ppermute | solution.py:107
  83.4 0.8 collective-permute-start.27
  84.2 1.1 collective-permute-done.27
  87.9 0.6 multiply_reduce_fusion.17
  88.5 1.3 %collective-permute-start.31 = (f32[]{:T(128)}, f32[]{:T(128)}, u32[]{:S(2)}, u32[]{:S(2)}) collective-permute-start(f32[]{:T(128)} %get-tuple-element.12), channel_id=1, source_target_pairs={{0,2},{1,3},{2,0},{3,1},{4,6},{5,7},{6,4},{7,5},{8,10},{9,11},{10,... | collective-permute-start | bytes 20 | tf_op jit(solution)/shard_map/ppermute | solution.py:107
  90.7 1.1 collective-permute-done.30
  96.4 1.7 %fusion.18 = f32[64,192]{0,1:T(8,128)S(1)} fusion(bf16[192,4096]{1,0:T(8,128)(2,1)S(1)} %bitcast.151, bf16[192,4096]{1,0:T(8,128)(2,1)S(1)} %bitcast.150, bf16[192,4096]{1,0:T(8,128)(2,1)S(1)} %bitcast.149, bf16[64,4096]{1,0:T(8,128)(2,1)S(1)} %get-tuple-element.110), kind=kOutput, calls=%fused_computation.18 | convolution fusion | flops 320864256 | bytes 5292032 | tf_op jit(solution)/shard_map/dot_general | solution.py:46
  98.7 1.3 %collective-permute-start.34 = (f32[3,4096]{1,0:T(4,128)S(1)}, f32[3,4096]{1,0:T(4,128)S(1)}, u32[]{:S(2)}, u32[]{:S(2)}) collective-permute-start(f32[3,4096]{1,0:T(4,128)S(1)} %reshape.975), channel_id=1, source_target_pairs={{0,2},{1,3},{2,0},{3,1},{4,6},{5,7},{6,4},{7,5},{8,10},{9,11},{10,... | collective-permute-start | bytes 147464 | tf_op jit(solution)/shard_map/ppermute | solution.py:107
  100.2 2.7 %collective-permute-done.34 = f32[3,4096]{1,0:T(4,128)S(1)} collective-permute-done((f32[3,4096]{1,0:T(4,128)S(1)}, f32[3,4096]{1,0:T(4,128)S(1)}, u32[]{:S(2)}, u32[]{:S(2)}) %collective-permute-start.34) | collective-permute-done | bytes 49184 | tf_op jit(solution)/shard_map/ppermute | solution.py:107
  102.9 1.3 %collective-permute-done.35 = f32[3,4096]{1,0:T(4,128)S(1)} collective-permute-done((f32[3,4096]{1,0:T(4,128)S(1)}, f32[3,4096]{1,0:T(4,128)S(1)}, u32[]{:S(2)}, u32[]{:S(2)}) %collective-permute-start.35) | collective-permute-done | bytes 49184 | tf_op jit(solution)/shard_map/ppermute | solution.py:107
  104.7 0.6 fusion.49
  106.8 1.1 fusion.42
  108.1 0.7 collective-permute-start.36
  108.8 3.4 %collective-permute-start.37 = (f32[9,512]{1,0:T(8,128)S(1)}, f32[9,512]{1,0:T(8,128)S(1)}, u32[]{:S(2)}, u32[]{:S(2)}) collective-permute-start(f32[9,512]{1,0:T(8,128)S(1)} %reshape.980), channel_id=1, source_target_pairs={{0,8},{4,12},{8,0},{12,4},{1,9},{5,13},{9,1},{13,5},{2,10},{6,14},... | collective-permute-start | bytes 55304 | tf_op jit(solution)/shard_map/ppermute | solution.py:107
  112.5 1.5 %collective-permute-done.37 = f32[9,512]{1,0:T(8,128)S(1)} collective-permute-done((f32[9,512]{1,0:T(8,128)S(1)}, f32[9,512]{1,0:T(8,128)S(1)}, u32[]{:S(2)}, u32[]{:S(2)}) %collective-permute-start.37) | collective-permute-done | bytes 18464 | tf_op jit(solution)/shard_map/ppermute | solution.py:107
  114.0 3.8 %collective-permute-done.38 = f32[9,512]{1,0:T(8,128)S(1)} collective-permute-done((f32[9,512]{1,0:T(8,128)S(1)}, f32[9,512]{1,0:T(8,128)S(1)}, u32[]{:S(2)}, u32[]{:S(2)}) %collective-permute-start.38) | collective-permute-done | bytes 18464 | tf_op jit(solution)/shard_map/ppermute | solution.py:107
  117.9 0.6 multiply_reduce_fusion.16
  118.5 0.8 collective-permute-start.40
  119.3 1.3 %collective-permute-start.39 = (f32[]{:T(128)}, f32[]{:T(128)}, u32[]{:S(2)}, u32[]{:S(2)}) collective-permute-start(f32[]{:T(128)} %get-tuple-element.10), channel_id=1, source_target_pairs={{0,1},{1,0},{2,3},{3,2},{4,5},{5,4},{6,7},{7,6},{8,9},{9,8},{10,11... | collective-permute-start | bytes 20 | tf_op jit(solution)/shard_map/ppermute | solution.py:107
  120.6 1.1 collective-permute-done.39
  124.3 0.6 multiply_add_fusion
  124.9 0.6 multiply_subtract_fusion
  (155 shorter events, 18.2 us)
Async XLA Ops:
  3.3 7.0 %copy-start.1 = (f32[2,3,4096]{2,0,1:T(2,128)S(1)}, f32[2,3,4096]{2,0,1:T(2,128)}, u32[]{:S(2)}) copy-start(f32[2,3,4096]{2,0,1:T(2,128)} %param.8) | copy-start | bytes 294916
  3.3 7.5 %copy-start.4 = (s32[4096]{0:T(1024)S(1)}, s32[4096]{0:T(1024)}, u32[]{:S(2)}) copy-start(s32[4096]{0:T(1024)} %param.10) | copy-start | bytes 49156
  4.6 12.5 %collective-permute-start = (f32[9,512]{1,0:T(8,128)S(1)}, f32[9,512]{1,0:T(8,128)S(1)}, u32[]{:S(2)}, u32[]{:S(2)}) collective-permute-start(f32[9,512]{1,0:T(8,128)S(1)} %reshape.948), channel_id=1, source_target_pairs={{0,4},{4,0},{8,12},{12,8},{1,5},{5,1},{9,13},{13,9},{2,6},{6,2},{1... | collective-permute-start | bytes 55304 | tf_op jit(solution)/shard_map/ppermute | solution.py:107
  7.7 9.4 %collective-permute-start.1 = (f32[9,512]{1,0:T(8,128)S(1)}, f32[9,512]{1,0:T(8,128)S(1)}, u32[]{:S(2)}, u32[]{:S(2)}) collective-permute-start(f32[9,512]{1,0:T(8,128)S(1)} %reshape.948), channel_id=1, source_target_pairs={{0,8},{4,12},{8,0},{12,4},{1,9},{5,13},{9,1},{13,5},{2,10},{6,14},... | collective-permute-start | bytes 55304 | tf_op jit(solution)/shard_map/ppermute | solution.py:107
  10.3 6.8 %collective-permute-start.2 = (f32[9,512]{1,0:T(8,128)S(1)}, f32[9,512]{1,0:T(8,128)S(1)}, u32[]{:S(2)}, u32[]{:S(2)}) collective-permute-start(f32[9,512]{1,0:T(8,128)S(1)} %reshape.948), channel_id=1, source_target_pairs={{0,12},{4,8},{8,4},{12,0},{1,13},{5,9},{9,5},{13,1},{2,14},{6,10},... | collective-permute-start | bytes 55304 | tf_op jit(solution)/shard_map/ppermute | solution.py:107
  11.9 5.2 %copy-start.2 = (f32[9,512]{1,0:T(8,128)S(1)}, f32[9,512]{1,0:T(8,128)}, u32[]{:S(2)}) copy-start(f32[9,512]{1,0:T(8,128)} %param.13) | copy-start | bytes 55300
  12.0 5.2 %copy-start.3 = (f32[512]{0:T(512)S(1)}, f32[512]{0:T(512)}, u32[]{:S(2)}) copy-start(f32[512]{0:T(512)} %param.12) | copy-start | bytes 6148
  15.2 11.1 %collective-permute-start.6 = (f32[6,4096]{1,0:T(8,128)S(1)}, f32[6,4096]{1,0:T(8,128)S(1)}, u32[]{:S(2)}, u32[]{:S(2)}) collective-permute-start(f32[6,4096]{1,0:T(8,128)S(1)} %reshape.953), channel_id=1, source_target_pairs={{0,1},{1,0},{2,3},{3,2},{4,5},{5,4},{6,7},{7,6},{8,9},{9,8},{10,11... | collective-permute-start | bytes 294920 | tf_op jit(solution)/shard_map/ppermute | solution.py:107
  15.3 11.0 %collective-permute-start.7 = (f32[6,4096]{1,0:T(8,128)S(1)}, f32[6,4096]{1,0:T(8,128)S(1)}, u32[]{:S(2)}, u32[]{:S(2)}) collective-permute-start(f32[6,4096]{1,0:T(8,128)S(1)} %reshape.953), channel_id=1, source_target_pairs={{0,2},{1,3},{2,0},{3,1},{4,6},{5,7},{6,4},{7,5},{8,10},{9,11},{10,... | collective-permute-start | bytes 294920 | tf_op jit(solution)/shard_map/ppermute | solution.py:107
  17.9 1.0 copy-start
  21.1 9.8 %copy-start.5 = (f32[4096]{0:T(1024)S(1)}, f32[4096]{0:T(1024)}, u32[]{:S(2)}) copy-start(f32[4096]{0:T(1024)} %param.11) | copy-start | bytes 49156
  21.3 4.9 %collective-permute-start.10 = (f32[3,4096]{1,0:T(4,128)S(1)}, f32[3,4096]{1,0:T(4,128)S(1)}, u32[]{:S(2)}, u32[]{:S(2)}) collective-permute-start(f32[3,4096]{1,0:T(4,128)S(1)} %reshape.955), channel_id=1, source_target_pairs={{0,2},{1,3},{2,0},{3,1},{4,6},{5,7},{6,4},{7,5},{8,10},{9,11},{10,... | collective-permute-start | bytes 147464 | tf_op jit(solution)/shard_map/ppermute | solution.py:107
  21.8 4.5 %collective-permute-start.11 = (f32[3,4096]{1,0:T(4,128)S(1)}, f32[3,4096]{1,0:T(4,128)S(1)}, u32[]{:S(2)}, u32[]{:S(2)}) collective-permute-start(f32[3,4096]{1,0:T(4,128)S(1)} %reshape.955), channel_id=1, source_target_pairs={{0,3},{1,2},{2,1},{3,0},{4,7},{5,6},{6,5},{7,4},{8,11},{9,10},{10,... | collective-permute-start | bytes 147464 | tf_op jit(solution)/shard_map/ppermute | solution.py:107
  22.9 3.4 %collective-permute-start.9 = (f32[3,4096]{1,0:T(4,128)S(1)}, f32[3,4096]{1,0:T(4,128)S(1)}, u32[]{:S(2)}, u32[]{:S(2)}) collective-permute-start(f32[3,4096]{1,0:T(4,128)S(1)} %reshape.955), channel_id=1, source_target_pairs={{0,1},{1,0},{2,3},{3,2},{4,5},{5,4},{6,7},{7,6},{8,9},{9,8},{10,11... | collective-permute-start | bytes 147464 | tf_op jit(solution)/shard_map/ppermute | solution.py:107
  26.3 4.4 %collective-permute-start.8 = (f32[6,4096]{1,0:T(8,128)S(1)}, f32[6,4096]{1,0:T(8,128)S(1)}, u32[]{:S(2)}, u32[]{:S(2)}) collective-permute-start(f32[6,4096]{1,0:T(8,128)S(1)} %reshape.953), channel_id=1, source_target_pairs={{0,3},{1,2},{2,1},{3,0},{4,7},{5,6},{6,5},{7,4},{8,11},{9,10},{10,... | collective-permute-start | bytes 294920 | tf_op jit(solution)/shard_map/ppermute | solution.py:107
  35.3 4.5 %collective-permute-start.12 = (f32[9,512]{1,0:T(8,128)S(1)}, f32[9,512]{1,0:T(8,128)S(1)}, u32[]{:S(2)}, u32[]{:S(2)}) collective-permute-start(f32[9,512]{1,0:T(8,128)S(1)} %reshape.960), channel_id=1, source_target_pairs={{0,4},{4,0},{8,12},{12,8},{1,5},{5,1},{9,13},{13,9},{2,6},{6,2},{1... | collective-permute-start | bytes 55304 | tf_op jit(solution)/shard_map/ppermute | solution.py:107
  36.2 6.1 %collective-permute-start.13 = (f32[9,512]{1,0:T(8,128)S(1)}, f32[9,512]{1,0:T(8,128)S(1)}, u32[]{:S(2)}, u32[]{:S(2)}) collective-permute-start(f32[9,512]{1,0:T(8,128)S(1)} %reshape.960), channel_id=1, source_target_pairs={{0,8},{4,12},{8,0},{12,4},{1,9},{5,13},{9,1},{13,5},{2,10},{6,14},... | collective-permute-start | bytes 55304 | tf_op jit(solution)/shard_map/ppermute | solution.py:107
  39.7 5.7 %collective-permute-start.14 = (f32[9,512]{1,0:T(8,128)S(1)}, f32[9,512]{1,0:T(8,128)S(1)}, u32[]{:S(2)}, u32[]{:S(2)}) collective-permute-start(f32[9,512]{1,0:T(8,128)S(1)} %reshape.960), channel_id=1, source_target_pairs={{0,12},{4,8},{8,4},{12,0},{1,13},{5,9},{9,5},{13,1},{2,14},{6,10},... | collective-permute-start | bytes 55304 | tf_op jit(solution)/shard_map/ppermute | solution.py:107
  46.0 5.6 %collective-permute-start.16 = (f32[]{:T(128)}, f32[]{:T(128)}, u32[]{:S(2)}, u32[]{:S(2)}) collective-permute-start(f32[]{:T(128)} %get-tuple-element.8), channel_id=1, source_target_pairs={{0,2},{1,3},{2,0},{3,1},{4,6},{5,7},{6,4},{7,5},{8,10},{9,11},{10,... | collective-permute-start | bytes 20 | tf_op jit(solution)/shard_map/ppermute | solution.py:107
  46.6 5.0 %collective-permute-start.17 = (f32[]{:T(128)}, f32[]{:T(128)}, u32[]{:S(2)}, u32[]{:S(2)}) collective-permute-start(f32[]{:T(128)} %get-tuple-element.8), channel_id=1, source_target_pairs={{0,3},{1,2},{2,1},{3,0},{4,7},{5,6},{6,5},{7,4},{8,11},{9,10},{10,... | collective-permute-start | bytes 20 | tf_op jit(solution)/shard_map/ppermute | solution.py:107
  46.6 2.9 %collective-permute-start.15 = (f32[]{:T(128)}, f32[]{:T(128)}, u32[]{:S(2)}, u32[]{:S(2)}) collective-permute-start(f32[]{:T(128)} %get-tuple-element.8), channel_id=1, source_target_pairs={{0,1},{1,0},{2,3},{3,2},{4,5},{5,4},{6,7},{7,6},{8,9},{9,8},{10,11... | collective-permute-start | bytes 20 | tf_op jit(solution)/shard_map/ppermute | solution.py:107
  48.1 6.0 %collective-permute-start.4 = (f32[]{:T(128)}, f32[]{:T(128)}, u32[]{:S(2)}, u32[]{:S(2)}) collective-permute-start(f32[]{:T(128)} %get-tuple-element.9), channel_id=1, source_target_pairs={{0,2},{1,3},{2,0},{3,1},{4,6},{5,7},{6,4},{7,5},{8,10},{9,11},{10,... | collective-permute-start | bytes 20 | tf_op jit(solution)/shard_map/ppermute | solution.py:107
  48.7 5.4 %collective-permute-start.5 = (f32[]{:T(128)}, f32[]{:T(128)}, u32[]{:S(2)}, u32[]{:S(2)}) collective-permute-start(f32[]{:T(128)} %get-tuple-element.9), channel_id=1, source_target_pairs={{0,3},{1,2},{2,1},{3,0},{4,7},{5,6},{6,5},{7,4},{8,11},{9,10},{10,... | collective-permute-start | bytes 20 | tf_op jit(solution)/shard_map/ppermute | solution.py:107
  49.5 3.3 %collective-permute-start.3 = (f32[]{:T(128)}, f32[]{:T(128)}, u32[]{:S(2)}, u32[]{:S(2)}) collective-permute-start(f32[]{:T(128)} %get-tuple-element.9), channel_id=1, source_target_pairs={{0,1},{1,0},{2,3},{3,2},{4,5},{5,4},{6,7},{7,6},{8,9},{9,8},{10,11... | collective-permute-start | bytes 20 | tf_op jit(solution)/shard_map/ppermute | solution.py:107
  56.0 4.5 %collective-permute-start.19 = (f32[]{:T(128)}, f32[]{:T(128)}, u32[]{:S(2)}, u32[]{:S(2)}) collective-permute-start(f32[]{:T(128)} %get-tuple-element.17), channel_id=1, source_target_pairs={{0,2},{1,3},{2,0},{3,1},{4,6},{5,7},{6,4},{7,5},{8,10},{9,11},{10,... | collective-permute-start | bytes 20 | tf_op jit(solution)/shard_map/ppermute | solution.py:107
  56.6 4.0 %collective-permute-start.20 = (f32[]{:T(128)}, f32[]{:T(128)}, u32[]{:S(2)}, u32[]{:S(2)}) collective-permute-start(f32[]{:T(128)} %get-tuple-element.17), channel_id=1, source_target_pairs={{0,3},{1,2},{2,1},{3,0},{4,7},{5,6},{6,5},{7,4},{8,11},{9,10},{10,... | collective-permute-start | bytes 20 | tf_op jit(solution)/shard_map/ppermute | solution.py:107
  57.4 1.9 %collective-permute-start.18 = (f32[]{:T(128)}, f32[]{:T(128)}, u32[]{:S(2)}, u32[]{:S(2)}) collective-permute-start(f32[]{:T(128)} %get-tuple-element.17), channel_id=1, source_target_pairs={{0,1},{1,0},{2,3},{3,2},{4,5},{5,4},{6,7},{7,6},{8,9},{9,8},{10,11... | collective-permute-start | bytes 20 | tf_op jit(solution)/shard_map/ppermute | solution.py:107
  65.6 1.9 %collective-permute-start.21 = (f32[3,4096]{1,0:T(4,128)S(1)}, f32[3,4096]{1,0:T(4,128)S(1)}, u32[]{:S(2)}, u32[]{:S(2)}) collective-permute-start(f32[3,4096]{1,0:T(4,128)S(1)} %reshape.965), channel_id=1, source_target_pairs={{0,1},{1,0},{2,3},{3,2},{4,5},{5,4},{6,7},{7,6},{8,9},{9,8},{10,11... | collective-permute-start | bytes 147464 | tf_op jit(solution)/shard_map/ppermute | solution.py:107
  66.0 5.0 %collective-permute-start.22 = (f32[3,4096]{1,0:T(4,128)S(1)}, f32[3,4096]{1,0:T(4,128)S(1)}, u32[]{:S(2)}, u32[]{:S(2)}) collective-permute-start(f32[3,4096]{1,0:T(4,128)S(1)} %reshape.965), channel_id=1, source_target_pairs={{0,2},{1,3},{2,0},{3,1},{4,6},{5,7},{6,4},{7,5},{8,10},{9,11},{10,... | collective-permute-start | bytes 147464 | tf_op jit(solution)/shard_map/ppermute | solution.py:107
  66.5 4.4 %collective-permute-start.23 = (f32[3,4096]{1,0:T(4,128)S(1)}, f32[3,4096]{1,0:T(4,128)S(1)}, u32[]{:S(2)}, u32[]{:S(2)}) collective-permute-start(f32[3,4096]{1,0:T(4,128)S(1)} %reshape.965), channel_id=1, source_target_pairs={{0,3},{1,2},{2,1},{3,0},{4,7},{5,6},{6,5},{7,4},{8,11},{9,10},{10,... | collective-permute-start | bytes 147464 | tf_op jit(solution)/shard_map/ppermute | solution.py:107
  74.7 4.5 %collective-permute-start.24 = (f32[9,512]{1,0:T(8,128)S(1)}, f32[9,512]{1,0:T(8,128)S(1)}, u32[]{:S(2)}, u32[]{:S(2)}) collective-permute-start(f32[9,512]{1,0:T(8,128)S(1)} %reshape.970), channel_id=1, source_target_pairs={{0,4},{4,0},{8,12},{12,8},{1,5},{5,1},{9,13},{13,9},{2,6},{6,2},{1... | collective-permute-start | bytes 55304 | tf_op jit(solution)/shard_map/ppermute | solution.py:107
  74.8 5.1 %collective-permute-start.25 = (f32[9,512]{1,0:T(8,128)S(1)}, f32[9,512]{1,0:T(8,128)S(1)}, u32[]{:S(2)}, u32[]{:S(2)}) collective-permute-start(f32[9,512]{1,0:T(8,128)S(1)} %reshape.970), channel_id=1, source_target_pairs={{0,8},{4,12},{8,0},{12,4},{1,9},{5,13},{9,1},{13,5},{2,10},{6,14},... | collective-permute-start | bytes 55304 | tf_op jit(solution)/shard_map/ppermute | solution.py:107
  75.7 5.7 %collective-permute-start.26 = (f32[9,512]{1,0:T(8,128)S(1)}, f32[9,512]{1,0:T(8,128)S(1)}, u32[]{:S(2)}, u32[]{:S(2)}) collective-permute-start(f32[9,512]{1,0:T(8,128)S(1)} %reshape.970), channel_id=1, source_target_pairs={{0,12},{4,8},{8,4},{12,0},{1,13},{5,9},{9,5},{13,1},{2,14},{6,10},... | collective-permute-start | bytes 55304 | tf_op jit(solution)/shard_map/ppermute | solution.py:107
  82.1 4.5 %collective-permute-start.28 = (f32[]{:T(128)}, f32[]{:T(128)}, u32[]{:S(2)}, u32[]{:S(2)}) collective-permute-start(f32[]{:T(128)} %get-tuple-element.15), channel_id=1, source_target_pairs={{0,2},{1,3},{2,0},{3,1},{4,6},{5,7},{6,4},{7,5},{8,10},{9,11},{10,... | collective-permute-start | bytes 20 | tf_op jit(solution)/shard_map/ppermute | solution.py:107
  83.4 3.2 %collective-permute-start.29 = (f32[]{:T(128)}, f32[]{:T(128)}, u32[]{:S(2)}, u32[]{:S(2)}) collective-permute-start(f32[]{:T(128)} %get-tuple-element.15), channel_id=1, source_target_pairs={{0,3},{1,2},{2,1},{3,0},{4,7},{5,6},{6,5},{7,4},{8,11},{9,10},{10,... | collective-permute-start | bytes 20 | tf_op jit(solution)/shard_map/ppermute | solution.py:107
  83.4 1.9 %collective-permute-start.27 = (f32[]{:T(128)}, f32[]{:T(128)}, u32[]{:S(2)}, u32[]{:S(2)}) collective-permute-start(f32[]{:T(128)} %get-tuple-element.15), channel_id=1, source_target_pairs={{0,1},{1,0},{2,3},{3,2},{4,5},{5,4},{6,7},{7,6},{8,9},{9,8},{10,11... | collective-permute-start | bytes 20 | tf_op jit(solution)/shard_map/ppermute | solution.py:107
  88.5 4.5 %collective-permute-start.31 = (f32[]{:T(128)}, f32[]{:T(128)}, u32[]{:S(2)}, u32[]{:S(2)}) collective-permute-start(f32[]{:T(128)} %get-tuple-element.12), channel_id=1, source_target_pairs={{0,2},{1,3},{2,0},{3,1},{4,6},{5,7},{6,4},{7,5},{8,10},{9,11},{10,... | collective-permute-start | bytes 20 | tf_op jit(solution)/shard_map/ppermute | solution.py:107
  89.8 3.2 %collective-permute-start.32 = (f32[]{:T(128)}, f32[]{:T(128)}, u32[]{:S(2)}, u32[]{:S(2)}) collective-permute-start(f32[]{:T(128)} %get-tuple-element.12), channel_id=1, source_target_pairs={{0,3},{1,2},{2,1},{3,0},{4,7},{5,6},{6,5},{7,4},{8,11},{9,10},{10,... | collective-permute-start | bytes 20 | tf_op jit(solution)/shard_map/ppermute | solution.py:107
  90.2 1.5 %collective-permute-start.30 = (f32[]{:T(128)}, f32[]{:T(128)}, u32[]{:S(2)}, u32[]{:S(2)}) collective-permute-start(f32[]{:T(128)} %get-tuple-element.12), channel_id=1, source_target_pairs={{0,1},{1,0},{2,3},{3,2},{4,5},{5,4},{6,7},{7,6},{8,9},{9,8},{10,11... | collective-permute-start | bytes 20 | tf_op jit(solution)/shard_map/ppermute | solution.py:107
  98.3 1.9 %collective-permute-start.33 = (f32[3,4096]{1,0:T(4,128)S(1)}, f32[3,4096]{1,0:T(4,128)S(1)}, u32[]{:S(2)}, u32[]{:S(2)}) collective-permute-start(f32[3,4096]{1,0:T(4,128)S(1)} %reshape.975), channel_id=1, source_target_pairs={{0,1},{1,0},{2,3},{3,2},{4,5},{5,4},{6,7},{7,6},{8,9},{9,8},{10,11... | collective-permute-start | bytes 147464 | tf_op jit(solution)/shard_map/ppermute | solution.py:107
  98.7 4.3 %collective-permute-start.34 = (f32[3,4096]{1,0:T(4,128)S(1)}, f32[3,4096]{1,0:T(4,128)S(1)}, u32[]{:S(2)}, u32[]{:S(2)}) collective-permute-start(f32[3,4096]{1,0:T(4,128)S(1)} %reshape.975), channel_id=1, source_target_pairs={{0,2},{1,3},{2,0},{3,1},{4,6},{5,7},{6,4},{7,5},{8,10},{9,11},{10,... | collective-permute-start | bytes 147464 | tf_op jit(solution)/shard_map/ppermute | solution.py:107
  100.0 4.3 %collective-permute-start.35 = (f32[3,4096]{1,0:T(4,128)S(1)}, f32[3,4096]{1,0:T(4,128)S(1)}, u32[]{:S(2)}, u32[]{:S(2)}) collective-permute-start(f32[3,4096]{1,0:T(4,128)S(1)} %reshape.975), channel_id=1, source_target_pairs={{0,3},{1,2},{2,1},{3,0},{4,7},{5,6},{6,5},{7,4},{8,11},{9,10},{10,... | collective-permute-start | bytes 147464 | tf_op jit(solution)/shard_map/ppermute | solution.py:107
  108.1 4.5 %collective-permute-start.36 = (f32[9,512]{1,0:T(8,128)S(1)}, f32[9,512]{1,0:T(8,128)S(1)}, u32[]{:S(2)}, u32[]{:S(2)}) collective-permute-start(f32[9,512]{1,0:T(8,128)S(1)} %reshape.980), channel_id=1, source_target_pairs={{0,4},{4,0},{8,12},{12,8},{1,5},{5,1},{9,13},{13,9},{2,6},{6,2},{1... | collective-permute-start | bytes 55304 | tf_op jit(solution)/shard_map/ppermute | solution.py:107
  108.8 5.3 %collective-permute-start.37 = (f32[9,512]{1,0:T(8,128)S(1)}, f32[9,512]{1,0:T(8,128)S(1)}, u32[]{:S(2)}, u32[]{:S(2)}) collective-permute-start(f32[9,512]{1,0:T(8,128)S(1)} %reshape.980), channel_id=1, source_target_pairs={{0,8},{4,12},{8,0},{12,4},{1,9},{5,13},{9,1},{13,5},{2,10},{6,14},... | collective-permute-start | bytes 55304 | tf_op jit(solution)/shard_map/ppermute | solution.py:107
  112.2 5.7 %collective-permute-start.38 = (f32[9,512]{1,0:T(8,128)S(1)}, f32[9,512]{1,0:T(8,128)S(1)}, u32[]{:S(2)}, u32[]{:S(2)}) collective-permute-start(f32[9,512]{1,0:T(8,128)S(1)} %reshape.980), channel_id=1, source_target_pairs={{0,12},{4,8},{8,4},{12,0},{1,13},{5,9},{9,5},{13,1},{2,14},{6,10},... | collective-permute-start | bytes 55304 | tf_op jit(solution)/shard_map/ppermute | solution.py:107
  118.5 4.5 %collective-permute-start.40 = (f32[]{:T(128)}, f32[]{:T(128)}, u32[]{:S(2)}, u32[]{:S(2)}) collective-permute-start(f32[]{:T(128)} %get-tuple-element.10), channel_id=1, source_target_pairs={{0,2},{1,3},{2,0},{3,1},{4,6},{5,7},{6,4},{7,5},{8,10},{9,11},{10,... | collective-permute-start | bytes 20 | tf_op jit(solution)/shard_map/ppermute | solution.py:107
  119.3 3.7 %collective-permute-start.41 = (f32[]{:T(128)}, f32[]{:T(128)}, u32[]{:S(2)}, u32[]{:S(2)}) collective-permute-start(f32[]{:T(128)} %get-tuple-element.10), channel_id=1, source_target_pairs={{0,3},{1,2},{2,1},{3,0},{4,7},{5,6},{6,5},{7,4},{8,11},{9,10},{10,... | collective-permute-start | bytes 20 | tf_op jit(solution)/shard_map/ppermute | solution.py:107
  119.3 2.4 %collective-permute-start.39 = (f32[]{:T(128)}, f32[]{:T(128)}, u32[]{:S(2)}, u32[]{:S(2)}) collective-permute-start(f32[]{:T(128)} %get-tuple-element.10), channel_id=1, source_target_pairs={{0,1},{1,0},{2,3},{3,2},{4,5},{5,4},{6,7},{7,6},{8,9},{9,8},{10,11... | collective-permute-start | bytes 20 | tf_op jit(solution)/shard_map/ppermute | solution.py:107

commit v5 on v4

--- a/solution.py
+++ b/solution.py
@@ -129,27 +129,37 @@
     inv = point_inverse(six_terms, point_damp)
     diag_terms = by_cam.segsum(jnp.sum(cam_jac * cam_jac, axis=0))
     cam_diag = allsum(diag_terms, "pts") + cam_damp[None, :]
+
+    def operate(vec):
+        y = jnp.sum(cam_jac * by_cam.gather(vec)[None], axis=1)
+        u = allsum(by_point.segsum(jnp.sum(point_jac * y[:, None, :], axis=0)), "cam")
+        w = jnp.sum(inv * u[None, :, :], axis=1)
+        z = y - jnp.sum(point_jac * by_point.gather(w)[None], axis=1)
+        return cam_damp[None, :] * vec + allsum(
+            by_cam.segsum(jnp.sum(cam_jac * z[:, None, :], axis=0)), "pts"
+        )
+
     solution = jnp.zeros_like(reduced_rhs)
     residual = reduced_rhs
     pre = residual / cam_diag
     direction = pre
-    rz = norm_sum(jnp.sum(residual * pre))
-    for step in range(ITERS):
-        dir_obs = by_cam.gather(direction)
-        y = jnp.sum(cam_jac * dir_obs[None], axis=1)
-        u = allsum(by_point.segsum(jnp.sum(point_jac * y[:, None, :], axis=0)), "cam")
-        w = jnp.sum(inv * u[None, :, :], axis=1)
-        z = y - jnp.sum(point_jac * by_point.gather(w)[None], axis=1)
-        image = cam_damp[None, :] * direction + allsum(
-            by_cam.segsum(jnp.sum(cam_jac * z[:, None, :], axis=0)), "pts"
-        )
-        alpha = rz / allsum(jnp.sum(direction * image), "cam")
+    image = operate(direction)
+    sums = norm_sum(jnp.stack([jnp.sum(residual * pre), jnp.sum(direction * image)]))
+    rz = sums[0]
+    alpha = rz / sums[1]
+    solution = solution + alpha * direction
+    residual = residual - alpha * image
+    for step in range(1, ITERS):
+        pre = residual / cam_diag
+        new_rz = norm_sum(jnp.sum(residual * pre))
+        image_pre = operate(pre)
+        beta = new_rz / rz
+        direction = pre + beta * direction
+        image = image_pre + beta * image
+        alpha = new_rz / norm_sum(jnp.sum(direction * image))
+        rz = new_rz
         solution = solution + alpha * direction
         residual = residual - alpha * image
-        pre = residual / cam_diag
-        new_rz = norm_sum(jnp.sum(residual * pre))
-        direction = pre + new_rz / rz * direction
-        rz = new_rz
     return (solution, residual)
 
 

time: 126 us -> 117 us (0.929)
  waiting for transfers between devices: 32.2 us -> 26.5 us
  starting transfers between devices: 39.8 us -> 36.6 us
  between operations: 16.9 us -> 13.9 us
  other arithmetic: 17.8 us -> 20.5 us
    ppermute x42 -> x39, waiting for transfers between devices: 32.2 us -> 26.5 us  [allsum(): lax.ppermute(value, axis, [(i, i ^ mask) for i in range(size)])]
    ppermute x42 -> x39, starting transfers between devices: 39.8 us -> 36.6 us  [allsum(): lax.ppermute(value, axis, [(i, i ^ mask) for i in range(size)])]
    add x4 -> x5, other arithmetic: 0.15 us -> 1.53 us  [allsum(): return value + peers[0] + (peers[1] + peers[2])]
    another operation x0 -> x1, other arithmetic: none -> 1.37 us  [on_device(): jnp.stack([jnp.sum(residual * pre), jnp.sum(direction * image)])]
  transfers between devices with their start and end apart: 42 -> 39, of which waited for: 15 -> 18; matrix products, arithmetic and copies ran while one was open for 7% -> 7% of each run, Pallas kernels for 0% -> 0%
where the time goes in v5:
time: 117 us
  starting transfers between devices  36.6 us (31%)
  waiting for transfers between devices  26.5 us (23%)
  other arithmetic  20.5 us (18%)
  matrix products  15.2 us (13%)
  between operations  13.9 us (12%)
  local copies, waits for them, and re-layouts  4.23 us (4%)
    ppermute x39, starting transfers between devices, allsum(): lax.ppermute(value, axis, [(i, i ^ mask) for i in range(size)])  36.6 us
    ppermute x39, waiting for transfers between devices, allsum(): lax.ppermute(value, axis, [(i, i ^ mask) for i in range(size)])  26.5 us
    dot_general x8, matrix products, segsum(): lax.dot_general(self.hot3, spread, (((1,), (1,)), ((), ())), preferred_el...  11.8 us
    select_n x8, other arithmetic, segsum(): jnp.where(self.low[None], part[:, None, :], jnp.zeros((), BF))  3.86 us
    dot_general x6, matrix products, gather(): lax.dot_general(stacked, self.hot3t, (((1,), (0,)), ((), ())), preferred_...  3.4 us
    reduce_sum x6, other arithmetic, gather(): return jnp.sum(jnp.where(self.low[None], spread, 0.0), axis=1)  2.61 us
  transfers between devices with their start and end apart: 39, of which 18 were waited for; matrix products, arithmetic and copies ran while one was open for 7% of the time, Pallas kernels for 0%

profile of v5, /device:TPU:0, one launch (start us, length us, event | category | flops | bytes accessed | tf_op | source)
XLA Modules:
  0.0 116.9 jit_solution(12980234774882885152)
XLA Ops:
  0.6 0.7 add_select_fusion.3
  1.4 1.4 %multiply_reduce_fusion.6 = f32[9,4096]{1,0:T(8,128)S(1)} fusion(f32[2,9,4096]{2,0,1:T(2,128)} %param.7), kind=kLoop, calls=%fused_computation.115 | loop fusion | flops 110592 | bytes 442368 | tf_op jit(solution)/shard_map/reduce_sum | solution.py:130
  3.3 1.1 fusion.24
  4.6 3.1 %collective-permute-start = (f32[9,512]{1,0:T(8,128)S(1)}, f32[9,512]{1,0:T(8,128)S(1)}, u32[]{:S(2)}, u32[]{:S(2)}) collective-permute-start(f32[9,512]{1,0:T(8,128)S(1)} %reshape.948), channel_id=1, source_target_pairs={{0,4},{4,0},{8,12},{12,8},{1,5},{5,1},{9,13},{13,9},{2,6},{6,2},{1... | collective-permute-start | bytes 55304 | tf_op jit(solution)/shard_map/ppermute | solution.py:107
  7.7 2.6 %collective-permute-start.1 = (f32[9,512]{1,0:T(8,128)S(1)}, f32[9,512]{1,0:T(8,128)S(1)}, u32[]{:S(2)}, u32[]{:S(2)}) collective-permute-start(f32[9,512]{1,0:T(8,128)S(1)} %reshape.948), channel_id=1, source_target_pairs={{0,8},{4,12},{8,0},{12,4},{1,9},{5,13},{9,1},{13,5},{2,10},{6,14},... | collective-permute-start | bytes 55304 | tf_op jit(solution)/shard_map/ppermute | solution.py:107
  11.0 0.9 broadcast_select_fusion.2
  12.0 3.0 %fusion = f32[64,384]{1,0:T(8,128)S(1)} fusion(bf16[384,4096]{1,0:T(8,128)(2,1)S(1)} %bitcast.146, bf16[384,4096]{1,0:T(8,128)(2,1)S(1)} %bitcast.145, bf16[384,4096]{1,0:T(8,128)(2,1)S(1)} %bitcast.144, bf16[64,4096]{1,0:T(8,128)(2,1)S(1)} %get-tuple-element.112), kind=kOutput, calls=%fused_computation | convolution fusion | flops 637009920 | bytes 10059776 | tf_op jit(solution)/shard_map/dot_general | solution.py:46
  15.3 1.8 %collective-permute-start.4 = (f32[6,4096]{1,0:T(8,128)S(1)}, f32[6,4096]{1,0:T(8,128)S(1)}, u32[]{:S(2)}, u32[]{:S(2)}) collective-permute-start(f32[6,4096]{1,0:T(8,128)S(1)} %reshape.953), channel_id=1, source_target_pairs={{0,2},{1,3},{2,0},{3,1},{4,6},{5,7},{6,4},{7,5},{8,10},{9,11},{10,... | collective-permute-start | bytes 294920 | tf_op jit(solution)/shard_map/ppermute | solution.py:107
  19.7 1.4 %fusion.6 = f32[64,192]{0,1:T(8,128)S(1)} fusion(bf16[192,4096]{1,0:T(8,128)(2,1)S(1)} %bitcast.149, bf16[192,4096]{1,0:T(8,128)(2,1)S(1)} %bitcast.148, bf16[192,4096]{1,0:T(8,128)(2,1)S(1)} %bitcast.147, bf16[64,4096]{1,0:T(8,128)(2,1)S(1)} %get-tuple-element.112), kind=kOutput, calls=%fused_computation.6 | convolution fusion | flops 320864256 | bytes 5292032 | tf_op jit(solution)/shard_map/dot_general | solution.py:46
  21.9 1.4 %collective-permute-start.8 = (f32[3,4096]{1,0:T(4,128)S(1)}, f32[3,4096]{1,0:T(4,128)S(1)}, u32[]{:S(2)}, u32[]{:S(2)}) collective-permute-start(f32[3,4096]{1,0:T(4,128)S(1)} %reshape.955), channel_id=1, source_target_pairs={{0,3},{1,2},{2,1},{3,0},{4,7},{5,6},{6,5},{7,4},{8,11},{9,10},{10,... | collective-permute-start | bytes 147464 | tf_op jit(solution)/shard_map/ppermute | solution.py:107
  23.6 2.9 %collective-permute-done.7 = f32[3,4096]{1,0:T(4,128)S(1)} collective-permute-done((f32[3,4096]{1,0:T(4,128)S(1)}, f32[3,4096]{1,0:T(4,128)S(1)}, u32[]{:S(2)}, u32[]{:S(2)}) %collective-permute-start.7) | collective-permute-done | bytes 49184 | tf_op jit(solution)/shard_map/ppermute | solution.py:107
  26.8 2.7 %collective-permute-done.5 = f32[6,4096]{1,0:T(8,128)S(1)} collective-permute-done((f32[6,4096]{1,0:T(8,128)S(1)}, f32[6,4096]{1,0:T(8,128)S(1)}, u32[]{:S(2)}, u32[]{:S(2)}) %collective-permute-start.5) | collective-permute-done | bytes 98336 | tf_op jit(solution)/shard_map/ppermute | solution.py:107
  30.7 0.6 fusion.51
  31.9 0.6 multiply_reduce_fusion.4
  32.9 1.1 fusion.30
  34.2 1.8 %collective-permute-start.10 = (f32[9,512]{1,0:T(8,128)S(1)}, f32[9,512]{1,0:T(8,128)S(1)}, u32[]{:S(2)}, u32[]{:S(2)}) collective-permute-start(f32[9,512]{1,0:T(8,128)S(1)} %reshape.960), channel_id=1, source_target_pairs={{0,8},{4,12},{8,0},{12,4},{1,9},{5,13},{9,1},{13,5},{2,10},{6,14},... | collective-permute-start | bytes 55304 | tf_op jit(solution)/shard_map/ppermute | solution.py:107
  36.0 2.0 %collective-permute-start.11 = (f32[9,512]{1,0:T(8,128)S(1)}, f32[9,512]{1,0:T(8,128)S(1)}, u32[]{:S(2)}, u32[]{:S(2)}) collective-permute-start(f32[9,512]{1,0:T(8,128)S(1)} %reshape.960), channel_id=1, source_target_pairs={{0,12},{4,8},{8,4},{12,0},{1,13},{5,9},{9,5},{13,1},{2,14},{6,10},... | collective-permute-start | bytes 55304 | tf_op jit(solution)/shard_map/ppermute | solution.py:107
  38.5 0.6 collective-permute-done.10
  39.1 2.6 %collective-permute-done.11 = f32[9,512]{1,0:T(8,128)S(1)} collective-permute-done((f32[9,512]{1,0:T(8,128)S(1)}, f32[9,512]{1,0:T(8,128)S(1)}, u32[]{:S(2)}, u32[]{:S(2)}) %collective-permute-start.11) | collective-permute-done | bytes 18464 | tf_op jit(solution)/shard_map/ppermute | solution.py:107
  42.0 0.6 multiply_reduce_fusion.27
  42.7 1.4 %pad_maximum_fusion.18 = f32[2]{0:T(128)S(1)} fusion(f32[1]{0:T(128)} %bitcast.48, f32[1]{0:T(128)} %bitcast.5), kind=kLoop, calls=%fused_computation.272 | loop fusion | flops 2 | bytes 16 | tf_op jit(solution)/shard_map/stack | solution.py:147
  44.0 1.1 collective-permute-start.13
  45.1 0.8 collective-permute-start.14
  45.9 1.8 %collective-permute-done.13 = f32[2]{0:T(128)S(1)} collective-permute-done((f32[2]{0:T(128)S(1)}, f32[2]{0:T(128)S(1)}, u32[]{:S(2)}, u32[]{:S(2)}) %collective-permute-start.13) | collective-permute-done | bytes 40 | tf_op jit(solution)/shard_map/ppermute | solution.py:107
  48.1 1.4 %add_add_fusion.6 = f32[2]{0:T(128)S(1)} fusion(f32[2]{0:T(128)S(1)} %collective-permute-done.13, f32[2]{0:T(128)S(1)} %collective-permute-done.14, f32[2]{0:T(128)S(1)} %collective-permute-done.12, f32[1]{0:T(128)} %bitcast.48, f32[1]{0:T(128)} %bitcast.5), kind=kLoop, calls=%fused_computation.273 | loop fusion | flops 8 | bytes 40 | tf_op jit(solution)/shard_map/add | solution.py:109
  49.5 0.6 fusion.122
  51.4 0.6 multiply_reduce_fusion.19
  54.1 1.4 %fusion.12 = f32[64,192]{0,1:T(8,128)S(1)} fusion(bf16[192,4096]{1,0:T(8,128)(2,1)S(1)} %bitcast.152, bf16[192,4096]{1,0:T(8,128)(2,1)S(1)} %bitcast.151, bf16[192,4096]{1,0:T(8,128)(2,1)S(1)} %bitcast.150, bf16[64,4096]{1,0:T(8,128)(2,1)S(1)} %get-tuple-element.112), kind=kOutput, calls=%fused_computation.12 | convolution fusion | flops 320864256 | bytes 5292032 | tf_op jit(solution)/shard_map/dot_general | solution.py:46
  55.9 1.0 collective-permute-start.19
  56.9 0.7 collective-permute-start.20
  57.6 3.0 %collective-permute-done.19 = f32[3,4096]{1,0:T(4,128)S(1)} collective-permute-done((f32[3,4096]{1,0:T(4,128)S(1)}, f32[3,4096]{1,0:T(4,128)S(1)}, u32[]{:S(2)}, u32[]{:S(2)}) %collective-permute-start.19) | collective-permute-done | bytes 49184 | tf_op jit(solution)/shard_map/ppermute | solution.py:107
  60.6 0.7 collective-permute-done.20
  61.8 0.6 fusion.50
  63.8 1.1 fusion.36
  65.1 0.6 collective-permute-start.21
  65.7 2.0 %collective-permute-start.22 = (f32[9,512]{1,0:T(8,128)S(1)}, f32[9,512]{1,0:T(8,128)S(1)}, u32[]{:S(2)}, u32[]{:S(2)}) collective-permute-start(f32[9,512]{1,0:T(8,128)S(1)} %reshape.970), channel_id=1, source_target_pairs={{0,8},{4,12},{8,0},{12,4},{1,9},{5,13},{9,1},{13,5},{2,10},{6,14},... | collective-permute-start | bytes 55304 | tf_op jit(solution)/shard_map/ppermute | solution.py:107
  67.7 1.8 %collective-permute-start.23 = (f32[9,512]{1,0:T(8,128)S(1)}, f32[9,512]{1,0:T(8,128)S(1)}, u32[]{:S(2)}, u32[]{:S(2)}) collective-permute-start(f32[9,512]{1,0:T(8,128)S(1)} %reshape.970), channel_id=1, source_target_pairs={{0,12},{4,8},{8,4},{12,0},{1,13},{5,9},{9,5},{13,1},{2,14},{6,10},... | collective-permute-start | bytes 55304 | tf_op jit(solution)/shard_map/ppermute | solution.py:107
  69.5 1.0 collective-permute-start.16
  70.6 1.4 %collective-permute-done.15 = f32[]{:T(128)} collective-permute-done((f32[]{:T(128)}, f32[]{:T(128)}, u32[]{:S(2)}, u32[]{:S(2)}) %collective-permute-start.15) | collective-permute-done | bytes 36 | tf_op jit(solution)/shard_map/ppermute | solution.py:107
  72.0 0.8 collective-permute-start.17
  74.1 1.1 collective-permute-done.17
  77.2 0.6 multiply_reduce_fusion.18
  77.8 1.0 collective-permute-start.25
  79.2 0.8 collective-permute-start.24
  80.0 1.1 collective-permute-done.24
  83.6 0.6 multiply_reduce_fusion.17
  86.3 1.7 %fusion.18 = f32[64,192]{0,1:T(8,128)S(1)} fusion(bf16[192,4096]{1,0:T(8,128)(2,1)S(1)} %bitcast.155, bf16[192,4096]{1,0:T(8,128)(2,1)S(1)} %bitcast.154, bf16[192,4096]{1,0:T(8,128)(2,1)S(1)} %bitcast.153, bf16[64,4096]{1,0:T(8,128)(2,1)S(1)} %get-tuple-element.112), kind=kOutput, calls=%fused_computation.18 | convolution fusion | flops 320864256 | bytes 5292032 | tf_op jit(solution)/shard_map/dot_general | solution.py:46
  88.6 1.0 collective-permute-start.31
  90.1 3.0 %collective-permute-done.31 = f32[3,4096]{1,0:T(4,128)S(1)} collective-permute-done((f32[3,4096]{1,0:T(4,128)S(1)}, f32[3,4096]{1,0:T(4,128)S(1)}, u32[]{:S(2)}, u32[]{:S(2)}) %collective-permute-start.31) | collective-permute-done | bytes 49184 | tf_op jit(solution)/shard_map/ppermute | solution.py:107
  93.1 0.9 collective-permute-done.32
  94.4 0.6 fusion.49
  96.4 1.1 fusion.42
  97.8 2.5 %collective-permute-start.34 = (f32[9,512]{1,0:T(8,128)S(1)}, f32[9,512]{1,0:T(8,128)S(1)}, u32[]{:S(2)}, u32[]{:S(2)}) collective-permute-start(f32[9,512]{1,0:T(8,128)S(1)} %reshape.980), channel_id=1, source_target_pairs={{0,8},{4,12},{8,0},{12,4},{1,9},{5,13},{9,1},{13,5},{2,10},{6,14},... | collective-permute-start | bytes 55304 | tf_op jit(solution)/shard_map/ppermute | solution.py:107
  100.4 1.8 %collective-permute-start.35 = (f32[9,512]{1,0:T(8,128)S(1)}, f32[9,512]{1,0:T(8,128)S(1)}, u32[]{:S(2)}, u32[]{:S(2)}) collective-permute-start(f32[9,512]{1,0:T(8,128)S(1)} %reshape.980), channel_id=1, source_target_pairs={{0,12},{4,8},{8,4},{12,0},{1,13},{5,9},{9,5},{13,1},{2,14},{6,10},... | collective-permute-start | bytes 55304 | tf_op jit(solution)/shard_map/ppermute | solution.py:107
  102.2 1.0 collective-permute-start.28
  103.2 1.4 %collective-permute-done.27 = f32[]{:T(128)} collective-permute-done((f32[]{:T(128)}, f32[]{:T(128)}, u32[]{:S(2)}, u32[]{:S(2)}) %collective-permute-start.27) | collective-permute-done | bytes 36 | tf_op jit(solution)/shard_map/ppermute | solution.py:107
  104.6 0.8 collective-permute-start.29
  106.7 1.1 collective-permute-done.29
  109.2 0.6 multiply_reduce_fusion.16
  109.8 1.0 collective-permute-start.37
  111.2 0.8 collective-permute-start.36
  112.0 1.1 collective-permute-done.36
  115.6 0.6 multiply_add_fusion
  116.3 0.6 multiply_subtract_fusion
  (150 shorter events, 19.5 us)
Async XLA Ops:
  3.3 7.0 %copy-start.1 = (f32[2,3,4096]{2,0,1:T(2,128)S(1)}, f32[2,3,4096]{2,0,1:T(2,128)}, u32[]{:S(2)}) copy-start(f32[2,3,4096]{2,0,1:T(2,128)} %param.8) | copy-start | bytes 294916
  3.3 7.5 %copy-start.4 = (s32[4096]{0:T(1024)S(1)}, s32[4096]{0:T(1024)}, u32[]{:S(2)}) copy-start(s32[4096]{0:T(1024)} %param.10) | copy-start | bytes 49156
  4.6 12.5 %collective-permute-start = (f32[9,512]{1,0:T(8,128)S(1)}, f32[9,512]{1,0:T(8,128)S(1)}, u32[]{:S(2)}, u32[]{:S(2)}) collective-permute-start(f32[9,512]{1,0:T(8,128)S(1)} %reshape.948), channel_id=1, source_target_pairs={{0,4},{4,0},{8,12},{12,8},{1,5},{5,1},{9,13},{13,9},{2,6},{6,2},{1... | collective-permute-start | bytes 55304 | tf_op jit(solution)/shard_map/ppermute | solution.py:107
  7.7 9.4 %collective-permute-start.1 = (f32[9,512]{1,0:T(8,128)S(1)}, f32[9,512]{1,0:T(8,128)S(1)}, u32[]{:S(2)}, u32[]{:S(2)}) collective-permute-start(f32[9,512]{1,0:T(8,128)S(1)} %reshape.948), channel_id=1, source_target_pairs={{0,8},{4,12},{8,0},{12,4},{1,9},{5,13},{9,1},{13,5},{2,10},{6,14},... | collective-permute-start | bytes 55304 | tf_op jit(solution)/shard_map/ppermute | solution.py:107
  10.3 6.8 %collective-permute-start.2 = (f32[9,512]{1,0:T(8,128)S(1)}, f32[9,512]{1,0:T(8,128)S(1)}, u32[]{:S(2)}, u32[]{:S(2)}) collective-permute-start(f32[9,512]{1,0:T(8,128)S(1)} %reshape.948), channel_id=1, source_target_pairs={{0,12},{4,8},{8,4},{12,0},{1,13},{5,9},{9,5},{13,1},{2,14},{6,10},... | collective-permute-start | bytes 55304 | tf_op jit(solution)/shard_map/ppermute | solution.py:107
  11.9 5.2 %copy-start.2 = (f32[9,512]{1,0:T(8,128)S(1)}, f32[9,512]{1,0:T(8,128)}, u32[]{:S(2)}) copy-start(f32[9,512]{1,0:T(8,128)} %param.13) | copy-start | bytes 55300
  12.0 5.2 %copy-start.3 = (f32[512]{0:T(512)S(1)}, f32[512]{0:T(512)}, u32[]{:S(2)}) copy-start(f32[512]{0:T(512)} %param.12) | copy-start | bytes 6148
  15.2 11.5 %collective-permute-start.3 = (f32[6,4096]{1,0:T(8,128)S(1)}, f32[6,4096]{1,0:T(8,128)S(1)}, u32[]{:S(2)}, u32[]{:S(2)}) collective-permute-start(f32[6,4096]{1,0:T(8,128)S(1)} %reshape.953), channel_id=1, source_target_pairs={{0,1},{1,0},{2,3},{3,2},{4,5},{5,4},{6,7},{7,6},{8,9},{9,8},{10,11... | collective-permute-start | bytes 294920 | tf_op jit(solution)/shard_map/ppermute | solution.py:107
  15.3 11.4 %collective-permute-start.4 = (f32[6,4096]{1,0:T(8,128)S(1)}, f32[6,4096]{1,0:T(8,128)S(1)}, u32[]{:S(2)}, u32[]{:S(2)}) collective-permute-start(f32[6,4096]{1,0:T(8,128)S(1)} %reshape.953), channel_id=1, source_target_pairs={{0,2},{1,3},{2,0},{3,1},{4,6},{5,7},{6,4},{7,5},{8,10},{9,11},{10,... | collective-permute-start | bytes 294920 | tf_op jit(solution)/shard_map/ppermute | solution.py:107
  17.9 1.0 copy-start
  21.1 8.6 %copy-start.5 = (f32[4096]{0:T(1024)S(1)}, f32[4096]{0:T(1024)}, u32[]{:S(2)}) copy-start(f32[4096]{0:T(1024)} %param.11) | copy-start | bytes 49156
  21.3 1.9 %collective-permute-start.6 = (f32[3,4096]{1,0:T(4,128)S(1)}, f32[3,4096]{1,0:T(4,128)S(1)}, u32[]{:S(2)}, u32[]{:S(2)}) collective-permute-start(f32[3,4096]{1,0:T(4,128)S(1)} %reshape.955), channel_id=1, source_target_pairs={{0,1},{1,0},{2,3},{3,2},{4,5},{5,4},{6,7},{7,6},{8,9},{9,8},{10,11... | collective-permute-start | bytes 147464 | tf_op jit(solution)/shard_map/ppermute | solution.py:107
  21.6 5.0 %collective-permute-start.7 = (f32[3,4096]{1,0:T(4,128)S(1)}, f32[3,4096]{1,0:T(4,128)S(1)}, u32[]{:S(2)}, u32[]{:S(2)}) collective-permute-start(f32[3,4096]{1,0:T(4,128)S(1)} %reshape.955), channel_id=1, source_target_pairs={{0,2},{1,3},{2,0},{3,1},{4,6},{5,7},{6,4},{7,5},{8,10},{9,11},{10,... | collective-permute-start | bytes 147464 | tf_op jit(solution)/shard_map/ppermute | solution.py:107
  21.9 4.8 %collective-permute-start.8 = (f32[3,4096]{1,0:T(4,128)S(1)}, f32[3,4096]{1,0:T(4,128)S(1)}, u32[]{:S(2)}, u32[]{:S(2)}) collective-permute-start(f32[3,4096]{1,0:T(4,128)S(1)} %reshape.955), channel_id=1, source_target_pairs={{0,3},{1,2},{2,1},{3,0},{4,7},{5,6},{6,5},{7,4},{8,11},{9,10},{10,... | collective-permute-start | bytes 147464 | tf_op jit(solution)/shard_map/ppermute | solution.py:107
  23.3 6.2 %collective-permute-start.5 = (f32[6,4096]{1,0:T(8,128)S(1)}, f32[6,4096]{1,0:T(8,128)S(1)}, u32[]{:S(2)}, u32[]{:S(2)}) collective-permute-start(f32[6,4096]{1,0:T(8,128)S(1)} %reshape.953), channel_id=1, source_target_pairs={{0,3},{1,2},{2,1},{3,0},{4,7},{5,6},{6,5},{7,4},{8,11},{9,10},{10,... | collective-permute-start | bytes 294920 | tf_op jit(solution)/shard_map/ppermute | solution.py:107
  34.2 4.9 %collective-permute-start.10 = (f32[9,512]{1,0:T(8,128)S(1)}, f32[9,512]{1,0:T(8,128)S(1)}, u32[]{:S(2)}, u32[]{:S(2)}) collective-permute-start(f32[9,512]{1,0:T(8,128)S(1)} %reshape.960), channel_id=1, source_target_pairs={{0,8},{4,12},{8,0},{12,4},{1,9},{5,13},{9,1},{13,5},{2,10},{6,14},... | collective-permute-start | bytes 55304 | tf_op jit(solution)/shard_map/ppermute | solution.py:107
  36.0 5.7 %collective-permute-start.11 = (f32[9,512]{1,0:T(8,128)S(1)}, f32[9,512]{1,0:T(8,128)S(1)}, u32[]{:S(2)}, u32[]{:S(2)}) collective-permute-start(f32[9,512]{1,0:T(8,128)S(1)} %reshape.960), channel_id=1, source_target_pairs={{0,12},{4,8},{8,4},{12,0},{1,13},{5,9},{9,5},{13,1},{2,14},{6,10},... | collective-permute-start | bytes 55304 | tf_op jit(solution)/shard_map/ppermute | solution.py:107
  38.0 4.1 %collective-permute-start.9 = (f32[9,512]{1,0:T(8,128)S(1)}, f32[9,512]{1,0:T(8,128)S(1)}, u32[]{:S(2)}, u32[]{:S(2)}) collective-permute-start(f32[9,512]{1,0:T(8,128)S(1)} %reshape.960), channel_id=1, source_target_pairs={{0,4},{4,0},{8,12},{12,8},{1,5},{5,1},{9,13},{13,9},{2,6},{6,2},{1... | collective-permute-start | bytes 55304 | tf_op jit(solution)/shard_map/ppermute | solution.py:107
  44.0 1.9 %collective-permute-start.12 = (f32[2]{0:T(128)S(1)}, f32[2]{0:T(128)S(1)}, u32[]{:S(2)}, u32[]{:S(2)}) collective-permute-start(f32[2]{0:T(128)S(1)} %pad_maximum_fusion.18), channel_id=1, source_target_pairs={{0,1},{1,0},{2,3},{3,2},{4,5},{5,4},{6,7},{7,6},{8,9},{9,8},{10,11... | collective-permute-start | bytes 32 | tf_op jit(solution)/shard_map/ppermute | solution.py:107
  44.0 3.6 %collective-permute-start.13 = (f32[2]{0:T(128)S(1)}, f32[2]{0:T(128)S(1)}, u32[]{:S(2)}, u32[]{:S(2)}) collective-permute-start(f32[2]{0:T(128)S(1)} %pad_maximum_fusion.18), channel_id=1, source_target_pairs={{0,2},{1,3},{2,0},{3,1},{4,6},{5,7},{6,4},{7,5},{8,10},{9,11},{10,... | collective-permute-start | bytes 32 | tf_op jit(solution)/shard_map/ppermute | solution.py:107
  45.1 3.0 %collective-permute-start.14 = (f32[2]{0:T(128)S(1)}, f32[2]{0:T(128)S(1)}, u32[]{:S(2)}, u32[]{:S(2)}) collective-permute-start(f32[2]{0:T(128)S(1)} %pad_maximum_fusion.18), channel_id=1, source_target_pairs={{0,3},{1,2},{2,1},{3,0},{4,7},{5,6},{6,5},{7,4},{8,11},{9,10},{10,... | collective-permute-start | bytes 32 | tf_op jit(solution)/shard_map/ppermute | solution.py:107
  55.7 1.9 %collective-permute-start.18 = (f32[3,4096]{1,0:T(4,128)S(1)}, f32[3,4096]{1,0:T(4,128)S(1)}, u32[]{:S(2)}, u32[]{:S(2)}) collective-permute-start(f32[3,4096]{1,0:T(4,128)S(1)} %reshape.965), channel_id=1, source_target_pairs={{0,1},{1,0},{2,3},{3,2},{4,5},{5,4},{6,7},{7,6},{8,9},{9,8},{10,11... | collective-permute-start | bytes 147464 | tf_op jit(solution)/shard_map/ppermute | solution.py:107
  55.9 4.7 %collective-permute-start.19 = (f32[3,4096]{1,0:T(4,128)S(1)}, f32[3,4096]{1,0:T(4,128)S(1)}, u32[]{:S(2)}, u32[]{:S(2)}) collective-permute-start(f32[3,4096]{1,0:T(4,128)S(1)} %reshape.965), channel_id=1, source_target_pairs={{0,2},{1,3},{2,0},{3,1},{4,6},{5,7},{6,4},{7,5},{8,10},{9,11},{10,... | collective-permute-start | bytes 147464 | tf_op jit(solution)/shard_map/ppermute | solution.py:107
  56.9 4.4 %collective-permute-start.20 = (f32[3,4096]{1,0:T(4,128)S(1)}, f32[3,4096]{1,0:T(4,128)S(1)}, u32[]{:S(2)}, u32[]{:S(2)}) collective-permute-start(f32[3,4096]{1,0:T(4,128)S(1)} %reshape.965), channel_id=1, source_target_pairs={{0,3},{1,2},{2,1},{3,0},{4,7},{5,6},{6,5},{7,4},{8,11},{9,10},{10,... | collective-permute-start | bytes 147464 | tf_op jit(solution)/shard_map/ppermute | solution.py:107
  65.1 12.1 %collective-permute-start.21 = (f32[9,512]{1,0:T(8,128)S(1)}, f32[9,512]{1,0:T(8,128)S(1)}, u32[]{:S(2)}, u32[]{:S(2)}) collective-permute-start(f32[9,512]{1,0:T(8,128)S(1)} %reshape.970), channel_id=1, source_target_pairs={{0,4},{4,0},{8,12},{12,8},{1,5},{5,1},{9,13},{13,9},{2,6},{6,2},{1... | collective-permute-start | bytes 55304 | tf_op jit(solution)/shard_map/ppermute | solution.py:107
  65.7 11.5 %collective-permute-start.22 = (f32[9,512]{1,0:T(8,128)S(1)}, f32[9,512]{1,0:T(8,128)S(1)}, u32[]{:S(2)}, u32[]{:S(2)}) collective-permute-start(f32[9,512]{1,0:T(8,128)S(1)} %reshape.970), channel_id=1, source_target_pairs={{0,8},{4,12},{8,0},{12,4},{1,9},{5,13},{9,1},{13,5},{2,10},{6,14},... | collective-permute-start | bytes 55304 | tf_op jit(solution)/shard_map/ppermute | solution.py:107
  67.7 9.5 %collective-permute-start.23 = (f32[9,512]{1,0:T(8,128)S(1)}, f32[9,512]{1,0:T(8,128)S(1)}, u32[]{:S(2)}, u32[]{:S(2)}) collective-permute-start(f32[9,512]{1,0:T(8,128)S(1)} %reshape.970), channel_id=1, source_target_pairs={{0,12},{4,8},{8,4},{12,0},{1,13},{5,9},{9,5},{13,1},{2,14},{6,10},... | collective-permute-start | bytes 55304 | tf_op jit(solution)/shard_map/ppermute | solution.py:107
  69.5 4.5 %collective-permute-start.16 = (f32[]{:T(128)}, f32[]{:T(128)}, u32[]{:S(2)}, u32[]{:S(2)}) collective-permute-start(f32[]{:T(128)} %get-tuple-element.17), channel_id=1, source_target_pairs={{0,2},{1,3},{2,0},{3,1},{4,6},{5,7},{6,4},{7,5},{8,10},{9,11},{10,... | collective-permute-start | bytes 20 | tf_op jit(solution)/shard_map/ppermute | solution.py:107
  70.6 1.4 %collective-permute-start.15 = (f32[]{:T(128)}, f32[]{:T(128)}, u32[]{:S(2)}, u32[]{:S(2)}) collective-permute-start(f32[]{:T(128)} %get-tuple-element.17), channel_id=1, source_target_pairs={{0,1},{1,0},{2,3},{3,2},{4,5},{5,4},{6,7},{7,6},{8,9},{9,8},{10,11... | collective-permute-start | bytes 20 | tf_op jit(solution)/shard_map/ppermute | solution.py:107
  72.0 3.2 %collective-permute-start.17 = (f32[]{:T(128)}, f32[]{:T(128)}, u32[]{:S(2)}, u32[]{:S(2)}) collective-permute-start(f32[]{:T(128)} %get-tuple-element.17), channel_id=1, source_target_pairs={{0,3},{1,2},{2,1},{3,0},{4,7},{5,6},{6,5},{7,4},{8,11},{9,10},{10,... | collective-permute-start | bytes 20 | tf_op jit(solution)/shard_map/ppermute | solution.py:107
  77.8 4.5 %collective-permute-start.25 = (f32[]{:T(128)}, f32[]{:T(128)}, u32[]{:S(2)}, u32[]{:S(2)}) collective-permute-start(f32[]{:T(128)} %get-tuple-element.15), channel_id=1, source_target_pairs={{0,2},{1,3},{2,0},{3,1},{4,6},{5,7},{6,4},{7,5},{8,10},{9,11},{10,... | collective-permute-start | bytes 20 | tf_op jit(solution)/shard_map/ppermute | solution.py:107
  78.8 3.5 %collective-permute-start.26 = (f32[]{:T(128)}, f32[]{:T(128)}, u32[]{:S(2)}, u32[]{:S(2)}) collective-permute-start(f32[]{:T(128)} %get-tuple-element.15), channel_id=1, source_target_pairs={{0,3},{1,2},{2,1},{3,0},{4,7},{5,6},{6,5},{7,4},{8,11},{9,10},{10,... | collective-permute-start | bytes 20 | tf_op jit(solution)/shard_map/ppermute | solution.py:107
  79.2 1.9 %collective-permute-start.24 = (f32[]{:T(128)}, f32[]{:T(128)}, u32[]{:S(2)}, u32[]{:S(2)}) collective-permute-start(f32[]{:T(128)} %get-tuple-element.15), channel_id=1, source_target_pairs={{0,1},{1,0},{2,3},{3,2},{4,5},{5,4},{6,7},{7,6},{8,9},{9,8},{10,11... | collective-permute-start | bytes 20 | tf_op jit(solution)/shard_map/ppermute | solution.py:107
  88.2 1.9 %collective-permute-start.30 = (f32[3,4096]{1,0:T(4,128)S(1)}, f32[3,4096]{1,0:T(4,128)S(1)}, u32[]{:S(2)}, u32[]{:S(2)}) collective-permute-start(f32[3,4096]{1,0:T(4,128)S(1)} %reshape.975), channel_id=1, source_target_pairs={{0,1},{1,0},{2,3},{3,2},{4,5},{5,4},{6,7},{7,6},{8,9},{9,8},{10,11... | collective-permute-start | bytes 147464 | tf_op jit(solution)/shard_map/ppermute | solution.py:107
  88.6 4.5 %collective-permute-start.31 = (f32[3,4096]{1,0:T(4,128)S(1)}, f32[3,4096]{1,0:T(4,128)S(1)}, u32[]{:S(2)}, u32[]{:S(2)}) collective-permute-start(f32[3,4096]{1,0:T(4,128)S(1)} %reshape.975), channel_id=1, source_target_pairs={{0,2},{1,3},{2,0},{3,1},{4,6},{5,7},{6,4},{7,5},{8,10},{9,11},{10,... | collective-permute-start | bytes 147464 | tf_op jit(solution)/shard_map/ppermute | solution.py:107
  89.6 4.4 %collective-permute-start.32 = (f32[3,4096]{1,0:T(4,128)S(1)}, f32[3,4096]{1,0:T(4,128)S(1)}, u32[]{:S(2)}, u32[]{:S(2)}) collective-permute-start(f32[3,4096]{1,0:T(4,128)S(1)} %reshape.975), channel_id=1, source_target_pairs={{0,3},{1,2},{2,1},{3,0},{4,7},{5,6},{6,5},{7,4},{8,11},{9,10},{10,... | collective-permute-start | bytes 147464 | tf_op jit(solution)/shard_map/ppermute | solution.py:107
  97.7 11.4 %collective-permute-start.33 = (f32[9,512]{1,0:T(8,128)S(1)}, f32[9,512]{1,0:T(8,128)S(1)}, u32[]{:S(2)}, u32[]{:S(2)}) collective-permute-start(f32[9,512]{1,0:T(8,128)S(1)} %reshape.980), channel_id=1, source_target_pairs={{0,4},{4,0},{8,12},{12,8},{1,5},{5,1},{9,13},{13,9},{2,6},{6,2},{1... | collective-permute-start | bytes 55304 | tf_op jit(solution)/shard_map/ppermute | solution.py:107
  97.8 11.4 %collective-permute-start.34 = (f32[9,512]{1,0:T(8,128)S(1)}, f32[9,512]{1,0:T(8,128)S(1)}, u32[]{:S(2)}, u32[]{:S(2)}) collective-permute-start(f32[9,512]{1,0:T(8,128)S(1)} %reshape.980), channel_id=1, source_target_pairs={{0,8},{4,12},{8,0},{12,4},{1,9},{5,13},{9,1},{13,5},{2,10},{6,14},... | collective-permute-start | bytes 55304 | tf_op jit(solution)/shard_map/ppermute | solution.py:107
  100.4 8.8 %collective-permute-start.35 = (f32[9,512]{1,0:T(8,128)S(1)}, f32[9,512]{1,0:T(8,128)S(1)}, u32[]{:S(2)}, u32[]{:S(2)}) collective-permute-start(f32[9,512]{1,0:T(8,128)S(1)} %reshape.980), channel_id=1, source_target_pairs={{0,12},{4,8},{8,4},{12,0},{1,13},{5,9},{9,5},{13,1},{2,14},{6,10},... | collective-permute-start | bytes 55304 | tf_op jit(solution)/shard_map/ppermute | solution.py:107
  102.2 4.5 %collective-permute-start.28 = (f32[]{:T(128)}, f32[]{:T(128)}, u32[]{:S(2)}, u32[]{:S(2)}) collective-permute-start(f32[]{:T(128)} %get-tuple-element.12), channel_id=1, source_target_pairs={{0,2},{1,3},{2,0},{3,1},{4,6},{5,7},{6,4},{7,5},{8,10},{9,11},{10,... | collective-permute-start | bytes 20 | tf_op jit(solution)/shard_map/ppermute | solution.py:107
  103.2 1.4 %collective-permute-start.27 = (f32[]{:T(128)}, f32[]{:T(128)}, u32[]{:S(2)}, u32[]{:S(2)}) collective-permute-start(f32[]{:T(128)} %get-tuple-element.12), channel_id=1, source_target_pairs={{0,1},{1,0},{2,3},{3,2},{4,5},{5,4},{6,7},{7,6},{8,9},{9,8},{10,11... | collective-permute-start | bytes 20 | tf_op jit(solution)/shard_map/ppermute | solution.py:107
  104.6 3.2 %collective-permute-start.29 = (f32[]{:T(128)}, f32[]{:T(128)}, u32[]{:S(2)}, u32[]{:S(2)}) collective-permute-start(f32[]{:T(128)} %get-tuple-element.12), channel_id=1, source_target_pairs={{0,3},{1,2},{2,1},{3,0},{4,7},{5,6},{6,5},{7,4},{8,11},{9,10},{10,... | collective-permute-start | bytes 20 | tf_op jit(solution)/shard_map/ppermute | solution.py:107
  109.8 4.5 %collective-permute-start.37 = (f32[]{:T(128)}, f32[]{:T(128)}, u32[]{:S(2)}, u32[]{:S(2)}) collective-permute-start(f32[]{:T(128)} %get-tuple-element.10), channel_id=1, source_target_pairs={{0,2},{1,3},{2,0},{3,1},{4,6},{5,7},{6,4},{7,5},{8,10},{9,11},{10,... | collective-permute-start | bytes 20 | tf_op jit(solution)/shard_map/ppermute | solution.py:107
  110.8 3.5 %collective-permute-start.38 = (f32[]{:T(128)}, f32[]{:T(128)}, u32[]{:S(2)}, u32[]{:S(2)}) collective-permute-start(f32[]{:T(128)} %get-tuple-element.10), channel_id=1, source_target_pairs={{0,3},{1,2},{2,1},{3,0},{4,7},{5,6},{6,5},{7,4},{8,11},{9,10},{10,... | collective-permute-start | bytes 20 | tf_op jit(solution)/shard_map/ppermute | solution.py:107
  111.2 1.9 %collective-permute-start.36 = (f32[]{:T(128)}, f32[]{:T(128)}, u32[]{:S(2)}, u32[]{:S(2)}) collective-permute-start(f32[]{:T(128)} %get-tuple-element.10), channel_id=1, source_target_pairs={{0,1},{1,0},{2,3},{3,2},{4,5},{5,4},{6,7},{7,6},{8,9},{9,8},{10,11... | collective-permute-start | bytes 20 | tf_op jit(solution)/shard_map/ppermute | solution.py:107

commit v6 on v5

--- a/solution.py
+++ b/solution.py
@@ -102,7 +102,7 @@
 
 def allsum(value, axis):
     size = SIZES[axis]
-    if size == 4:
+    if size == 4 and axis == "cam":
         peers = [
             lax.ppermute(value, axis, [(i, i ^ mask) for i in range(size)]) for mask in (1, 2, 3)
         ]
@@ -130,29 +130,30 @@
     diag_terms = by_cam.segsum(jnp.sum(cam_jac * cam_jac, axis=0))
     cam_diag = allsum(diag_terms, "pts") + cam_damp[None, :]
 
-    def operate(vec):
+    def operate(vec, extra):
         y = jnp.sum(cam_jac * by_cam.gather(vec)[None], axis=1)
-        u = allsum(by_point.segsum(jnp.sum(point_jac * y[:, None, :], axis=0)), "cam")
+        u_part = by_point.segsum(jnp.sum(point_jac * y[:, None, :], axis=0))
+        extra_row = jnp.zeros((1, npts), F32).at[0, 0].set(extra)
+        u_all = allsum(jnp.concatenate([u_part, extra_row], axis=0), "cam")
+        u = u_all[:3]
         w = jnp.sum(inv * u[None, :, :], axis=1)
         z = y - jnp.sum(point_jac * by_point.gather(w)[None], axis=1)
-        return cam_damp[None, :] * vec + allsum(
+        image = cam_damp[None, :] * vec + allsum(
             by_cam.segsum(jnp.sum(cam_jac * z[:, None, :], axis=0)), "pts"
         )
+        return image, u_all[3, 0]
 
     solution = jnp.zeros_like(reduced_rhs)
     residual = reduced_rhs
     pre = residual / cam_diag
     direction = pre
-    image = operate(direction)
-    sums = norm_sum(jnp.stack([jnp.sum(residual * pre), jnp.sum(direction * image)]))
-    rz = sums[0]
-    alpha = rz / sums[1]
+    image, rz = operate(direction, jnp.sum(residual * pre))
+    alpha = rz / norm_sum(jnp.sum(direction * image))
     solution = solution + alpha * direction
     residual = residual - alpha * image
     for step in range(1, ITERS):
         pre = residual / cam_diag
-        new_rz = norm_sum(jnp.sum(residual * pre))
-        image_pre = operate(pre)
+        image_pre, new_rz = operate(pre, jnp.sum(residual * pre))
         beta = new_rz / rz
         direction = pre + beta * direction
         image = image_pre + beta * image

time: 117 us -> 115 us (0.983)
  starting transfers between devices: 36.6 us -> 27.3 us
  between operations: 13.9 us -> 17.6 us
  waiting for transfers between devices: 26.5 us -> 30 us
    ppermute x39 -> x21, starting transfers between devices: 36.6 us -> 14.1 us  [allsum(): lax.ppermute(value, axis, [(i, i ^ mask) for i in range(size)])]
    ppermute x0 -> x8, waiting for transfers between devices: none -> 16.3 us  [allsum(): lax.ppermute(value, axis, [(i, i ^ step) for i in range(size)])]
    ppermute x0 -> x8, starting transfers between devices: none -> 13.2 us  [allsum(): lax.ppermute(value, axis, [(i, i ^ step) for i in range(size)])]
    ppermute x39 -> x21, waiting for transfers between devices: 26.5 us -> 13.7 us  [allsum(): lax.ppermute(value, axis, [(i, i ^ mask) for i in range(size)])]
    add x5 -> x4, other arithmetic: 1.53 us -> 0.15 us  [allsum(): return value + peers[0] + (peers[1] + peers[2])]
    reduce_sum x6 -> x7, other arithmetic: 2.28 us -> 2.98 us  [the longest x2 1.32 us: on_device(): image_pre, new_rz = operate(pre, jnp.sum(residual * pre))]
  transfers between devices with their start and end apart: 39 -> 29, of which waited for: 18 -> 17; matrix products, arithmetic and copies ran while one was open for 7% -> 11% of each run, Pallas kernels for 0% -> 0%
where the time goes in v6:
time: 115 us
  waiting for transfers between devices  30 us (26%)
  starting transfers between devices  27.3 us (24%)
  other arithmetic  19.5 us (17%)
  between operations  17.6 us (15%)
  matrix products  14.9 us (13%)
  local copies, waits for them, and re-layouts  5.26 us (5%)
    ppermute x8, waiting for transfers between devices, allsum(): lax.ppermute(value, axis, [(i, i ^ step) for i in range(size)])  16.3 us
    ppermute x21, starting transfers between devices, allsum(): lax.ppermute(value, axis, [(i, i ^ mask) for i in range(size)])  14.1 us
    ppermute x21, waiting for transfers between devices, allsum(): lax.ppermute(value, axis, [(i, i ^ mask) for i in range(size)])  13.7 us
    ppermute x8, starting transfers between devices, allsum(): lax.ppermute(value, axis, [(i, i ^ step) for i in range(size)])  13.2 us
    dot_general x8, matrix products, segsum(): lax.dot_general(self.hot3, spread, (((1,), (1,)), ((), ())), preferred_el...  11.5 us
    select_n x8, other arithmetic, segsum(): jnp.where(self.low[None], part[:, None, :], jnp.zeros((), BF))  3.86 us
    dot_general x6, matrix products, gather(): lax.dot_general(stacked, self.hot3t, (((1,), (0,)), ((), ())), preferred_...  3.4 us
    reduce_sum x6, other arithmetic, gather(): return jnp.sum(jnp.where(self.low[None], spread, 0.0), axis=1)  2.83 us
  transfers between devices with their start and end apart: 29, of which 17 were waited for; matrix products, arithmetic and copies ran while one was open for 11% of the time, Pallas kernels for 0%

profile of v6, /device:TPU:0, one launch (start us, length us, event | category | flops | bytes accessed | tf_op | source)
XLA Modules:
  0.0 114.6 jit_solution(2502583160147653854)
XLA Ops:
  0.6 0.7 add_select_fusion
  1.4 1.4 %multiply_reduce_fusion.6 = f32[9,4096]{1,0:T(8,128)S(1)} fusion(f32[2,9,4096]{2,0,1:T(2,128)} %param.13), kind=kLoop, calls=%fused_computation.115 | loop fusion | flops 110592 | bytes 442368 | tf_op jit(solution)/shard_map/reduce_sum | solution.py:130
  3.3 1.1 fusion.24
  4.6 3.1 %collective-permute-start = (f32[9,512]{1,0:T(8,128)S(1)}, f32[9,512]{1,0:T(8,128)S(1)}, u32[]{:S(2)}, u32[]{:S(2)}) collective-permute-start(f32[9,512]{1,0:T(8,128)S(1)} %reshape.1036), channel_id=1, source_target_pairs={{0,4},{4,0},{8,12},{12,8},{1,5},{5,1},{9,13},{13,9},{2,6},{6,2},{1... | collective-permute-start | bytes 55304 | tf_op jit(solution)/shard_map/ppermute | solution.py:114
  8.5 0.9 broadcast_select_fusion.2
  9.4 3.0 %fusion = f32[64,384]{1,0:T(8,128)S(1)} fusion(bf16[384,4096]{1,0:T(8,128)(2,1)S(1)} %bitcast.151, bf16[384,4096]{1,0:T(8,128)(2,1)S(1)} %bitcast.150, bf16[384,4096]{1,0:T(8,128)(2,1)S(1)} %bitcast.149, bf16[64,4096]{1,0:T(8,128)(2,1)S(1)} %get-tuple-element.146), kind=kOutput, calls=%fused_computation | convolution fusion | flops 637009920 | bytes 10059776 | tf_op jit(solution)/shard_map/dot_general | solution.py:46
  12.7 1.6 %collective-permute-start.6 = (f32[6,4096]{1,0:T(8,128)S(1)}, f32[6,4096]{1,0:T(8,128)S(1)}, u32[]{:S(2)}, u32[]{:S(2)}) collective-permute-start(f32[6,4096]{1,0:T(8,128)S(1)} %reshape.1044), channel_id=1, source_target_pairs={{0,2},{1,3},{2,0},{3,1},{4,6},{5,7},{6,4},{7,5},{8,10},{9,11},{10,... | collective-permute-start | bytes 294920 | tf_op jit(solution)/shard_map/ppermute | solution.py:107
  14.6 2.7 %collective-permute-start.1 = (f32[9,512]{1,0:T(8,128)S(1)}, f32[9,512]{1,0:T(8,128)S(1)}, u32[]{:S(2)}, u32[]{:S(2)}) collective-permute-start(f32[9,512]{1,0:T(8,128)S(1)} %add.159), channel_id=1, source_target_pairs={{0,8},{4,12},{8,0},{12,4},{1,9},{5,13},{9,1},{13,5},{2,10},{6,14},... | collective-permute-start | bytes 55304 | tf_op jit(solution)/shard_map/ppermute | solution.py:114
  17.2 0.8 compare_reduce_fusion
  18.1 1.7 %collective-permute-done.1 = f32[9,512]{1,0:T(8,128)S(1)} collective-permute-done((f32[9,512]{1,0:T(8,128)S(1)}, f32[9,512]{1,0:T(8,128)S(1)}, u32[]{:S(2)}, u32[]{:S(2)}) %collective-permute-start.1) | collective-permute-done | bytes 18464 | tf_op jit(solution)/shard_map/ppermute | solution.py:114
  19.7 0.6 multiply_reduce_fusion.27
  20.6 0.5 fusion.55
  21.1 0.5 select_reduce_fusion.5
  21.6 0.5 copy-done
  22.9 1.4 %fusion.6 = f32[64,192]{0,1:T(8,128)S(1)} fusion(bf16[192,4096]{1,0:T(8,128)(2,1)S(1)} %bitcast.154, bf16[192,4096]{1,0:T(8,128)(2,1)S(1)} %bitcast.153, bf16[192,4096]{1,0:T(8,128)(2,1)S(1)} %bitcast.152, bf16[64,4096]{1,0:T(8,128)(2,1)S(1)} %get-tuple-element.146), kind=kOutput, calls=%fused_computation.6 | convolution fusion | flops 320864256 | bytes 5292032 | tf_op jit(solution)/shard_map/dot_general | solution.py:46
  26.0 1.6 %collective-permute-start.3 = (f32[4,4096]{1,0:T(4,128)S(1)}, f32[4,4096]{1,0:T(4,128)S(1)}, u32[]{:S(2)}, u32[]{:S(2)}) collective-permute-start(f32[4,4096]{1,0:T(4,128)S(1)} %select_maximum_fusion.2), channel_id=1, source_target_pairs={{0,2},{1,3},{2,0},{3,1},{4,6},{5,7},{6,4},{7,5},{8,10},{9,11},{10,... | collective-permute-start | bytes 196616 | tf_op jit(solution)/shard_map/ppermute | solution.py:107
  28.6 1.9 %collective-permute-done.3 = f32[4,4096]{1,0:T(4,128)S(1)} collective-permute-done((f32[4,4096]{1,0:T(4,128)S(1)}, f32[4,4096]{1,0:T(4,128)S(1)}, u32[]{:S(2)}, u32[]{:S(2)}) %collective-permute-start.3) | collective-permute-done | bytes 65568 | tf_op jit(solution)/shard_map/ppermute | solution.py:107
  30.4 1.2 %collective-permute-done.4 = f32[4,4096]{1,0:T(4,128)S(1)} collective-permute-done((f32[4,4096]{1,0:T(4,128)S(1)}, f32[4,4096]{1,0:T(4,128)S(1)}, u32[]{:S(2)}, u32[]{:S(2)}) %collective-permute-start.4) | collective-permute-done | bytes 65568 | tf_op jit(solution)/shard_map/ppermute | solution.py:107
  32.1 0.6 fusion.51
  34.1 1.1 fusion.30
  35.6 3.8 %collective-permute-done.8 = f32[9,512]{1,0:T(8,128)S(1)} collective-permute-done((f32[9,512]{1,0:T(8,128)S(1)}, f32[9,512]{1,0:T(8,128)S(1)}, u32[]{:S(2)}, u32[]{:S(2)}) %collective-permute-start.8) | collective-permute-done | bytes 18464 | tf_op jit(solution)/shard_map/ppermute | solution.py:114
  39.4 2.3 %collective-permute-start.9 = (f32[9,512]{1,0:T(8,128)S(1)}, f32[9,512]{1,0:T(8,128)S(1)}, u32[]{:S(2)}, u32[]{:S(2)}) collective-permute-start(f32[9,512]{1,0:T(8,128)S(1)} %add.172), channel_id=1, source_target_pairs={{0,8},{4,12},{8,0},{12,4},{1,9},{5,13},{9,1},{13,5},{2,10},{6,14},... | collective-permute-start | bytes 55304 | tf_op jit(solution)/shard_map/ppermute | solution.py:114
  41.7 0.6 slice.186
  42.3 1.9 %collective-permute-done.9 = f32[9,512]{1,0:T(8,128)S(1)} collective-permute-done((f32[9,512]{1,0:T(8,128)S(1)}, f32[9,512]{1,0:T(8,128)S(1)}, u32[]{:S(2)}, u32[]{:S(2)}) %collective-permute-start.9) | collective-permute-done | bytes 18464 | tf_op jit(solution)/shard_map/ppermute | solution.py:114
  44.2 0.6 multiply_reduce_fusion.20
  44.8 1.2 %collective-permute-start.11 = (f32[]{:T(128)}, f32[]{:T(128)}, u32[]{:S(2)}, u32[]{:S(2)}) collective-permute-start(f32[]{:T(128)} %get-tuple-element.54), channel_id=1, source_target_pairs={{0,2},{1,3},{2,0},{3,1},{4,6},{5,7},{6,4},{7,5},{8,10},{9,11},{10,... | collective-permute-start | bytes 20 | tf_op jit(solution)/shard_map/ppermute | solution.py:107
  46.0 0.9 collective-permute-start.10
  47.0 1.0 collective-permute-done.10
  51.2 0.6 multiply_reduce_fusion.19
  52.0 0.5 fusion.54
  52.5 0.5 select_reduce_fusion.4
  53.8 1.4 %fusion.12 = f32[64,192]{0,1:T(8,128)S(1)} fusion(bf16[192,4096]{1,0:T(8,128)(2,1)S(1)} %bitcast.157, bf16[192,4096]{1,0:T(8,128)(2,1)S(1)} %bitcast.156, bf16[192,4096]{1,0:T(8,128)(2,1)S(1)} %bitcast.155, bf16[64,4096]{1,0:T(8,128)(2,1)S(1)} %get-tuple-element.146), kind=kOutput, calls=%fused_computation.12 | convolution fusion | flops 320864256 | bytes 5292032 | tf_op jit(solution)/shard_map/dot_general | solution.py:46
  57.1 1.2 %collective-permute-start.14 = (f32[4,4096]{1,0:T(4,128)S(1)}, f32[4,4096]{1,0:T(4,128)S(1)}, u32[]{:S(2)}, u32[]{:S(2)}) collective-permute-start(f32[4,4096]{1,0:T(4,128)S(1)} %select_maximum_fusion.1), channel_id=1, source_target_pairs={{0,2},{1,3},{2,0},{3,1},{4,6},{5,7},{6,4},{7,5},{8,10},{9,11},{10,... | collective-permute-start | bytes 196616 | tf_op jit(solution)/shard_map/ppermute | solution.py:107
  58.7 2.7 %collective-permute-done.14 = f32[4,4096]{1,0:T(4,128)S(1)} collective-permute-done((f32[4,4096]{1,0:T(4,128)S(1)}, f32[4,4096]{1,0:T(4,128)S(1)}, u32[]{:S(2)}, u32[]{:S(2)}) %collective-permute-start.14) | collective-permute-done | bytes 65568 | tf_op jit(solution)/shard_map/ppermute | solution.py:107
  61.4 1.3 %collective-permute-done.15 = f32[4,4096]{1,0:T(4,128)S(1)} collective-permute-done((f32[4,4096]{1,0:T(4,128)S(1)}, f32[4,4096]{1,0:T(4,128)S(1)}, u32[]{:S(2)}, u32[]{:S(2)}) %collective-permute-start.15) | collective-permute-done | bytes 65568 | tf_op jit(solution)/shard_map/ppermute | solution.py:107
  63.2 0.6 fusion.50
  63.8 0.6 select_reduce_fusion.1
  65.4 1.1 fusion.36
  66.9 3.8 %collective-permute-done.16 = f32[9,512]{1,0:T(8,128)S(1)} collective-permute-done((f32[9,512]{1,0:T(8,128)S(1)}, f32[9,512]{1,0:T(8,128)S(1)}, u32[]{:S(2)}, u32[]{:S(2)}) %collective-permute-start.16) | collective-permute-done | bytes 18464 | tf_op jit(solution)/shard_map/ppermute | solution.py:114
  70.7 2.3 %collective-permute-start.17 = (f32[9,512]{1,0:T(8,128)S(1)}, f32[9,512]{1,0:T(8,128)S(1)}, u32[]{:S(2)}, u32[]{:S(2)}) collective-permute-start(f32[9,512]{1,0:T(8,128)S(1)} %add.182), channel_id=1, source_target_pairs={{0,8},{4,12},{8,0},{12,4},{1,9},{5,13},{9,1},{13,5},{2,10},{6,14},... | collective-permute-start | bytes 55304 | tf_op jit(solution)/shard_map/ppermute | solution.py:114
  73.0 0.5 slice.202
  74.8 0.7 collective-permute-done.17
  75.5 0.7 multiply_reduce_fusion.18
  76.2 0.8 collective-permute-start.19
  77.0 1.3 %collective-permute-start.18 = (f32[]{:T(128)}, f32[]{:T(128)}, u32[]{:S(2)}, u32[]{:S(2)}) collective-permute-start(f32[]{:T(128)} %get-tuple-element.49), channel_id=1, source_target_pairs={{0,1},{1,0},{2,3},{3,2},{4,5},{5,4},{6,7},{7,6},{8,9},{9,8},{10,11... | collective-permute-start | bytes 20 | tf_op jit(solution)/shard_map/ppermute | solution.py:107
  78.3 0.9 collective-permute-done.18
  82.4 0.7 multiply_reduce_fusion.17
  83.3 0.5 fusion.53
  85.1 1.4 %fusion.18 = f32[64,192]{0,1:T(8,128)S(1)} fusion(bf16[192,4096]{1,0:T(8,128)(2,1)S(1)} %bitcast.160, bf16[192,4096]{1,0:T(8,128)(2,1)S(1)} %bitcast.159, bf16[192,4096]{1,0:T(8,128)(2,1)S(1)} %bitcast.158, bf16[64,4096]{1,0:T(8,128)(2,1)S(1)} %get-tuple-element.146), kind=kOutput, calls=%fused_computation.18 | convolution fusion | flops 320864256 | bytes 5292032 | tf_op jit(solution)/shard_map/dot_general | solution.py:46
  88.5 0.8 collective-permute-start.22
  89.3 0.7 collective-permute-start.23
  90.1 3.2 %collective-permute-done.22 = f32[4,4096]{1,0:T(4,128)S(1)} collective-permute-done((f32[4,4096]{1,0:T(4,128)S(1)}, f32[4,4096]{1,0:T(4,128)S(1)}, u32[]{:S(2)}, u32[]{:S(2)}) %collective-permute-start.22) | collective-permute-done | bytes 65568 | tf_op jit(solution)/shard_map/ppermute | solution.py:107
  94.2 0.6 fusion.49
  96.2 1.1 fusion.42
  97.7 3.8 %collective-permute-done.24 = f32[9,512]{1,0:T(8,128)S(1)} collective-permute-done((f32[9,512]{1,0:T(8,128)S(1)}, f32[9,512]{1,0:T(8,128)S(1)}, u32[]{:S(2)}, u32[]{:S(2)}) %collective-permute-start.24) | collective-permute-done | bytes 18464 | tf_op jit(solution)/shard_map/ppermute | solution.py:114
  101.5 2.3 %collective-permute-start.25 = (f32[9,512]{1,0:T(8,128)S(1)}, f32[9,512]{1,0:T(8,128)S(1)}, u32[]{:S(2)}, u32[]{:S(2)}) collective-permute-start(f32[9,512]{1,0:T(8,128)S(1)} %add.194), channel_id=1, source_target_pairs={{0,8},{4,12},{8,0},{12,4},{1,9},{5,13},{9,1},{13,5},{2,10},{6,14},... | collective-permute-start | bytes 55304 | tf_op jit(solution)/shard_map/ppermute | solution.py:114
  103.7 0.5 slice.204
  105.6 0.7 collective-permute-done.25
  106.3 0.6 multiply_reduce_fusion.16
  106.9 1.2 %collective-permute-start.27 = (f32[]{:T(128)}, f32[]{:T(128)}, u32[]{:S(2)}, u32[]{:S(2)}) collective-permute-start(f32[]{:T(128)} %get-tuple-element.44), channel_id=1, source_target_pairs={{0,2},{1,3},{2,0},{3,1},{4,6},{5,7},{6,4},{7,5},{8,10},{9,11},{10,... | collective-permute-start | bytes 20 | tf_op jit(solution)/shard_map/ppermute | solution.py:107
  108.1 0.9 collective-permute-start.26
  109.0 1.1 collective-permute-done.26
  113.3 0.6 multiply_add_fusion
  114.0 0.6 multiply_subtract_fusion
  (138 shorter events, 15.1 us)
Async XLA Ops:
  3.3 4.4 %copy-start.1 = (f32[2,3,4096]{2,0,1:T(2,128)S(1)}, f32[2,3,4096]{2,0,1:T(2,128)}, u32[]{:S(2)}) copy-start(f32[2,3,4096]{2,0,1:T(2,128)} %param.14) | copy-start | bytes 294916
  3.3 4.9 %copy-start.4 = (s32[4096]{0:T(1024)S(1)}, s32[4096]{0:T(1024)}, u32[]{:S(2)}) copy-start(s32[4096]{0:T(1024)} %param.16) | copy-start | bytes 49156
  4.6 9.9 %collective-permute-start = (f32[9,512]{1,0:T(8,128)S(1)}, f32[9,512]{1,0:T(8,128)S(1)}, u32[]{:S(2)}, u32[]{:S(2)}) collective-permute-start(f32[9,512]{1,0:T(8,128)S(1)} %reshape.1036), channel_id=1, source_target_pairs={{0,4},{4,0},{8,12},{12,8},{1,5},{5,1},{9,13},{13,9},{2,6},{6,2},{1... | collective-permute-start | bytes 55304 | tf_op jit(solution)/shard_map/ppermute | solution.py:114
  9.3 10.4 %copy-start.2 = (f32[9,512]{1,0:T(8,128)S(1)}, f32[9,512]{1,0:T(8,128)}, u32[]{:S(2)}) copy-start(f32[9,512]{1,0:T(8,128)} %param.19) | copy-start | bytes 55300
  9.4 10.4 %copy-start.3 = (f32[512]{0:T(512)S(1)}, f32[512]{0:T(512)}, u32[]{:S(2)}) copy-start(f32[512]{0:T(512)} %param.18) | copy-start | bytes 6148
  12.6 14.9 %collective-permute-start.5 = (f32[6,4096]{1,0:T(8,128)S(1)}, f32[6,4096]{1,0:T(8,128)S(1)}, u32[]{:S(2)}, u32[]{:S(2)}) collective-permute-start(f32[6,4096]{1,0:T(8,128)S(1)} %reshape.1044), channel_id=1, source_target_pairs={{0,1},{1,0},{2,3},{3,2},{4,5},{5,4},{6,7},{7,6},{8,9},{9,8},{10,11... | collective-permute-start | bytes 294920 | tf_op jit(solution)/shard_map/ppermute | solution.py:107
  12.7 15.1 %collective-permute-start.6 = (f32[6,4096]{1,0:T(8,128)S(1)}, f32[6,4096]{1,0:T(8,128)S(1)}, u32[]{:S(2)}, u32[]{:S(2)}) collective-permute-start(f32[6,4096]{1,0:T(8,128)S(1)} %reshape.1044), channel_id=1, source_target_pairs={{0,2},{1,3},{2,0},{3,1},{4,6},{5,7},{6,4},{7,5},{8,10},{9,11},{10,... | collective-permute-start | bytes 294920 | tf_op jit(solution)/shard_map/ppermute | solution.py:107
  14.3 13.5 %collective-permute-start.7 = (f32[6,4096]{1,0:T(8,128)S(1)}, f32[6,4096]{1,0:T(8,128)S(1)}, u32[]{:S(2)}, u32[]{:S(2)}) collective-permute-start(f32[6,4096]{1,0:T(8,128)S(1)} %reshape.1044), channel_id=1, source_target_pairs={{0,3},{1,2},{2,1},{3,0},{4,7},{5,6},{6,5},{7,4},{8,11},{9,10},{10,... | collective-permute-start | bytes 294920 | tf_op jit(solution)/shard_map/ppermute | solution.py:107
  14.6 5.2 %collective-permute-start.1 = (f32[9,512]{1,0:T(8,128)S(1)}, f32[9,512]{1,0:T(8,128)S(1)}, u32[]{:S(2)}, u32[]{:S(2)}) collective-permute-start(f32[9,512]{1,0:T(8,128)S(1)} %add.159), channel_id=1, source_target_pairs={{0,8},{4,12},{8,0},{12,4},{1,9},{5,13},{9,1},{13,5},{2,10},{6,14},... | collective-permute-start | bytes 55304 | tf_op jit(solution)/shard_map/ppermute | solution.py:114
  21.1 1.0 copy-start
  24.3 3.7 %copy-start.5 = (f32[4096]{0:T(1024)S(1)}, f32[4096]{0:T(1024)}, u32[]{:S(2)}) copy-start(f32[4096]{0:T(1024)} %param.17) | copy-start | bytes 49156
  25.9 2.7 %collective-permute-start.2 = (f32[4,4096]{1,0:T(4,128)S(1)}, f32[4,4096]{1,0:T(4,128)S(1)}, u32[]{:S(2)}, u32[]{:S(2)}) collective-permute-start(f32[4,4096]{1,0:T(4,128)S(1)} %select_maximum_fusion.2), channel_id=1, source_target_pairs={{0,1},{1,0},{2,3},{3,2},{4,5},{5,4},{6,7},{7,6},{8,9},{9,8},{10,11... | collective-permute-start | bytes 196616 | tf_op jit(solution)/shard_map/ppermute | solution.py:107
  26.0 4.5 %collective-permute-start.3 = (f32[4,4096]{1,0:T(4,128)S(1)}, f32[4,4096]{1,0:T(4,128)S(1)}, u32[]{:S(2)}, u32[]{:S(2)}) collective-permute-start(f32[4,4096]{1,0:T(4,128)S(1)} %select_maximum_fusion.2), channel_id=1, source_target_pairs={{0,2},{1,3},{2,0},{3,1},{4,6},{5,7},{6,4},{7,5},{8,10},{9,11},{10,... | collective-permute-start | bytes 196616 | tf_op jit(solution)/shard_map/ppermute | solution.py:107
  27.6 4.1 %collective-permute-start.4 = (f32[4,4096]{1,0:T(4,128)S(1)}, f32[4,4096]{1,0:T(4,128)S(1)}, u32[]{:S(2)}, u32[]{:S(2)}) collective-permute-start(f32[4,4096]{1,0:T(4,128)S(1)} %select_maximum_fusion.2), channel_id=1, source_target_pairs={{0,3},{1,2},{2,1},{3,0},{4,7},{5,6},{6,5},{7,4},{8,11},{9,10},{10,... | collective-permute-start | bytes 196616 | tf_op jit(solution)/shard_map/ppermute | solution.py:107
  35.4 4.0 %collective-permute-start.8 = (f32[9,512]{1,0:T(8,128)S(1)}, f32[9,512]{1,0:T(8,128)S(1)}, u32[]{:S(2)}, u32[]{:S(2)}) collective-permute-start(f32[9,512]{1,0:T(8,128)S(1)} %reshape.1049), channel_id=1, source_target_pairs={{0,4},{4,0},{8,12},{12,8},{1,5},{5,1},{9,13},{13,9},{2,6},{6,2},{1... | collective-permute-start | bytes 55304 | tf_op jit(solution)/shard_map/ppermute | solution.py:114
  39.4 4.8 %collective-permute-start.9 = (f32[9,512]{1,0:T(8,128)S(1)}, f32[9,512]{1,0:T(8,128)S(1)}, u32[]{:S(2)}, u32[]{:S(2)}) collective-permute-start(f32[9,512]{1,0:T(8,128)S(1)} %add.172), channel_id=1, source_target_pairs={{0,8},{4,12},{8,0},{12,4},{1,9},{5,13},{9,1},{13,5},{2,10},{6,14},... | collective-permute-start | bytes 55304 | tf_op jit(solution)/shard_map/ppermute | solution.py:114
  44.8 4.4 %collective-permute-start.11 = (f32[]{:T(128)}, f32[]{:T(128)}, u32[]{:S(2)}, u32[]{:S(2)}) collective-permute-start(f32[]{:T(128)} %get-tuple-element.54), channel_id=1, source_target_pairs={{0,2},{1,3},{2,0},{3,1},{4,6},{5,7},{6,4},{7,5},{8,10},{9,11},{10,... | collective-permute-start | bytes 20 | tf_op jit(solution)/shard_map/ppermute | solution.py:107
  46.0 3.2 %collective-permute-start.12 = (f32[]{:T(128)}, f32[]{:T(128)}, u32[]{:S(2)}, u32[]{:S(2)}) collective-permute-start(f32[]{:T(128)} %get-tuple-element.54), channel_id=1, source_target_pairs={{0,3},{1,2},{2,1},{3,0},{4,7},{5,6},{6,5},{7,4},{8,11},{9,10},{10,... | collective-permute-start | bytes 20 | tf_op jit(solution)/shard_map/ppermute | solution.py:107
  46.0 1.9 %collective-permute-start.10 = (f32[]{:T(128)}, f32[]{:T(128)}, u32[]{:S(2)}, u32[]{:S(2)}) collective-permute-start(f32[]{:T(128)} %get-tuple-element.54), channel_id=1, source_target_pairs={{0,1},{1,0},{2,3},{3,2},{4,5},{5,4},{6,7},{7,6},{8,9},{9,8},{10,11... | collective-permute-start | bytes 20 | tf_op jit(solution)/shard_map/ppermute | solution.py:107
  56.8 1.9 %collective-permute-start.13 = (f32[4,4096]{1,0:T(4,128)S(1)}, f32[4,4096]{1,0:T(4,128)S(1)}, u32[]{:S(2)}, u32[]{:S(2)}) collective-permute-start(f32[4,4096]{1,0:T(4,128)S(1)} %select_maximum_fusion.1), channel_id=1, source_target_pairs={{0,1},{1,0},{2,3},{3,2},{4,5},{5,4},{6,7},{7,6},{8,9},{9,8},{10,11... | collective-permute-start | bytes 196616 | tf_op jit(solution)/shard_map/ppermute | solution.py:107
  57.1 4.3 %collective-permute-start.14 = (f32[4,4096]{1,0:T(4,128)S(1)}, f32[4,4096]{1,0:T(4,128)S(1)}, u32[]{:S(2)}, u32[]{:S(2)}) collective-permute-start(f32[4,4096]{1,0:T(4,128)S(1)} %select_maximum_fusion.1), channel_id=1, source_target_pairs={{0,2},{1,3},{2,0},{3,1},{4,6},{5,7},{6,4},{7,5},{8,10},{9,11},{10,... | collective-permute-start | bytes 196616 | tf_op jit(solution)/shard_map/ppermute | solution.py:107
  58.3 4.4 %collective-permute-start.15 = (f32[4,4096]{1,0:T(4,128)S(1)}, f32[4,4096]{1,0:T(4,128)S(1)}, u32[]{:S(2)}, u32[]{:S(2)}) collective-permute-start(f32[4,4096]{1,0:T(4,128)S(1)} %select_maximum_fusion.1), channel_id=1, source_target_pairs={{0,3},{1,2},{2,1},{3,0},{4,7},{5,6},{6,5},{7,4},{8,11},{9,10},{10,... | collective-permute-start | bytes 196616 | tf_op jit(solution)/shard_map/ppermute | solution.py:107
  66.7 4.0 %collective-permute-start.16 = (f32[9,512]{1,0:T(8,128)S(1)}, f32[9,512]{1,0:T(8,128)S(1)}, u32[]{:S(2)}, u32[]{:S(2)}) collective-permute-start(f32[9,512]{1,0:T(8,128)S(1)} %reshape.1060), channel_id=1, source_target_pairs={{0,4},{4,0},{8,12},{12,8},{1,5},{5,1},{9,13},{13,9},{2,6},{6,2},{1... | collective-permute-start | bytes 55304 | tf_op jit(solution)/shard_map/ppermute | solution.py:114
  70.7 4.8 %collective-permute-start.17 = (f32[9,512]{1,0:T(8,128)S(1)}, f32[9,512]{1,0:T(8,128)S(1)}, u32[]{:S(2)}, u32[]{:S(2)}) collective-permute-start(f32[9,512]{1,0:T(8,128)S(1)} %add.182), channel_id=1, source_target_pairs={{0,8},{4,12},{8,0},{12,4},{1,9},{5,13},{9,1},{13,5},{2,10},{6,14},... | collective-permute-start | bytes 55304 | tf_op jit(solution)/shard_map/ppermute | solution.py:114
  76.2 4.3 %collective-permute-start.19 = (f32[]{:T(128)}, f32[]{:T(128)}, u32[]{:S(2)}, u32[]{:S(2)}) collective-permute-start(f32[]{:T(128)} %get-tuple-element.49), channel_id=1, source_target_pairs={{0,2},{1,3},{2,0},{3,1},{4,6},{5,7},{6,4},{7,5},{8,10},{9,11},{10,... | collective-permute-start | bytes 20 | tf_op jit(solution)/shard_map/ppermute | solution.py:107
  77.0 3.6 %collective-permute-start.20 = (f32[]{:T(128)}, f32[]{:T(128)}, u32[]{:S(2)}, u32[]{:S(2)}) collective-permute-start(f32[]{:T(128)} %get-tuple-element.49), channel_id=1, source_target_pairs={{0,3},{1,2},{2,1},{3,0},{4,7},{5,6},{6,5},{7,4},{8,11},{9,10},{10,... | collective-permute-start | bytes 20 | tf_op jit(solution)/shard_map/ppermute | solution.py:107
  77.0 2.2 %collective-permute-start.18 = (f32[]{:T(128)}, f32[]{:T(128)}, u32[]{:S(2)}, u32[]{:S(2)}) collective-permute-start(f32[]{:T(128)} %get-tuple-element.49), channel_id=1, source_target_pairs={{0,1},{1,0},{2,3},{3,2},{4,5},{5,4},{6,7},{7,6},{8,9},{9,8},{10,11... | collective-permute-start | bytes 20 | tf_op jit(solution)/shard_map/ppermute | solution.py:107
  88.1 1.9 %collective-permute-start.21 = (f32[4,4096]{1,0:T(4,128)S(1)}, f32[4,4096]{1,0:T(4,128)S(1)}, u32[]{:S(2)}, u32[]{:S(2)}) collective-permute-start(f32[4,4096]{1,0:T(4,128)S(1)} %select_maximum_fusion), channel_id=1, source_target_pairs={{0,1},{1,0},{2,3},{3,2},{4,5},{5,4},{6,7},{7,6},{8,9},{9,8},{10,11... | collective-permute-start | bytes 196616 | tf_op jit(solution)/shard_map/ppermute | solution.py:107
  88.5 4.7 %collective-permute-start.22 = (f32[4,4096]{1,0:T(4,128)S(1)}, f32[4,4096]{1,0:T(4,128)S(1)}, u32[]{:S(2)}, u32[]{:S(2)}) collective-permute-start(f32[4,4096]{1,0:T(4,128)S(1)} %select_maximum_fusion), channel_id=1, source_target_pairs={{0,2},{1,3},{2,0},{3,1},{4,6},{5,7},{6,4},{7,5},{8,10},{9,11},{10,... | collective-permute-start | bytes 196616 | tf_op jit(solution)/shard_map/ppermute | solution.py:107
  89.3 4.4 %collective-permute-start.23 = (f32[4,4096]{1,0:T(4,128)S(1)}, f32[4,4096]{1,0:T(4,128)S(1)}, u32[]{:S(2)}, u32[]{:S(2)}) collective-permute-start(f32[4,4096]{1,0:T(4,128)S(1)} %select_maximum_fusion), channel_id=1, source_target_pairs={{0,3},{1,2},{2,1},{3,0},{4,7},{5,6},{6,5},{7,4},{8,11},{9,10},{10,... | collective-permute-start | bytes 196616 | tf_op jit(solution)/shard_map/ppermute | solution.py:107
  97.5 4.0 %collective-permute-start.24 = (f32[9,512]{1,0:T(8,128)S(1)}, f32[9,512]{1,0:T(8,128)S(1)}, u32[]{:S(2)}, u32[]{:S(2)}) collective-permute-start(f32[9,512]{1,0:T(8,128)S(1)} %reshape.1071), channel_id=1, source_target_pairs={{0,4},{4,0},{8,12},{12,8},{1,5},{5,1},{9,13},{13,9},{2,6},{6,2},{1... | collective-permute-start | bytes 55304 | tf_op jit(solution)/shard_map/ppermute | solution.py:114
  101.5 4.8 %collective-permute-start.25 = (f32[9,512]{1,0:T(8,128)S(1)}, f32[9,512]{1,0:T(8,128)S(1)}, u32[]{:S(2)}, u32[]{:S(2)}) collective-permute-start(f32[9,512]{1,0:T(8,128)S(1)} %add.194), channel_id=1, source_target_pairs={{0,8},{4,12},{8,0},{12,4},{1,9},{5,13},{9,1},{13,5},{2,10},{6,14},... | collective-permute-start | bytes 55304 | tf_op jit(solution)/shard_map/ppermute | solution.py:114
  106.9 4.5 %collective-permute-start.27 = (f32[]{:T(128)}, f32[]{:T(128)}, u32[]{:S(2)}, u32[]{:S(2)}) collective-permute-start(f32[]{:T(128)} %get-tuple-element.44), channel_id=1, source_target_pairs={{0,2},{1,3},{2,0},{3,1},{4,6},{5,7},{6,4},{7,5},{8,10},{9,11},{10,... | collective-permute-start | bytes 20 | tf_op jit(solution)/shard_map/ppermute | solution.py:107
  108.1 3.3 %collective-permute-start.28 = (f32[]{:T(128)}, f32[]{:T(128)}, u32[]{:S(2)}, u32[]{:S(2)}) collective-permute-start(f32[]{:T(128)} %get-tuple-element.44), channel_id=1, source_target_pairs={{0,3},{1,2},{2,1},{3,0},{4,7},{5,6},{6,5},{7,4},{8,11},{9,10},{10,... | collective-permute-start | bytes 20 | tf_op jit(solution)/shard_map/ppermute | solution.py:107
  108.1 2.0 %collective-permute-start.26 = (f32[]{:T(128)}, f32[]{:T(128)}, u32[]{:S(2)}, u32[]{:S(2)}) collective-permute-start(f32[]{:T(128)} %get-tuple-element.44), channel_id=1, source_target_pairs={{0,1},{1,0},{2,3},{3,2},{4,5},{5,4},{6,7},{7,6},{8,9},{9,8},{10,11... | collective-permute-start | bytes 20 | tf_op jit(solution)/shard_map/ppermute | solution.py:107

commit v7 on v6

--- a/solution.py
+++ b/solution.py
@@ -130,34 +130,43 @@
     diag_terms = by_cam.segsum(jnp.sum(cam_jac * cam_jac, axis=0))
     cam_diag = allsum(diag_terms, "pts") + cam_damp[None, :]
 
-    def operate(vec, extra):
+    def operate(vec, extras):
         y = jnp.sum(cam_jac * by_cam.gather(vec)[None], axis=1)
         u_part = by_point.segsum(jnp.sum(point_jac * y[:, None, :], axis=0))
-        extra_row = jnp.zeros((1, npts), F32).at[0, 0].set(extra)
+        extras = extras + [jnp.sum(cam_damp[None, :] * vec * vec), jnp.sum(y * y)]
+        count = len(extras)
+        extra_row = jnp.zeros((1, npts), F32).at[0, :count].set(jnp.stack(extras))
         u_all = allsum(jnp.concatenate([u_part, extra_row], axis=0), "cam")
         u = u_all[:3]
+        got = u_all[3, :count]
         w = jnp.sum(inv * u[None, :, :], axis=1)
+        point_energy = got[count - 1] - jnp.sum(u * w)
         z = y - jnp.sum(point_jac * by_point.gather(w)[None], axis=1)
-        image = cam_damp[None, :] * vec + allsum(
-            by_cam.segsum(jnp.sum(cam_jac * z[:, None, :], axis=0)), "pts"
-        )
-        return image, u_all[3, 0]
+        img_part = by_cam.segsum(jnp.sum(cam_jac * z[:, None, :], axis=0))
+        pt_row = jnp.zeros((1, ncam), F32).at[0, 0].set(point_energy)
+        img_all = allsum(jnp.concatenate([img_part, pt_row], axis=0), "pts")
+        image = cam_damp[None, :] * vec + img_all[:-1]
+        energy = got[count - 2] + img_all[-1, 0]
+        return image, got, energy
 
     solution = jnp.zeros_like(reduced_rhs)
     residual = reduced_rhs
     pre = residual / cam_diag
     direction = pre
-    image, rz = operate(direction, jnp.sum(residual * pre))
-    alpha = rz / norm_sum(jnp.sum(direction * image))
+    image, got, curv = operate(direction, [jnp.sum(residual * pre)])
+    rz = got[0]
+    alpha = rz / curv
     solution = solution + alpha * direction
     residual = residual - alpha * image
     for step in range(1, ITERS):
         pre = residual / cam_diag
-        image_pre, new_rz = operate(pre, jnp.sum(residual * pre))
+        image_pre, got, energy = operate(pre, [jnp.sum(residual * pre), jnp.sum(pre * image)])
+        new_rz = got[0]
         beta = new_rz / rz
         direction = pre + beta * direction
         image = image_pre + beta * image
-        alpha = new_rz / norm_sum(jnp.sum(direction * image))
+        curv = energy + beta * (2.0 * got[1] + beta * curv)
+        alpha = new_rz / curv
         rz = new_rz
         solution = solution + alpha * direction
         residual = residual - alpha * image

time: 115 us -> 117 us (1.017)
  other arithmetic: 19.5 us -> 30.7 us
  starting transfers between devices: 27.3 us -> 21 us
  waiting for transfers between devices: 30 us -> 26 us
  local copies, waits for them, and re-layouts: 5.26 us -> 7.05 us
    another operation x1 -> x6, other arithmetic: 0.81 us -> 10.8 us
    ppermute x21 -> x12, starting transfers between devices: 14.1 us -> 7.68 us  [allsum(): lax.ppermute(value, axis, [(i, i ^ mask) for i in range(size)])]
    ppermute x21 -> x12, waiting for transfers between devices: 13.7 us -> 10.4 us  [allsum(): lax.ppermute(value, axis, [(i, i ^ mask) for i in range(size)])]
    reduce_sum x9 -> x12, other arithmetic: 5.02 us -> 7.02 us  [the longest x3 1.97 us: operate(): extras = extras + [jnp.sum(cam_damp[None, :] * vec * vec), jnp.sum(y * y)]]
    slice x3 -> x6, local copies, waits for them, and re-layouts: 1.62 us -> 3.4 us  [the longest x3 1.54 us: operate(): energy = got[count - 2] + img_all[-1, 0]]
  transfers between devices with their start and end apart: 29 -> 20, of which waited for: 17 -> 13; matrix products, arithmetic and copies ran while one was open for 11% -> 13% of each run, Pallas kernels for 0% -> 0%
where the time goes in v7:
time: 117 us; the launch traced here: 116 us
  other arithmetic  30.7 us (26%)
  waiting for transfers between devices  26 us (22%)
  starting transfers between devices  21 us (18%)
  between operations  16.8 us (14%)
  matrix products  14.9 us (13%)
  local copies, waits for them, and re-layouts  7.05 us (6%)
    ppermute x8, waiting for transfers between devices, allsum(): lax.ppermute(value, axis, [(i, i ^ step) for i in range(size)])  15.6 us
    ppermute x8, starting transfers between devices, allsum(): lax.ppermute(value, axis, [(i, i ^ step) for i in range(size)])  13.3 us
    dot_general x8, matrix products, segsum(): lax.dot_general(self.hot3, spread, (((1,), (1,)), ((), ())), preferred_el...  11.5 us
    another operation x6, other arithmetic  10.8 us
    ppermute x12, waiting for transfers between devices, allsum(): lax.ppermute(value, axis, [(i, i ^ mask) for i in range(size)])  10.4 us
    ppermute x12, starting transfers between devices, allsum(): lax.ppermute(value, axis, [(i, i ^ mask) for i in range(size)])  7.68 us
    select_n x8, other arithmetic, segsum(): jnp.where(self.low[None], part[:, None, :], jnp.zeros((), BF))  3.86 us
    dot_general x6, matrix products, gather(): lax.dot_general(stacked, self.hot3t, (((1,), (0,)), ((), ())), preferred_...  3.41 us
  transfers between devices with their start and end apart: 20, of which 13 were waited for; matrix products, arithmetic and copies ran while one was open for 13% of the time, Pallas kernels for 0%

profile of v7, /device:TPU:0, one launch (start us, length us, event | category | flops | bytes accessed | tf_op | source)
XLA Modules:
  0.0 116.5 jit_solution(117433908245177137)
XLA Ops:
  0.6 0.7 add_select_fusion
  1.4 1.4 %multiply_reduce_fusion.6 = f32[9,4096]{1,0:T(8,128)S(1)} fusion(f32[2,9,4096]{2,0,1:T(2,128)} %param.19), kind=kLoop, calls=%fused_computation.115 | loop fusion | flops 110592 | bytes 442368 | tf_op jit(solution)/shard_map/reduce_sum | solution.py:130
  3.3 1.1 fusion.24
  4.6 3.1 %collective-permute-start = (f32[9,512]{1,0:T(8,128)S(1)}, f32[9,512]{1,0:T(8,128)S(1)}, u32[]{:S(2)}, u32[]{:S(2)}) collective-permute-start(f32[9,512]{1,0:T(8,128)S(1)} %reshape.1253), channel_id=1, source_target_pairs={{0,4},{4,0},{8,12},{12,8},{1,5},{5,1},{9,13},{13,9},{2,6},{6,2},{1... | collective-permute-start | bytes 55304 | tf_op jit(solution)/shard_map/ppermute | solution.py:114
  8.5 0.9 broadcast_select_fusion.2
  9.4 3.0 %fusion = f32[64,384]{1,0:T(8,128)S(1)} fusion(bf16[384,4096]{1,0:T(8,128)(2,1)S(1)} %bitcast.173, bf16[384,4096]{1,0:T(8,128)(2,1)S(1)} %bitcast.172, bf16[384,4096]{1,0:T(8,128)(2,1)S(1)} %bitcast.171, bf16[64,4096]{1,0:T(8,128)(2,1)S(1)} %get-tuple-element.195), kind=kOutput, calls=%fused_computation | convolution fusion | flops 637009920 | bytes 10059776 | tf_op jit(solution)/shard_map/dot_general | solution.py:46
  12.7 1.6 %collective-permute-start.6 = (f32[6,4096]{1,0:T(8,128)S(1)}, f32[6,4096]{1,0:T(8,128)S(1)}, u32[]{:S(2)}, u32[]{:S(2)}) collective-permute-start(f32[6,4096]{1,0:T(8,128)S(1)} %reshape.1260), channel_id=1, source_target_pairs={{0,2},{1,3},{2,0},{3,1},{4,6},{5,7},{6,4},{7,5},{8,10},{9,11},{10,... | collective-permute-start | bytes 294920 | tf_op jit(solution)/shard_map/ppermute | solution.py:107
  14.6 2.7 %collective-permute-start.1 = (f32[9,512]{1,0:T(8,128)S(1)}, f32[9,512]{1,0:T(8,128)S(1)}, u32[]{:S(2)}, u32[]{:S(2)}) collective-permute-start(f32[9,512]{1,0:T(8,128)S(1)} %add.174), channel_id=1, source_target_pairs={{0,8},{4,12},{8,0},{12,4},{1,9},{5,13},{9,1},{13,5},{2,10},{6,14},... | collective-permute-start | bytes 55304 | tf_op jit(solution)/shard_map/ppermute | solution.py:114
  17.2 0.6 compare_reduce_fusion.2
  17.9 0.7 compare_reduce_fusion.1
  18.6 1.1 collective-permute-done.1
  19.7 0.6 multiply_reduce_fusion.32
  20.6 0.5 fusion.55
  21.1 0.5 select_reduce_fusion.5
  21.6 0.5 copy-done
  22.4 0.7 multiply_reduce_fusion.31
  23.6 1.4 %fusion.6 = f32[64,192]{0,1:T(8,128)S(1)} fusion(bf16[192,4096]{1,0:T(8,128)(2,1)S(1)} %bitcast.176, bf16[192,4096]{1,0:T(8,128)(2,1)S(1)} %bitcast.175, bf16[192,4096]{1,0:T(8,128)(2,1)S(1)} %bitcast.174, bf16[64,4096]{1,0:T(8,128)(2,1)S(1)} %get-tuple-element.195), kind=kOutput, calls=%fused_computation.6 | convolution fusion | flops 320864256 | bytes 5292032 | tf_op jit(solution)/shard_map/dot_general | solution.py:46
  25.2 2.6 %broadcast_select_fusion.26 = f32[1,3]{1,0:T(1,128)S(1)} fusion(pred[]{:T(512)} %compare_reduce_fusion.2, f32[1,1]{1,0:T(1,128)} %bitcast.15, f32[1,1]{1,0:T(1,128)} %bitcast.14, f32[1,1]{1,0:T(1,128)} %bitcast.13), kind=kLoop, calls=%fused_computation.298 | loop fusion | flops 9 | bytes 25 | tf_op jit(solution)/shard_map/select.39
  27.9 1.6 %collective-permute-start.3 = (f32[4,4096]{1,0:T(4,128)S(1)}, f32[4,4096]{1,0:T(4,128)S(1)}, u32[]{:S(2)}, u32[]{:S(2)}) collective-permute-start(f32[4,4096]{1,0:T(4,128)S(1)} %select_maximum_fusion.2), channel_id=1, source_target_pairs={{0,2},{1,3},{2,0},{3,1},{4,6},{5,7},{6,4},{7,5},{8,10},{9,11},{10,... | collective-permute-start | bytes 196616 | tf_op jit(solution)/shard_map/ppermute | solution.py:107
  30.5 1.9 %collective-permute-done.3 = f32[4,4096]{1,0:T(4,128)S(1)} collective-permute-done((f32[4,4096]{1,0:T(4,128)S(1)}, f32[4,4096]{1,0:T(4,128)S(1)}, u32[]{:S(2)}, u32[]{:S(2)}) %collective-permute-start.3) | collective-permute-done | bytes 65568 | tf_op jit(solution)/shard_map/ppermute | solution.py:107
  32.4 1.2 collective-permute-done.4
  33.9 0.6 multiply_reduce_fusion.18
  34.5 0.6 fusion.133
  35.3 0.6 fusion.51
  37.3 1.1 fusion.30
  40.7 3.8 %collective-permute-done.8 = f32[10,512]{1,0:T(8,128)S(1)} collective-permute-done((f32[10,512]{1,0:T(8,128)S(1)}, f32[10,512]{1,0:T(8,128)S(1)}, u32[]{:S(2)}, u32[]{:S(2)}) %collective-permute-start.8) | collective-permute-done | bytes 20512 | tf_op jit(solution)/shard_map/ppermute | solution.py:114
  44.5 2.3 %collective-permute-start.9 = (f32[10,512]{1,0:T(8,128)S(1)}, f32[10,512]{1,0:T(8,128)S(1)}, u32[]{:S(2)}, u32[]{:S(2)}) collective-permute-start(f32[10,512]{1,0:T(8,128)S(1)} %fusion.136), channel_id=1, source_target_pairs={{0,8},{4,12},{8,0},{12,4},{1,9},{5,13},{9,1},{13,5},{2,10},{6,14},... | collective-permute-start | bytes 61448 | tf_op jit(solution)/shard_map/ppermute | solution.py:114
  46.8 0.6 compare_reduce_fusion
  47.5 1.9 %collective-permute-done.9 = f32[10,512]{1,0:T(8,128)S(1)} collective-permute-done((f32[10,512]{1,0:T(8,128)S(1)}, f32[10,512]{1,0:T(8,128)S(1)}, u32[]{:S(2)}, u32[]{:S(2)}) %collective-permute-start.9) | collective-permute-done | bytes 20512 | tf_op jit(solution)/shard_map/ppermute | solution.py:114
  49.4 0.5 slice.333
  51.9 0.7 multiply_reduce_fusion.24
  52.8 0.5 fusion.54
  54.0 0.6 multiply_reduce_fusion.22
  55.2 1.4 %fusion.12 = f32[64,192]{0,1:T(8,128)S(1)} fusion(bf16[192,4096]{1,0:T(8,128)(2,1)S(1)} %bitcast.179, bf16[192,4096]{1,0:T(8,128)(2,1)S(1)} %bitcast.178, bf16[192,4096]{1,0:T(8,128)(2,1)S(1)} %bitcast.177, bf16[64,4096]{1,0:T(8,128)(2,1)S(1)} %get-tuple-element.195), kind=kOutput, calls=%fused_computation.12 | convolution fusion | flops 320864256 | bytes 5292032 | tf_op jit(solution)/shard_map/dot_general | solution.py:46
  56.8 3.1 %broadcast_select_fusion.25 = f32[1,4]{1,0:T(1,128)S(1)} fusion(pred[]{:T(512)} %compare_reduce_fusion, f32[1,1]{1,0:T(1,128)} %bitcast.66, f32[1,1]{1,0:T(1,128)} %bitcast.65, f32[1,1]{1,0:T(1,128)} %bitcast.64, f32[1,1]{1,0:T(1,128)} %bitcast.63), kind=kLoop, calls=%fused_computation.297 | loop fusion | flops 16 | bytes 33 | tf_op jit(solution)/shard_map/select.40
  60.1 1.3 %collective-permute-start.11 = (f32[4,4096]{1,0:T(4,128)S(1)}, f32[4,4096]{1,0:T(4,128)S(1)}, u32[]{:S(2)}, u32[]{:S(2)}) collective-permute-start(f32[4,4096]{1,0:T(4,128)S(1)} %select_maximum_fusion.1), channel_id=1, source_target_pairs={{0,2},{1,3},{2,0},{3,1},{4,6},{5,7},{6,4},{7,5},{8,10},{9,11},{10,... | collective-permute-start | bytes 196616 | tf_op jit(solution)/shard_map/ppermute | solution.py:107
  61.4 0.6 collective-permute-start.12
  61.9 2.9 %collective-permute-done.11 = f32[4,4096]{1,0:T(4,128)S(1)} collective-permute-done((f32[4,4096]{1,0:T(4,128)S(1)}, f32[4,4096]{1,0:T(4,128)S(1)}, u32[]{:S(2)}, u32[]{:S(2)}) %collective-permute-start.11) | collective-permute-done | bytes 65568 | tf_op jit(solution)/shard_map/ppermute | solution.py:107
  64.8 1.0 collective-permute-done.12
  65.8 0.6 fusion.132
  66.7 0.6 multiply_reduce_fusion.17
  67.4 0.6 fusion.50
  69.5 1.1 fusion.36
  72.8 3.8 %collective-permute-done.13 = f32[10,512]{1,0:T(8,128)S(1)} collective-permute-done((f32[10,512]{1,0:T(8,128)S(1)}, f32[10,512]{1,0:T(8,128)S(1)}, u32[]{:S(2)}, u32[]{:S(2)}) %collective-permute-start.13) | collective-permute-done | bytes 20512 | tf_op jit(solution)/shard_map/ppermute | solution.py:114
  76.6 2.3 %collective-permute-start.14 = (f32[10,512]{1,0:T(8,128)S(1)}, f32[10,512]{1,0:T(8,128)S(1)}, u32[]{:S(2)}, u32[]{:S(2)}) collective-permute-start(f32[10,512]{1,0:T(8,128)S(1)} %fusion.135), channel_id=1, source_target_pairs={{0,8},{4,12},{8,0},{12,4},{1,9},{5,13},{9,1},{13,5},{2,10},{6,14},... | collective-permute-start | bytes 61448 | tf_op jit(solution)/shard_map/ppermute | solution.py:114
  80.9 0.6 collective-permute-done.14
  81.5 0.5 slice.339
  83.9 0.7 multiply_reduce_fusion.21
  84.9 0.5 fusion.53
  86.2 0.7 multiply_reduce_fusion.19
  87.3 1.4 %fusion.18 = f32[64,192]{0,1:T(8,128)S(1)} fusion(bf16[192,4096]{1,0:T(8,128)(2,1)S(1)} %bitcast.182, bf16[192,4096]{1,0:T(8,128)(2,1)S(1)} %bitcast.181, bf16[192,4096]{1,0:T(8,128)(2,1)S(1)} %bitcast.180, bf16[64,4096]{1,0:T(8,128)(2,1)S(1)} %get-tuple-element.195), kind=kOutput, calls=%fused_computation.18 | convolution fusion | flops 320864256 | bytes 5292032 | tf_op jit(solution)/shard_map/dot_general | solution.py:46
  89.0 3.2 %broadcast_select_fusion.24 = f32[1,4]{1,0:T(1,128)S(1)} fusion(pred[]{:T(512)} %compare_reduce_fusion, f32[1,1]{1,0:T(1,128)} %bitcast.92, f32[1,1]{1,0:T(1,128)} %bitcast.91, f32[1,1]{1,0:T(1,128)} %bitcast.90, f32[1,1]{1,0:T(1,128)} %bitcast.89), kind=kLoop, calls=%fused_computation.296 | loop fusion | flops 16 | bytes 33 | tf_op jit(solution)/shard_map/select.41
  92.2 1.0 collective-permute-start.16
  93.2 0.9 collective-permute-start.17
  94.1 3.2 %collective-permute-done.16 = f32[4,4096]{1,0:T(4,128)S(1)} collective-permute-done((f32[4,4096]{1,0:T(4,128)S(1)}, f32[4,4096]{1,0:T(4,128)S(1)}, u32[]{:S(2)}, u32[]{:S(2)}) %collective-permute-start.16) | collective-permute-done | bytes 65568 | tf_op jit(solution)/shard_map/ppermute | solution.py:107
  97.6 0.6 fusion.131
  98.5 0.7 multiply_reduce_fusion.16
  99.3 0.6 fusion.49
  101.3 1.1 fusion.42
  104.7 3.8 %collective-permute-done.18 = f32[10,512]{1,0:T(8,128)S(1)} collective-permute-done((f32[10,512]{1,0:T(8,128)S(1)}, f32[10,512]{1,0:T(8,128)S(1)}, u32[]{:S(2)}, u32[]{:S(2)}) %collective-permute-start.18) | collective-permute-done | bytes 20512 | tf_op jit(solution)/shard_map/ppermute | solution.py:114
  108.6 2.3 %collective-permute-start.19 = (f32[10,512]{1,0:T(8,128)S(1)}, f32[10,512]{1,0:T(8,128)S(1)}, u32[]{:S(2)}, u32[]{:S(2)}) collective-permute-start(f32[10,512]{1,0:T(8,128)S(1)} %fusion.134), channel_id=1, source_target_pairs={{0,8},{4,12},{8,0},{12,4},{1,9},{5,13},{9,1},{13,5},{2,10},{6,14},... | collective-permute-start | bytes 61448 | tf_op jit(solution)/shard_map/ppermute | solution.py:114
  112.8 0.6 collective-permute-done.19
  113.4 0.5 slice.346
  115.8 0.7 fusion.106
  (136 shorter events, 14.9 us)
Async XLA Ops:
  3.3 4.4 %copy-start.1 = (f32[2,3,4096]{2,0,1:T(2,128)S(1)}, f32[2,3,4096]{2,0,1:T(2,128)}, u32[]{:S(2)}) copy-start(f32[2,3,4096]{2,0,1:T(2,128)} %param.20) | copy-start | bytes 294916
  3.3 4.9 %copy-start.4 = (s32[4096]{0:T(1024)S(1)}, s32[4096]{0:T(1024)}, u32[]{:S(2)}) copy-start(s32[4096]{0:T(1024)} %param.22) | copy-start | bytes 49156
  4.6 9.9 %collective-permute-start = (f32[9,512]{1,0:T(8,128)S(1)}, f32[9,512]{1,0:T(8,128)S(1)}, u32[]{:S(2)}, u32[]{:S(2)}) collective-permute-start(f32[9,512]{1,0:T(8,128)S(1)} %reshape.1253), channel_id=1, source_target_pairs={{0,4},{4,0},{8,12},{12,8},{1,5},{5,1},{9,13},{13,9},{2,6},{6,2},{1... | collective-permute-start | bytes 55304 | tf_op jit(solution)/shard_map/ppermute | solution.py:114
  9.3 10.4 %copy-start.2 = (f32[9,512]{1,0:T(8,128)S(1)}, f32[9,512]{1,0:T(8,128)}, u32[]{:S(2)}) copy-start(f32[9,512]{1,0:T(8,128)} %param.25) | copy-start | bytes 55300
  9.4 10.4 %copy-start.3 = (f32[512]{0:T(512)S(1)}, f32[512]{0:T(512)}, u32[]{:S(2)}) copy-start(f32[512]{0:T(512)} %param.24) | copy-start | bytes 6148
  12.6 16.8 %collective-permute-start.5 = (f32[6,4096]{1,0:T(8,128)S(1)}, f32[6,4096]{1,0:T(8,128)S(1)}, u32[]{:S(2)}, u32[]{:S(2)}) collective-permute-start(f32[6,4096]{1,0:T(8,128)S(1)} %reshape.1260), channel_id=1, source_target_pairs={{0,1},{1,0},{2,3},{3,2},{4,5},{5,4},{6,7},{7,6},{8,9},{9,8},{10,11... | collective-permute-start | bytes 294920 | tf_op jit(solution)/shard_map/ppermute | solution.py:107
  12.7 17.0 %collective-permute-start.6 = (f32[6,4096]{1,0:T(8,128)S(1)}, f32[6,4096]{1,0:T(8,128)S(1)}, u32[]{:S(2)}, u32[]{:S(2)}) collective-permute-start(f32[6,4096]{1,0:T(8,128)S(1)} %reshape.1260), channel_id=1, source_target_pairs={{0,2},{1,3},{2,0},{3,1},{4,6},{5,7},{6,4},{7,5},{8,10},{9,11},{10,... | collective-permute-start | bytes 294920 | tf_op jit(solution)/shard_map/ppermute | solution.py:107
  14.3 15.5 %collective-permute-start.7 = (f32[6,4096]{1,0:T(8,128)S(1)}, f32[6,4096]{1,0:T(8,128)S(1)}, u32[]{:S(2)}, u32[]{:S(2)}) collective-permute-start(f32[6,4096]{1,0:T(8,128)S(1)} %reshape.1260), channel_id=1, source_target_pairs={{0,3},{1,2},{2,1},{3,0},{4,7},{5,6},{6,5},{7,4},{8,11},{9,10},{10,... | collective-permute-start | bytes 294920 | tf_op jit(solution)/shard_map/ppermute | solution.py:107
  14.6 5.2 %collective-permute-start.1 = (f32[9,512]{1,0:T(8,128)S(1)}, f32[9,512]{1,0:T(8,128)S(1)}, u32[]{:S(2)}, u32[]{:S(2)}) collective-permute-start(f32[9,512]{1,0:T(8,128)S(1)} %add.174), channel_id=1, source_target_pairs={{0,8},{4,12},{8,0},{12,4},{1,9},{5,13},{9,1},{13,5},{2,10},{6,14},... | collective-permute-start | bytes 55304 | tf_op jit(solution)/shard_map/ppermute | solution.py:114
  21.1 1.0 copy-start
  25.0 5.0 %copy-start.5 = (f32[4096]{0:T(1024)S(1)}, f32[4096]{0:T(1024)}, u32[]{:S(2)}) copy-start(f32[4096]{0:T(1024)} %param.23) | copy-start | bytes 49156
  27.8 2.7 %collective-permute-start.2 = (f32[4,4096]{1,0:T(4,128)S(1)}, f32[4,4096]{1,0:T(4,128)S(1)}, u32[]{:S(2)}, u32[]{:S(2)}) collective-permute-start(f32[4,4096]{1,0:T(4,128)S(1)} %select_maximum_fusion.2), channel_id=1, source_target_pairs={{0,1},{1,0},{2,3},{3,2},{4,5},{5,4},{6,7},{7,6},{8,9},{9,8},{10,11... | collective-permute-start | bytes 196616 | tf_op jit(solution)/shard_map/ppermute | solution.py:107
  27.9 4.5 %collective-permute-start.3 = (f32[4,4096]{1,0:T(4,128)S(1)}, f32[4,4096]{1,0:T(4,128)S(1)}, u32[]{:S(2)}, u32[]{:S(2)}) collective-permute-start(f32[4,4096]{1,0:T(4,128)S(1)} %select_maximum_fusion.2), channel_id=1, source_target_pairs={{0,2},{1,3},{2,0},{3,1},{4,6},{5,7},{6,4},{7,5},{8,10},{9,11},{10,... | collective-permute-start | bytes 196616 | tf_op jit(solution)/shard_map/ppermute | solution.py:107
  29.5 4.1 %collective-permute-start.4 = (f32[4,4096]{1,0:T(4,128)S(1)}, f32[4,4096]{1,0:T(4,128)S(1)}, u32[]{:S(2)}, u32[]{:S(2)}) collective-permute-start(f32[4,4096]{1,0:T(4,128)S(1)} %select_maximum_fusion.2), channel_id=1, source_target_pairs={{0,3},{1,2},{2,1},{3,0},{4,7},{5,6},{6,5},{7,4},{8,11},{9,10},{10,... | collective-permute-start | bytes 196616 | tf_op jit(solution)/shard_map/ppermute | solution.py:107
  40.5 4.0 %collective-permute-start.8 = (f32[10,512]{1,0:T(8,128)S(1)}, f32[10,512]{1,0:T(8,128)S(1)}, u32[]{:S(2)}, u32[]{:S(2)}) collective-permute-start(f32[10,512]{1,0:T(8,128)S(1)} %select_maximum_fusion.5), channel_id=1, source_target_pairs={{0,4},{4,0},{8,12},{12,8},{1,5},{5,1},{9,13},{13,9},{2,6},{6,2},{1... | collective-permute-start | bytes 61448 | tf_op jit(solution)/shard_map/ppermute | solution.py:114
  44.5 4.9 %collective-permute-start.9 = (f32[10,512]{1,0:T(8,128)S(1)}, f32[10,512]{1,0:T(8,128)S(1)}, u32[]{:S(2)}, u32[]{:S(2)}) collective-permute-start(f32[10,512]{1,0:T(8,128)S(1)} %fusion.136), channel_id=1, source_target_pairs={{0,8},{4,12},{8,0},{12,4},{1,9},{5,13},{9,1},{13,5},{2,10},{6,14},... | collective-permute-start | bytes 61448 | tf_op jit(solution)/shard_map/ppermute | solution.py:114
  60.0 1.9 %collective-permute-start.10 = (f32[4,4096]{1,0:T(4,128)S(1)}, f32[4,4096]{1,0:T(4,128)S(1)}, u32[]{:S(2)}, u32[]{:S(2)}) collective-permute-start(f32[4,4096]{1,0:T(4,128)S(1)} %select_maximum_fusion.1), channel_id=1, source_target_pairs={{0,1},{1,0},{2,3},{3,2},{4,5},{5,4},{6,7},{7,6},{8,9},{9,8},{10,11... | collective-permute-start | bytes 196616 | tf_op jit(solution)/shard_map/ppermute | solution.py:107
  60.1 4.7 %collective-permute-start.11 = (f32[4,4096]{1,0:T(4,128)S(1)}, f32[4,4096]{1,0:T(4,128)S(1)}, u32[]{:S(2)}, u32[]{:S(2)}) collective-permute-start(f32[4,4096]{1,0:T(4,128)S(1)} %select_maximum_fusion.1), channel_id=1, source_target_pairs={{0,2},{1,3},{2,0},{3,1},{4,6},{5,7},{6,4},{7,5},{8,10},{9,11},{10,... | collective-permute-start | bytes 196616 | tf_op jit(solution)/shard_map/ppermute | solution.py:107
  61.4 4.4 %collective-permute-start.12 = (f32[4,4096]{1,0:T(4,128)S(1)}, f32[4,4096]{1,0:T(4,128)S(1)}, u32[]{:S(2)}, u32[]{:S(2)}) collective-permute-start(f32[4,4096]{1,0:T(4,128)S(1)} %select_maximum_fusion.1), channel_id=1, source_target_pairs={{0,3},{1,2},{2,1},{3,0},{4,7},{5,6},{6,5},{7,4},{8,11},{9,10},{10,... | collective-permute-start | bytes 196616 | tf_op jit(solution)/shard_map/ppermute | solution.py:107
  72.6 4.0 %collective-permute-start.13 = (f32[10,512]{1,0:T(8,128)S(1)}, f32[10,512]{1,0:T(8,128)S(1)}, u32[]{:S(2)}, u32[]{:S(2)}) collective-permute-start(f32[10,512]{1,0:T(8,128)S(1)} %select_maximum_fusion.4), channel_id=1, source_target_pairs={{0,4},{4,0},{8,12},{12,8},{1,5},{5,1},{9,13},{13,9},{2,6},{6,2},{1... | collective-permute-start | bytes 61448 | tf_op jit(solution)/shard_map/ppermute | solution.py:114
  76.6 4.9 %collective-permute-start.14 = (f32[10,512]{1,0:T(8,128)S(1)}, f32[10,512]{1,0:T(8,128)S(1)}, u32[]{:S(2)}, u32[]{:S(2)}) collective-permute-start(f32[10,512]{1,0:T(8,128)S(1)} %fusion.135), channel_id=1, source_target_pairs={{0,8},{4,12},{8,0},{12,4},{1,9},{5,13},{9,1},{13,5},{2,10},{6,14},... | collective-permute-start | bytes 61448 | tf_op jit(solution)/shard_map/ppermute | solution.py:114
  92.2 1.9 %collective-permute-start.15 = (f32[4,4096]{1,0:T(4,128)S(1)}, f32[4,4096]{1,0:T(4,128)S(1)}, u32[]{:S(2)}, u32[]{:S(2)}) collective-permute-start(f32[4,4096]{1,0:T(4,128)S(1)} %select_maximum_fusion), channel_id=1, source_target_pairs={{0,1},{1,0},{2,3},{3,2},{4,5},{5,4},{6,7},{7,6},{8,9},{9,8},{10,11... | collective-permute-start | bytes 196616 | tf_op jit(solution)/shard_map/ppermute | solution.py:107
  92.2 5.0 %collective-permute-start.16 = (f32[4,4096]{1,0:T(4,128)S(1)}, f32[4,4096]{1,0:T(4,128)S(1)}, u32[]{:S(2)}, u32[]{:S(2)}) collective-permute-start(f32[4,4096]{1,0:T(4,128)S(1)} %select_maximum_fusion), channel_id=1, source_target_pairs={{0,2},{1,3},{2,0},{3,1},{4,6},{5,7},{6,4},{7,5},{8,10},{9,11},{10,... | collective-permute-start | bytes 196616 | tf_op jit(solution)/shard_map/ppermute | solution.py:107
  93.2 4.4 %collective-permute-start.17 = (f32[4,4096]{1,0:T(4,128)S(1)}, f32[4,4096]{1,0:T(4,128)S(1)}, u32[]{:S(2)}, u32[]{:S(2)}) collective-permute-start(f32[4,4096]{1,0:T(4,128)S(1)} %select_maximum_fusion), channel_id=1, source_target_pairs={{0,3},{1,2},{2,1},{3,0},{4,7},{5,6},{6,5},{7,4},{8,11},{9,10},{10,... | collective-permute-start | bytes 196616 | tf_op jit(solution)/shard_map/ppermute | solution.py:107
  104.6 4.0 %collective-permute-start.18 = (f32[10,512]{1,0:T(8,128)S(1)}, f32[10,512]{1,0:T(8,128)S(1)}, u32[]{:S(2)}, u32[]{:S(2)}) collective-permute-start(f32[10,512]{1,0:T(8,128)S(1)} %select_maximum_fusion.3), channel_id=1, source_target_pairs={{0,4},{4,0},{8,12},{12,8},{1,5},{5,1},{9,13},{13,9},{2,6},{6,2},{1... | collective-permute-start | bytes 61448 | tf_op jit(solution)/shard_map/ppermute | solution.py:114
  108.6 4.9 %collective-permute-start.19 = (f32[10,512]{1,0:T(8,128)S(1)}, f32[10,512]{1,0:T(8,128)S(1)}, u32[]{:S(2)}, u32[]{:S(2)}) collective-permute-start(f32[10,512]{1,0:T(8,128)S(1)} %fusion.134), channel_id=1, source_target_pairs={{0,8},{4,12},{8,0},{12,4},{1,9},{5,13},{9,1},{13,5},{2,10},{6,14},... | collective-permute-start | bytes 61448 | tf_op jit(solution)/shard_map/ppermute | solution.py:114

commit v8 on v7

--- a/solution.py
+++ b/solution.py
@@ -100,18 +100,22 @@
 SIZES = {}
 
 
+def add(first, second):
+    return jax.tree.map(jnp.add, first, second)
+
+
 def allsum(value, axis):
     size = SIZES[axis]
     if size == 4 and axis == "cam":
         peers = [
             lax.ppermute(value, axis, [(i, i ^ mask) for i in range(size)]) for mask in (1, 2, 3)
         ]
-        return (value + peers[0]) + (peers[1] + peers[2])
+        return add(add(value, peers[0]), add(peers[1], peers[2]))
     if size & (size - 1):
         return lax.psum(value, axis)
     step = 1
     while step < size:
-        value = value + lax.ppermute(value, axis, [(i, i ^ step) for i in range(size)])
+        value = add(value, lax.ppermute(value, axis, [(i, i ^ step) for i in range(size)]))
         step *= 2
     return value
 
@@ -135,18 +139,14 @@
         u_part = by_point.segsum(jnp.sum(point_jac * y[:, None, :], axis=0))
         extras = extras + [jnp.sum(cam_damp[None, :] * vec * vec), jnp.sum(y * y)]
         count = len(extras)
-        extra_row = jnp.zeros((1, npts), F32).at[0, :count].set(jnp.stack(extras))
-        u_all = allsum(jnp.concatenate([u_part, extra_row], axis=0), "cam")
-        u = u_all[:3]
-        got = u_all[3, :count]
+        u, got = allsum((u_part, jnp.stack(extras)), "cam")
         w = jnp.sum(inv * u[None, :, :], axis=1)
         point_energy = got[count - 1] - jnp.sum(u * w)
         z = y - jnp.sum(point_jac * by_point.gather(w)[None], axis=1)
         img_part = by_cam.segsum(jnp.sum(cam_jac * z[:, None, :], axis=0))
-        pt_row = jnp.zeros((1, ncam), F32).at[0, 0].set(point_energy)
-        img_all = allsum(jnp.concatenate([img_part, pt_row], axis=0), "pts")
-        image = cam_damp[None, :] * vec + img_all[:-1]
-        energy = got[count - 2] + img_all[-1, 0]
+        img_sum, pt_sum = allsum((img_part, point_energy), "pts")
+        image = cam_damp[None, :] * vec + img_sum
+        energy = got[count - 2] + pt_sum
         return image, got, energy
 
     solution = jnp.zeros_like(reduced_rhs)

time: 117 us -> 139 us (1.19)
  starting transfers between devices: 21 us -> 45.3 us
  waiting for transfers between devices: 26 us -> 21.3 us
  other arithmetic: 30.7 us -> 34.4 us
  local copies, waits for them, and re-layouts: 7.05 us -> 5.43 us
    ppermute x8 -> x14, starting transfers between devices: 13.3 us -> 31.8 us  [allsum(): lax.ppermute(value, axis, [(i, i ^ step) for i in range(size)])]
    ppermute x8 -> x14, waiting for transfers between devices: 15.6 us -> 7.86 us  [allsum(): lax.ppermute(value, axis, [(i, i ^ step) for i in range(size)])]
    add x11, other arithmetic: 0.21 us -> 7.34 us  [add(): return jax.tree.map(jnp.add, first, second)]
    ppermute x12 -> x21, starting transfers between devices: 7.68 us -> 13.5 us  [allsum(): lax.ppermute(value, axis, [(i, i ^ mask) for i in range(size)])]
    another operation x6 -> x3, other arithmetic: 10.8 us -> 7.18 us  [operate(): u, got = allsum((u_part, jnp.stack(extras)), 'cam')]
    ppermute x12 -> x21, waiting for transfers between devices: 10.4 us -> 13.4 us  [allsum(): lax.ppermute(value, axis, [(i, i ^ mask) for i in range(size)])]
    reduce_sum x3 -> x0, other arithmetic: 1.97 us -> none  [operate(): extras = extras + [jnp.sum(cam_damp[None, :] * vec * vec), jnp.sum(y * y)]]
    sub x3, other arithmetic: 0.06 us -> 1.95 us  [operate(): z = y - jnp.sum(point_jac * by_point.gather(w)[None], axis=1)]
  transfers between devices with their start and end apart: 20 -> 35, of which waited for: 13 -> 16; matrix products, arithmetic and copies ran while one was open for 13% -> 19% of each run, Pallas kernels for 0% -> 0%
where the time goes in v8:
time: 139 us
  starting transfers between devices  45.3 us (33%)
  other arithmetic  34.4 us (25%)
  waiting for transfers between devices  21.3 us (15%)
  between operations  16.9 us (12%)
  matrix products  15.2 us (11%)
  local copies, waits for them, and re-layouts  5.43 us (4%)
    ppermute x14, starting transfers between devices, allsum(): lax.ppermute(value, axis, [(i, i ^ step) for i in range(size)])  31.8 us
    ppermute x21, starting transfers between devices, allsum(): lax.ppermute(value, axis, [(i, i ^ mask) for i in range(size)])  13.5 us
    ppermute x21, waiting for transfers between devices, allsum(): lax.ppermute(value, axis, [(i, i ^ mask) for i in range(size)])  13.4 us
    dot_general x8, matrix products, segsum(): lax.dot_general(self.hot3, spread, (((1,), (1,)), ((), ())), preferred_el...  11.8 us
    ppermute x14, waiting for transfers between devices, allsum(): lax.ppermute(value, axis, [(i, i ^ step) for i in range(size)])  7.86 us
    add x11, other arithmetic, add(): return jax.tree.map(jnp.add, first, second)  7.34 us
    another operation x3, other arithmetic, operate(): u, got = allsum((u_part, jnp.stack(extras)), 'cam')  7.18 us
    select_n x8, other arithmetic, segsum(): jnp.where(self.low[None], part[:, None, :], jnp.zeros((), BF))  3.86 us
  transfers between devices with their start and end apart: 35, of which 16 were waited for; matrix products, arithmetic and copies ran while one was open for 19% of the time, Pallas kernels for 0%

profile of v8, /device:TPU:0, one launch (start us, length us, event | category | flops | bytes accessed | tf_op | source)
XLA Modules:
  0.0 138.5 jit_solution(17366105447388700533)
XLA Ops:
  0.6 0.7 add_select_fusion.3
  1.4 1.4 multiply_reduce_fusion.6
  3.3 1.1 fusion.24
  4.6 3.1 %collective-permute-start = (f32[9,512]{1,0:T(8,128)S(1)}, f32[9,512]{1,0:T(8,128)S(1)}, u32[]{:S(2)}, u32[]{:S(2)}) collective-permute-start(f32[9,512]{1,0:T(8,128)S(1)} %reshape.952), channel_id=1, source_target_pairs={{0,4},{4,0},{8,12},{12,8},{1,5},{5,1},{9,13},{13,9},{2,6},{6,2},{1... | collective-permute-start | bytes 55304 | tf_op jit(solution)/shard_map/ppermute | solution.py:118
  8.5 0.9 broadcast_select_fusion.2
  9.6 3.0 %collective-permute-start.1 = (f32[9,512]{1,0:T(8,128)S(1)}, f32[9,512]{1,0:T(8,128)S(1)}, u32[]{:S(2)}, u32[]{:S(2)}) collective-permute-start(f32[9,512]{1,0:T(8,128)S(1)} %add.185), channel_id=1, source_target_pairs={{0,8},{4,12},{8,0},{12,4},{1,9},{5,13},{9,1},{13,5},{2,10},{6,14},... | collective-permute-start | bytes 55304 | tf_op jit(solution)/shard_map/ppermute | solution.py:118
  12.7 3.0 %fusion = f32[64,384]{1,0:T(8,128)S(1)} fusion(bf16[384,4096]{1,0:T(8,128)(2,1)S(1)} %bitcast.167, bf16[384,4096]{1,0:T(8,128)(2,1)S(1)} %bitcast.166, bf16[384,4096]{1,0:T(8,128)(2,1)S(1)} %bitcast.165, bf16[64,4096]{1,0:T(8,128)(2,1)S(1)} %get-tuple-element.129), kind=kOutput, calls=%fused_computation | convolution fusion | flops 637009920 | bytes 10059776 | tf_op jit(solution)/shard_map/dot_general | solution.py:46
  16.0 1.6 %collective-permute-start.8 = (f32[6,4096]{1,0:T(8,128)S(1)}, f32[6,4096]{1,0:T(8,128)S(1)}, u32[]{:S(2)}, u32[]{:S(2)}) collective-permute-start(f32[6,4096]{1,0:T(8,128)S(1)} %reshape.959), channel_id=1, source_target_pairs={{0,1},{1,0},{2,3},{3,2},{4,5},{5,4},{6,7},{7,6},{8,9},{9,8},{10,11... | collective-permute-start | bytes 294920 | tf_op jit(solution)/shard_map/ppermute | solution.py:111
  17.6 0.6 multiply_reduce_fusion.32
  20.8 1.4 %fusion.6 = f32[64,192]{0,1:T(8,128)S(1)} fusion(bf16[192,4096]{1,0:T(8,128)(2,1)S(1)} %bitcast.170, bf16[192,4096]{1,0:T(8,128)(2,1)S(1)} %bitcast.169, bf16[192,4096]{1,0:T(8,128)(2,1)S(1)} %bitcast.168, bf16[64,4096]{1,0:T(8,128)(2,1)S(1)} %get-tuple-element.129), kind=kOutput, calls=%fused_computation.6 | convolution fusion | flops 320864256 | bytes 5292032 | tf_op jit(solution)/shard_map/dot_general | solution.py:46
  23.1 1.2 collective-permute-start.7
  24.9 2.6 %collective-permute-done.6 = f32[3,4096]{1,0:T(4,128)S(1)} collective-permute-done((f32[3,4096]{1,0:T(4,128)S(1)}, f32[3,4096]{1,0:T(4,128)S(1)}, u32[]{:S(2)}, u32[]{:S(2)}) %collective-permute-start.6) | collective-permute-done | bytes 49184 | tf_op jit(solution)/shard_map/ppermute | solution.py:111
  27.9 3.3 %collective-permute-done.9 = f32[6,4096]{1,0:T(8,128)S(1)} collective-permute-done((f32[6,4096]{1,0:T(8,128)S(1)}, f32[6,4096]{1,0:T(8,128)S(1)}, u32[]{:S(2)}, u32[]{:S(2)}) %collective-permute-start.9) | collective-permute-done | bytes 98336 | tf_op jit(solution)/shard_map/ppermute | solution.py:111
  32.3 0.7 multiply_reduce_fusion.18
  33.1 0.6 fusion.51
  34.3 0.6 fusion.133
  34.9 1.9 %pad_maximum_fusion.18 = f32[3]{0:T(128)S(1)} fusion(f32[1]{0:T(128)} %bitcast.10, f32[1]{0:T(128)} %bitcast.6, f32[1]{0:T(128)} %bitcast.5), kind=kLoop, calls=%fused_computation.285 | loop fusion | flops 6 | bytes 24 | tf_op jit(solution)/shard_map/stack | solution.py:142
  36.8 0.7 collective-permute-start.3
  37.5 1.2 collective-permute-start.4
  39.7 1.1 fusion.30
  41.0 1.6 %collective-permute-start.13 = (f32[9,512]{1,0:T(8,128)S(1)}, f32[9,512]{1,0:T(8,128)S(1)}, u32[]{:S(2)}, u32[]{:S(2)}) collective-permute-start(f32[9,512]{1,0:T(8,128)S(1)} %reshape.964), channel_id=1, source_target_pairs={{0,4},{4,0},{8,12},{12,8},{1,5},{5,1},{9,13},{13,9},{2,6},{6,2},{1... | collective-permute-start | bytes 55304 | tf_op jit(solution)/shard_map/ppermute | solution.py:118
  42.7 1.9 %add_add_fusion.7 = f32[3]{0:T(128)S(1)} fusion(f32[3]{0:T(128)S(1)} %collective-permute-done.3, f32[3]{0:T(128)S(1)} %collective-permute-done.4, f32[3]{0:T(128)S(1)} %collective-permute-done.2, f32[1]{0:T(128)} %bitcast.10, f32[1]{0:T(128)} %bitcast.6, f32[1]{0:T(128)} %bitcast.5), kind=kLoop, calls=%fused_computation.290 | loop fusion | flops 15 | bytes 60 | tf_op jit(solution)/shard_map/add | solution.py:104
  47.3 2.9 %collective-permute-start.11 = (f32[]{:T(128)}, f32[]{:T(128)}, u32[]{:S(2)}, u32[]{:S(2)}) collective-permute-start(f32[]{:T(128)} %sub.369), channel_id=1, source_target_pairs={{0,4},{4,0},{8,12},{12,8},{1,5},{5,1},{9,13},{13,9},{2,6},{6,2},{1... | collective-permute-start | bytes 20 | tf_op jit(solution)/shard_map/ppermute | solution.py:118
  50.2 0.6 collective-permute-done.11
  51.6 4.0 %collective-permute-start.12 = (f32[]{:T(128)}, f32[]{:T(128)}, u32[]{:S(2)}, u32[]{:S(2)}) collective-permute-start(f32[]{:T(128)} %add.202), channel_id=1, source_target_pairs={{0,8},{4,12},{8,0},{12,4},{1,9},{5,13},{9,1},{13,5},{2,10},{6,14},... | collective-permute-start | bytes 20 | tf_op jit(solution)/shard_map/ppermute | solution.py:118
  58.0 0.7 multiply_reduce_fusion.24
  60.7 1.4 %fusion.12 = f32[64,192]{0,1:T(8,128)S(1)} fusion(bf16[192,4096]{1,0:T(8,128)(2,1)S(1)} %bitcast.173, bf16[192,4096]{1,0:T(8,128)(2,1)S(1)} %bitcast.172, bf16[192,4096]{1,0:T(8,128)(2,1)S(1)} %bitcast.171, bf16[64,4096]{1,0:T(8,128)(2,1)S(1)} %get-tuple-element.129), kind=kOutput, calls=%fused_computation.12 | convolution fusion | flops 320864256 | bytes 5292032 | tf_op jit(solution)/shard_map/dot_general | solution.py:46
  62.4 1.1 collective-permute-start.19
  63.5 0.8 collective-permute-start.20
  64.3 3.1 %collective-permute-done.19 = f32[3,4096]{1,0:T(4,128)S(1)} collective-permute-done((f32[3,4096]{1,0:T(4,128)S(1)}, f32[3,4096]{1,0:T(4,128)S(1)}, u32[]{:S(2)}, u32[]{:S(2)}) %collective-permute-start.19) | collective-permute-done | bytes 49184 | tf_op jit(solution)/shard_map/ppermute | solution.py:111
  68.4 0.6 fusion.50
  69.5 0.7 fusion.132
  70.1 2.7 %pad_maximum_fusion.19 = f32[4]{0:T(128)S(1)} fusion(f32[1]{0:T(128)} %bitcast.60, f32[1]{0:T(128)} %bitcast.56, f32[1]{0:T(128)} %bitcast.55, f32[1]{0:T(128)} %bitcast.54), kind=kLoop, calls=%fused_computation.286 | loop fusion | flops 12 | bytes 32 | tf_op jit(solution)/shard_map/stack | solution.py:142
  73.1 1.0 collective-permute-start.16
  74.7 0.7 multiply_reduce_fusion.17
  76.3 1.1 fusion.36
  77.5 1.9 %collective-permute-start.23 = (f32[9,512]{1,0:T(8,128)S(1)}, f32[9,512]{1,0:T(8,128)S(1)}, u32[]{:S(2)}, u32[]{:S(2)}) collective-permute-start(f32[9,512]{1,0:T(8,128)S(1)} %reshape.974), channel_id=1, source_target_pairs={{0,4},{4,0},{8,12},{12,8},{1,5},{5,1},{9,13},{13,9},{2,6},{6,2},{1... | collective-permute-start | bytes 55304 | tf_op jit(solution)/shard_map/ppermute | solution.py:118
  79.4 2.7 %add_add_fusion.6 = f32[4]{0:T(128)S(1)} fusion(f32[4]{0:T(128)S(1)} %collective-permute-done.16, f32[4]{0:T(128)S(1)} %collective-permute-done.17, f32[4]{0:T(128)S(1)} %collective-permute-done.15, f32[1]{0:T(128)} %bitcast.60, f32[1]{0:T(128)} %bitcast.56, f32[1]{0:T(128)} %bitcast.55, f32[1]{0:T(128)} %bitcast.54), kind=kLoop, calls=%fused_computation.289 | loop fusion | flops 24 | bytes 80 | tf_op jit(solution)/shard_map/add | solution.py:104
  82.1 2.3 %collective-permute-start.24 = (f32[9,512]{1,0:T(8,128)S(1)}, f32[9,512]{1,0:T(8,128)S(1)}, u32[]{:S(2)}, u32[]{:S(2)}) collective-permute-start(f32[9,512]{1,0:T(8,128)S(1)} %add.221), channel_id=1, source_target_pairs={{0,8},{4,12},{8,0},{12,4},{1,9},{5,13},{9,1},{13,5},{2,10},{6,14},... | collective-permute-start | bytes 55304 | tf_op jit(solution)/shard_map/ppermute | solution.py:118
  84.4 0.6 fusion.135
  88.3 2.5 %collective-permute-start.21 = (f32[]{:T(128)}, f32[]{:T(128)}, u32[]{:S(2)}, u32[]{:S(2)}) collective-permute-start(f32[]{:T(128)} %sub.380), channel_id=1, source_target_pairs={{0,4},{4,0},{8,12},{12,8},{1,5},{5,1},{9,13},{13,9},{2,6},{6,2},{1... | collective-permute-start | bytes 20 | tf_op jit(solution)/shard_map/ppermute | solution.py:118
  90.8 1.2 collective-permute-done.21
  92.6 2.1 %collective-permute-start.22 = (f32[]{:T(128)}, f32[]{:T(128)}, u32[]{:S(2)}, u32[]{:S(2)}) collective-permute-start(f32[]{:T(128)} %add.214), channel_id=1, source_target_pairs={{0,8},{4,12},{8,0},{12,4},{1,9},{5,13},{9,1},{13,5},{2,10},{6,14},... | collective-permute-start | bytes 20 | tf_op jit(solution)/shard_map/ppermute | solution.py:118
  94.6 2.6 %collective-permute-done.22 = f32[]{:T(128)} collective-permute-done((f32[]{:T(128)}, f32[]{:T(128)}, u32[]{:S(2)}, u32[]{:S(2)}) %collective-permute-start.22) | collective-permute-done | bytes 36 | tf_op jit(solution)/shard_map/ppermute | solution.py:118
  99.1 0.6 multiply_reduce_fusion.21
  101.8 1.7 %fusion.18 = f32[64,192]{0,1:T(8,128)S(1)} fusion(bf16[192,4096]{1,0:T(8,128)(2,1)S(1)} %bitcast.176, bf16[192,4096]{1,0:T(8,128)(2,1)S(1)} %bitcast.175, bf16[192,4096]{1,0:T(8,128)(2,1)S(1)} %bitcast.174, bf16[64,4096]{1,0:T(8,128)(2,1)S(1)} %get-tuple-element.129), kind=kOutput, calls=%fused_computation.18 | convolution fusion | flops 320864256 | bytes 5292032 | tf_op jit(solution)/shard_map/dot_general | solution.py:46
  103.7 0.9 collective-permute-start.29
  104.6 1.0 collective-permute-start.30
  105.6 3.2 %collective-permute-done.29 = f32[3,4096]{1,0:T(4,128)S(1)} collective-permute-done((f32[3,4096]{1,0:T(4,128)S(1)}, f32[3,4096]{1,0:T(4,128)S(1)}, u32[]{:S(2)}, u32[]{:S(2)}) %collective-permute-start.29) | collective-permute-done | bytes 49184 | tf_op jit(solution)/shard_map/ppermute | solution.py:111
  109.5 0.6 fusion.49
  110.6 0.7 fusion.131
  111.3 2.6 %pad_maximum_fusion.20 = f32[4]{0:T(128)S(1)} fusion(f32[1]{0:T(128)} %bitcast.85, f32[1]{0:T(128)} %bitcast.81, f32[1]{0:T(128)} %bitcast.80, f32[1]{0:T(128)} %bitcast.79), kind=kLoop, calls=%fused_computation.287 | loop fusion | flops 12 | bytes 32 | tf_op jit(solution)/shard_map/stack | solution.py:142
  114.2 0.9 collective-permute-start.26
  115.1 0.6 collective-permute-start.27
  115.7 0.7 multiply_reduce_fusion.16
  117.3 1.1 fusion.42
  118.6 1.2 collective-permute-start.33
  119.8 2.6 %add_add_fusion.5 = f32[4]{0:T(128)S(1)} fusion(f32[4]{0:T(128)S(1)} %collective-permute-done.26, f32[4]{0:T(128)S(1)} %collective-permute-done.27, f32[4]{0:T(128)S(1)} %collective-permute-done.25, f32[1]{0:T(128)} %bitcast.85, f32[1]{0:T(128)} %bitcast.81, f32[1]{0:T(128)} %bitcast.80, f32[1]{0:T(128)} %bitcast.79), kind=kLoop, calls=%fused_computation.288 | loop fusion | flops 24 | bytes 80 | tf_op jit(solution)/shard_map/add | solution.py:104
  122.6 0.7 collective-permute-start.34
  127.2 2.5 %collective-permute-start.31 = (f32[]{:T(128)}, f32[]{:T(128)}, u32[]{:S(2)}, u32[]{:S(2)}) collective-permute-start(f32[]{:T(128)} %sub.391), channel_id=1, source_target_pairs={{0,4},{4,0},{8,12},{12,8},{1,5},{5,1},{9,13},{13,9},{2,6},{6,2},{1... | collective-permute-start | bytes 20 | tf_op jit(solution)/shard_map/ppermute | solution.py:118
  129.7 1.1 collective-permute-done.31
  131.5 3.6 %collective-permute-start.32 = (f32[]{:T(128)}, f32[]{:T(128)}, u32[]{:S(2)}, u32[]{:S(2)}) collective-permute-start(f32[]{:T(128)} %add.231), channel_id=1, source_target_pairs={{0,8},{4,12},{8,0},{12,4},{1,9},{5,13},{9,1},{13,5},{2,10},{6,14},... | collective-permute-start | bytes 20 | tf_op jit(solution)/shard_map/ppermute | solution.py:118
  135.0 0.9 collective-permute-done.32
  137.8 0.7 fusion.106
  (151 shorter events, 22.4 us)
Async XLA Ops:
  3.3 4.4 %copy-start.1 = (f32[2,3,4096]{2,0,1:T(2,128)S(1)}, f32[2,3,4096]{2,0,1:T(2,128)}, u32[]{:S(2)}) copy-start(f32[2,3,4096]{2,0,1:T(2,128)} %param.8) | copy-start | bytes 294916
  3.3 4.9 %copy-start.4 = (s32[4096]{0:T(1024)S(1)}, s32[4096]{0:T(1024)}, u32[]{:S(2)}) copy-start(s32[4096]{0:T(1024)} %param.10) | copy-start | bytes 49156
  4.6 5.0 %collective-permute-start = (f32[9,512]{1,0:T(8,128)S(1)}, f32[9,512]{1,0:T(8,128)S(1)}, u32[]{:S(2)}, u32[]{:S(2)}) collective-permute-start(f32[9,512]{1,0:T(8,128)S(1)} %reshape.952), channel_id=1, source_target_pairs={{0,4},{4,0},{8,12},{12,8},{1,5},{5,1},{9,13},{13,9},{2,6},{6,2},{1... | collective-permute-start | bytes 55304 | tf_op jit(solution)/shard_map/ppermute | solution.py:118
  9.6 8.0 %collective-permute-start.1 = (f32[9,512]{1,0:T(8,128)S(1)}, f32[9,512]{1,0:T(8,128)S(1)}, u32[]{:S(2)}, u32[]{:S(2)}) collective-permute-start(f32[9,512]{1,0:T(8,128)S(1)} %add.185), channel_id=1, source_target_pairs={{0,8},{4,12},{8,0},{12,4},{1,9},{5,13},{9,1},{13,5},{2,10},{6,14},... | collective-permute-start | bytes 55304 | tf_op jit(solution)/shard_map/ppermute | solution.py:118
  12.7 5.0 %copy-start.2 = (f32[9,512]{1,0:T(8,128)S(1)}, f32[9,512]{1,0:T(8,128)}, u32[]{:S(2)}) copy-start(f32[9,512]{1,0:T(8,128)} %param.13) | copy-start | bytes 55300
  12.7 5.0 %copy-start.3 = (f32[512]{0:T(512)S(1)}, f32[512]{0:T(512)}, u32[]{:S(2)}) copy-start(f32[512]{0:T(512)} %param.12) | copy-start | bytes 6148
  16.0 12.0 %collective-permute-start.10 = (f32[6,4096]{1,0:T(8,128)S(1)}, f32[6,4096]{1,0:T(8,128)S(1)}, u32[]{:S(2)}, u32[]{:S(2)}) collective-permute-start(f32[6,4096]{1,0:T(8,128)S(1)} %reshape.959), channel_id=1, source_target_pairs={{0,3},{1,2},{2,1},{3,0},{4,7},{5,6},{6,5},{7,4},{8,11},{9,10},{10,... | collective-permute-start | bytes 294920 | tf_op jit(solution)/shard_map/ppermute | solution.py:111
  16.0 11.9 %collective-permute-start.8 = (f32[6,4096]{1,0:T(8,128)S(1)}, f32[6,4096]{1,0:T(8,128)S(1)}, u32[]{:S(2)}, u32[]{:S(2)}) collective-permute-start(f32[6,4096]{1,0:T(8,128)S(1)} %reshape.959), channel_id=1, source_target_pairs={{0,1},{1,0},{2,3},{3,2},{4,5},{5,4},{6,7},{7,6},{8,9},{9,8},{10,11... | collective-permute-start | bytes 294920 | tf_op jit(solution)/shard_map/ppermute | solution.py:111
  19.0 1.0 copy-start
  22.2 9.2 %copy-start.5 = (f32[4096]{0:T(1024)S(1)}, f32[4096]{0:T(1024)}, u32[]{:S(2)}) copy-start(f32[4096]{0:T(1024)} %param.11) | copy-start | bytes 49156
  22.4 1.9 %collective-permute-start.5 = (f32[3,4096]{1,0:T(4,128)S(1)}, f32[3,4096]{1,0:T(4,128)S(1)}, u32[]{:S(2)}, u32[]{:S(2)}) collective-permute-start(f32[3,4096]{1,0:T(4,128)S(1)} %reshape.957), channel_id=1, source_target_pairs={{0,1},{1,0},{2,3},{3,2},{4,5},{5,4},{6,7},{7,6},{8,9},{9,8},{10,11... | collective-permute-start | bytes 147464 | tf_op jit(solution)/shard_map/ppermute | solution.py:111
  22.5 5.0 %collective-permute-start.6 = (f32[3,4096]{1,0:T(4,128)S(1)}, f32[3,4096]{1,0:T(4,128)S(1)}, u32[]{:S(2)}, u32[]{:S(2)}) collective-permute-start(f32[3,4096]{1,0:T(4,128)S(1)} %reshape.957), channel_id=1, source_target_pairs={{0,2},{1,3},{2,0},{3,1},{4,6},{5,7},{6,4},{7,5},{8,10},{9,11},{10,... | collective-permute-start | bytes 147464 | tf_op jit(solution)/shard_map/ppermute | solution.py:111
  23.1 4.8 %collective-permute-start.7 = (f32[3,4096]{1,0:T(4,128)S(1)}, f32[3,4096]{1,0:T(4,128)S(1)}, u32[]{:S(2)}, u32[]{:S(2)}) collective-permute-start(f32[3,4096]{1,0:T(4,128)S(1)} %reshape.957), channel_id=1, source_target_pairs={{0,3},{1,2},{2,1},{3,0},{4,7},{5,6},{6,5},{7,4},{8,11},{9,10},{10,... | collective-permute-start | bytes 147464 | tf_op jit(solution)/shard_map/ppermute | solution.py:111
  24.4 6.9 %collective-permute-start.9 = (f32[6,4096]{1,0:T(8,128)S(1)}, f32[6,4096]{1,0:T(8,128)S(1)}, u32[]{:S(2)}, u32[]{:S(2)}) collective-permute-start(f32[6,4096]{1,0:T(8,128)S(1)} %reshape.959), channel_id=1, source_target_pairs={{0,2},{1,3},{2,0},{3,1},{4,6},{5,7},{6,4},{7,5},{8,10},{9,11},{10,... | collective-permute-start | bytes 294920 | tf_op jit(solution)/shard_map/ppermute | solution.py:111
  36.8 5.9 %collective-permute-start.2 = (f32[3]{0:T(128)S(1)}, f32[3]{0:T(128)S(1)}, u32[]{:S(2)}, u32[]{:S(2)}) collective-permute-start(f32[3]{0:T(128)S(1)} %pad_maximum_fusion.18), channel_id=1, source_target_pairs={{0,1},{1,0},{2,3},{3,2},{4,5},{5,4},{6,7},{7,6},{8,9},{9,8},{10,11... | collective-permute-start | bytes 44 | tf_op jit(solution)/shard_map/ppermute | solution.py:111
  36.8 5.8 %collective-permute-start.3 = (f32[3]{0:T(128)S(1)}, f32[3]{0:T(128)S(1)}, u32[]{:S(2)}, u32[]{:S(2)}) collective-permute-start(f32[3]{0:T(128)S(1)} %pad_maximum_fusion.18), channel_id=1, source_target_pairs={{0,2},{1,3},{2,0},{3,1},{4,6},{5,7},{6,4},{7,5},{8,10},{9,11},{10,... | collective-permute-start | bytes 44 | tf_op jit(solution)/shard_map/ppermute | solution.py:111
  37.5 5.2 %collective-permute-start.4 = (f32[3]{0:T(128)S(1)}, f32[3]{0:T(128)S(1)}, u32[]{:S(2)}, u32[]{:S(2)}) collective-permute-start(f32[3]{0:T(128)S(1)} %pad_maximum_fusion.18), channel_id=1, source_target_pairs={{0,3},{1,2},{2,1},{3,0},{4,7},{5,6},{6,5},{7,4},{8,11},{9,10},{10,... | collective-permute-start | bytes 44 | tf_op jit(solution)/shard_map/ppermute | solution.py:111
  41.0 4.0 %collective-permute-start.13 = (f32[9,512]{1,0:T(8,128)S(1)}, f32[9,512]{1,0:T(8,128)S(1)}, u32[]{:S(2)}, u32[]{:S(2)}) collective-permute-start(f32[9,512]{1,0:T(8,128)S(1)} %reshape.964), channel_id=1, source_target_pairs={{0,4},{4,0},{8,12},{12,8},{1,5},{5,1},{9,13},{13,9},{2,6},{6,2},{1... | collective-permute-start | bytes 55304 | tf_op jit(solution)/shard_map/ppermute | solution.py:118
  45.0 12.9 %collective-permute-start.14 = (f32[9,512]{1,0:T(8,128)S(1)}, f32[9,512]{1,0:T(8,128)S(1)}, u32[]{:S(2)}, u32[]{:S(2)}) collective-permute-start(f32[9,512]{1,0:T(8,128)S(1)} %add.205), channel_id=1, source_target_pairs={{0,8},{4,12},{8,0},{12,4},{1,9},{5,13},{9,1},{13,5},{2,10},{6,14},... | collective-permute-start | bytes 55304 | tf_op jit(solution)/shard_map/ppermute | solution.py:118
  47.3 3.6 %collective-permute-start.11 = (f32[]{:T(128)}, f32[]{:T(128)}, u32[]{:S(2)}, u32[]{:S(2)}) collective-permute-start(f32[]{:T(128)} %sub.369), channel_id=1, source_target_pairs={{0,4},{4,0},{8,12},{12,8},{1,5},{5,1},{9,13},{13,9},{2,6},{6,2},{1... | collective-permute-start | bytes 20 | tf_op jit(solution)/shard_map/ppermute | solution.py:118
  51.6 4.5 %collective-permute-start.12 = (f32[]{:T(128)}, f32[]{:T(128)}, u32[]{:S(2)}, u32[]{:S(2)}) collective-permute-start(f32[]{:T(128)} %add.202), channel_id=1, source_target_pairs={{0,8},{4,12},{8,0},{12,4},{1,9},{5,13},{9,1},{13,5},{2,10},{6,14},... | collective-permute-start | bytes 20 | tf_op jit(solution)/shard_map/ppermute | solution.py:118
  62.4 1.9 %collective-permute-start.18 = (f32[3,4096]{1,0:T(4,128)S(1)}, f32[3,4096]{1,0:T(4,128)S(1)}, u32[]{:S(2)}, u32[]{:S(2)}) collective-permute-start(f32[3,4096]{1,0:T(4,128)S(1)} %reshape.969), channel_id=1, source_target_pairs={{0,1},{1,0},{2,3},{3,2},{4,5},{5,4},{6,7},{7,6},{8,9},{9,8},{10,11... | collective-permute-start | bytes 147464 | tf_op jit(solution)/shard_map/ppermute | solution.py:111
  62.4 4.9 %collective-permute-start.19 = (f32[3,4096]{1,0:T(4,128)S(1)}, f32[3,4096]{1,0:T(4,128)S(1)}, u32[]{:S(2)}, u32[]{:S(2)}) collective-permute-start(f32[3,4096]{1,0:T(4,128)S(1)} %reshape.969), channel_id=1, source_target_pairs={{0,2},{1,3},{2,0},{3,1},{4,6},{5,7},{6,4},{7,5},{8,10},{9,11},{10,... | collective-permute-start | bytes 147464 | tf_op jit(solution)/shard_map/ppermute | solution.py:111
  63.5 4.4 %collective-permute-start.20 = (f32[3,4096]{1,0:T(4,128)S(1)}, f32[3,4096]{1,0:T(4,128)S(1)}, u32[]{:S(2)}, u32[]{:S(2)}) collective-permute-start(f32[3,4096]{1,0:T(4,128)S(1)} %reshape.969), channel_id=1, source_target_pairs={{0,3},{1,2},{2,1},{3,0},{4,7},{5,6},{6,5},{7,4},{8,11},{9,10},{10,... | collective-permute-start | bytes 147464 | tf_op jit(solution)/shard_map/ppermute | solution.py:111
  72.8 6.6 %collective-permute-start.15 = (f32[4]{0:T(128)S(1)}, f32[4]{0:T(128)S(1)}, u32[]{:S(2)}, u32[]{:S(2)}) collective-permute-start(f32[4]{0:T(128)S(1)} %pad_maximum_fusion.19), channel_id=1, source_target_pairs={{0,1},{1,0},{2,3},{3,2},{4,5},{5,4},{6,7},{7,6},{8,9},{9,8},{10,11... | collective-permute-start | bytes 56 | tf_op jit(solution)/shard_map/ppermute | solution.py:111
  73.1 6.4 %collective-permute-start.16 = (f32[4]{0:T(128)S(1)}, f32[4]{0:T(128)S(1)}, u32[]{:S(2)}, u32[]{:S(2)}) collective-permute-start(f32[4]{0:T(128)S(1)} %pad_maximum_fusion.19), channel_id=1, source_target_pairs={{0,2},{1,3},{2,0},{3,1},{4,6},{5,7},{6,4},{7,5},{8,10},{9,11},{10,... | collective-permute-start | bytes 56 | tf_op jit(solution)/shard_map/ppermute | solution.py:111
  74.1 5.3 %collective-permute-start.17 = (f32[4]{0:T(128)S(1)}, f32[4]{0:T(128)S(1)}, u32[]{:S(2)}, u32[]{:S(2)}) collective-permute-start(f32[4]{0:T(128)S(1)} %pad_maximum_fusion.19), channel_id=1, source_target_pairs={{0,3},{1,2},{2,1},{3,0},{4,7},{5,6},{6,5},{7,4},{8,11},{9,10},{10,... | collective-permute-start | bytes 56 | tf_op jit(solution)/shard_map/ppermute | solution.py:111
  77.5 4.6 %collective-permute-start.23 = (f32[9,512]{1,0:T(8,128)S(1)}, f32[9,512]{1,0:T(8,128)S(1)}, u32[]{:S(2)}, u32[]{:S(2)}) collective-permute-start(f32[9,512]{1,0:T(8,128)S(1)} %reshape.974), channel_id=1, source_target_pairs={{0,4},{4,0},{8,12},{12,8},{1,5},{5,1},{9,13},{13,9},{2,6},{6,2},{1... | collective-permute-start | bytes 55304 | tf_op jit(solution)/shard_map/ppermute | solution.py:118
  82.1 17.0 %collective-permute-start.24 = (f32[9,512]{1,0:T(8,128)S(1)}, f32[9,512]{1,0:T(8,128)S(1)}, u32[]{:S(2)}, u32[]{:S(2)}) collective-permute-start(f32[9,512]{1,0:T(8,128)S(1)} %add.221), channel_id=1, source_target_pairs={{0,8},{4,12},{8,0},{12,4},{1,9},{5,13},{9,1},{13,5},{2,10},{6,14},... | collective-permute-start | bytes 55304 | tf_op jit(solution)/shard_map/ppermute | solution.py:118
  88.3 3.7 %collective-permute-start.21 = (f32[]{:T(128)}, f32[]{:T(128)}, u32[]{:S(2)}, u32[]{:S(2)}) collective-permute-start(f32[]{:T(128)} %sub.380), channel_id=1, source_target_pairs={{0,4},{4,0},{8,12},{12,8},{1,5},{5,1},{9,13},{13,9},{2,6},{6,2},{1... | collective-permute-start | bytes 20 | tf_op jit(solution)/shard_map/ppermute | solution.py:118
  92.6 4.6 %collective-permute-start.22 = (f32[]{:T(128)}, f32[]{:T(128)}, u32[]{:S(2)}, u32[]{:S(2)}) collective-permute-start(f32[]{:T(128)} %add.214), channel_id=1, source_target_pairs={{0,8},{4,12},{8,0},{12,4},{1,9},{5,13},{9,1},{13,5},{2,10},{6,14},... | collective-permute-start | bytes 20 | tf_op jit(solution)/shard_map/ppermute | solution.py:118
  103.6 1.9 %collective-permute-start.28 = (f32[3,4096]{1,0:T(4,128)S(1)}, f32[3,4096]{1,0:T(4,128)S(1)}, u32[]{:S(2)}, u32[]{:S(2)}) collective-permute-start(f32[3,4096]{1,0:T(4,128)S(1)} %reshape.979), channel_id=1, source_target_pairs={{0,1},{1,0},{2,3},{3,2},{4,5},{5,4},{6,7},{7,6},{8,9},{9,8},{10,11... | collective-permute-start | bytes 147464 | tf_op jit(solution)/shard_map/ppermute | solution.py:111
  103.7 5.0 %collective-permute-start.29 = (f32[3,4096]{1,0:T(4,128)S(1)}, f32[3,4096]{1,0:T(4,128)S(1)}, u32[]{:S(2)}, u32[]{:S(2)}) collective-permute-start(f32[3,4096]{1,0:T(4,128)S(1)} %reshape.979), channel_id=1, source_target_pairs={{0,2},{1,3},{2,0},{3,1},{4,6},{5,7},{6,4},{7,5},{8,10},{9,11},{10,... | collective-permute-start | bytes 147464 | tf_op jit(solution)/shard_map/ppermute | solution.py:111
  104.6 4.5 %collective-permute-start.30 = (f32[3,4096]{1,0:T(4,128)S(1)}, f32[3,4096]{1,0:T(4,128)S(1)}, u32[]{:S(2)}, u32[]{:S(2)}) collective-permute-start(f32[3,4096]{1,0:T(4,128)S(1)} %reshape.979), channel_id=1, source_target_pairs={{0,3},{1,2},{2,1},{3,0},{4,7},{5,6},{6,5},{7,4},{8,11},{9,10},{10,... | collective-permute-start | bytes 147464 | tf_op jit(solution)/shard_map/ppermute | solution.py:111
  113.8 6.0 %collective-permute-start.25 = (f32[4]{0:T(128)S(1)}, f32[4]{0:T(128)S(1)}, u32[]{:S(2)}, u32[]{:S(2)}) collective-permute-start(f32[4]{0:T(128)S(1)} %pad_maximum_fusion.20), channel_id=1, source_target_pairs={{0,1},{1,0},{2,3},{3,2},{4,5},{5,4},{6,7},{7,6},{8,9},{9,8},{10,11... | collective-permute-start | bytes 56 | tf_op jit(solution)/shard_map/ppermute | solution.py:111
  114.2 5.6 %collective-permute-start.26 = (f32[4]{0:T(128)S(1)}, f32[4]{0:T(128)S(1)}, u32[]{:S(2)}, u32[]{:S(2)}) collective-permute-start(f32[4]{0:T(128)S(1)} %pad_maximum_fusion.20), channel_id=1, source_target_pairs={{0,2},{1,3},{2,0},{3,1},{4,6},{5,7},{6,4},{7,5},{8,10},{9,11},{10,... | collective-permute-start | bytes 56 | tf_op jit(solution)/shard_map/ppermute | solution.py:111
  115.1 4.7 %collective-permute-start.27 = (f32[4]{0:T(128)S(1)}, f32[4]{0:T(128)S(1)}, u32[]{:S(2)}, u32[]{:S(2)}) collective-permute-start(f32[4]{0:T(128)S(1)} %pad_maximum_fusion.20), channel_id=1, source_target_pairs={{0,3},{1,2},{2,1},{3,0},{4,7},{5,6},{6,5},{7,4},{8,11},{9,10},{10,... | collective-permute-start | bytes 56 | tf_op jit(solution)/shard_map/ppermute | solution.py:111
  118.6 4.0 %collective-permute-start.33 = (f32[9,512]{1,0:T(8,128)S(1)}, f32[9,512]{1,0:T(8,128)S(1)}, u32[]{:S(2)}, u32[]{:S(2)}) collective-permute-start(f32[9,512]{1,0:T(8,128)S(1)} %reshape.984), channel_id=1, source_target_pairs={{0,4},{4,0},{8,12},{12,8},{1,5},{5,1},{9,13},{13,9},{2,6},{6,2},{1... | collective-permute-start | bytes 55304 | tf_op jit(solution)/shard_map/ppermute | solution.py:118
  122.6 15.2 %collective-permute-start.34 = (f32[9,512]{1,0:T(8,128)S(1)}, f32[9,512]{1,0:T(8,128)S(1)}, u32[]{:S(2)}, u32[]{:S(2)}) collective-permute-start(f32[9,512]{1,0:T(8,128)S(1)} %add.238), channel_id=1, source_target_pairs={{0,8},{4,12},{8,0},{12,4},{1,9},{5,13},{9,1},{13,5},{2,10},{6,14},... | collective-permute-start | bytes 55304 | tf_op jit(solution)/shard_map/ppermute | solution.py:118
  127.2 3.6 %collective-permute-start.31 = (f32[]{:T(128)}, f32[]{:T(128)}, u32[]{:S(2)}, u32[]{:S(2)}) collective-permute-start(f32[]{:T(128)} %sub.391), channel_id=1, source_target_pairs={{0,4},{4,0},{8,12},{12,8},{1,5},{5,1},{9,13},{13,9},{2,6},{6,2},{1... | collective-permute-start | bytes 20 | tf_op jit(solution)/shard_map/ppermute | solution.py:118
  131.5 4.5 %collective-permute-start.32 = (f32[]{:T(128)}, f32[]{:T(128)}, u32[]{:S(2)}, u32[]{:S(2)}) collective-permute-start(f32[]{:T(128)} %add.231), channel_id=1, source_target_pairs={{0,8},{4,12},{8,0},{12,4},{1,9},{5,13},{9,1},{13,5},{2,10},{6,14},... | collective-permute-start | bytes 20 | tf_op jit(solution)/shard_map/ppermute | solution.py:118

commit v9 on v7

--- a/solution.py
+++ b/solution.py
@@ -130,37 +130,45 @@
     diag_terms = by_cam.segsum(jnp.sum(cam_jac * cam_jac, axis=0))
     cam_diag = allsum(diag_terms, "pts") + cam_damp[None, :]
 
+    def as_row(rows, width):
+        flat = rows.reshape(-1)
+        count = -(-flat.shape[0] // width)
+        return jnp.pad(flat, (0, count * width - flat.shape[0])).reshape(count, width)
+
+    def lanes(terms):
+        return jnp.sum(terms.reshape(-1, ncam), axis=0)
+
     def operate(vec, extras):
         y = jnp.sum(cam_jac * by_cam.gather(vec)[None], axis=1)
         u_part = by_point.segsum(jnp.sum(point_jac * y[:, None, :], axis=0))
-        extras = extras + [jnp.sum(cam_damp[None, :] * vec * vec), jnp.sum(y * y)]
-        count = len(extras)
-        extra_row = jnp.zeros((1, npts), F32).at[0, :count].set(jnp.stack(extras))
-        u_all = allsum(jnp.concatenate([u_part, extra_row], axis=0), "cam")
+        extras = jnp.stack([lanes(t) for t in extras] + [lanes(cam_damp[None, :] * vec * vec), lanes(y * y)])
+        count = extras.shape[0]
+        rows = as_row(extras, npts)
+        u_all = allsum(jnp.concatenate([u_part, rows], axis=0), "cam")
         u = u_all[:3]
-        got = u_all[3, :count]
+        got = jnp.sum(u_all[3:].reshape(-1)[: count * ncam].reshape(count, ncam), axis=1)
         w = jnp.sum(inv * u[None, :, :], axis=1)
-        point_energy = got[count - 1] - jnp.sum(u * w)
+        pt_terms = jnp.sum(u * w, axis=0).reshape(-1, ncam)
+        pt_row = u_all[3:].reshape(-1)[(count - 1) * ncam : count * ncam] - jnp.sum(pt_terms, axis=0)
         z = y - jnp.sum(point_jac * by_point.gather(w)[None], axis=1)
         img_part = by_cam.segsum(jnp.sum(cam_jac * z[:, None, :], axis=0))
-        pt_row = jnp.zeros((1, ncam), F32).at[0, 0].set(point_energy)
-        img_all = allsum(jnp.concatenate([img_part, pt_row], axis=0), "pts")
+        img_all = allsum(jnp.concatenate([img_part, pt_row[None]], axis=0), "pts")
         image = cam_damp[None, :] * vec + img_all[:-1]
-        energy = got[count - 2] + img_all[-1, 0]
+        energy = got[count - 2] + jnp.sum(img_all[-1])
         return image, got, energy
 
     solution = jnp.zeros_like(reduced_rhs)
     residual = reduced_rhs
     pre = residual / cam_diag
     direction = pre
-    image, got, curv = operate(direction, [jnp.sum(residual * pre)])
+    image, got, curv = operate(direction, [residual * pre])
     rz = got[0]
     alpha = rz / curv
     solution = solution + alpha * direction
     residual = residual - alpha * image
     for step in range(1, ITERS):
         pre = residual / cam_diag
-        image_pre, got, energy = operate(pre, [jnp.sum(residual * pre), jnp.sum(pre * image)])
+        image_pre, got, energy = operate(pre, [residual * pre, pre * image])
         new_rz = got[0]
         beta = new_rz / rz
         direction = pre + beta * direction

time: 117 us -> 96.7 us (0.83)
  other arithmetic: 30.7 us -> 17.1 us
  between operations: 16.8 us -> 11.4 us
    another operation x6 -> x1, other arithmetic: 10.8 us -> 0.01 us  [operate(): jnp.stack([lanes(t) for t in extras] + [lanes(cam_damp[None, :] * vec * v...]
    reduce_sum x9 -> x18, other arithmetic: 5.85 us -> 2.63 us  [the longest x3 1.9 us: operate(): energy = got[count - 2] + jnp.sum(img_all[-1])]
    slice x4, local copies, waits for them, and re-layouts: 2.19 us -> 0.66 us  [the longest x1 0.58 us: operate(): energy = got[count - 2] + jnp.sum(img_all[-1])]
  transfers between devices with their start and end apart: 20 -> 20, of which waited for: 13 -> 12; matrix products, arithmetic and copies ran while one was open for 13% -> 12% of each run, Pallas kernels for 0% -> 0%
where the time goes in v9:
time: 96.7 us; the launch traced here: 96.3 us
  waiting for transfers between devices  25.8 us (27%)
  starting transfers between devices  21.2 us (22%)
  other arithmetic  17.1 us (18%)
  matrix products  14.9 us (15%)
  between operations  11.4 us (12%)
  local copies, waits for them, and re-layouts  5.94 us (6%)
    ppermute x8, waiting for transfers between devices, allsum(): lax.ppermute(value, axis, [(i, i ^ step) for i in range(size)])  15.4 us
    ppermute x8, starting transfers between devices, allsum(): lax.ppermute(value, axis, [(i, i ^ step) for i in range(size)])  13.5 us
    dot_general x8, matrix products, segsum(): lax.dot_general(self.hot3, spread, (((1,), (1,)), ((), ())), preferred_el...  11.5 us
    ppermute x12, waiting for transfers between devices, allsum(): lax.ppermute(value, axis, [(i, i ^ mask) for i in range(size)])  10.4 us
    ppermute x12, starting transfers between devices, allsum(): lax.ppermute(value, axis, [(i, i ^ mask) for i in range(size)])  7.68 us
    select_n x8, other arithmetic, segsum(): jnp.where(self.low[None], part[:, None, :], jnp.zeros((), BF))  3.86 us
    dot_general x6, matrix products, gather(): lax.dot_general(stacked, self.hot3t, (((1,), (0,)), ((), ())), preferred_...  3.41 us
    reduce_sum x6, other arithmetic, gather(): return jnp.sum(jnp.where(self.low[None], spread, 0.0), axis=1)  2.61 us
  transfers between devices with their start and end apart: 20, of which 12 were waited for; matrix products, arithmetic and copies ran while one was open for 12% of the time, Pallas kernels for 0%

profile of v9, /device:TPU:0, one launch (start us, length us, event | category | flops | bytes accessed | tf_op | source)
XLA Modules:
  0.0 96.3 jit_solution(10607798855327151243)
XLA Ops:
  0.6 0.7 add_select_fusion
  1.4 1.4 %multiply_reduce_fusion.6 = f32[9,4096]{1,0:T(8,128)S(1)} fusion(f32[2,9,4096]{2,0,1:T(2,128)} %param.7), kind=kLoop, calls=%fused_computation.115 | loop fusion | flops 110592 | bytes 442368 | tf_op jit(solution)/shard_map/reduce_sum | solution.py:130
  2.9 0.4 broadcast_select_fusion.23
  3.3 1.1 %fusion.24 = f32[32,144]{0,1:T(8,128)S(1)} fusion(bf16[144,4096]{1,0:T(8,128)(2,1)S(1)} %bitcast.194, bf16[144,4096]{1,0:T(8,128)(2,1)S(1)} %bitcast.193, bf16[144,4096]{1,0:T(8,128)(2,1)S(1)} %bitcast.192, bf16[32,4096]{1,0:T(8,128)(2,1)S(1)} %fusion.52), kind=kOutput, calls=%fused_computation.24 | convolution fusion | flops 126222336 | bytes 3819520 | tf_op jit(solution)/shard_map/dot_general | solution.py:46
  4.6 3.1 %collective-permute-start = (f32[9,512]{1,0:T(8,128)S(1)}, f32[9,512]{1,0:T(8,128)S(1)}, u32[]{:S(2)}, u32[]{:S(2)}) collective-permute-start(f32[9,512]{1,0:T(8,128)S(1)} %reshape.1015), channel_id=1, source_target_pairs={{0,4},{4,0},{8,12},{12,8},{1,5},{5,1},{9,13},{13,9},{2,6},{6,2},{1... | collective-permute-start | bytes 55304 | tf_op jit(solution)/shard_map/ppermute | solution.py:114
  8.5 0.9 broadcast_select_fusion.2
  9.4 3.0 %fusion = f32[64,384]{1,0:T(8,128)S(1)} fusion(bf16[384,4096]{1,0:T(8,128)(2,1)S(1)} %bitcast.179, bf16[384,4096]{1,0:T(8,128)(2,1)S(1)} %bitcast.178, bf16[384,4096]{1,0:T(8,128)(2,1)S(1)} %bitcast.177, bf16[64,4096]{1,0:T(8,128)(2,1)S(1)} %get-tuple-element.120), kind=kOutput, calls=%fused_computation | convolution fusion | flops 637009920 | bytes 10059776 | tf_op jit(solution)/shard_map/dot_general | solution.py:46
  12.7 1.6 %collective-permute-start.6 = (f32[6,4096]{1,0:T(8,128)S(1)}, f32[6,4096]{1,0:T(8,128)S(1)}, u32[]{:S(2)}, u32[]{:S(2)}) collective-permute-start(f32[6,4096]{1,0:T(8,128)S(1)} %reshape.1025), channel_id=1, source_target_pairs={{0,2},{1,3},{2,0},{3,1},{4,6},{5,7},{6,4},{7,5},{8,10},{9,11},{10,... | collective-permute-start | bytes 294920 | tf_op jit(solution)/shard_map/ppermute | solution.py:107
  14.6 2.7 %collective-permute-start.1 = (f32[9,512]{1,0:T(8,128)S(1)}, f32[9,512]{1,0:T(8,128)S(1)}, u32[]{:S(2)}, u32[]{:S(2)}) collective-permute-start(f32[9,512]{1,0:T(8,128)S(1)} %add.147), channel_id=1, source_target_pairs={{0,8},{4,12},{8,0},{12,4},{1,9},{5,13},{9,1},{13,5},{2,10},{6,14},... | collective-permute-start | bytes 55304 | tf_op jit(solution)/shard_map/ppermute | solution.py:114
  17.2 2.5 %collective-permute-done.1 = f32[9,512]{1,0:T(8,128)S(1)} collective-permute-done((f32[9,512]{1,0:T(8,128)S(1)}, f32[9,512]{1,0:T(8,128)S(1)}, u32[]{:S(2)}, u32[]{:S(2)}) %collective-permute-start.1) | collective-permute-done | bytes 18464 | tf_op jit(solution)/shard_map/ppermute | solution.py:114
  20.0 0.5 fusion.55
  20.6 0.5 select_reduce_fusion.5
  21.0 0.5 copy-done
  21.9 0.4 broadcast_select_fusion.11
  22.3 1.4 %fusion.6 = f32[64,192]{0,1:T(8,128)S(1)} fusion(bf16[192,4096]{1,0:T(8,128)(2,1)S(1)} %bitcast.182, bf16[192,4096]{1,0:T(8,128)(2,1)S(1)} %bitcast.181, bf16[192,4096]{1,0:T(8,128)(2,1)S(1)} %bitcast.180, bf16[64,4096]{1,0:T(8,128)(2,1)S(1)} %get-tuple-element.120), kind=kOutput, calls=%fused_computation.6 | convolution fusion | flops 320864256 | bytes 5292032 | tf_op jit(solution)/shard_map/dot_general | solution.py:46
  24.2 1.6 %collective-permute-start.3 = (f32[4,4096]{1,0:T(4,128)S(1)}, f32[4,4096]{1,0:T(4,128)S(1)}, u32[]{:S(2)}, u32[]{:S(2)}) collective-permute-start(f32[4,4096]{1,0:T(4,128)S(1)} %pad_maximum_fusion.18), channel_id=1, source_target_pairs={{0,2},{1,3},{2,0},{3,1},{4,6},{5,7},{6,4},{7,5},{8,10},{9,11},{10,... | collective-permute-start | bytes 196616 | tf_op jit(solution)/shard_map/ppermute | solution.py:107
  26.9 1.9 %collective-permute-done.3 = f32[4,4096]{1,0:T(4,128)S(1)} collective-permute-done((f32[4,4096]{1,0:T(4,128)S(1)}, f32[4,4096]{1,0:T(4,128)S(1)}, u32[]{:S(2)}, u32[]{:S(2)}) %collective-permute-start.3) | collective-permute-done | bytes 65568 | tf_op jit(solution)/shard_map/ppermute | solution.py:107
  28.7 1.2 %collective-permute-done.4 = f32[4,4096]{1,0:T(4,128)S(1)} collective-permute-done((f32[4,4096]{1,0:T(4,128)S(1)}, f32[4,4096]{1,0:T(4,128)S(1)}, u32[]{:S(2)}, u32[]{:S(2)}) %collective-permute-start.4) | collective-permute-done | bytes 65568 | tf_op jit(solution)/shard_map/ppermute | solution.py:107
  30.4 0.6 fusion.51
  31.1 0.4 select_reduce_fusion.2
  31.6 0.6 multiply_reduce_fusion.4
  32.2 0.4 broadcast_select_fusion.20
  32.6 1.1 %fusion.30 = f32[32,144]{0,1:T(8,128)S(1)} fusion(bf16[144,4096]{1,0:T(8,128)(2,1)S(1)} %bitcast.197, bf16[144,4096]{1,0:T(8,128)(2,1)S(1)} %bitcast.196, bf16[144,4096]{1,0:T(8,128)(2,1)S(1)} %bitcast.195, bf16[32,4096]{1,0:T(8,128)(2,1)S(1)} %fusion.52), kind=kOutput, calls=%fused_computation.30 | convolution fusion | flops 126222336 | bytes 3819520 | tf_op jit(solution)/shard_map/dot_general | solution.py:46
  34.3 3.6 %collective-permute-done.8 = f32[10,512]{1,0:T(8,128)S(1)} collective-permute-done((f32[10,512]{1,0:T(8,128)S(1)}, f32[10,512]{1,0:T(8,128)S(1)}, u32[]{:S(2)}, u32[]{:S(2)}) %collective-permute-start.8) | collective-permute-done | bytes 20512 | tf_op jit(solution)/shard_map/ppermute | solution.py:114
  38.0 2.3 %collective-permute-start.9 = (f32[10,512]{1,0:T(8,128)S(1)}, f32[10,512]{1,0:T(8,128)S(1)}, u32[]{:S(2)}, u32[]{:S(2)}) collective-permute-start(f32[10,512]{1,0:T(8,128)S(1)} %fusion.136), channel_id=1, source_target_pairs={{0,8},{4,12},{8,0},{12,4},{1,9},{5,13},{9,1},{13,5},{2,10},{6,14},... | collective-permute-start | bytes 61448 | tf_op jit(solution)/shard_map/ppermute | solution.py:114
  40.3 0.6 fusion.133
  40.9 2.0 %collective-permute-done.9 = f32[10,512]{1,0:T(8,128)S(1)} collective-permute-done((f32[10,512]{1,0:T(8,128)S(1)}, f32[10,512]{1,0:T(8,128)S(1)}, u32[]{:S(2)}, u32[]{:S(2)}) %collective-permute-start.9) | collective-permute-done | bytes 20512 | tf_op jit(solution)/shard_map/ppermute | solution.py:114
  42.9 0.7 slice_reduce_fusion.5
  45.8 0.5 fusion.54
  46.3 0.5 select_reduce_fusion.4
  47.2 0.4 broadcast_select_fusion.8
  47.6 1.4 %fusion.12 = f32[64,192]{0,1:T(8,128)S(1)} fusion(bf16[192,4096]{1,0:T(8,128)(2,1)S(1)} %bitcast.185, bf16[192,4096]{1,0:T(8,128)(2,1)S(1)} %bitcast.184, bf16[192,4096]{1,0:T(8,128)(2,1)S(1)} %bitcast.183, bf16[64,4096]{1,0:T(8,128)(2,1)S(1)} %get-tuple-element.120), kind=kOutput, calls=%fused_computation.12 | convolution fusion | flops 320864256 | bytes 5292032 | tf_op jit(solution)/shard_map/dot_general | solution.py:46
  49.5 1.3 %collective-permute-start.11 = (f32[4,4096]{1,0:T(4,128)S(1)}, f32[4,4096]{1,0:T(4,128)S(1)}, u32[]{:S(2)}, u32[]{:S(2)}) collective-permute-start(f32[4,4096]{1,0:T(4,128)S(1)} %pad_maximum_fusion.19), channel_id=1, source_target_pairs={{0,2},{1,3},{2,0},{3,1},{4,6},{5,7},{6,4},{7,5},{8,10},{9,11},{10,... | collective-permute-start | bytes 196616 | tf_op jit(solution)/shard_map/ppermute | solution.py:107
  50.8 0.6 collective-permute-start.12
  51.4 2.9 %collective-permute-done.11 = f32[4,4096]{1,0:T(4,128)S(1)} collective-permute-done((f32[4,4096]{1,0:T(4,128)S(1)}, f32[4,4096]{1,0:T(4,128)S(1)}, u32[]{:S(2)}, u32[]{:S(2)}) %collective-permute-start.11) | collective-permute-done | bytes 65568 | tf_op jit(solution)/shard_map/ppermute | solution.py:107
  54.2 1.0 %collective-permute-done.12 = f32[4,4096]{1,0:T(4,128)S(1)} collective-permute-done((f32[4,4096]{1,0:T(4,128)S(1)}, f32[4,4096]{1,0:T(4,128)S(1)}, u32[]{:S(2)}, u32[]{:S(2)}) %collective-permute-start.12) | collective-permute-done | bytes 65568 | tf_op jit(solution)/shard_map/ppermute | solution.py:107
  55.7 0.6 fusion.50
  56.3 0.4 select_reduce_fusion.1
  56.8 0.4 multiply_reduce_fusion.2
  57.3 0.4 broadcast_select_fusion.17
  57.7 1.1 %fusion.36 = f32[32,144]{0,1:T(8,128)S(1)} fusion(bf16[144,4096]{1,0:T(8,128)(2,1)S(1)} %bitcast.200, bf16[144,4096]{1,0:T(8,128)(2,1)S(1)} %bitcast.199, bf16[144,4096]{1,0:T(8,128)(2,1)S(1)} %bitcast.198, bf16[32,4096]{1,0:T(8,128)(2,1)S(1)} %fusion.52), kind=kOutput, calls=%fused_computation.36 | convolution fusion | flops 126222336 | bytes 3819520 | tf_op jit(solution)/shard_map/dot_general | solution.py:46
  59.4 3.6 %collective-permute-done.13 = f32[10,512]{1,0:T(8,128)S(1)} collective-permute-done((f32[10,512]{1,0:T(8,128)S(1)}, f32[10,512]{1,0:T(8,128)S(1)}, u32[]{:S(2)}, u32[]{:S(2)}) %collective-permute-start.13) | collective-permute-done | bytes 20512 | tf_op jit(solution)/shard_map/ppermute | solution.py:114
  63.1 2.3 %collective-permute-start.14 = (f32[10,512]{1,0:T(8,128)S(1)}, f32[10,512]{1,0:T(8,128)S(1)}, u32[]{:S(2)}, u32[]{:S(2)}) collective-permute-start(f32[10,512]{1,0:T(8,128)S(1)} %fusion.135), channel_id=1, source_target_pairs={{0,8},{4,12},{8,0},{12,4},{1,9},{5,13},{9,1},{13,5},{2,10},{6,14},... | collective-permute-start | bytes 61448 | tf_op jit(solution)/shard_map/ppermute | solution.py:114
  65.4 0.7 fusion.132
  68.1 0.6 slice_reduce_fusion.4
  70.9 0.5 fusion.53
  71.5 0.5 select_reduce_fusion.3
  72.3 0.4 broadcast_select_fusion.5
  72.8 1.4 %fusion.18 = f32[64,192]{0,1:T(8,128)S(1)} fusion(bf16[192,4096]{1,0:T(8,128)(2,1)S(1)} %bitcast.188, bf16[192,4096]{1,0:T(8,128)(2,1)S(1)} %bitcast.187, bf16[192,4096]{1,0:T(8,128)(2,1)S(1)} %bitcast.186, bf16[64,4096]{1,0:T(8,128)(2,1)S(1)} %get-tuple-element.120), kind=kOutput, calls=%fused_computation.18 | convolution fusion | flops 320864256 | bytes 5292032 | tf_op jit(solution)/shard_map/dot_general | solution.py:46
  74.8 1.0 %collective-permute-start.16 = (f32[4,4096]{1,0:T(4,128)S(1)}, f32[4,4096]{1,0:T(4,128)S(1)}, u32[]{:S(2)}, u32[]{:S(2)}) collective-permute-start(f32[4,4096]{1,0:T(4,128)S(1)} %pad_maximum_fusion.20), channel_id=1, source_target_pairs={{0,2},{1,3},{2,0},{3,1},{4,6},{5,7},{6,4},{7,5},{8,10},{9,11},{10,... | collective-permute-start | bytes 196616 | tf_op jit(solution)/shard_map/ppermute | solution.py:107
  75.8 0.9 collective-permute-start.17
  76.7 3.2 %collective-permute-done.16 = f32[4,4096]{1,0:T(4,128)S(1)} collective-permute-done((f32[4,4096]{1,0:T(4,128)S(1)}, f32[4,4096]{1,0:T(4,128)S(1)}, u32[]{:S(2)}, u32[]{:S(2)}) %collective-permute-start.16) | collective-permute-done | bytes 65568 | tf_op jit(solution)/shard_map/ppermute | solution.py:107
  80.7 0.6 fusion.49
  81.3 0.4 select_reduce_fusion
  81.8 0.4 multiply_reduce_fusion
  82.3 0.4 broadcast_select_fusion.14
  82.7 1.1 %fusion.42 = f32[32,144]{0,1:T(8,128)S(1)} fusion(bf16[144,4096]{1,0:T(8,128)(2,1)S(1)} %bitcast.191, bf16[144,4096]{1,0:T(8,128)(2,1)S(1)} %bitcast.190, bf16[144,4096]{1,0:T(8,128)(2,1)S(1)} %bitcast.189, bf16[32,4096]{1,0:T(8,128)(2,1)S(1)} %fusion.52), kind=kOutput, calls=%fused_computation.42 | convolution fusion | flops 126222336 | bytes 3819520 | tf_op jit(solution)/shard_map/dot_general | solution.py:46
  84.1 0.5 collective-permute-start.18
  84.8 3.3 %collective-permute-done.18 = f32[10,512]{1,0:T(8,128)S(1)} collective-permute-done((f32[10,512]{1,0:T(8,128)S(1)}, f32[10,512]{1,0:T(8,128)S(1)}, u32[]{:S(2)}, u32[]{:S(2)}) %collective-permute-start.18) | collective-permute-done | bytes 20512 | tf_op jit(solution)/shard_map/ppermute | solution.py:114
  88.1 2.2 %collective-permute-start.19 = (f32[10,512]{1,0:T(8,128)S(1)}, f32[10,512]{1,0:T(8,128)S(1)}, u32[]{:S(2)}, u32[]{:S(2)}) collective-permute-start(f32[10,512]{1,0:T(8,128)S(1)} %fusion.134), channel_id=1, source_target_pairs={{0,8},{4,12},{8,0},{12,4},{1,9},{5,13},{9,1},{13,5},{2,10},{6,14},... | collective-permute-start | bytes 61448 | tf_op jit(solution)/shard_map/ppermute | solution.py:114
  90.2 0.6 fusion.131
  92.8 0.4 collective-permute-done.19
  93.2 0.6 slice_reduce_fusion.3
  95.7 0.7 fusion.106
  (163 shorter events, 9.8 us)
Async XLA Ops:
  3.3 4.4 %copy-start.1 = (f32[2,3,4096]{2,0,1:T(2,128)S(1)}, f32[2,3,4096]{2,0,1:T(2,128)}, u32[]{:S(2)}) copy-start(f32[2,3,4096]{2,0,1:T(2,128)} %param.8) | copy-start | bytes 294916
  3.3 4.9 %copy-start.4 = (s32[4096]{0:T(1024)S(1)}, s32[4096]{0:T(1024)}, u32[]{:S(2)}) copy-start(s32[4096]{0:T(1024)} %param.10) | copy-start | bytes 49156
  4.6 9.9 %collective-permute-start = (f32[9,512]{1,0:T(8,128)S(1)}, f32[9,512]{1,0:T(8,128)S(1)}, u32[]{:S(2)}, u32[]{:S(2)}) collective-permute-start(f32[9,512]{1,0:T(8,128)S(1)} %reshape.1015), channel_id=1, source_target_pairs={{0,4},{4,0},{8,12},{12,8},{1,5},{5,1},{9,13},{13,9},{2,6},{6,2},{1... | collective-permute-start | bytes 55304 | tf_op jit(solution)/shard_map/ppermute | solution.py:114
  9.3 10.4 %copy-start.2 = (f32[9,512]{1,0:T(8,128)S(1)}, f32[9,512]{1,0:T(8,128)}, u32[]{:S(2)}) copy-start(f32[9,512]{1,0:T(8,128)} %param.13) | copy-start | bytes 55300
  9.4 10.4 %copy-start.3 = (f32[512]{0:T(512)S(1)}, f32[512]{0:T(512)}, u32[]{:S(2)}) copy-start(f32[512]{0:T(512)} %param.12) | copy-start | bytes 6148
  12.6 13.2 %collective-permute-start.5 = (f32[6,4096]{1,0:T(8,128)S(1)}, f32[6,4096]{1,0:T(8,128)S(1)}, u32[]{:S(2)}, u32[]{:S(2)}) collective-permute-start(f32[6,4096]{1,0:T(8,128)S(1)} %reshape.1025), channel_id=1, source_target_pairs={{0,1},{1,0},{2,3},{3,2},{4,5},{5,4},{6,7},{7,6},{8,9},{9,8},{10,11... | collective-permute-start | bytes 294920 | tf_op jit(solution)/shard_map/ppermute | solution.py:107
  12.7 13.4 %collective-permute-start.6 = (f32[6,4096]{1,0:T(8,128)S(1)}, f32[6,4096]{1,0:T(8,128)S(1)}, u32[]{:S(2)}, u32[]{:S(2)}) collective-permute-start(f32[6,4096]{1,0:T(8,128)S(1)} %reshape.1025), channel_id=1, source_target_pairs={{0,2},{1,3},{2,0},{3,1},{4,6},{5,7},{6,4},{7,5},{8,10},{9,11},{10,... | collective-permute-start | bytes 294920 | tf_op jit(solution)/shard_map/ppermute | solution.py:107
  14.3 11.8 %collective-permute-start.7 = (f32[6,4096]{1,0:T(8,128)S(1)}, f32[6,4096]{1,0:T(8,128)S(1)}, u32[]{:S(2)}, u32[]{:S(2)}) collective-permute-start(f32[6,4096]{1,0:T(8,128)S(1)} %reshape.1025), channel_id=1, source_target_pairs={{0,3},{1,2},{2,1},{3,0},{4,7},{5,6},{6,5},{7,4},{8,11},{9,10},{10,... | collective-permute-start | bytes 294920 | tf_op jit(solution)/shard_map/ppermute | solution.py:107
  14.6 5.2 %collective-permute-start.1 = (f32[9,512]{1,0:T(8,128)S(1)}, f32[9,512]{1,0:T(8,128)S(1)}, u32[]{:S(2)}, u32[]{:S(2)}) collective-permute-start(f32[9,512]{1,0:T(8,128)S(1)} %add.147), channel_id=1, source_target_pairs={{0,8},{4,12},{8,0},{12,4},{1,9},{5,13},{9,1},{13,5},{2,10},{6,14},... | collective-permute-start | bytes 55304 | tf_op jit(solution)/shard_map/ppermute | solution.py:114
  20.5 1.0 %copy-start = (f32[2,9,4096]{2,0,1:T(2,128)S(1)}, f32[2,9,4096]{2,0,1:T(2,128)}, u32[]{:S(2)}) copy-start(f32[2,9,4096]{2,0,1:T(2,128)} %param.7) | copy-start | bytes 884740
  23.8 2.5 %copy-start.5 = (f32[4096]{0:T(1024)S(1)}, f32[4096]{0:T(1024)}, u32[]{:S(2)}) copy-start(f32[4096]{0:T(1024)} %param.11) | copy-start | bytes 49156
  24.1 2.7 %collective-permute-start.2 = (f32[4,4096]{1,0:T(4,128)S(1)}, f32[4,4096]{1,0:T(4,128)S(1)}, u32[]{:S(2)}, u32[]{:S(2)}) collective-permute-start(f32[4,4096]{1,0:T(4,128)S(1)} %pad_maximum_fusion.18), channel_id=1, source_target_pairs={{0,1},{1,0},{2,3},{3,2},{4,5},{5,4},{6,7},{7,6},{8,9},{9,8},{10,11... | collective-permute-start | bytes 196616 | tf_op jit(solution)/shard_map/ppermute | solution.py:107
  24.2 4.5 %collective-permute-start.3 = (f32[4,4096]{1,0:T(4,128)S(1)}, f32[4,4096]{1,0:T(4,128)S(1)}, u32[]{:S(2)}, u32[]{:S(2)}) collective-permute-start(f32[4,4096]{1,0:T(4,128)S(1)} %pad_maximum_fusion.18), channel_id=1, source_target_pairs={{0,2},{1,3},{2,0},{3,1},{4,6},{5,7},{6,4},{7,5},{8,10},{9,11},{10,... | collective-permute-start | bytes 196616 | tf_op jit(solution)/shard_map/ppermute | solution.py:107
  25.8 4.1 %collective-permute-start.4 = (f32[4,4096]{1,0:T(4,128)S(1)}, f32[4,4096]{1,0:T(4,128)S(1)}, u32[]{:S(2)}, u32[]{:S(2)}) collective-permute-start(f32[4,4096]{1,0:T(4,128)S(1)} %pad_maximum_fusion.18), channel_id=1, source_target_pairs={{0,3},{1,2},{2,1},{3,0},{4,7},{5,6},{6,5},{7,4},{8,11},{9,10},{10,... | collective-permute-start | bytes 196616 | tf_op jit(solution)/shard_map/ppermute | solution.py:107
  34.0 4.0 %collective-permute-start.8 = (f32[10,512]{1,0:T(8,128)S(1)}, f32[10,512]{1,0:T(8,128)S(1)}, u32[]{:S(2)}, u32[]{:S(2)}) collective-permute-start(f32[10,512]{1,0:T(8,128)S(1)} %pad_maximum_fusion.21), channel_id=1, source_target_pairs={{0,4},{4,0},{8,12},{12,8},{1,5},{5,1},{9,13},{13,9},{2,6},{6,2},{1... | collective-permute-start | bytes 61448 | tf_op jit(solution)/shard_map/ppermute | solution.py:114
  38.0 4.9 %collective-permute-start.9 = (f32[10,512]{1,0:T(8,128)S(1)}, f32[10,512]{1,0:T(8,128)S(1)}, u32[]{:S(2)}, u32[]{:S(2)}) collective-permute-start(f32[10,512]{1,0:T(8,128)S(1)} %fusion.136), channel_id=1, source_target_pairs={{0,8},{4,12},{8,0},{12,4},{1,9},{5,13},{9,1},{13,5},{2,10},{6,14},... | collective-permute-start | bytes 61448 | tf_op jit(solution)/shard_map/ppermute | solution.py:114
  49.4 1.9 %collective-permute-start.10 = (f32[4,4096]{1,0:T(4,128)S(1)}, f32[4,4096]{1,0:T(4,128)S(1)}, u32[]{:S(2)}, u32[]{:S(2)}) collective-permute-start(f32[4,4096]{1,0:T(4,128)S(1)} %pad_maximum_fusion.19), channel_id=1, source_target_pairs={{0,1},{1,0},{2,3},{3,2},{4,5},{5,4},{6,7},{7,6},{8,9},{9,8},{10,11... | collective-permute-start | bytes 196616 | tf_op jit(solution)/shard_map/ppermute | solution.py:107
  49.5 4.7 %collective-permute-start.11 = (f32[4,4096]{1,0:T(4,128)S(1)}, f32[4,4096]{1,0:T(4,128)S(1)}, u32[]{:S(2)}, u32[]{:S(2)}) collective-permute-start(f32[4,4096]{1,0:T(4,128)S(1)} %pad_maximum_fusion.19), channel_id=1, source_target_pairs={{0,2},{1,3},{2,0},{3,1},{4,6},{5,7},{6,4},{7,5},{8,10},{9,11},{10,... | collective-permute-start | bytes 196616 | tf_op jit(solution)/shard_map/ppermute | solution.py:107
  50.8 4.4 %collective-permute-start.12 = (f32[4,4096]{1,0:T(4,128)S(1)}, f32[4,4096]{1,0:T(4,128)S(1)}, u32[]{:S(2)}, u32[]{:S(2)}) collective-permute-start(f32[4,4096]{1,0:T(4,128)S(1)} %pad_maximum_fusion.19), channel_id=1, source_target_pairs={{0,3},{1,2},{2,1},{3,0},{4,7},{5,6},{6,5},{7,4},{8,11},{9,10},{10,... | collective-permute-start | bytes 196616 | tf_op jit(solution)/shard_map/ppermute | solution.py:107
  59.1 4.0 %collective-permute-start.13 = (f32[10,512]{1,0:T(8,128)S(1)}, f32[10,512]{1,0:T(8,128)S(1)}, u32[]{:S(2)}, u32[]{:S(2)}) collective-permute-start(f32[10,512]{1,0:T(8,128)S(1)} %pad_maximum_fusion.22), channel_id=1, source_target_pairs={{0,4},{4,0},{8,12},{12,8},{1,5},{5,1},{9,13},{13,9},{2,6},{6,2},{1... | collective-permute-start | bytes 61448 | tf_op jit(solution)/shard_map/ppermute | solution.py:114
  63.1 5.0 %collective-permute-start.14 = (f32[10,512]{1,0:T(8,128)S(1)}, f32[10,512]{1,0:T(8,128)S(1)}, u32[]{:S(2)}, u32[]{:S(2)}) collective-permute-start(f32[10,512]{1,0:T(8,128)S(1)} %fusion.135), channel_id=1, source_target_pairs={{0,8},{4,12},{8,0},{12,4},{1,9},{5,13},{9,1},{13,5},{2,10},{6,14},... | collective-permute-start | bytes 61448 | tf_op jit(solution)/shard_map/ppermute | solution.py:114
  74.8 1.9 %collective-permute-start.15 = (f32[4,4096]{1,0:T(4,128)S(1)}, f32[4,4096]{1,0:T(4,128)S(1)}, u32[]{:S(2)}, u32[]{:S(2)}) collective-permute-start(f32[4,4096]{1,0:T(4,128)S(1)} %pad_maximum_fusion.20), channel_id=1, source_target_pairs={{0,1},{1,0},{2,3},{3,2},{4,5},{5,4},{6,7},{7,6},{8,9},{9,8},{10,11... | collective-permute-start | bytes 196616 | tf_op jit(solution)/shard_map/ppermute | solution.py:107
  74.8 5.0 %collective-permute-start.16 = (f32[4,4096]{1,0:T(4,128)S(1)}, f32[4,4096]{1,0:T(4,128)S(1)}, u32[]{:S(2)}, u32[]{:S(2)}) collective-permute-start(f32[4,4096]{1,0:T(4,128)S(1)} %pad_maximum_fusion.20), channel_id=1, source_target_pairs={{0,2},{1,3},{2,0},{3,1},{4,6},{5,7},{6,4},{7,5},{8,10},{9,11},{10,... | collective-permute-start | bytes 196616 | tf_op jit(solution)/shard_map/ppermute | solution.py:107
  75.8 4.4 %collective-permute-start.17 = (f32[4,4096]{1,0:T(4,128)S(1)}, f32[4,4096]{1,0:T(4,128)S(1)}, u32[]{:S(2)}, u32[]{:S(2)}) collective-permute-start(f32[4,4096]{1,0:T(4,128)S(1)} %pad_maximum_fusion.20), channel_id=1, source_target_pairs={{0,3},{1,2},{2,1},{3,0},{4,7},{5,6},{6,5},{7,4},{8,11},{9,10},{10,... | collective-permute-start | bytes 196616 | tf_op jit(solution)/shard_map/ppermute | solution.py:107
  84.1 4.0 %collective-permute-start.18 = (f32[10,512]{1,0:T(8,128)S(1)}, f32[10,512]{1,0:T(8,128)S(1)}, u32[]{:S(2)}, u32[]{:S(2)}) collective-permute-start(f32[10,512]{1,0:T(8,128)S(1)} %pad_maximum_fusion.23), channel_id=1, source_target_pairs={{0,4},{4,0},{8,12},{12,8},{1,5},{5,1},{9,13},{13,9},{2,6},{6,2},{1... | collective-permute-start | bytes 61448 | tf_op jit(solution)/shard_map/ppermute | solution.py:114
  88.1 5.1 %collective-permute-start.19 = (f32[10,512]{1,0:T(8,128)S(1)}, f32[10,512]{1,0:T(8,128)S(1)}, u32[]{:S(2)}, u32[]{:S(2)}) collective-permute-start(f32[10,512]{1,0:T(8,128)S(1)} %fusion.134), channel_id=1, source_target_pairs={{0,8},{4,12},{8,0},{12,4},{1,9},{5,13},{9,1},{13,5},{2,10},{6,14},... | collective-permute-start | bytes 61448 | tf_op jit(solution)/shard_map/ppermute | solution.py:114

commit v10 on v9

--- a/solution.py
+++ b/solution.py
@@ -146,7 +146,7 @@
         rows = as_row(extras, npts)
         u_all = allsum(jnp.concatenate([u_part, rows], axis=0), "cam")
         u = u_all[:3]
-        got = jnp.sum(u_all[3:].reshape(-1)[: count * ncam].reshape(count, ncam), axis=1)
+        got = jnp.sum(u_all[3:].reshape(-1)[: count * ncam].reshape(count, ncam), axis=1, keepdims=True)
         w = jnp.sum(inv * u[None, :, :], axis=1)
         pt_terms = jnp.sum(u * w, axis=0).reshape(-1, ncam)
         pt_row = u_all[3:].reshape(-1)[(count - 1) * ncam : count * ncam] - jnp.sum(pt_terms, axis=0)
@@ -154,7 +154,7 @@
         img_part = by_cam.segsum(jnp.sum(cam_jac * z[:, None, :], axis=0))
         img_all = allsum(jnp.concatenate([img_part, pt_row[None]], axis=0), "pts")
         image = cam_damp[None, :] * vec + img_all[:-1]
-        energy = got[count - 2] + jnp.sum(img_all[-1])
+        energy = got[count - 2 : count - 1] + jnp.sum(img_all[-1:], axis=1, keepdims=True)
         return image, got, energy
 
     solution = jnp.zeros_like(reduced_rhs)
@@ -162,18 +162,18 @@
     pre = residual / cam_diag
     direction = pre
     image, got, curv = operate(direction, [residual * pre])
-    rz = got[0]
+    rz = got[0:1]
     alpha = rz / curv
     solution = solution + alpha * direction
     residual = residual - alpha * image
     for step in range(1, ITERS):
         pre = residual / cam_diag
         image_pre, got, energy = operate(pre, [residual * pre, pre * image])
-        new_rz = got[0]
+        new_rz = got[0:1]
         beta = new_rz / rz
         direction = pre + beta * direction
         image = image_pre + beta * image
-        curv = energy + beta * (2.0 * got[1] + beta * curv)
+        curv = energy + beta * (2.0 * got[1:2] + beta * curv)
         alpha = new_rz / curv
         rz = new_rz
         solution = solution + alpha * direction

time: 96.7 us -> 96.6 us (level)
  no operation moved by 1% of the time
where the time goes in v10:
time: 96.6 us; the launch traced here: 96.3 us
  waiting for transfers between devices  25.7 us (27%)
  starting transfers between devices  21.3 us (22%)
  other arithmetic  17.1 us (18%)
  matrix products  14.9 us (15%)
  between operations  11.3 us (12%)
  local copies, waits for them, and re-layouts  5.9 us (6%)
    ppermute x8, waiting for transfers between devices, allsum(): lax.ppermute(value, axis, [(i, i ^ step) for i in range(size)])  15.3 us
    ppermute x8, starting transfers between devices, allsum(): lax.ppermute(value, axis, [(i, i ^ step) for i in range(size)])  13.6 us
    dot_general x8, matrix products, segsum(): lax.dot_general(self.hot3, spread, (((1,), (1,)), ((), ())), preferred_el...  11.5 us
    ppermute x12, waiting for transfers between devices, allsum(): lax.ppermute(value, axis, [(i, i ^ mask) for i in range(size)])  10.4 us
    ppermute x12, starting transfers between devices, allsum(): lax.ppermute(value, axis, [(i, i ^ mask) for i in range(size)])  7.68 us
    select_n x8, other arithmetic, segsum(): jnp.where(self.low[None], part[:, None, :], jnp.zeros((), BF))  3.86 us
    dot_general x6, matrix products, gather(): lax.dot_general(stacked, self.hot3t, (((1,), (0,)), ((), ())), preferred_...  3.41 us
    reduce_sum x6, other arithmetic, gather(): return jnp.sum(jnp.where(self.low[None], spread, 0.0), axis=1)  2.61 us
  transfers between devices with their start and end apart: 20, of which 12 were waited for; matrix products, arithmetic and copies ran while one was open for 12% of the time, Pallas kernels for 0%

profile of v10, /device:TPU:0, one launch (start us, length us, event | category | flops | bytes accessed | tf_op | source)
XLA Modules:
  0.0 96.3 jit_solution(8989217765137513850)
XLA Ops:
  0.6 0.7 add_select_fusion
  1.4 1.4 %multiply_reduce_fusion.6 = f32[9,4096]{1,0:T(8,128)S(1)} fusion(f32[2,9,4096]{2,0,1:T(2,128)} %param.7), kind=kLoop, calls=%fused_computation.115 | loop fusion | flops 110592 | bytes 442368 | tf_op jit(solution)/shard_map/reduce_sum | solution.py:130
  2.9 0.4 broadcast_select_fusion.23
  3.3 1.1 %fusion.24 = f32[32,144]{0,1:T(8,128)S(1)} fusion(bf16[144,4096]{1,0:T(8,128)(2,1)S(1)} %bitcast.202, bf16[144,4096]{1,0:T(8,128)(2,1)S(1)} %bitcast.201, bf16[144,4096]{1,0:T(8,128)(2,1)S(1)} %bitcast.200, bf16[32,4096]{1,0:T(8,128)(2,1)S(1)} %fusion.52), kind=kOutput, calls=%fused_computation.24 | convolution fusion | flops 126222336 | bytes 3819520 | tf_op jit(solution)/shard_map/dot_general | solution.py:46
  4.6 3.1 %collective-permute-start = (f32[9,512]{1,0:T(8,128)S(1)}, f32[9,512]{1,0:T(8,128)S(1)}, u32[]{:S(2)}, u32[]{:S(2)}) collective-permute-start(f32[9,512]{1,0:T(8,128)S(1)} %reshape.1029), channel_id=1, source_target_pairs={{0,4},{4,0},{8,12},{12,8},{1,5},{5,1},{9,13},{13,9},{2,6},{6,2},{1... | collective-permute-start | bytes 55304 | tf_op jit(solution)/shard_map/ppermute | solution.py:114
  8.5 0.9 broadcast_select_fusion.2
  9.4 3.0 %fusion = f32[64,384]{1,0:T(8,128)S(1)} fusion(bf16[384,4096]{1,0:T(8,128)(2,1)S(1)} %bitcast.187, bf16[384,4096]{1,0:T(8,128)(2,1)S(1)} %bitcast.186, bf16[384,4096]{1,0:T(8,128)(2,1)S(1)} %bitcast.185, bf16[64,4096]{1,0:T(8,128)(2,1)S(1)} %get-tuple-element.120), kind=kOutput, calls=%fused_computation | convolution fusion | flops 637009920 | bytes 10059776 | tf_op jit(solution)/shard_map/dot_general | solution.py:46
  12.7 1.6 %collective-permute-start.6 = (f32[6,4096]{1,0:T(8,128)S(1)}, f32[6,4096]{1,0:T(8,128)S(1)}, u32[]{:S(2)}, u32[]{:S(2)}) collective-permute-start(f32[6,4096]{1,0:T(8,128)S(1)} %reshape.1039), channel_id=1, source_target_pairs={{0,2},{1,3},{2,0},{3,1},{4,6},{5,7},{6,4},{7,5},{8,10},{9,11},{10,... | collective-permute-start | bytes 294920 | tf_op jit(solution)/shard_map/ppermute | solution.py:107
  14.6 2.7 %collective-permute-start.1 = (f32[9,512]{1,0:T(8,128)S(1)}, f32[9,512]{1,0:T(8,128)S(1)}, u32[]{:S(2)}, u32[]{:S(2)}) collective-permute-start(f32[9,512]{1,0:T(8,128)S(1)} %add.147), channel_id=1, source_target_pairs={{0,8},{4,12},{8,0},{12,4},{1,9},{5,13},{9,1},{13,5},{2,10},{6,14},... | collective-permute-start | bytes 55304 | tf_op jit(solution)/shard_map/ppermute | solution.py:114
  17.2 2.5 %collective-permute-done.1 = f32[9,512]{1,0:T(8,128)S(1)} collective-permute-done((f32[9,512]{1,0:T(8,128)S(1)}, f32[9,512]{1,0:T(8,128)S(1)}, u32[]{:S(2)}, u32[]{:S(2)}) %collective-permute-start.1) | collective-permute-done | bytes 18464 | tf_op jit(solution)/shard_map/ppermute | solution.py:114
  20.0 0.5 fusion.55
  20.6 0.5 select_reduce_fusion.5
  21.0 0.5 copy-done
  21.9 0.4 broadcast_select_fusion.11
  22.3 1.4 %fusion.6 = f32[64,192]{0,1:T(8,128)S(1)} fusion(bf16[192,4096]{1,0:T(8,128)(2,1)S(1)} %bitcast.190, bf16[192,4096]{1,0:T(8,128)(2,1)S(1)} %bitcast.189, bf16[192,4096]{1,0:T(8,128)(2,1)S(1)} %bitcast.188, bf16[64,4096]{1,0:T(8,128)(2,1)S(1)} %get-tuple-element.120), kind=kOutput, calls=%fused_computation.6 | convolution fusion | flops 320864256 | bytes 5292032 | tf_op jit(solution)/shard_map/dot_general | solution.py:46
  24.2 1.6 %collective-permute-start.3 = (f32[4,4096]{1,0:T(4,128)S(1)}, f32[4,4096]{1,0:T(4,128)S(1)}, u32[]{:S(2)}, u32[]{:S(2)}) collective-permute-start(f32[4,4096]{1,0:T(4,128)S(1)} %pad_maximum_fusion.18), channel_id=1, source_target_pairs={{0,2},{1,3},{2,0},{3,1},{4,6},{5,7},{6,4},{7,5},{8,10},{9,11},{10,... | collective-permute-start | bytes 196616 | tf_op jit(solution)/shard_map/ppermute | solution.py:107
  26.9 1.9 %collective-permute-done.3 = f32[4,4096]{1,0:T(4,128)S(1)} collective-permute-done((f32[4,4096]{1,0:T(4,128)S(1)}, f32[4,4096]{1,0:T(4,128)S(1)}, u32[]{:S(2)}, u32[]{:S(2)}) %collective-permute-start.3) | collective-permute-done | bytes 65568 | tf_op jit(solution)/shard_map/ppermute | solution.py:107
  28.7 1.2 %collective-permute-done.4 = f32[4,4096]{1,0:T(4,128)S(1)} collective-permute-done((f32[4,4096]{1,0:T(4,128)S(1)}, f32[4,4096]{1,0:T(4,128)S(1)}, u32[]{:S(2)}, u32[]{:S(2)}) %collective-permute-start.4) | collective-permute-done | bytes 65568 | tf_op jit(solution)/shard_map/ppermute | solution.py:107
  30.4 0.6 fusion.51
  31.1 0.4 select_reduce_fusion.2
  31.6 0.6 multiply_reduce_fusion.4
  32.2 0.4 broadcast_select_fusion.20
  32.6 1.1 %fusion.30 = f32[32,144]{0,1:T(8,128)S(1)} fusion(bf16[144,4096]{1,0:T(8,128)(2,1)S(1)} %bitcast.205, bf16[144,4096]{1,0:T(8,128)(2,1)S(1)} %bitcast.204, bf16[144,4096]{1,0:T(8,128)(2,1)S(1)} %bitcast.203, bf16[32,4096]{1,0:T(8,128)(2,1)S(1)} %fusion.52), kind=kOutput, calls=%fused_computation.30 | convolution fusion | flops 126222336 | bytes 3819520 | tf_op jit(solution)/shard_map/dot_general | solution.py:46
  34.3 3.6 %collective-permute-done.8 = f32[10,512]{1,0:T(8,128)S(1)} collective-permute-done((f32[10,512]{1,0:T(8,128)S(1)}, f32[10,512]{1,0:T(8,128)S(1)}, u32[]{:S(2)}, u32[]{:S(2)}) %collective-permute-start.8) | collective-permute-done | bytes 20512 | tf_op jit(solution)/shard_map/ppermute | solution.py:114
  38.0 2.3 %collective-permute-start.9 = (f32[10,512]{1,0:T(8,128)S(1)}, f32[10,512]{1,0:T(8,128)S(1)}, u32[]{:S(2)}, u32[]{:S(2)}) collective-permute-start(f32[10,512]{1,0:T(8,128)S(1)} %fusion.136), channel_id=1, source_target_pairs={{0,8},{4,12},{8,0},{12,4},{1,9},{5,13},{9,1},{13,5},{2,10},{6,14},... | collective-permute-start | bytes 61448 | tf_op jit(solution)/shard_map/ppermute | solution.py:114
  40.3 0.6 fusion.133
  40.9 2.0 %collective-permute-done.9 = f32[10,512]{1,0:T(8,128)S(1)} collective-permute-done((f32[10,512]{1,0:T(8,128)S(1)}, f32[10,512]{1,0:T(8,128)S(1)}, u32[]{:S(2)}, u32[]{:S(2)}) %collective-permute-start.9) | collective-permute-done | bytes 20512 | tf_op jit(solution)/shard_map/ppermute | solution.py:114
  42.9 0.7 slice_reduce_fusion.5
  45.8 0.5 fusion.54
  46.3 0.5 select_reduce_fusion.4
  47.2 0.4 broadcast_select_fusion.8
  47.6 1.4 %fusion.12 = f32[64,192]{0,1:T(8,128)S(1)} fusion(bf16[192,4096]{1,0:T(8,128)(2,1)S(1)} %bitcast.193, bf16[192,4096]{1,0:T(8,128)(2,1)S(1)} %bitcast.192, bf16[192,4096]{1,0:T(8,128)(2,1)S(1)} %bitcast.191, bf16[64,4096]{1,0:T(8,128)(2,1)S(1)} %get-tuple-element.120), kind=kOutput, calls=%fused_computation.12 | convolution fusion | flops 320864256 | bytes 5292032 | tf_op jit(solution)/shard_map/dot_general | solution.py:46
  49.5 1.3 %collective-permute-start.11 = (f32[4,4096]{1,0:T(4,128)S(1)}, f32[4,4096]{1,0:T(4,128)S(1)}, u32[]{:S(2)}, u32[]{:S(2)}) collective-permute-start(f32[4,4096]{1,0:T(4,128)S(1)} %pad_maximum_fusion.19), channel_id=1, source_target_pairs={{0,2},{1,3},{2,0},{3,1},{4,6},{5,7},{6,4},{7,5},{8,10},{9,11},{10,... | collective-permute-start | bytes 196616 | tf_op jit(solution)/shard_map/ppermute | solution.py:107
  50.8 0.6 collective-permute-start.12
  51.4 2.9 %collective-permute-done.11 = f32[4,4096]{1,0:T(4,128)S(1)} collective-permute-done((f32[4,4096]{1,0:T(4,128)S(1)}, f32[4,4096]{1,0:T(4,128)S(1)}, u32[]{:S(2)}, u32[]{:S(2)}) %collective-permute-start.11) | collective-permute-done | bytes 65568 | tf_op jit(solution)/shard_map/ppermute | solution.py:107
  54.2 1.0 %collective-permute-done.12 = f32[4,4096]{1,0:T(4,128)S(1)} collective-permute-done((f32[4,4096]{1,0:T(4,128)S(1)}, f32[4,4096]{1,0:T(4,128)S(1)}, u32[]{:S(2)}, u32[]{:S(2)}) %collective-permute-start.12) | collective-permute-done | bytes 65568 | tf_op jit(solution)/shard_map/ppermute | solution.py:107
  55.7 0.6 fusion.50
  56.3 0.4 select_reduce_fusion.1
  56.8 0.4 multiply_reduce_fusion.2
  57.3 0.4 broadcast_select_fusion.17
  57.7 1.1 %fusion.36 = f32[32,144]{0,1:T(8,128)S(1)} fusion(bf16[144,4096]{1,0:T(8,128)(2,1)S(1)} %bitcast.208, bf16[144,4096]{1,0:T(8,128)(2,1)S(1)} %bitcast.207, bf16[144,4096]{1,0:T(8,128)(2,1)S(1)} %bitcast.206, bf16[32,4096]{1,0:T(8,128)(2,1)S(1)} %fusion.52), kind=kOutput, calls=%fused_computation.36 | convolution fusion | flops 126222336 | bytes 3819520 | tf_op jit(solution)/shard_map/dot_general | solution.py:46
  59.4 3.6 %collective-permute-done.13 = f32[10,512]{1,0:T(8,128)S(1)} collective-permute-done((f32[10,512]{1,0:T(8,128)S(1)}, f32[10,512]{1,0:T(8,128)S(1)}, u32[]{:S(2)}, u32[]{:S(2)}) %collective-permute-start.13) | collective-permute-done | bytes 20512 | tf_op jit(solution)/shard_map/ppermute | solution.py:114
  63.1 2.3 %collective-permute-start.14 = (f32[10,512]{1,0:T(8,128)S(1)}, f32[10,512]{1,0:T(8,128)S(1)}, u32[]{:S(2)}, u32[]{:S(2)}) collective-permute-start(f32[10,512]{1,0:T(8,128)S(1)} %fusion.135), channel_id=1, source_target_pairs={{0,8},{4,12},{8,0},{12,4},{1,9},{5,13},{9,1},{13,5},{2,10},{6,14},... | collective-permute-start | bytes 61448 | tf_op jit(solution)/shard_map/ppermute | solution.py:114
  65.4 0.6 fusion.132
  68.0 0.6 slice_reduce_fusion.4
  70.8 0.5 fusion.53
  71.3 0.5 select_reduce_fusion.3
  72.2 0.4 broadcast_select_fusion.5
  72.6 1.4 %fusion.18 = f32[64,192]{0,1:T(8,128)S(1)} fusion(bf16[192,4096]{1,0:T(8,128)(2,1)S(1)} %bitcast.196, bf16[192,4096]{1,0:T(8,128)(2,1)S(1)} %bitcast.195, bf16[192,4096]{1,0:T(8,128)(2,1)S(1)} %bitcast.194, bf16[64,4096]{1,0:T(8,128)(2,1)S(1)} %get-tuple-element.120), kind=kOutput, calls=%fused_computation.18 | convolution fusion | flops 320864256 | bytes 5292032 | tf_op jit(solution)/shard_map/dot_general | solution.py:46
  74.7 1.0 %collective-permute-start.16 = (f32[4,4096]{1,0:T(4,128)S(1)}, f32[4,4096]{1,0:T(4,128)S(1)}, u32[]{:S(2)}, u32[]{:S(2)}) collective-permute-start(f32[4,4096]{1,0:T(4,128)S(1)} %pad_maximum_fusion.20), channel_id=1, source_target_pairs={{0,2},{1,3},{2,0},{3,1},{4,6},{5,7},{6,4},{7,5},{8,10},{9,11},{10,... | collective-permute-start | bytes 196616 | tf_op jit(solution)/shard_map/ppermute | solution.py:107
  75.7 0.9 collective-permute-start.17
  76.6 3.2 %collective-permute-done.16 = f32[4,4096]{1,0:T(4,128)S(1)} collective-permute-done((f32[4,4096]{1,0:T(4,128)S(1)}, f32[4,4096]{1,0:T(4,128)S(1)}, u32[]{:S(2)}, u32[]{:S(2)}) %collective-permute-start.16) | collective-permute-done | bytes 65568 | tf_op jit(solution)/shard_map/ppermute | solution.py:107
  79.7 0.3 collective-permute-done.17
  80.6 0.6 fusion.49
  81.2 0.4 select_reduce_fusion
  81.7 0.4 multiply_reduce_fusion
  82.2 0.4 broadcast_select_fusion.14
  82.6 1.1 %fusion.42 = f32[32,144]{0,1:T(8,128)S(1)} fusion(bf16[144,4096]{1,0:T(8,128)(2,1)S(1)} %bitcast.199, bf16[144,4096]{1,0:T(8,128)(2,1)S(1)} %bitcast.198, bf16[144,4096]{1,0:T(8,128)(2,1)S(1)} %bitcast.197, bf16[32,4096]{1,0:T(8,128)(2,1)S(1)} %fusion.52), kind=kOutput, calls=%fused_computation.42 | convolution fusion | flops 126222336 | bytes 3819520 | tf_op jit(solution)/shard_map/dot_general | solution.py:46
  84.0 0.5 collective-permute-start.18
  84.6 3.3 %collective-permute-done.18 = f32[10,512]{1,0:T(8,128)S(1)} collective-permute-done((f32[10,512]{1,0:T(8,128)S(1)}, f32[10,512]{1,0:T(8,128)S(1)}, u32[]{:S(2)}, u32[]{:S(2)}) %collective-permute-start.18) | collective-permute-done | bytes 20512 | tf_op jit(solution)/shard_map/ppermute | solution.py:114
  87.9 2.3 %collective-permute-start.19 = (f32[10,512]{1,0:T(8,128)S(1)}, f32[10,512]{1,0:T(8,128)S(1)}, u32[]{:S(2)}, u32[]{:S(2)}) collective-permute-start(f32[10,512]{1,0:T(8,128)S(1)} %fusion.134), channel_id=1, source_target_pairs={{0,8},{4,12},{8,0},{12,4},{1,9},{5,13},{9,1},{13,5},{2,10},{6,14},... | collective-permute-start | bytes 61448 | tf_op jit(solution)/shard_map/ppermute | solution.py:114
  90.2 0.6 fusion.131
  93.1 0.6 slice_reduce_fusion.3
  95.6 0.7 fusion.106
  (163 shorter events, 9.8 us)
Async XLA Ops:
  3.3 4.4 %copy-start.1 = (f32[2,3,4096]{2,0,1:T(2,128)S(1)}, f32[2,3,4096]{2,0,1:T(2,128)}, u32[]{:S(2)}) copy-start(f32[2,3,4096]{2,0,1:T(2,128)} %param.8) | copy-start | bytes 294916
  3.3 4.9 %copy-start.4 = (s32[4096]{0:T(1024)S(1)}, s32[4096]{0:T(1024)}, u32[]{:S(2)}) copy-start(s32[4096]{0:T(1024)} %param.10) | copy-start | bytes 49156
  4.6 9.9 %collective-permute-start = (f32[9,512]{1,0:T(8,128)S(1)}, f32[9,512]{1,0:T(8,128)S(1)}, u32[]{:S(2)}, u32[]{:S(2)}) collective-permute-start(f32[9,512]{1,0:T(8,128)S(1)} %reshape.1029), channel_id=1, source_target_pairs={{0,4},{4,0},{8,12},{12,8},{1,5},{5,1},{9,13},{13,9},{2,6},{6,2},{1... | collective-permute-start | bytes 55304 | tf_op jit(solution)/shard_map/ppermute | solution.py:114
  9.3 10.4 %copy-start.2 = (f32[9,512]{1,0:T(8,128)S(1)}, f32[9,512]{1,0:T(8,128)}, u32[]{:S(2)}) copy-start(f32[9,512]{1,0:T(8,128)} %param.13) | copy-start | bytes 55300
  9.4 10.4 %copy-start.3 = (f32[512]{0:T(512)S(1)}, f32[512]{0:T(512)}, u32[]{:S(2)}) copy-start(f32[512]{0:T(512)} %param.12) | copy-start | bytes 6148
  12.6 13.2 %collective-permute-start.5 = (f32[6,4096]{1,0:T(8,128)S(1)}, f32[6,4096]{1,0:T(8,128)S(1)}, u32[]{:S(2)}, u32[]{:S(2)}) collective-permute-start(f32[6,4096]{1,0:T(8,128)S(1)} %reshape.1039), channel_id=1, source_target_pairs={{0,1},{1,0},{2,3},{3,2},{4,5},{5,4},{6,7},{7,6},{8,9},{9,8},{10,11... | collective-permute-start | bytes 294920 | tf_op jit(solution)/shard_map/ppermute | solution.py:107
  12.7 13.4 %collective-permute-start.6 = (f32[6,4096]{1,0:T(8,128)S(1)}, f32[6,4096]{1,0:T(8,128)S(1)}, u32[]{:S(2)}, u32[]{:S(2)}) collective-permute-start(f32[6,4096]{1,0:T(8,128)S(1)} %reshape.1039), channel_id=1, source_target_pairs={{0,2},{1,3},{2,0},{3,1},{4,6},{5,7},{6,4},{7,5},{8,10},{9,11},{10,... | collective-permute-start | bytes 294920 | tf_op jit(solution)/shard_map/ppermute | solution.py:107
  14.3 11.8 %collective-permute-start.7 = (f32[6,4096]{1,0:T(8,128)S(1)}, f32[6,4096]{1,0:T(8,128)S(1)}, u32[]{:S(2)}, u32[]{:S(2)}) collective-permute-start(f32[6,4096]{1,0:T(8,128)S(1)} %reshape.1039), channel_id=1, source_target_pairs={{0,3},{1,2},{2,1},{3,0},{4,7},{5,6},{6,5},{7,4},{8,11},{9,10},{10,... | collective-permute-start | bytes 294920 | tf_op jit(solution)/shard_map/ppermute | solution.py:107
  14.6 5.2 %collective-permute-start.1 = (f32[9,512]{1,0:T(8,128)S(1)}, f32[9,512]{1,0:T(8,128)S(1)}, u32[]{:S(2)}, u32[]{:S(2)}) collective-permute-start(f32[9,512]{1,0:T(8,128)S(1)} %add.147), channel_id=1, source_target_pairs={{0,8},{4,12},{8,0},{12,4},{1,9},{5,13},{9,1},{13,5},{2,10},{6,14},... | collective-permute-start | bytes 55304 | tf_op jit(solution)/shard_map/ppermute | solution.py:114
  20.5 1.0 %copy-start = (f32[2,9,4096]{2,0,1:T(2,128)S(1)}, f32[2,9,4096]{2,0,1:T(2,128)}, u32[]{:S(2)}) copy-start(f32[2,9,4096]{2,0,1:T(2,128)} %param.7) | copy-start | bytes 884740
  23.8 2.5 %copy-start.5 = (f32[4096]{0:T(1024)S(1)}, f32[4096]{0:T(1024)}, u32[]{:S(2)}) copy-start(f32[4096]{0:T(1024)} %param.11) | copy-start | bytes 49156
  24.1 2.7 %collective-permute-start.2 = (f32[4,4096]{1,0:T(4,128)S(1)}, f32[4,4096]{1,0:T(4,128)S(1)}, u32[]{:S(2)}, u32[]{:S(2)}) collective-permute-start(f32[4,4096]{1,0:T(4,128)S(1)} %pad_maximum_fusion.18), channel_id=1, source_target_pairs={{0,1},{1,0},{2,3},{3,2},{4,5},{5,4},{6,7},{7,6},{8,9},{9,8},{10,11... | collective-permute-start | bytes 196616 | tf_op jit(solution)/shard_map/ppermute | solution.py:107
  24.2 4.5 %collective-permute-start.3 = (f32[4,4096]{1,0:T(4,128)S(1)}, f32[4,4096]{1,0:T(4,128)S(1)}, u32[]{:S(2)}, u32[]{:S(2)}) collective-permute-start(f32[4,4096]{1,0:T(4,128)S(1)} %pad_maximum_fusion.18), channel_id=1, source_target_pairs={{0,2},{1,3},{2,0},{3,1},{4,6},{5,7},{6,4},{7,5},{8,10},{9,11},{10,... | collective-permute-start | bytes 196616 | tf_op jit(solution)/shard_map/ppermute | solution.py:107
  25.8 4.1 %collective-permute-start.4 = (f32[4,4096]{1,0:T(4,128)S(1)}, f32[4,4096]{1,0:T(4,128)S(1)}, u32[]{:S(2)}, u32[]{:S(2)}) collective-permute-start(f32[4,4096]{1,0:T(4,128)S(1)} %pad_maximum_fusion.18), channel_id=1, source_target_pairs={{0,3},{1,2},{2,1},{3,0},{4,7},{5,6},{6,5},{7,4},{8,11},{9,10},{10,... | collective-permute-start | bytes 196616 | tf_op jit(solution)/shard_map/ppermute | solution.py:107
  34.0 4.0 %collective-permute-start.8 = (f32[10,512]{1,0:T(8,128)S(1)}, f32[10,512]{1,0:T(8,128)S(1)}, u32[]{:S(2)}, u32[]{:S(2)}) collective-permute-start(f32[10,512]{1,0:T(8,128)S(1)} %pad_maximum_fusion.21), channel_id=1, source_target_pairs={{0,4},{4,0},{8,12},{12,8},{1,5},{5,1},{9,13},{13,9},{2,6},{6,2},{1... | collective-permute-start | bytes 61448 | tf_op jit(solution)/shard_map/ppermute | solution.py:114
  38.0 4.9 %collective-permute-start.9 = (f32[10,512]{1,0:T(8,128)S(1)}, f32[10,512]{1,0:T(8,128)S(1)}, u32[]{:S(2)}, u32[]{:S(2)}) collective-permute-start(f32[10,512]{1,0:T(8,128)S(1)} %fusion.136), channel_id=1, source_target_pairs={{0,8},{4,12},{8,0},{12,4},{1,9},{5,13},{9,1},{13,5},{2,10},{6,14},... | collective-permute-start | bytes 61448 | tf_op jit(solution)/shard_map/ppermute | solution.py:114
  49.4 1.9 %collective-permute-start.10 = (f32[4,4096]{1,0:T(4,128)S(1)}, f32[4,4096]{1,0:T(4,128)S(1)}, u32[]{:S(2)}, u32[]{:S(2)}) collective-permute-start(f32[4,4096]{1,0:T(4,128)S(1)} %pad_maximum_fusion.19), channel_id=1, source_target_pairs={{0,1},{1,0},{2,3},{3,2},{4,5},{5,4},{6,7},{7,6},{8,9},{9,8},{10,11... | collective-permute-start | bytes 196616 | tf_op jit(solution)/shard_map/ppermute | solution.py:107
  49.5 4.7 %collective-permute-start.11 = (f32[4,4096]{1,0:T(4,128)S(1)}, f32[4,4096]{1,0:T(4,128)S(1)}, u32[]{:S(2)}, u32[]{:S(2)}) collective-permute-start(f32[4,4096]{1,0:T(4,128)S(1)} %pad_maximum_fusion.19), channel_id=1, source_target_pairs={{0,2},{1,3},{2,0},{3,1},{4,6},{5,7},{6,4},{7,5},{8,10},{9,11},{10,... | collective-permute-start | bytes 196616 | tf_op jit(solution)/shard_map/ppermute | solution.py:107
  50.8 4.4 %collective-permute-start.12 = (f32[4,4096]{1,0:T(4,128)S(1)}, f32[4,4096]{1,0:T(4,128)S(1)}, u32[]{:S(2)}, u32[]{:S(2)}) collective-permute-start(f32[4,4096]{1,0:T(4,128)S(1)} %pad_maximum_fusion.19), channel_id=1, source_target_pairs={{0,3},{1,2},{2,1},{3,0},{4,7},{5,6},{6,5},{7,4},{8,11},{9,10},{10,... | collective-permute-start | bytes 196616 | tf_op jit(solution)/shard_map/ppermute | solution.py:107
  59.1 4.0 %collective-permute-start.13 = (f32[10,512]{1,0:T(8,128)S(1)}, f32[10,512]{1,0:T(8,128)S(1)}, u32[]{:S(2)}, u32[]{:S(2)}) collective-permute-start(f32[10,512]{1,0:T(8,128)S(1)} %pad_maximum_fusion.22), channel_id=1, source_target_pairs={{0,4},{4,0},{8,12},{12,8},{1,5},{5,1},{9,13},{13,9},{2,6},{6,2},{1... | collective-permute-start | bytes 61448 | tf_op jit(solution)/shard_map/ppermute | solution.py:114
  63.1 4.9 %collective-permute-start.14 = (f32[10,512]{1,0:T(8,128)S(1)}, f32[10,512]{1,0:T(8,128)S(1)}, u32[]{:S(2)}, u32[]{:S(2)}) collective-permute-start(f32[10,512]{1,0:T(8,128)S(1)} %fusion.135), channel_id=1, source_target_pairs={{0,8},{4,12},{8,0},{12,4},{1,9},{5,13},{9,1},{13,5},{2,10},{6,14},... | collective-permute-start | bytes 61448 | tf_op jit(solution)/shard_map/ppermute | solution.py:114
  74.6 1.9 %collective-permute-start.15 = (f32[4,4096]{1,0:T(4,128)S(1)}, f32[4,4096]{1,0:T(4,128)S(1)}, u32[]{:S(2)}, u32[]{:S(2)}) collective-permute-start(f32[4,4096]{1,0:T(4,128)S(1)} %pad_maximum_fusion.20), channel_id=1, source_target_pairs={{0,1},{1,0},{2,3},{3,2},{4,5},{5,4},{6,7},{7,6},{8,9},{9,8},{10,11... | collective-permute-start | bytes 196616 | tf_op jit(solution)/shard_map/ppermute | solution.py:107
  74.7 5.0 %collective-permute-start.16 = (f32[4,4096]{1,0:T(4,128)S(1)}, f32[4,4096]{1,0:T(4,128)S(1)}, u32[]{:S(2)}, u32[]{:S(2)}) collective-permute-start(f32[4,4096]{1,0:T(4,128)S(1)} %pad_maximum_fusion.20), channel_id=1, source_target_pairs={{0,2},{1,3},{2,0},{3,1},{4,6},{5,7},{6,4},{7,5},{8,10},{9,11},{10,... | collective-permute-start | bytes 196616 | tf_op jit(solution)/shard_map/ppermute | solution.py:107
  75.7 4.4 %collective-permute-start.17 = (f32[4,4096]{1,0:T(4,128)S(1)}, f32[4,4096]{1,0:T(4,128)S(1)}, u32[]{:S(2)}, u32[]{:S(2)}) collective-permute-start(f32[4,4096]{1,0:T(4,128)S(1)} %pad_maximum_fusion.20), channel_id=1, source_target_pairs={{0,3},{1,2},{2,1},{3,0},{4,7},{5,6},{6,5},{7,4},{8,11},{9,10},{10,... | collective-permute-start | bytes 196616 | tf_op jit(solution)/shard_map/ppermute | solution.py:107
  84.0 4.0 %collective-permute-start.18 = (f32[10,512]{1,0:T(8,128)S(1)}, f32[10,512]{1,0:T(8,128)S(1)}, u32[]{:S(2)}, u32[]{:S(2)}) collective-permute-start(f32[10,512]{1,0:T(8,128)S(1)} %pad_maximum_fusion.23), channel_id=1, source_target_pairs={{0,4},{4,0},{8,12},{12,8},{1,5},{5,1},{9,13},{13,9},{2,6},{6,2},{1... | collective-permute-start | bytes 61448 | tf_op jit(solution)/shard_map/ppermute | solution.py:114
  87.9 5.1 %collective-permute-start.19 = (f32[10,512]{1,0:T(8,128)S(1)}, f32[10,512]{1,0:T(8,128)S(1)}, u32[]{:S(2)}, u32[]{:S(2)}) collective-permute-start(f32[10,512]{1,0:T(8,128)S(1)} %fusion.134), channel_id=1, source_target_pairs={{0,8},{4,12},{8,0},{12,4},{1,9},{5,13},{9,1},{13,5},{2,10},{6,14},... | collective-permute-start | bytes 61448 | tf_op jit(solution)/shard_map/ppermute | solution.py:114

commit v11 on v9

--- a/solution.py
+++ b/solution.py
@@ -136,7 +136,7 @@
         return jnp.pad(flat, (0, count * width - flat.shape[0])).reshape(count, width)
 
     def lanes(terms):
-        return jnp.sum(terms.reshape(-1, ncam), axis=0)
+        return jnp.broadcast_to(jnp.sum(terms), (ncam,))
 
     def operate(vec, extras):
         y = jnp.sum(cam_jac * by_cam.gather(vec)[None], axis=1)
@@ -146,15 +146,14 @@
         rows = as_row(extras, npts)
         u_all = allsum(jnp.concatenate([u_part, rows], axis=0), "cam")
         u = u_all[:3]
-        got = jnp.sum(u_all[3:].reshape(-1)[: count * ncam].reshape(count, ncam), axis=1)
+        got = u_all[3:].reshape(-1)[: count * ncam].reshape(count, ncam)
         w = jnp.sum(inv * u[None, :, :], axis=1)
-        pt_terms = jnp.sum(u * w, axis=0).reshape(-1, ncam)
-        pt_row = u_all[3:].reshape(-1)[(count - 1) * ncam : count * ncam] - jnp.sum(pt_terms, axis=0)
+        pt_row = got[count - 1] - lanes(u * w)
         z = y - jnp.sum(point_jac * by_point.gather(w)[None], axis=1)
         img_part = by_cam.segsum(jnp.sum(cam_jac * z[:, None, :], axis=0))
         img_all = allsum(jnp.concatenate([img_part, pt_row[None]], axis=0), "pts")
         image = cam_damp[None, :] * vec + img_all[:-1]
-        energy = got[count - 2] + jnp.sum(img_all[-1])
+        energy = got[count - 2] + img_all[-1]
         return image, got, energy
 
     solution = jnp.zeros_like(reduced_rhs)

time: 96.7 us -> 103 us (1.065)
  other arithmetic: 17.1 us -> 29.5 us
  between operations: 11.4 us -> 1.45 us
  waiting for transfers between devices: 25.8 us -> 32.1 us
  local copies, waits for them, and re-layouts: 5.94 us -> 3.9 us
    another operation x1 -> x3, other arithmetic: 0.01 us -> 7.29 us  [operate(): jnp.stack([lanes(t) for t in extras] + [lanes(cam_damp[None, :] * vec * v...]
    ppermute x8, waiting for transfers between devices: 15.4 us -> 21.5 us  [allsum(): lax.ppermute(value, axis, [(i, i ^ step) for i in range(size)])]
    reduce_sum x18 -> x9, other arithmetic: 2.63 us -> 5.91 us  [lanes(): return jnp.broadcast_to(jnp.sum(terms), (ncam,))]
    sub x3, other arithmetic: 0.02 us -> 1.96 us  [operate(): pt_row = got[count - 1] - lanes(u * w)]
    slice x6 -> x0, local copies, waits for them, and re-layouts: 1.91 us -> none  [the longest x2 1.26 us: on_device(): curv = energy + beta * (2.0 * got[1] + beta * curv)]
  transfers between devices with their start and end apart: 20 -> 20, of which waited for: 12 -> 13; matrix products, arithmetic and copies ran while one was open for 12% -> 12% of each run, Pallas kernels for 0% -> 0%
where the time goes in v11:
time: 103 us
  waiting for transfers between devices  32.1 us (31%)
  other arithmetic  29.5 us (29%)
  starting transfers between devices  21 us (20%)
  matrix products  14.9 us (14%)
  local copies, waits for them, and re-layouts  3.9 us (4%)
  between operations  1.45 us (1%)
    ppermute x8, waiting for transfers between devices, allsum(): lax.ppermute(value, axis, [(i, i ^ step) for i in range(size)])  21.5 us
    ppermute x8, starting transfers between devices, allsum(): lax.ppermute(value, axis, [(i, i ^ step) for i in range(size)])  13.3 us
    dot_general x8, matrix products, segsum(): lax.dot_general(self.hot3, spread, (((1,), (1,)), ((), ())), preferred_el...  11.5 us
    ppermute x12, waiting for transfers between devices, allsum(): lax.ppermute(value, axis, [(i, i ^ mask) for i in range(size)])  10.6 us
    ppermute x12, starting transfers between devices, allsum(): lax.ppermute(value, axis, [(i, i ^ mask) for i in range(size)])  7.68 us
    another operation x3, other arithmetic, operate(): jnp.stack([lanes(t) for t in extras] + [lanes(cam_damp[None, :] * vec * v...  7.29 us
    reduce_sum x9, other arithmetic, lanes(): return jnp.broadcast_to(jnp.sum(terms), (ncam,))  5.91 us
    select_n x8, other arithmetic, segsum(): jnp.where(self.low[None], part[:, None, :], jnp.zeros((), BF))  3.86 us
  transfers between devices with their start and end apart: 20, of which 13 were waited for; matrix products, arithmetic and copies ran while one was open for 12% of the time, Pallas kernels for 0%

profile of v11, /device:TPU:0, one launch (start us, length us, event | category | flops | bytes accessed | tf_op | source)
XLA Modules:
  0.0 102.9 jit_solution(6056068899453843546)
XLA Ops:
  0.6 0.7 add_select_fusion
  1.4 1.4 %multiply_reduce_fusion.6 = f32[9,4096]{1,0:T(8,128)S(1)} fusion(f32[2,9,4096]{2,0,1:T(2,128)} %param.7), kind=kLoop, calls=%fused_computation.115 | loop fusion | flops 110592 | bytes 442368 | tf_op jit(solution)/shard_map/reduce_sum | solution.py:130
  3.3 1.1 %fusion.24 = f32[32,144]{0,1:T(8,128)S(1)} fusion(bf16[144,4096]{1,0:T(8,128)(2,1)S(1)} %bitcast.188, bf16[144,4096]{1,0:T(8,128)(2,1)S(1)} %bitcast.187, bf16[144,4096]{1,0:T(8,128)(2,1)S(1)} %bitcast.186, bf16[32,4096]{1,0:T(8,128)(2,1)S(1)} %fusion.52), kind=kOutput, calls=%fused_computation.24 | convolution fusion | flops 126222336 | bytes 3819520 | tf_op jit(solution)/shard_map/dot_general | solution.py:46
  4.6 3.1 %collective-permute-start = (f32[9,512]{1,0:T(8,128)S(1)}, f32[9,512]{1,0:T(8,128)S(1)}, u32[]{:S(2)}, u32[]{:S(2)}) collective-permute-start(f32[9,512]{1,0:T(8,128)S(1)} %reshape.1000), channel_id=1, source_target_pairs={{0,4},{4,0},{8,12},{12,8},{1,5},{5,1},{9,13},{13,9},{2,6},{6,2},{1... | collective-permute-start | bytes 55304 | tf_op jit(solution)/shard_map/ppermute | solution.py:114
  8.5 0.9 broadcast_select_fusion.2
  9.4 3.0 %fusion = f32[64,384]{1,0:T(8,128)S(1)} fusion(bf16[384,4096]{1,0:T(8,128)(2,1)S(1)} %bitcast.173, bf16[384,4096]{1,0:T(8,128)(2,1)S(1)} %bitcast.172, bf16[384,4096]{1,0:T(8,128)(2,1)S(1)} %bitcast.171, bf16[64,4096]{1,0:T(8,128)(2,1)S(1)} %get-tuple-element.117), kind=kOutput, calls=%fused_computation | convolution fusion | flops 637009920 | bytes 10059776 | tf_op jit(solution)/shard_map/dot_general | solution.py:46
  12.7 1.6 %collective-permute-start.6 = (f32[6,4096]{1,0:T(8,128)S(1)}, f32[6,4096]{1,0:T(8,128)S(1)}, u32[]{:S(2)}, u32[]{:S(2)}) collective-permute-start(f32[6,4096]{1,0:T(8,128)S(1)} %reshape.1009), channel_id=1, source_target_pairs={{0,2},{1,3},{2,0},{3,1},{4,6},{5,7},{6,4},{7,5},{8,10},{9,11},{10,... | collective-permute-start | bytes 294920 | tf_op jit(solution)/shard_map/ppermute | solution.py:107
  14.6 2.7 %collective-permute-start.1 = (f32[9,512]{1,0:T(8,128)S(1)}, f32[9,512]{1,0:T(8,128)S(1)}, u32[]{:S(2)}, u32[]{:S(2)}) collective-permute-start(f32[9,512]{1,0:T(8,128)S(1)} %add.159), channel_id=1, source_target_pairs={{0,8},{4,12},{8,0},{12,4},{1,9},{5,13},{9,1},{13,5},{2,10},{6,14},... | collective-permute-start | bytes 55304 | tf_op jit(solution)/shard_map/ppermute | solution.py:114
  17.2 2.5 %collective-permute-done.1 = f32[9,512]{1,0:T(8,128)S(1)} collective-permute-done((f32[9,512]{1,0:T(8,128)S(1)}, f32[9,512]{1,0:T(8,128)S(1)}, u32[]{:S(2)}, u32[]{:S(2)}) %collective-permute-start.1) | collective-permute-done | bytes 18464 | tf_op jit(solution)/shard_map/ppermute | solution.py:114
  19.7 0.6 multiply_reduce_fusion.32
  20.6 0.5 fusion.55
  21.1 0.5 select_reduce_fusion.5
  21.6 0.5 copy-done
  22.4 0.7 multiply_reduce_fusion.31
  23.2 0.4 broadcast_select_fusion.11
  23.6 1.4 %fusion.6 = f32[64,192]{0,1:T(8,128)S(1)} fusion(bf16[192,4096]{1,0:T(8,128)(2,1)S(1)} %bitcast.176, bf16[192,4096]{1,0:T(8,128)(2,1)S(1)} %bitcast.175, bf16[192,4096]{1,0:T(8,128)(2,1)S(1)} %bitcast.174, bf16[64,4096]{1,0:T(8,128)(2,1)S(1)} %get-tuple-element.117), kind=kOutput, calls=%fused_computation.6 | convolution fusion | flops 320864256 | bytes 5292032 | tf_op jit(solution)/shard_map/dot_general | solution.py:46
  25.3 2.1 %maximum_maximum_fusion.2 = f32[3]{0:T(128)S(1)} fusion(f32[1]{0:T(128)} %bitcast.99, f32[1]{0:T(128)} %bitcast.98, f32[1]{0:T(128)} %bitcast.97), kind=kLoop, calls=%fused_computation.313 | loop fusion | flops 6 | bytes 24 | tf_op jit(solution)/shard_map/stack | solution.py:144
  27.6 1.6 %collective-permute-start.3 = (f32[4,4096]{1,0:T(4,128)S(1)}, f32[4,4096]{1,0:T(4,128)S(1)}, u32[]{:S(2)}, u32[]{:S(2)}) collective-permute-start(f32[4,4096]{1,0:T(4,128)S(1)} %pad_maximum_fusion.18), channel_id=1, source_target_pairs={{0,2},{1,3},{2,0},{3,1},{4,6},{5,7},{6,4},{7,5},{8,10},{9,11},{10,... | collective-permute-start | bytes 196616 | tf_op jit(solution)/shard_map/ppermute | solution.py:107
  30.2 1.9 %collective-permute-done.3 = f32[4,4096]{1,0:T(4,128)S(1)} collective-permute-done((f32[4,4096]{1,0:T(4,128)S(1)}, f32[4,4096]{1,0:T(4,128)S(1)}, u32[]{:S(2)}, u32[]{:S(2)}) %collective-permute-start.3) | collective-permute-done | bytes 65568 | tf_op jit(solution)/shard_map/ppermute | solution.py:107
  32.0 1.2 %collective-permute-done.4 = f32[4,4096]{1,0:T(4,128)S(1)} collective-permute-done((f32[4,4096]{1,0:T(4,128)S(1)}, f32[4,4096]{1,0:T(4,128)S(1)}, u32[]{:S(2)}, u32[]{:S(2)}) %collective-permute-start.4) | collective-permute-done | bytes 65568 | tf_op jit(solution)/shard_map/ppermute | solution.py:107
  33.6 0.6 multiply_reduce_fusion.18
  34.3 0.6 fusion.51
  35.5 0.6 multiply_reduce_fusion.4
  36.5 1.1 %fusion.30 = f32[32,144]{0,1:T(8,128)S(1)} fusion(bf16[144,4096]{1,0:T(8,128)(2,1)S(1)} %bitcast.191, bf16[144,4096]{1,0:T(8,128)(2,1)S(1)} %bitcast.190, bf16[144,4096]{1,0:T(8,128)(2,1)S(1)} %bitcast.189, bf16[32,4096]{1,0:T(8,128)(2,1)S(1)} %fusion.52), kind=kOutput, calls=%fused_computation.30 | convolution fusion | flops 126222336 | bytes 3819520 | tf_op jit(solution)/shard_map/dot_general | solution.py:46
  37.8 0.7 slice_subtract_fusion.2
  38.7 3.8 %collective-permute-done.8 = f32[10,512]{1,0:T(8,128)S(1)} collective-permute-done((f32[10,512]{1,0:T(8,128)S(1)}, f32[10,512]{1,0:T(8,128)S(1)}, u32[]{:S(2)}, u32[]{:S(2)}) %collective-permute-start.8) | collective-permute-done | bytes 20512 | tf_op jit(solution)/shard_map/ppermute | solution.py:114
  42.5 2.3 %collective-permute-start.9 = (f32[10,512]{1,0:T(8,128)S(1)}, f32[10,512]{1,0:T(8,128)S(1)}, u32[]{:S(2)}, u32[]{:S(2)}) collective-permute-start(f32[10,512]{1,0:T(8,128)S(1)} %fusion.141), channel_id=1, source_target_pairs={{0,8},{4,12},{8,0},{12,4},{1,9},{5,13},{9,1},{13,5},{2,10},{6,14},... | collective-permute-start | bytes 61448 | tf_op jit(solution)/shard_map/ppermute | solution.py:114
  44.8 2.5 %collective-permute-done.9 = f32[10,512]{1,0:T(8,128)S(1)} collective-permute-done((f32[10,512]{1,0:T(8,128)S(1)}, f32[10,512]{1,0:T(8,128)S(1)}, u32[]{:S(2)}, u32[]{:S(2)}) %collective-permute-start.9) | collective-permute-done | bytes 20512 | tf_op jit(solution)/shard_map/ppermute | solution.py:114
  47.4 0.7 multiply_reduce_fusion.24
  48.3 0.5 fusion.54
  48.8 0.5 select_reduce_fusion.4
  49.6 0.6 multiply_reduce_fusion.22
  50.8 1.4 %fusion.12 = f32[64,192]{0,1:T(8,128)S(1)} fusion(bf16[192,4096]{1,0:T(8,128)(2,1)S(1)} %bitcast.179, bf16[192,4096]{1,0:T(8,128)(2,1)S(1)} %bitcast.178, bf16[192,4096]{1,0:T(8,128)(2,1)S(1)} %bitcast.177, bf16[64,4096]{1,0:T(8,128)(2,1)S(1)} %get-tuple-element.117), kind=kOutput, calls=%fused_computation.12 | convolution fusion | flops 320864256 | bytes 5292032 | tf_op jit(solution)/shard_map/dot_general | solution.py:46
  52.4 2.6 %maximum_maximum_fusion.1 = f32[4]{0:T(128)S(1)} fusion(f32[1]{0:T(128)} %bitcast.103, f32[1]{0:T(128)} %bitcast.102, f32[1]{0:T(128)} %bitcast.101, f32[1]{0:T(128)} %bitcast.100), kind=kLoop, calls=%fused_computation.312 | loop fusion | flops 12 | bytes 32 | tf_op jit(solution)/shard_map/stack | solution.py:144
  55.2 1.3 %collective-permute-start.11 = (f32[4,4096]{1,0:T(4,128)S(1)}, f32[4,4096]{1,0:T(4,128)S(1)}, u32[]{:S(2)}, u32[]{:S(2)}) collective-permute-start(f32[4,4096]{1,0:T(4,128)S(1)} %pad_maximum_fusion.19), channel_id=1, source_target_pairs={{0,2},{1,3},{2,0},{3,1},{4,6},{5,7},{6,4},{7,5},{8,10},{9,11},{10,... | collective-permute-start | bytes 196616 | tf_op jit(solution)/shard_map/ppermute | solution.py:107
  56.5 0.6 collective-permute-start.12
  57.1 2.9 %collective-permute-done.11 = f32[4,4096]{1,0:T(4,128)S(1)} collective-permute-done((f32[4,4096]{1,0:T(4,128)S(1)}, f32[4,4096]{1,0:T(4,128)S(1)}, u32[]{:S(2)}, u32[]{:S(2)}) %collective-permute-start.11) | collective-permute-done | bytes 65568 | tf_op jit(solution)/shard_map/ppermute | solution.py:107
  59.9 1.0 collective-permute-done.12
  61.2 0.6 multiply_reduce_fusion.17
  62.0 0.6 fusion.50
  64.0 1.1 %fusion.36 = f32[32,144]{0,1:T(8,128)S(1)} fusion(bf16[144,4096]{1,0:T(8,128)(2,1)S(1)} %bitcast.194, bf16[144,4096]{1,0:T(8,128)(2,1)S(1)} %bitcast.193, bf16[144,4096]{1,0:T(8,128)(2,1)S(1)} %bitcast.192, bf16[32,4096]{1,0:T(8,128)(2,1)S(1)} %fusion.52), kind=kOutput, calls=%fused_computation.36 | convolution fusion | flops 126222336 | bytes 3819520 | tf_op jit(solution)/shard_map/dot_general | solution.py:46
  65.3 0.7 slice_subtract_fusion.1
  66.2 3.8 %collective-permute-done.13 = f32[10,512]{1,0:T(8,128)S(1)} collective-permute-done((f32[10,512]{1,0:T(8,128)S(1)}, f32[10,512]{1,0:T(8,128)S(1)}, u32[]{:S(2)}, u32[]{:S(2)}) %collective-permute-start.13) | collective-permute-done | bytes 20512 | tf_op jit(solution)/shard_map/ppermute | solution.py:114
  70.0 2.3 %collective-permute-start.14 = (f32[10,512]{1,0:T(8,128)S(1)}, f32[10,512]{1,0:T(8,128)S(1)}, u32[]{:S(2)}, u32[]{:S(2)}) collective-permute-start(f32[10,512]{1,0:T(8,128)S(1)} %fusion.140), channel_id=1, source_target_pairs={{0,8},{4,12},{8,0},{12,4},{1,9},{5,13},{9,1},{13,5},{2,10},{6,14},... | collective-permute-start | bytes 61448 | tf_op jit(solution)/shard_map/ppermute | solution.py:114
  72.3 2.5 %collective-permute-done.14 = f32[10,512]{1,0:T(8,128)S(1)} collective-permute-done((f32[10,512]{1,0:T(8,128)S(1)}, f32[10,512]{1,0:T(8,128)S(1)}, u32[]{:S(2)}, u32[]{:S(2)}) %collective-permute-start.14) | collective-permute-done | bytes 20512 | tf_op jit(solution)/shard_map/ppermute | solution.py:114
  74.9 0.7 multiply_reduce_fusion.21
  75.8 0.5 fusion.53
  76.4 0.5 select_reduce_fusion.3
  77.1 0.6 multiply_reduce_fusion.19
  77.8 0.4 broadcast_select_fusion.5
  78.3 1.4 %fusion.18 = f32[64,192]{0,1:T(8,128)S(1)} fusion(bf16[192,4096]{1,0:T(8,128)(2,1)S(1)} %bitcast.182, bf16[192,4096]{1,0:T(8,128)(2,1)S(1)} %bitcast.181, bf16[192,4096]{1,0:T(8,128)(2,1)S(1)} %bitcast.180, bf16[64,4096]{1,0:T(8,128)(2,1)S(1)} %get-tuple-element.117), kind=kOutput, calls=%fused_computation.18 | convolution fusion | flops 320864256 | bytes 5292032 | tf_op jit(solution)/shard_map/dot_general | solution.py:46
  79.9 2.6 %maximum_maximum_fusion = f32[4]{0:T(128)S(1)} fusion(f32[1]{0:T(128)} %bitcast.107, f32[1]{0:T(128)} %bitcast.106, f32[1]{0:T(128)} %bitcast.105, f32[1]{0:T(128)} %bitcast.104), kind=kLoop, calls=%fused_computation.311 | loop fusion | flops 12 | bytes 32 | tf_op jit(solution)/shard_map/stack | solution.py:144
  82.7 1.2 %collective-permute-start.16 = (f32[4,4096]{1,0:T(4,128)S(1)}, f32[4,4096]{1,0:T(4,128)S(1)}, u32[]{:S(2)}, u32[]{:S(2)}) collective-permute-start(f32[4,4096]{1,0:T(4,128)S(1)} %pad_maximum_fusion.20), channel_id=1, source_target_pairs={{0,2},{1,3},{2,0},{3,1},{4,6},{5,7},{6,4},{7,5},{8,10},{9,11},{10,... | collective-permute-start | bytes 196616 | tf_op jit(solution)/shard_map/ppermute | solution.py:107
  83.9 0.7 collective-permute-start.17
  84.6 3.1 %collective-permute-done.16 = f32[4,4096]{1,0:T(4,128)S(1)} collective-permute-done((f32[4,4096]{1,0:T(4,128)S(1)}, f32[4,4096]{1,0:T(4,128)S(1)}, u32[]{:S(2)}, u32[]{:S(2)}) %collective-permute-start.16) | collective-permute-done | bytes 65568 | tf_op jit(solution)/shard_map/ppermute | solution.py:107
  87.7 0.6 collective-permute-done.17
  88.6 0.6 multiply_reduce_fusion.16
  89.4 0.6 fusion.49
  91.4 1.1 %fusion.42 = f32[32,144]{0,1:T(8,128)S(1)} fusion(bf16[144,4096]{1,0:T(8,128)(2,1)S(1)} %bitcast.185, bf16[144,4096]{1,0:T(8,128)(2,1)S(1)} %bitcast.184, bf16[144,4096]{1,0:T(8,128)(2,1)S(1)} %bitcast.183, bf16[32,4096]{1,0:T(8,128)(2,1)S(1)} %fusion.52), kind=kOutput, calls=%fused_computation.42 | convolution fusion | flops 126222336 | bytes 3819520 | tf_op jit(solution)/shard_map/dot_general | solution.py:46
  92.7 0.7 slice_subtract_fusion
  93.6 3.8 %collective-permute-done.18 = f32[10,512]{1,0:T(8,128)S(1)} collective-permute-done((f32[10,512]{1,0:T(8,128)S(1)}, f32[10,512]{1,0:T(8,128)S(1)}, u32[]{:S(2)}, u32[]{:S(2)}) %collective-permute-start.18) | collective-permute-done | bytes 20512 | tf_op jit(solution)/shard_map/ppermute | solution.py:114
  97.4 2.3 %collective-permute-start.19 = (f32[10,512]{1,0:T(8,128)S(1)}, f32[10,512]{1,0:T(8,128)S(1)}, u32[]{:S(2)}, u32[]{:S(2)}) collective-permute-start(f32[10,512]{1,0:T(8,128)S(1)} %fusion.139), channel_id=1, source_target_pairs={{0,8},{4,12},{8,0},{12,4},{1,9},{5,13},{9,1},{13,5},{2,10},{6,14},... | collective-permute-start | bytes 61448 | tf_op jit(solution)/shard_map/ppermute | solution.py:114
  99.7 2.6 %collective-permute-done.19 = f32[10,512]{1,0:T(8,128)S(1)} collective-permute-done((f32[10,512]{1,0:T(8,128)S(1)}, f32[10,512]{1,0:T(8,128)S(1)}, u32[]{:S(2)}, u32[]{:S(2)}) %collective-permute-start.19) | collective-permute-done | bytes 20512 | tf_op jit(solution)/shard_map/ppermute | solution.py:114
  102.3 0.7 fusion.106
  (142 shorter events, 12.8 us)
Async XLA Ops:
  3.3 4.4 %copy-start.1 = (f32[2,3,4096]{2,0,1:T(2,128)S(1)}, f32[2,3,4096]{2,0,1:T(2,128)}, u32[]{:S(2)}) copy-start(f32[2,3,4096]{2,0,1:T(2,128)} %param.8) | copy-start | bytes 294916
  3.3 4.9 %copy-start.4 = (s32[4096]{0:T(1024)S(1)}, s32[4096]{0:T(1024)}, u32[]{:S(2)}) copy-start(s32[4096]{0:T(1024)} %param.10) | copy-start | bytes 49156
  4.6 9.9 %collective-permute-start = (f32[9,512]{1,0:T(8,128)S(1)}, f32[9,512]{1,0:T(8,128)S(1)}, u32[]{:S(2)}, u32[]{:S(2)}) collective-permute-start(f32[9,512]{1,0:T(8,128)S(1)} %reshape.1000), channel_id=1, source_target_pairs={{0,4},{4,0},{8,12},{12,8},{1,5},{5,1},{9,13},{13,9},{2,6},{6,2},{1... | collective-permute-start | bytes 55304 | tf_op jit(solution)/shard_map/ppermute | solution.py:114
  9.3 10.4 %copy-start.2 = (f32[9,512]{1,0:T(8,128)S(1)}, f32[9,512]{1,0:T(8,128)}, u32[]{:S(2)}) copy-start(f32[9,512]{1,0:T(8,128)} %param.13) | copy-start | bytes 55300
  9.4 10.4 %copy-start.3 = (f32[512]{0:T(512)S(1)}, f32[512]{0:T(512)}, u32[]{:S(2)}) copy-start(f32[512]{0:T(512)} %param.12) | copy-start | bytes 6148
  12.6 16.5 %collective-permute-start.5 = (f32[6,4096]{1,0:T(8,128)S(1)}, f32[6,4096]{1,0:T(8,128)S(1)}, u32[]{:S(2)}, u32[]{:S(2)}) collective-permute-start(f32[6,4096]{1,0:T(8,128)S(1)} %reshape.1009), channel_id=1, source_target_pairs={{0,1},{1,0},{2,3},{3,2},{4,5},{5,4},{6,7},{7,6},{8,9},{9,8},{10,11... | collective-permute-start | bytes 294920 | tf_op jit(solution)/shard_map/ppermute | solution.py:107
  12.7 16.7 %collective-permute-start.6 = (f32[6,4096]{1,0:T(8,128)S(1)}, f32[6,4096]{1,0:T(8,128)S(1)}, u32[]{:S(2)}, u32[]{:S(2)}) collective-permute-start(f32[6,4096]{1,0:T(8,128)S(1)} %reshape.1009), channel_id=1, source_target_pairs={{0,2},{1,3},{2,0},{3,1},{4,6},{5,7},{6,4},{7,5},{8,10},{9,11},{10,... | collective-permute-start | bytes 294920 | tf_op jit(solution)/shard_map/ppermute | solution.py:107
  14.3 15.1 %collective-permute-start.7 = (f32[6,4096]{1,0:T(8,128)S(1)}, f32[6,4096]{1,0:T(8,128)S(1)}, u32[]{:S(2)}, u32[]{:S(2)}) collective-permute-start(f32[6,4096]{1,0:T(8,128)S(1)} %reshape.1009), channel_id=1, source_target_pairs={{0,3},{1,2},{2,1},{3,0},{4,7},{5,6},{6,5},{7,4},{8,11},{9,10},{10,... | collective-permute-start | bytes 294920 | tf_op jit(solution)/shard_map/ppermute | solution.py:107
  14.6 5.2 %collective-permute-start.1 = (f32[9,512]{1,0:T(8,128)S(1)}, f32[9,512]{1,0:T(8,128)S(1)}, u32[]{:S(2)}, u32[]{:S(2)}) collective-permute-start(f32[9,512]{1,0:T(8,128)S(1)} %add.159), channel_id=1, source_target_pairs={{0,8},{4,12},{8,0},{12,4},{1,9},{5,13},{9,1},{13,5},{2,10},{6,14},... | collective-permute-start | bytes 55304 | tf_op jit(solution)/shard_map/ppermute | solution.py:114
  21.1 1.0 copy-start
  25.0 4.6 %copy-start.5 = (f32[4096]{0:T(1024)S(1)}, f32[4096]{0:T(1024)}, u32[]{:S(2)}) copy-start(f32[4096]{0:T(1024)} %param.11) | copy-start | bytes 49156
  27.5 2.7 %collective-permute-start.2 = (f32[4,4096]{1,0:T(4,128)S(1)}, f32[4,4096]{1,0:T(4,128)S(1)}, u32[]{:S(2)}, u32[]{:S(2)}) collective-permute-start(f32[4,4096]{1,0:T(4,128)S(1)} %pad_maximum_fusion.18), channel_id=1, source_target_pairs={{0,1},{1,0},{2,3},{3,2},{4,5},{5,4},{6,7},{7,6},{8,9},{9,8},{10,11... | collective-permute-start | bytes 196616 | tf_op jit(solution)/shard_map/ppermute | solution.py:107
  27.6 4.5 %collective-permute-start.3 = (f32[4,4096]{1,0:T(4,128)S(1)}, f32[4,4096]{1,0:T(4,128)S(1)}, u32[]{:S(2)}, u32[]{:S(2)}) collective-permute-start(f32[4,4096]{1,0:T(4,128)S(1)} %pad_maximum_fusion.18), channel_id=1, source_target_pairs={{0,2},{1,3},{2,0},{3,1},{4,6},{5,7},{6,4},{7,5},{8,10},{9,11},{10,... | collective-permute-start | bytes 196616 | tf_op jit(solution)/shard_map/ppermute | solution.py:107
  29.1 4.1 %collective-permute-start.4 = (f32[4,4096]{1,0:T(4,128)S(1)}, f32[4,4096]{1,0:T(4,128)S(1)}, u32[]{:S(2)}, u32[]{:S(2)}) collective-permute-start(f32[4,4096]{1,0:T(4,128)S(1)} %pad_maximum_fusion.18), channel_id=1, source_target_pairs={{0,3},{1,2},{2,1},{3,0},{4,7},{5,6},{6,5},{7,4},{8,11},{9,10},{10,... | collective-permute-start | bytes 196616 | tf_op jit(solution)/shard_map/ppermute | solution.py:107
  38.5 4.0 %collective-permute-start.8 = (f32[10,512]{1,0:T(8,128)S(1)}, f32[10,512]{1,0:T(8,128)S(1)}, u32[]{:S(2)}, u32[]{:S(2)}) collective-permute-start(f32[10,512]{1,0:T(8,128)S(1)} %pad_maximum_fusion.21), channel_id=1, source_target_pairs={{0,4},{4,0},{8,12},{12,8},{1,5},{5,1},{9,13},{13,9},{2,6},{6,2},{1... | collective-permute-start | bytes 61448 | tf_op jit(solution)/shard_map/ppermute | solution.py:114
  42.5 4.9 %collective-permute-start.9 = (f32[10,512]{1,0:T(8,128)S(1)}, f32[10,512]{1,0:T(8,128)S(1)}, u32[]{:S(2)}, u32[]{:S(2)}) collective-permute-start(f32[10,512]{1,0:T(8,128)S(1)} %fusion.141), channel_id=1, source_target_pairs={{0,8},{4,12},{8,0},{12,4},{1,9},{5,13},{9,1},{13,5},{2,10},{6,14},... | collective-permute-start | bytes 61448 | tf_op jit(solution)/shard_map/ppermute | solution.py:114
  55.1 1.9 %collective-permute-start.10 = (f32[4,4096]{1,0:T(4,128)S(1)}, f32[4,4096]{1,0:T(4,128)S(1)}, u32[]{:S(2)}, u32[]{:S(2)}) collective-permute-start(f32[4,4096]{1,0:T(4,128)S(1)} %pad_maximum_fusion.19), channel_id=1, source_target_pairs={{0,1},{1,0},{2,3},{3,2},{4,5},{5,4},{6,7},{7,6},{8,9},{9,8},{10,11... | collective-permute-start | bytes 196616 | tf_op jit(solution)/shard_map/ppermute | solution.py:107
  55.2 4.7 %collective-permute-start.11 = (f32[4,4096]{1,0:T(4,128)S(1)}, f32[4,4096]{1,0:T(4,128)S(1)}, u32[]{:S(2)}, u32[]{:S(2)}) collective-permute-start(f32[4,4096]{1,0:T(4,128)S(1)} %pad_maximum_fusion.19), channel_id=1, source_target_pairs={{0,2},{1,3},{2,0},{3,1},{4,6},{5,7},{6,4},{7,5},{8,10},{9,11},{10,... | collective-permute-start | bytes 196616 | tf_op jit(solution)/shard_map/ppermute | solution.py:107
  56.5 4.4 %collective-permute-start.12 = (f32[4,4096]{1,0:T(4,128)S(1)}, f32[4,4096]{1,0:T(4,128)S(1)}, u32[]{:S(2)}, u32[]{:S(2)}) collective-permute-start(f32[4,4096]{1,0:T(4,128)S(1)} %pad_maximum_fusion.19), channel_id=1, source_target_pairs={{0,3},{1,2},{2,1},{3,0},{4,7},{5,6},{6,5},{7,4},{8,11},{9,10},{10,... | collective-permute-start | bytes 196616 | tf_op jit(solution)/shard_map/ppermute | solution.py:107
  66.0 4.0 %collective-permute-start.13 = (f32[10,512]{1,0:T(8,128)S(1)}, f32[10,512]{1,0:T(8,128)S(1)}, u32[]{:S(2)}, u32[]{:S(2)}) collective-permute-start(f32[10,512]{1,0:T(8,128)S(1)} %pad_maximum_fusion.22), channel_id=1, source_target_pairs={{0,4},{4,0},{8,12},{12,8},{1,5},{5,1},{9,13},{13,9},{2,6},{6,2},{1... | collective-permute-start | bytes 61448 | tf_op jit(solution)/shard_map/ppermute | solution.py:114
  70.0 4.9 %collective-permute-start.14 = (f32[10,512]{1,0:T(8,128)S(1)}, f32[10,512]{1,0:T(8,128)S(1)}, u32[]{:S(2)}, u32[]{:S(2)}) collective-permute-start(f32[10,512]{1,0:T(8,128)S(1)} %fusion.140), channel_id=1, source_target_pairs={{0,8},{4,12},{8,0},{12,4},{1,9},{5,13},{9,1},{13,5},{2,10},{6,14},... | collective-permute-start | bytes 61448 | tf_op jit(solution)/shard_map/ppermute | solution.py:114
  82.6 1.9 %collective-permute-start.15 = (f32[4,4096]{1,0:T(4,128)S(1)}, f32[4,4096]{1,0:T(4,128)S(1)}, u32[]{:S(2)}, u32[]{:S(2)}) collective-permute-start(f32[4,4096]{1,0:T(4,128)S(1)} %pad_maximum_fusion.20), channel_id=1, source_target_pairs={{0,1},{1,0},{2,3},{3,2},{4,5},{5,4},{6,7},{7,6},{8,9},{9,8},{10,11... | collective-permute-start | bytes 196616 | tf_op jit(solution)/shard_map/ppermute | solution.py:107
  82.7 4.9 %collective-permute-start.16 = (f32[4,4096]{1,0:T(4,128)S(1)}, f32[4,4096]{1,0:T(4,128)S(1)}, u32[]{:S(2)}, u32[]{:S(2)}) collective-permute-start(f32[4,4096]{1,0:T(4,128)S(1)} %pad_maximum_fusion.20), channel_id=1, source_target_pairs={{0,2},{1,3},{2,0},{3,1},{4,6},{5,7},{6,4},{7,5},{8,10},{9,11},{10,... | collective-permute-start | bytes 196616 | tf_op jit(solution)/shard_map/ppermute | solution.py:107
  83.9 4.4 %collective-permute-start.17 = (f32[4,4096]{1,0:T(4,128)S(1)}, f32[4,4096]{1,0:T(4,128)S(1)}, u32[]{:S(2)}, u32[]{:S(2)}) collective-permute-start(f32[4,4096]{1,0:T(4,128)S(1)} %pad_maximum_fusion.20), channel_id=1, source_target_pairs={{0,3},{1,2},{2,1},{3,0},{4,7},{5,6},{6,5},{7,4},{8,11},{9,10},{10,... | collective-permute-start | bytes 196616 | tf_op jit(solution)/shard_map/ppermute | solution.py:107
  93.4 4.0 %collective-permute-start.18 = (f32[10,512]{1,0:T(8,128)S(1)}, f32[10,512]{1,0:T(8,128)S(1)}, u32[]{:S(2)}, u32[]{:S(2)}) collective-permute-start(f32[10,512]{1,0:T(8,128)S(1)} %pad_maximum_fusion.23), channel_id=1, source_target_pairs={{0,4},{4,0},{8,12},{12,8},{1,5},{5,1},{9,13},{13,9},{2,6},{6,2},{1... | collective-permute-start | bytes 61448 | tf_op jit(solution)/shard_map/ppermute | solution.py:114
  97.4 4.9 %collective-permute-start.19 = (f32[10,512]{1,0:T(8,128)S(1)}, f32[10,512]{1,0:T(8,128)S(1)}, u32[]{:S(2)}, u32[]{:S(2)}) collective-permute-start(f32[10,512]{1,0:T(8,128)S(1)} %fusion.139), channel_id=1, source_target_pairs={{0,8},{4,12},{8,0},{12,4},{1,9},{5,13},{9,1},{13,5},{2,10},{6,14},... | collective-permute-start | bytes 61448 | tf_op jit(solution)/shard_map/ppermute | solution.py:114

commit v12 on v10

--- a/solution.py
+++ b/solution.py
@@ -10,7 +10,7 @@
 
 
 def split_of(count):
-    lo = 1 << (max(count.bit_length() - 1, 0) // 2)
+    lo = 1 << max((count.bit_length() - 1) // 2 - 1, 0)
     while count % lo:
         lo //= 2
     return count // lo, lo

time: 96.6 us -> 90.5 us (0.937)
  other arithmetic: 17.1 us -> 13.5 us
  matrix products: 14.9 us -> 11.6 us
    dot_general x8, matrix products: 11.5 us -> 7.72 us  [segsum(): lax.dot_general(self.hot3, spread, (((1,), (1,)), ((), ())), preferred_el...]
    reduce_sum x6 -> x3, other arithmetic: 2.61 us -> 0.75 us  [gather(): return jnp.sum(jnp.where(self.low[None], spread, 0.0), axis=1)]
    select_n x8, other arithmetic: 3.86 us -> 2.11 us  [segsum(): jnp.where(self.low[None], part[:, None, :], jnp.zeros((), BF))]
  transfers between devices with their start and end apart: 20 -> 20, of which waited for: 12 -> 12; matrix products, arithmetic and copies ran while one was open for 12% -> 10% of each run, Pallas kernels for 0% -> 0%
where the time goes in v12:
time: 90.5 us; the launch traced here: 90.1 us
  waiting for transfers between devices  25.7 us (28%)
  starting transfers between devices  21.3 us (24%)
  other arithmetic  13.5 us (15%)
  matrix products  11.6 us (13%)
  between operations  11.3 us (12%)
  local copies, waits for them, and re-layouts  6.67 us (7%)
    ppermute x8, waiting for transfers between devices, allsum(): lax.ppermute(value, axis, [(i, i ^ step) for i in range(size)])  15.3 us
    ppermute x8, starting transfers between devices, allsum(): lax.ppermute(value, axis, [(i, i ^ step) for i in range(size)])  13.6 us
    ppermute x12, waiting for transfers between devices, allsum(): lax.ppermute(value, axis, [(i, i ^ mask) for i in range(size)])  10.4 us
    dot_general x8, matrix products, segsum(): lax.dot_general(self.hot3, spread, (((1,), (1,)), ((), ())), preferred_el...  7.72 us
    ppermute x12, starting transfers between devices, allsum(): lax.ppermute(value, axis, [(i, i ^ mask) for i in range(size)])  7.68 us
    dot_general x6, matrix products, gather(): lax.dot_general(stacked, self.hot3t, (((1,), (0,)), ((), ())), preferred_...  3.9 us
    select_n x8, other arithmetic, segsum(): jnp.where(self.low[None], part[:, None, :], jnp.zeros((), BF))  2.11 us
    reshape x12, local copies, waits for them, and re-layouts, segsum(): out.reshape(self.hi, ncol, self.lo).transpose(1, 0, 2)  1.92 us
  transfers between devices with their start and end apart: 20, of which 12 were waited for; matrix products, arithmetic and copies ran while one was open for 10% of the time, Pallas kernels for 0%

profile of v12, /device:TPU:0, one launch (start us, length us, event | category | flops | bytes accessed | tf_op | source)
XLA Modules:
  0.0 90.1 jit_solution(381954774242407795)
XLA Ops:
  0.6 0.7 add_select_fusion
  1.4 1.4 %multiply_reduce_fusion.6 = f32[9,4096]{1,0:T(8,128)S(1)} fusion(f32[2,9,4096]{2,0,1:T(2,128)} %param.7), kind=kLoop, calls=%fused_computation.122 | loop fusion | flops 110592 | bytes 442368 | tf_op jit(solution)/shard_map/reduce_sum | solution.py:130
  2.9 0.2 select_bitcast_fusion.11
  3.2 0.7 fusion.67
  4.2 3.1 %collective-permute-start = (f32[9,512]{1,0:T(8,128)S(1)}, f32[9,512]{1,0:T(8,128)S(1)}, u32[]{:S(2)}, u32[]{:S(2)}) collective-permute-start(f32[9,512]{1,0:T(8,128)S(1)} %reshape.1029), channel_id=1, source_target_pairs={{0,4},{4,0},{8,12},{12,8},{1,5},{5,1},{9,13},{13,9},{2,6},{6,2},{1... | collective-permute-start | bytes 55304 | tf_op jit(solution)/shard_map/ppermute | solution.py:114
  7.3 0.2 multiply_reduce_fusion.23
  8.1 0.4 broadcast_select_fusion.2
  8.6 1.6 %fusion = f32[128,192]{0,1:T(8,128)S(1)} fusion(bf16[192,4096]{1,0:T(8,128)(2,1)S(1)} %bitcast.207, bf16[192,4096]{1,0:T(8,128)(2,1)S(1)} %bitcast.206, bf16[192,4096]{1,0:T(8,128)(2,1)S(1)} %bitcast.205, bf16[128,4096]{1,0:T(8,128)(2,1)S(1)} %fusion.27), kind=kOutput, calls=%fused_computation | convolution fusion | flops 627572736 | bytes 5865472 | tf_op jit(solution)/shard_map/dot_general | solution.py:46
  10.6 1.6 %collective-permute-start.6 = (f32[6,4096]{1,0:T(8,128)S(1)}, f32[6,4096]{1,0:T(8,128)S(1)}, u32[]{:S(2)}, u32[]{:S(2)}) collective-permute-start(f32[6,4096]{1,0:T(8,128)S(1)} %reshape.1039), channel_id=1, source_target_pairs={{0,2},{1,3},{2,0},{3,1},{4,6},{5,7},{6,4},{7,5},{8,10},{9,11},{10,... | collective-permute-start | bytes 294920 | tf_op jit(solution)/shard_map/ppermute | solution.py:107
  12.2 0.3 collective-permute-start.7
  12.5 2.7 %collective-permute-start.1 = (f32[9,512]{1,0:T(8,128)S(1)}, f32[9,512]{1,0:T(8,128)S(1)}, u32[]{:S(2)}, u32[]{:S(2)}) collective-permute-start(f32[9,512]{1,0:T(8,128)S(1)} %add.147), channel_id=1, source_target_pairs={{0,8},{4,12},{8,0},{12,4},{1,9},{5,13},{9,1},{13,5},{2,10},{6,14},... | collective-permute-start | bytes 55304 | tf_op jit(solution)/shard_map/ppermute | solution.py:114
  15.1 2.5 %collective-permute-done.1 = f32[9,512]{1,0:T(8,128)S(1)} collective-permute-done((f32[9,512]{1,0:T(8,128)S(1)}, f32[9,512]{1,0:T(8,128)S(1)}, u32[]{:S(2)}, u32[]{:S(2)}) %collective-permute-start.1) | collective-permute-done | bytes 18464 | tf_op jit(solution)/shard_map/ppermute | solution.py:114
  18.0 0.6 fusion.57
  18.6 0.4 copy-done
  19.4 0.2 broadcast_select_fusion.11
  19.6 1.1 %fusion.9 = f32[128,96]{0,1:T(8,128)S(1)} fusion(bf16[96,4096]{1,0:T(8,128)(2,1)S(1)} %bitcast.217, bf16[96,4096]{1,0:T(8,128)(2,1)S(1)} %bitcast.216, bf16[96,4096]{1,0:T(8,128)(2,1)S(1)} %bitcast.215, bf16[128,4096]{1,0:T(8,128)(2,1)S(1)} %fusion.27), kind=kOutput, calls=%fused_computation.14 | convolution fusion | flops 318504960 | bytes 3457024 | tf_op jit(solution)/shard_map/dot_general | solution.py:46
  21.2 1.6 %collective-permute-start.3 = (f32[4,4096]{1,0:T(4,128)S(1)}, f32[4,4096]{1,0:T(4,128)S(1)}, u32[]{:S(2)}, u32[]{:S(2)}) collective-permute-start(f32[4,4096]{1,0:T(4,128)S(1)} %pad_maximum_fusion.18), channel_id=1, source_target_pairs={{0,2},{1,3},{2,0},{3,1},{4,6},{5,7},{6,4},{7,5},{8,10},{9,11},{10,... | collective-permute-start | bytes 196616 | tf_op jit(solution)/shard_map/ppermute | solution.py:107
  22.8 0.2 collective-permute-start.4
  23.9 1.9 %collective-permute-done.3 = f32[4,4096]{1,0:T(4,128)S(1)} collective-permute-done((f32[4,4096]{1,0:T(4,128)S(1)}, f32[4,4096]{1,0:T(4,128)S(1)}, u32[]{:S(2)}, u32[]{:S(2)}) %collective-permute-start.3) | collective-permute-done | bytes 65568 | tf_op jit(solution)/shard_map/ppermute | solution.py:107
  25.7 1.2 %collective-permute-done.4 = f32[4,4096]{1,0:T(4,128)S(1)} collective-permute-done((f32[4,4096]{1,0:T(4,128)S(1)}, f32[4,4096]{1,0:T(4,128)S(1)}, u32[]{:S(2)}, u32[]{:S(2)}) %collective-permute-start.4) | collective-permute-done | bytes 65568 | tf_op jit(solution)/shard_map/ppermute | solution.py:107
  27.5 0.7 fusion.54
  28.2 0.2 select_reduce_fusion.2
  28.5 0.4 multiply_reduce_fusion.4
  29.0 0.2 select_bitcast_fusion.8
  29.2 0.7 fusion.64
  30.7 3.6 %collective-permute-done.8 = f32[10,512]{1,0:T(8,128)S(1)} collective-permute-done((f32[10,512]{1,0:T(8,128)S(1)}, f32[10,512]{1,0:T(8,128)S(1)}, u32[]{:S(2)}, u32[]{:S(2)}) %collective-permute-start.8) | collective-permute-done | bytes 20512 | tf_op jit(solution)/shard_map/ppermute | solution.py:114
  34.4 2.3 %collective-permute-start.9 = (f32[10,512]{1,0:T(8,128)S(1)}, f32[10,512]{1,0:T(8,128)S(1)}, u32[]{:S(2)}, u32[]{:S(2)}) collective-permute-start(f32[10,512]{1,0:T(8,128)S(1)} %fusion.151), channel_id=1, source_target_pairs={{0,8},{4,12},{8,0},{12,4},{1,9},{5,13},{9,1},{13,5},{2,10},{6,14},... | collective-permute-start | bytes 61448 | tf_op jit(solution)/shard_map/ppermute | solution.py:114
  36.7 0.6 fusion.148
  37.3 2.0 %collective-permute-done.9 = f32[10,512]{1,0:T(8,128)S(1)} collective-permute-done((f32[10,512]{1,0:T(8,128)S(1)}, f32[10,512]{1,0:T(8,128)S(1)}, u32[]{:S(2)}, u32[]{:S(2)}) %collective-permute-start.9) | collective-permute-done | bytes 20512 | tf_op jit(solution)/shard_map/ppermute | solution.py:114
  39.2 0.7 slice_reduce_fusion.5
  42.3 0.6 fusion.56
  42.9 0.3 multiply_reduce_fusion.3
  43.7 1.1 %fusion.15 = f32[128,96]{0,1:T(8,128)S(1)} fusion(bf16[96,4096]{1,0:T(8,128)(2,1)S(1)} %bitcast.220, bf16[96,4096]{1,0:T(8,128)(2,1)S(1)} %bitcast.219, bf16[96,4096]{1,0:T(8,128)(2,1)S(1)} %bitcast.218, bf16[128,4096]{1,0:T(8,128)(2,1)S(1)} %fusion.27), kind=kOutput, calls=%fused_computation.20 | convolution fusion | flops 318504960 | bytes 3457024 | tf_op jit(solution)/shard_map/dot_general | solution.py:46
  45.3 1.3 %collective-permute-start.11 = (f32[4,4096]{1,0:T(4,128)S(1)}, f32[4,4096]{1,0:T(4,128)S(1)}, u32[]{:S(2)}, u32[]{:S(2)}) collective-permute-start(f32[4,4096]{1,0:T(4,128)S(1)} %pad_maximum_fusion.19), channel_id=1, source_target_pairs={{0,2},{1,3},{2,0},{3,1},{4,6},{5,7},{6,4},{7,5},{8,10},{9,11},{10,... | collective-permute-start | bytes 196616 | tf_op jit(solution)/shard_map/ppermute | solution.py:107
  46.6 0.6 collective-permute-start.12
  47.2 2.9 %collective-permute-done.11 = f32[4,4096]{1,0:T(4,128)S(1)} collective-permute-done((f32[4,4096]{1,0:T(4,128)S(1)}, f32[4,4096]{1,0:T(4,128)S(1)}, u32[]{:S(2)}, u32[]{:S(2)}) %collective-permute-start.11) | collective-permute-done | bytes 65568 | tf_op jit(solution)/shard_map/ppermute | solution.py:107
  50.0 1.0 %collective-permute-done.12 = f32[4,4096]{1,0:T(4,128)S(1)} collective-permute-done((f32[4,4096]{1,0:T(4,128)S(1)}, f32[4,4096]{1,0:T(4,128)S(1)}, u32[]{:S(2)}, u32[]{:S(2)}) %collective-permute-start.12) | collective-permute-done | bytes 65568 | tf_op jit(solution)/shard_map/ppermute | solution.py:107
  51.5 0.7 fusion.53
  52.3 0.3 select_reduce_fusion.1
  52.6 0.4 multiply_reduce_fusion.2
  53.1 0.2 select_bitcast_fusion.5
  53.3 0.7 fusion.61
  54.8 3.6 %collective-permute-done.13 = f32[10,512]{1,0:T(8,128)S(1)} collective-permute-done((f32[10,512]{1,0:T(8,128)S(1)}, f32[10,512]{1,0:T(8,128)S(1)}, u32[]{:S(2)}, u32[]{:S(2)}) %collective-permute-start.13) | collective-permute-done | bytes 20512 | tf_op jit(solution)/shard_map/ppermute | solution.py:114
  58.4 2.3 %collective-permute-start.14 = (f32[10,512]{1,0:T(8,128)S(1)}, f32[10,512]{1,0:T(8,128)S(1)}, u32[]{:S(2)}, u32[]{:S(2)}) collective-permute-start(f32[10,512]{1,0:T(8,128)S(1)} %fusion.150), channel_id=1, source_target_pairs={{0,8},{4,12},{8,0},{12,4},{1,9},{5,13},{9,1},{13,5},{2,10},{6,14},... | collective-permute-start | bytes 61448 | tf_op jit(solution)/shard_map/ppermute | solution.py:114
  60.8 0.6 fusion.147
  63.4 0.6 slice_reduce_fusion.4
  66.3 0.6 fusion.55
  67.5 1.1 %fusion.21 = f32[128,96]{0,1:T(8,128)S(1)} fusion(bf16[96,4096]{1,0:T(8,128)(2,1)S(1)} %bitcast.223, bf16[96,4096]{1,0:T(8,128)(2,1)S(1)} %bitcast.222, bf16[96,4096]{1,0:T(8,128)(2,1)S(1)} %bitcast.221, bf16[128,4096]{1,0:T(8,128)(2,1)S(1)} %fusion.27), kind=kOutput, calls=%fused_computation.26 | convolution fusion | flops 318504960 | bytes 3457024 | tf_op jit(solution)/shard_map/dot_general | solution.py:46
  69.1 1.0 %collective-permute-start.16 = (f32[4,4096]{1,0:T(4,128)S(1)}, f32[4,4096]{1,0:T(4,128)S(1)}, u32[]{:S(2)}, u32[]{:S(2)}) collective-permute-start(f32[4,4096]{1,0:T(4,128)S(1)} %pad_maximum_fusion.20), channel_id=1, source_target_pairs={{0,2},{1,3},{2,0},{3,1},{4,6},{5,7},{6,4},{7,5},{8,10},{9,11},{10,... | collective-permute-start | bytes 196616 | tf_op jit(solution)/shard_map/ppermute | solution.py:107
  70.1 0.9 collective-permute-start.17
  71.0 3.2 %collective-permute-done.16 = f32[4,4096]{1,0:T(4,128)S(1)} collective-permute-done((f32[4,4096]{1,0:T(4,128)S(1)}, f32[4,4096]{1,0:T(4,128)S(1)}, u32[]{:S(2)}, u32[]{:S(2)}) %collective-permute-start.16) | collective-permute-done | bytes 65568 | tf_op jit(solution)/shard_map/ppermute | solution.py:107
  74.1 0.3 collective-permute-done.17
  75.0 0.7 fusion.52
  75.7 0.2 select_reduce_fusion
  76.0 0.4 multiply_reduce_fusion
  76.5 0.2 select_bitcast_fusion.2
  76.8 0.7 fusion.58
  77.8 0.5 collective-permute-start.18
  78.5 3.3 %collective-permute-done.18 = f32[10,512]{1,0:T(8,128)S(1)} collective-permute-done((f32[10,512]{1,0:T(8,128)S(1)}, f32[10,512]{1,0:T(8,128)S(1)}, u32[]{:S(2)}, u32[]{:S(2)}) %collective-permute-start.18) | collective-permute-done | bytes 20512 | tf_op jit(solution)/shard_map/ppermute | solution.py:114
  81.8 2.3 %collective-permute-start.19 = (f32[10,512]{1,0:T(8,128)S(1)}, f32[10,512]{1,0:T(8,128)S(1)}, u32[]{:S(2)}, u32[]{:S(2)}) collective-permute-start(f32[10,512]{1,0:T(8,128)S(1)} %fusion.149), channel_id=1, source_target_pairs={{0,8},{4,12},{8,0},{12,4},{1,9},{5,13},{9,1},{13,5},{2,10},{6,14},... | collective-permute-start | bytes 61448 | tf_op jit(solution)/shard_map/ppermute | solution.py:114
  84.1 0.6 fusion.146
  86.6 0.3 collective-permute-done.19
  86.9 0.6 slice_reduce_fusion.3
  89.5 0.7 fusion.121
  (159 shorter events, 10.0 us)
Async XLA Ops:
  3.2 4.1 %copy-start.1 = (f32[2,3,4096]{2,0,1:T(2,128)S(1)}, f32[2,3,4096]{2,0,1:T(2,128)}, u32[]{:S(2)}) copy-start(f32[2,3,4096]{2,0,1:T(2,128)} %param.8) | copy-start | bytes 294916
  3.2 4.6 %copy-start.4 = (s32[4096]{0:T(1024)S(1)}, s32[4096]{0:T(1024)}, u32[]{:S(2)}) copy-start(s32[4096]{0:T(1024)} %param.10) | copy-start | bytes 49156
  4.2 8.3 %collective-permute-start = (f32[9,512]{1,0:T(8,128)S(1)}, f32[9,512]{1,0:T(8,128)S(1)}, u32[]{:S(2)}, u32[]{:S(2)}) collective-permute-start(f32[9,512]{1,0:T(8,128)S(1)} %reshape.1029), channel_id=1, source_target_pairs={{0,4},{4,0},{8,12},{12,8},{1,5},{5,1},{9,13},{13,9},{2,6},{6,2},{1... | collective-permute-start | bytes 55304 | tf_op jit(solution)/shard_map/ppermute | solution.py:114
  8.5 9.1 %copy-start.2 = (f32[9,512]{1,0:T(8,128)S(1)}, f32[9,512]{1,0:T(8,128)}, u32[]{:S(2)}) copy-start(f32[9,512]{1,0:T(8,128)} %param.13) | copy-start | bytes 55300
  8.5 9.1 %copy-start.3 = (f32[512]{0:T(512)S(1)}, f32[512]{0:T(512)}, u32[]{:S(2)}) copy-start(f32[512]{0:T(512)} %param.12) | copy-start | bytes 6148
  10.5 12.3 %collective-permute-start.5 = (f32[6,4096]{1,0:T(8,128)S(1)}, f32[6,4096]{1,0:T(8,128)S(1)}, u32[]{:S(2)}, u32[]{:S(2)}) collective-permute-start(f32[6,4096]{1,0:T(8,128)S(1)} %reshape.1039), channel_id=1, source_target_pairs={{0,1},{1,0},{2,3},{3,2},{4,5},{5,4},{6,7},{7,6},{8,9},{9,8},{10,11... | collective-permute-start | bytes 294920 | tf_op jit(solution)/shard_map/ppermute | solution.py:107
  10.6 12.5 %collective-permute-start.6 = (f32[6,4096]{1,0:T(8,128)S(1)}, f32[6,4096]{1,0:T(8,128)S(1)}, u32[]{:S(2)}, u32[]{:S(2)}) collective-permute-start(f32[6,4096]{1,0:T(8,128)S(1)} %reshape.1039), channel_id=1, source_target_pairs={{0,2},{1,3},{2,0},{3,1},{4,6},{5,7},{6,4},{7,5},{8,10},{9,11},{10,... | collective-permute-start | bytes 294920 | tf_op jit(solution)/shard_map/ppermute | solution.py:107
  12.2 10.9 %collective-permute-start.7 = (f32[6,4096]{1,0:T(8,128)S(1)}, f32[6,4096]{1,0:T(8,128)S(1)}, u32[]{:S(2)}, u32[]{:S(2)}) collective-permute-start(f32[6,4096]{1,0:T(8,128)S(1)} %reshape.1039), channel_id=1, source_target_pairs={{0,3},{1,2},{2,1},{3,0},{4,7},{5,6},{6,5},{7,4},{8,11},{9,10},{10,... | collective-permute-start | bytes 294920 | tf_op jit(solution)/shard_map/ppermute | solution.py:107
  12.5 5.2 %collective-permute-start.1 = (f32[9,512]{1,0:T(8,128)S(1)}, f32[9,512]{1,0:T(8,128)S(1)}, u32[]{:S(2)}, u32[]{:S(2)}) collective-permute-start(f32[9,512]{1,0:T(8,128)S(1)} %add.147), channel_id=1, source_target_pairs={{0,8},{4,12},{8,0},{12,4},{1,9},{5,13},{9,1},{13,5},{2,10},{6,14},... | collective-permute-start | bytes 55304 | tf_op jit(solution)/shard_map/ppermute | solution.py:114
  18.0 1.0 %copy-start = (f32[2,9,4096]{2,0,1:T(2,128)S(1)}, f32[2,9,4096]{2,0,1:T(2,128)}, u32[]{:S(2)}) copy-start(f32[2,9,4096]{2,0,1:T(2,128)} %param.7) | copy-start | bytes 884740
  20.7 2.6 %copy-start.5 = (f32[4096]{0:T(1024)S(1)}, f32[4096]{0:T(1024)}, u32[]{:S(2)}) copy-start(f32[4096]{0:T(1024)} %param.11) | copy-start | bytes 49156
  21.2 2.7 %collective-permute-start.2 = (f32[4,4096]{1,0:T(4,128)S(1)}, f32[4,4096]{1,0:T(4,128)S(1)}, u32[]{:S(2)}, u32[]{:S(2)}) collective-permute-start(f32[4,4096]{1,0:T(4,128)S(1)} %pad_maximum_fusion.18), channel_id=1, source_target_pairs={{0,1},{1,0},{2,3},{3,2},{4,5},{5,4},{6,7},{7,6},{8,9},{9,8},{10,11... | collective-permute-start | bytes 196616 | tf_op jit(solution)/shard_map/ppermute | solution.py:107
  21.2 4.5 %collective-permute-start.3 = (f32[4,4096]{1,0:T(4,128)S(1)}, f32[4,4096]{1,0:T(4,128)S(1)}, u32[]{:S(2)}, u32[]{:S(2)}) collective-permute-start(f32[4,4096]{1,0:T(4,128)S(1)} %pad_maximum_fusion.18), channel_id=1, source_target_pairs={{0,2},{1,3},{2,0},{3,1},{4,6},{5,7},{6,4},{7,5},{8,10},{9,11},{10,... | collective-permute-start | bytes 196616 | tf_op jit(solution)/shard_map/ppermute | solution.py:107
  22.8 4.1 %collective-permute-start.4 = (f32[4,4096]{1,0:T(4,128)S(1)}, f32[4,4096]{1,0:T(4,128)S(1)}, u32[]{:S(2)}, u32[]{:S(2)}) collective-permute-start(f32[4,4096]{1,0:T(4,128)S(1)} %pad_maximum_fusion.18), channel_id=1, source_target_pairs={{0,3},{1,2},{2,1},{3,0},{4,7},{5,6},{6,5},{7,4},{8,11},{9,10},{10,... | collective-permute-start | bytes 196616 | tf_op jit(solution)/shard_map/ppermute | solution.py:107
  30.4 4.0 %collective-permute-start.8 = (f32[10,512]{1,0:T(8,128)S(1)}, f32[10,512]{1,0:T(8,128)S(1)}, u32[]{:S(2)}, u32[]{:S(2)}) collective-permute-start(f32[10,512]{1,0:T(8,128)S(1)} %pad_maximum_fusion.21), channel_id=1, source_target_pairs={{0,4},{4,0},{8,12},{12,8},{1,5},{5,1},{9,13},{13,9},{2,6},{6,2},{1... | collective-permute-start | bytes 61448 | tf_op jit(solution)/shard_map/ppermute | solution.py:114
  34.4 4.9 %collective-permute-start.9 = (f32[10,512]{1,0:T(8,128)S(1)}, f32[10,512]{1,0:T(8,128)S(1)}, u32[]{:S(2)}, u32[]{:S(2)}) collective-permute-start(f32[10,512]{1,0:T(8,128)S(1)} %fusion.151), channel_id=1, source_target_pairs={{0,8},{4,12},{8,0},{12,4},{1,9},{5,13},{9,1},{13,5},{2,10},{6,14},... | collective-permute-start | bytes 61448 | tf_op jit(solution)/shard_map/ppermute | solution.py:114
  45.3 1.9 %collective-permute-start.10 = (f32[4,4096]{1,0:T(4,128)S(1)}, f32[4,4096]{1,0:T(4,128)S(1)}, u32[]{:S(2)}, u32[]{:S(2)}) collective-permute-start(f32[4,4096]{1,0:T(4,128)S(1)} %pad_maximum_fusion.19), channel_id=1, source_target_pairs={{0,1},{1,0},{2,3},{3,2},{4,5},{5,4},{6,7},{7,6},{8,9},{9,8},{10,11... | collective-permute-start | bytes 196616 | tf_op jit(solution)/shard_map/ppermute | solution.py:107
  45.3 4.7 %collective-permute-start.11 = (f32[4,4096]{1,0:T(4,128)S(1)}, f32[4,4096]{1,0:T(4,128)S(1)}, u32[]{:S(2)}, u32[]{:S(2)}) collective-permute-start(f32[4,4096]{1,0:T(4,128)S(1)} %pad_maximum_fusion.19), channel_id=1, source_target_pairs={{0,2},{1,3},{2,0},{3,1},{4,6},{5,7},{6,4},{7,5},{8,10},{9,11},{10,... | collective-permute-start | bytes 196616 | tf_op jit(solution)/shard_map/ppermute | solution.py:107
  46.6 4.4 %collective-permute-start.12 = (f32[4,4096]{1,0:T(4,128)S(1)}, f32[4,4096]{1,0:T(4,128)S(1)}, u32[]{:S(2)}, u32[]{:S(2)}) collective-permute-start(f32[4,4096]{1,0:T(4,128)S(1)} %pad_maximum_fusion.19), channel_id=1, source_target_pairs={{0,3},{1,2},{2,1},{3,0},{4,7},{5,6},{6,5},{7,4},{8,11},{9,10},{10,... | collective-permute-start | bytes 196616 | tf_op jit(solution)/shard_map/ppermute | solution.py:107
  54.4 4.0 %collective-permute-start.13 = (f32[10,512]{1,0:T(8,128)S(1)}, f32[10,512]{1,0:T(8,128)S(1)}, u32[]{:S(2)}, u32[]{:S(2)}) collective-permute-start(f32[10,512]{1,0:T(8,128)S(1)} %pad_maximum_fusion.22), channel_id=1, source_target_pairs={{0,4},{4,0},{8,12},{12,8},{1,5},{5,1},{9,13},{13,9},{2,6},{6,2},{1... | collective-permute-start | bytes 61448 | tf_op jit(solution)/shard_map/ppermute | solution.py:114
  58.4 4.9 %collective-permute-start.14 = (f32[10,512]{1,0:T(8,128)S(1)}, f32[10,512]{1,0:T(8,128)S(1)}, u32[]{:S(2)}, u32[]{:S(2)}) collective-permute-start(f32[10,512]{1,0:T(8,128)S(1)} %fusion.150), channel_id=1, source_target_pairs={{0,8},{4,12},{8,0},{12,4},{1,9},{5,13},{9,1},{13,5},{2,10},{6,14},... | collective-permute-start | bytes 61448 | tf_op jit(solution)/shard_map/ppermute | solution.py:114
  69.0 1.9 %collective-permute-start.15 = (f32[4,4096]{1,0:T(4,128)S(1)}, f32[4,4096]{1,0:T(4,128)S(1)}, u32[]{:S(2)}, u32[]{:S(2)}) collective-permute-start(f32[4,4096]{1,0:T(4,128)S(1)} %pad_maximum_fusion.20), channel_id=1, source_target_pairs={{0,1},{1,0},{2,3},{3,2},{4,5},{5,4},{6,7},{7,6},{8,9},{9,8},{10,11... | collective-permute-start | bytes 196616 | tf_op jit(solution)/shard_map/ppermute | solution.py:107
  69.1 5.0 %collective-permute-start.16 = (f32[4,4096]{1,0:T(4,128)S(1)}, f32[4,4096]{1,0:T(4,128)S(1)}, u32[]{:S(2)}, u32[]{:S(2)}) collective-permute-start(f32[4,4096]{1,0:T(4,128)S(1)} %pad_maximum_fusion.20), channel_id=1, source_target_pairs={{0,2},{1,3},{2,0},{3,1},{4,6},{5,7},{6,4},{7,5},{8,10},{9,11},{10,... | collective-permute-start | bytes 196616 | tf_op jit(solution)/shard_map/ppermute | solution.py:107
  70.1 4.4 %collective-permute-start.17 = (f32[4,4096]{1,0:T(4,128)S(1)}, f32[4,4096]{1,0:T(4,128)S(1)}, u32[]{:S(2)}, u32[]{:S(2)}) collective-permute-start(f32[4,4096]{1,0:T(4,128)S(1)} %pad_maximum_fusion.20), channel_id=1, source_target_pairs={{0,3},{1,2},{2,1},{3,0},{4,7},{5,6},{6,5},{7,4},{8,11},{9,10},{10,... | collective-permute-start | bytes 196616 | tf_op jit(solution)/shard_map/ppermute | solution.py:107
  77.8 4.0 %collective-permute-start.18 = (f32[10,512]{1,0:T(8,128)S(1)}, f32[10,512]{1,0:T(8,128)S(1)}, u32[]{:S(2)}, u32[]{:S(2)}) collective-permute-start(f32[10,512]{1,0:T(8,128)S(1)} %pad_maximum_fusion.23), channel_id=1, source_target_pairs={{0,4},{4,0},{8,12},{12,8},{1,5},{5,1},{9,13},{13,9},{2,6},{6,2},{1... | collective-permute-start | bytes 61448 | tf_op jit(solution)/shard_map/ppermute | solution.py:114
  81.8 5.1 %collective-permute-start.19 = (f32[10,512]{1,0:T(8,128)S(1)}, f32[10,512]{1,0:T(8,128)S(1)}, u32[]{:S(2)}, u32[]{:S(2)}) collective-permute-start(f32[10,512]{1,0:T(8,128)S(1)} %fusion.149), channel_id=1, source_target_pairs={{0,8},{4,12},{8,0},{12,4},{1,9},{5,13},{9,1},{13,5},{2,10},{6,14},... | collective-permute-start | bytes 61448 | tf_op jit(solution)/shard_map/ppermute | solution.py:114

commit v13 on v12

--- a/solution.py
+++ b/solution.py
@@ -10,7 +10,7 @@
 
 
 def split_of(count):
-    lo = 1 << max((count.bit_length() - 1) // 2 - 1, 0)
+    lo = 1 << max((count.bit_length() - 1) // 2 - 2, 0)
     while count % lo:
         lo //= 2
     return count // lo, lo

time: 90.5 us -> 128 us (1.41)
  matrix products: 11.6 us -> 31.9 us
  local copies, waits for them, and re-layouts: 6.67 us -> 18.2 us
  other arithmetic: 13.5 us -> 20.1 us
    dot_general x6, matrix products: 3.9 us -> 14.2 us  [gather(): lax.dot_general(stacked, self.hot3t, (((1,), (0,)), ((), ())), preferred_...]
    dot_general x8, matrix products: 7.72 us -> 17.7 us  [segsum(): lax.dot_general(self.hot3, spread, (((1,), (1,)), ((), ())), preferred_el...]
    select_n x0 -> x12, local copies, waits for them, and re-layouts: none -> 7.18 us  [segsum(): jnp.where(self.low[None], part[:, None, :], jnp.zeros((), BF))]
    reshape x0 -> x3, local copies, waits for them, and re-layouts: none -> 3.81 us  [gather(): spread = lax.dot_general(stacked, self.hot3t, (((1,), (0,)), ((), ())), p...]
    select_n x8, other arithmetic: 2.11 us -> 3.99 us  [segsum(): jnp.where(self.low[None], part[:, None, :], jnp.zeros((), BF))]
    reduce_sum x6, other arithmetic: 0.19 us -> 1.94 us  [lanes(): return jnp.sum(terms.reshape(-1, ncam), axis=0)]
    reshape x12 -> x20, local copies, waits for them, and re-layouts: 1.92 us -> 3.02 us  [segsum(): out.reshape(self.hi, ncol, self.lo).transpose(1, 0, 2)]
  transfers between devices with their start and end apart: 20 -> 20, of which waited for: 12 -> 13; matrix products, arithmetic and copies ran while one was open for 10% -> 13% of each run, Pallas kernels for 0% -> 0%
where the time goes in v13:
time: 128 us; the launch traced here: 127 us
  matrix products  31.9 us (25%)
  waiting for transfers between devices  24.6 us (19%)
  starting transfers between devices  21.2 us (17%)
  other arithmetic  20.1 us (16%)
  local copies, waits for them, and re-layouts  18.2 us (14%)
  between operations  11.4 us (9%)
    dot_general x8, matrix products, segsum(): lax.dot_general(self.hot3, spread, (((1,), (1,)), ((), ())), preferred_el...  17.7 us
    ppermute x8, waiting for transfers between devices, allsum(): lax.ppermute(value, axis, [(i, i ^ step) for i in range(size)])  15.2 us
    dot_general x6, matrix products, gather(): lax.dot_general(stacked, self.hot3t, (((1,), (0,)), ((), ())), preferred_...  14.2 us
    ppermute x8, starting transfers between devices, allsum(): lax.ppermute(value, axis, [(i, i ^ step) for i in range(size)])  13.5 us
    ppermute x12, waiting for transfers between devices, allsum(): lax.ppermute(value, axis, [(i, i ^ mask) for i in range(size)])  9.36 us
    ppermute x12, starting transfers between devices, allsum(): lax.ppermute(value, axis, [(i, i ^ mask) for i in range(size)])  7.68 us
    select_n x12, local copies, waits for them, and re-layouts, segsum(): jnp.where(self.low[None], part[:, None, :], jnp.zeros((), BF))  7.18 us
    select_n x8, other arithmetic, segsum(): jnp.where(self.low[None], part[:, None, :], jnp.zeros((), BF))  3.99 us
  transfers between devices with their start and end apart: 20, of which 13 were waited for; matrix products, arithmetic and copies ran while one was open for 13% of the time, Pallas kernels for 0%

profile of v13, /device:TPU:0, one launch (start us, length us, event | category | flops | bytes accessed | tf_op | source)
XLA Modules:
  0.0 127.4 jit_solution(15799570430845765355)
XLA Ops:
  0.6 0.7 add_select_fusion
  1.4 1.4 %multiply_reduce_fusion.6 = f32[9,4096]{1,0:T(8,128)S(1)} fusion(f32[2,9,4096]{2,0,1:T(2,128)} %param.7), kind=kLoop, calls=%fused_computation.102 | loop fusion | flops 110592 | bytes 442368 | tf_op jit(solution)/shard_map/reduce_sum | solution.py:130
  2.8 0.5 broadcast_select_fusion.23
  3.8 1.2 fusion.32
  5.3 3.1 %collective-permute-start = (f32[9,512]{1,0:T(8,128)S(1)}, f32[9,512]{1,0:T(8,128)S(1)}, u32[]{:S(2)}, u32[]{:S(2)}) collective-permute-start(f32[9,512]{1,0:T(8,128)S(1)} %copy.130), channel_id=1, source_target_pairs={{0,4},{4,0},{8,12},{12,8},{1,5},{5,1},{9,13},{13,9},{2,6},{6,2},{1... | collective-permute-start | bytes 55304 | tf_op jit(solution)/shard_map/ppermute | solution.py:114
  8.9 0.4 fusion
  9.7 2.2 %fusion.4 = f32[256,96]{0,1:T(8,128)S(1)} fusion(bf16[96,4096]{1,0:T(8,128)(2,1)S(1)} %bitcast.171, bf16[96,4096]{1,0:T(8,128)(2,1)S(1)} %bitcast.170, bf16[96,4096]{1,0:T(8,128)(2,1)S(1)} %bitcast.169, bf16[256,4096]{1,0:T(8,128)(2,1)S(1)} %fusion), kind=kOutput, calls=%fused_computation.9 | convolution fusion | flops 629932032 | bytes 4554752 | tf_op jit(solution)/shard_map/dot_general | solution.py:46
  12.1 0.4 reshape.1039
  12.6 1.6 %collective-permute-start.6 = (f32[6,4096]{1,0:T(8,128)S(1)}, f32[6,4096]{1,0:T(8,128)}, u32[]{:S(2)}, u32[]{:S(2)}) collective-permute-start(f32[6,4096]{1,0:T(8,128)S(1)} %reshape.1039), channel_id=1, source_target_pairs={{0,2},{1,3},{2,0},{3,1},{4,6},{5,7},{6,4},{7,5},{8,10},{9,11},{10,... | collective-permute-start | bytes 294920 | tf_op jit(solution)/shard_map/ppermute | solution.py:107
  14.4 2.7 %collective-permute-start.1 = (f32[9,512]{1,0:T(8,128)S(1)}, f32[9,512]{1,0:T(8,128)S(1)}, u32[]{:S(2)}, u32[]{:S(2)}) collective-permute-start(f32[9,512]{1,0:T(8,128)S(1)} %add.147), channel_id=1, source_target_pairs={{0,8},{4,12},{8,0},{12,4},{1,9},{5,13},{9,1},{13,5},{2,10},{6,14},... | collective-permute-start | bytes 55304 | tf_op jit(solution)/shard_map/ppermute | solution.py:114
  17.1 2.5 %collective-permute-done.1 = f32[9,512]{1,0:T(8,128)S(1)} collective-permute-done((f32[9,512]{1,0:T(8,128)S(1)}, f32[9,512]{1,0:T(8,128)S(1)}, u32[]{:S(2)}, u32[]{:S(2)}) %collective-permute-start.1) | collective-permute-done | bytes 18464 | tf_op jit(solution)/shard_map/ppermute | solution.py:114
  19.9 3.6 %fusion.13 = f32[36,4096]{1,0:T(8,128)} fusion(bf16[128,4096]{1,0:T(8,128)(2,1)} %copy-done.2, bf16[36,128]{1,0:T(8,128)(2,1)S(1)} %get-tuple-element.101, bf16[36,128]{1,0:T(8,128)(2,1)S(1)} %get-tuple-element.102, bf16[36,128]{1,0:T(8,128)(2,1)S(1)} %get-tuple-element.100), kind=kOutput, calls=%fused_computation.19 | convolution fusion | flops 122766336 | bytes 1666048 | tf_op jit(solution)/shard_map/dot_general | solution.py:55
  23.5 1.3 %reshape.1032 = f32[9,4,4096]{2,1,0:T(4,128)S(1)} reshape(f32[36,4096]{1,0:T(8,128)} %fusion.13) | data formatting | bytes 1179648 | tf_op jit(solution)/shard_map/reshape | solution.py:57
  25.8 2.0 %fusion.16 = f32[256,48]{0,1:T(8,128)S(1)} fusion(bf16[256,4096]{1,0:T(8,128)(2,1)S(1)} %fusion, bf16[48,4096]{1,0:T(8,128)(2,1)S(1)} %bitcast.177, bf16[48,4096]{1,0:T(8,128)(2,1)S(1)} %bitcast.176, bf16[48,4096]{1,0:T(8,128)(2,1)S(1)} %bitcast.175), kind=kOutput, calls=%fused_computation.22 | convolution fusion | flops 324403200 | bytes 3325952 | tf_op jit(solution)/shard_map/dot_general | solution.py:46
  28.4 1.6 %collective-permute-start.3 = (f32[4,4096]{1,0:T(4,128)S(1)}, f32[4,4096]{1,0:T(4,128)S(1)}, u32[]{:S(2)}, u32[]{:S(2)}) collective-permute-start(f32[4,4096]{1,0:T(4,128)S(1)} %pad_maximum_fusion.18), channel_id=1, source_target_pairs={{0,2},{1,3},{2,0},{3,1},{4,6},{5,7},{6,4},{7,5},{8,10},{9,11},{10,... | collective-permute-start | bytes 196616 | tf_op jit(solution)/shard_map/ppermute | solution.py:107
  30.3 1.1 add_add_fusion
  32.1 0.8 collective-permute-done.3
  32.9 1.2 collective-permute-done.4
  34.7 1.2 fusion.3
  36.9 1.2 broadcast_select_fusion.20
  38.0 1.8 %select_n.235 = bf16[36,4096]{1,0:T(8,128)(2,1)} reshape(bf16[9,4,4096]{2,1,0:T(4,128)(2,1)} %get-tuple-element.109) | data formatting | bytes 589824 | tf_op jit(solution)/shard_map/jit(_where)/select_n | solution.py:42
  39.8 0.8 select_n.237
  40.6 0.8 select_n.239
  41.4 3.5 %fusion.38 = f32[128,36]{0,1:T(8,128)S(1)} fusion(bf16[36,4096]{1,0:T(8,128)(2,1)} %select_n.239, bf16[36,4096]{1,0:T(8,128)(2,1)} %select_n.237, bf16[36,4096]{1,0:T(8,128)(2,1)} %select_n.235, bf16[128,4096]{1,0:T(8,128)(2,1)} %copy-done.2), kind=kOutput, calls=%fused_computation.44 | convolution fusion | flops 125337600 | bytes 1951744 | tf_op jit(solution)/shard_map/dot_general | solution.py:46
  45.7 3.6 %collective-permute-done.8 = f32[10,512]{1,0:T(8,128)S(1)} collective-permute-done((f32[10,512]{1,0:T(8,128)S(1)}, f32[10,512]{1,0:T(8,128)S(1)}, u32[]{:S(2)}, u32[]{:S(2)}) %collective-permute-start.8) | collective-permute-done | bytes 20512 | tf_op jit(solution)/shard_map/ppermute | solution.py:114
  49.3 2.3 %collective-permute-start.9 = (f32[10,512]{1,0:T(8,128)S(1)}, f32[10,512]{1,0:T(8,128)S(1)}, u32[]{:S(2)}, u32[]{:S(2)}) collective-permute-start(f32[10,512]{1,0:T(8,128)S(1)} %fusion.136), channel_id=1, source_target_pairs={{0,8},{4,12},{8,0},{12,4},{1,9},{5,13},{9,1},{13,5},{2,10},{6,14},... | collective-permute-start | bytes 61448 | tf_op jit(solution)/shard_map/ppermute | solution.py:114
  51.6 0.6 fusion.133
  52.2 2.0 %collective-permute-done.9 = f32[10,512]{1,0:T(8,128)S(1)} collective-permute-done((f32[10,512]{1,0:T(8,128)S(1)}, f32[10,512]{1,0:T(8,128)S(1)}, u32[]{:S(2)}, u32[]{:S(2)}) %collective-permute-start.9) | collective-permute-done | bytes 20512 | tf_op jit(solution)/shard_map/ppermute | solution.py:114
  54.2 0.6 slice_reduce_fusion.5
  56.7 0.6 multiply_reduce_fusion.22
  57.6 3.6 %fusion.12 = f32[36,4096]{1,0:T(8,128)} fusion(bf16[128,4096]{1,0:T(8,128)(2,1)} %copy-done.2, bf16[36,128]{1,0:T(8,128)(2,1)S(1)} %get-tuple-element.98, bf16[36,128]{1,0:T(8,128)(2,1)S(1)} %get-tuple-element.99, bf16[36,128]{1,0:T(8,128)(2,1)S(1)} %get-tuple-element.97), kind=kOutput, calls=%fused_computation.18 | convolution fusion | flops 122766336 | bytes 1666048 | tf_op jit(solution)/shard_map/dot_general | solution.py:55
  61.2 1.3 reshape.1048
  63.4 2.0 %fusion.15 = f32[256,48]{0,1:T(8,128)S(1)} fusion(bf16[256,4096]{1,0:T(8,128)(2,1)S(1)} %fusion, bf16[48,4096]{1,0:T(8,128)(2,1)S(1)} %bitcast.180, bf16[48,4096]{1,0:T(8,128)(2,1)S(1)} %bitcast.179, bf16[48,4096]{1,0:T(8,128)(2,1)S(1)} %bitcast.178), kind=kOutput, calls=%fused_computation.21 | convolution fusion | flops 324403200 | bytes 3325952 | tf_op jit(solution)/shard_map/dot_general | solution.py:46
  66.0 1.3 %collective-permute-start.11 = (f32[4,4096]{1,0:T(4,128)S(1)}, f32[4,4096]{1,0:T(4,128)S(1)}, u32[]{:S(2)}, u32[]{:S(2)}) collective-permute-start(f32[4,4096]{1,0:T(4,128)S(1)} %pad_maximum_fusion.19), channel_id=1, source_target_pairs={{0,2},{1,3},{2,0},{3,1},{4,6},{5,7},{6,4},{7,5},{8,10},{9,11},{10,... | collective-permute-start | bytes 196616 | tf_op jit(solution)/shard_map/ppermute | solution.py:107
  67.3 0.6 collective-permute-start.12
  67.9 2.9 %collective-permute-done.11 = f32[4,4096]{1,0:T(4,128)S(1)} collective-permute-done((f32[4,4096]{1,0:T(4,128)S(1)}, f32[4,4096]{1,0:T(4,128)S(1)}, u32[]{:S(2)}, u32[]{:S(2)}) %collective-permute-start.11) | collective-permute-done | bytes 65568 | tf_op jit(solution)/shard_map/ppermute | solution.py:107
  70.7 1.0 collective-permute-done.12
  72.1 0.6 multiply_reduce_fusion.17
  72.9 1.2 fusion.2
  74.8 1.2 broadcast_select_fusion.17
  76.0 1.8 %select_n.249 = bf16[36,4096]{1,0:T(8,128)(2,1)} reshape(bf16[9,4,4096]{2,1,0:T(4,128)(2,1)} %get-tuple-element.106) | data formatting | bytes 589824 | tf_op jit(solution)/shard_map/jit(_where)/select_n | solution.py:42
  77.8 0.8 select_n.251
  78.6 0.8 select_n.253
  79.4 3.5 %fusion.44 = f32[128,36]{0,1:T(8,128)S(1)} fusion(bf16[36,4096]{1,0:T(8,128)(2,1)} %select_n.253, bf16[36,4096]{1,0:T(8,128)(2,1)} %select_n.251, bf16[36,4096]{1,0:T(8,128)(2,1)} %select_n.249, bf16[128,4096]{1,0:T(8,128)(2,1)} %copy-done.2), kind=kOutput, calls=%fused_computation.50 | convolution fusion | flops 125337600 | bytes 1951744 | tf_op jit(solution)/shard_map/dot_general | solution.py:46
  83.7 3.6 %collective-permute-done.13 = f32[10,512]{1,0:T(8,128)S(1)} collective-permute-done((f32[10,512]{1,0:T(8,128)S(1)}, f32[10,512]{1,0:T(8,128)S(1)}, u32[]{:S(2)}, u32[]{:S(2)}) %collective-permute-start.13) | collective-permute-done | bytes 20512 | tf_op jit(solution)/shard_map/ppermute | solution.py:114
  87.3 2.3 %collective-permute-start.14 = (f32[10,512]{1,0:T(8,128)S(1)}, f32[10,512]{1,0:T(8,128)S(1)}, u32[]{:S(2)}, u32[]{:S(2)}) collective-permute-start(f32[10,512]{1,0:T(8,128)S(1)} %fusion.135), channel_id=1, source_target_pairs={{0,8},{4,12},{8,0},{12,4},{1,9},{5,13},{9,1},{13,5},{2,10},{6,14},... | collective-permute-start | bytes 61448 | tf_op jit(solution)/shard_map/ppermute | solution.py:114
  89.6 0.6 fusion.132
  92.2 0.6 slice_reduce_fusion.4
  94.7 1.2 multiply_reduce_fusion.20
  96.2 3.6 %fusion.11 = f32[36,4096]{1,0:T(8,128)} fusion(bf16[128,4096]{1,0:T(8,128)(2,1)} %copy-done.2, bf16[36,128]{1,0:T(8,128)(2,1)S(1)} %get-tuple-element.95, bf16[36,128]{1,0:T(8,128)(2,1)S(1)} %get-tuple-element.96, bf16[36,128]{1,0:T(8,128)(2,1)S(1)} %get-tuple-element.94), kind=kOutput, calls=%fused_computation.17 | convolution fusion | flops 122766336 | bytes 1666048 | tf_op jit(solution)/shard_map/dot_general | solution.py:55
  99.8 1.3 reshape.1062
  102.2 2.0 %fusion.14 = f32[256,48]{0,1:T(8,128)S(1)} fusion(bf16[256,4096]{1,0:T(8,128)(2,1)S(1)} %fusion, bf16[48,4096]{1,0:T(8,128)(2,1)S(1)} %bitcast.183, bf16[48,4096]{1,0:T(8,128)(2,1)S(1)} %bitcast.182, bf16[48,4096]{1,0:T(8,128)(2,1)S(1)} %bitcast.181), kind=kOutput, calls=%fused_computation.20 | convolution fusion | flops 324403200 | bytes 3325952 | tf_op jit(solution)/shard_map/dot_general | solution.py:46
  104.9 1.0 collective-permute-start.16
  105.9 0.9 collective-permute-start.17
  106.7 3.2 %collective-permute-done.16 = f32[4,4096]{1,0:T(4,128)S(1)} collective-permute-done((f32[4,4096]{1,0:T(4,128)S(1)}, f32[4,4096]{1,0:T(4,128)S(1)}, u32[]{:S(2)}, u32[]{:S(2)}) %collective-permute-start.16) | collective-permute-done | bytes 65568 | tf_op jit(solution)/shard_map/ppermute | solution.py:107
  110.8 1.2 fusion.1
  112.8 0.5 broadcast_select_fusion.14
  113.5 1.2 fusion.50
  115.1 0.5 collective-permute-start.18
  115.7 3.4 %collective-permute-done.18 = f32[10,512]{1,0:T(8,128)S(1)} collective-permute-done((f32[10,512]{1,0:T(8,128)S(1)}, f32[10,512]{1,0:T(8,128)S(1)}, u32[]{:S(2)}, u32[]{:S(2)}) %collective-permute-start.18) | collective-permute-done | bytes 20512 | tf_op jit(solution)/shard_map/ppermute | solution.py:114
  119.1 2.3 %collective-permute-start.19 = (f32[10,512]{1,0:T(8,128)S(1)}, f32[10,512]{1,0:T(8,128)S(1)}, u32[]{:S(2)}, u32[]{:S(2)}) collective-permute-start(f32[10,512]{1,0:T(8,128)S(1)} %fusion.134), channel_id=1, source_target_pairs={{0,8},{4,12},{8,0},{12,4},{1,9},{5,13},{9,1},{13,5},{2,10},{6,14},... | collective-permute-start | bytes 61448 | tf_op jit(solution)/shard_map/ppermute | solution.py:114
  121.4 0.7 fusion.131
  124.2 0.6 slice_reduce_fusion.3
  126.7 0.7 fusion.88
  (212 shorter events, 15.2 us)
Async XLA Ops:
  3.8 1.2 copy-start.2
  3.8 4.6 %copy-start.1 = (f32[2,3,4096]{2,0,1:T(2,128)S(1)}, f32[2,3,4096]{2,0,1:T(2,128)}, u32[]{:S(2)}) copy-start(f32[2,3,4096]{2,0,1:T(2,128)} %param.8) | copy-start | bytes 294916
  3.8 5.1 %copy-start.15 = (s32[4096]{0:T(1024)S(1)}, s32[4096]{0:T(1024)}, u32[]{:S(2)}) copy-start(s32[4096]{0:T(1024)} %param.10) | copy-start | bytes 49156
  5.3 9.1 %collective-permute-start = (f32[9,512]{1,0:T(8,128)S(1)}, f32[9,512]{1,0:T(8,128)S(1)}, u32[]{:S(2)}, u32[]{:S(2)}) collective-permute-start(f32[9,512]{1,0:T(8,128)S(1)} %copy.130), channel_id=1, source_target_pairs={{0,4},{4,0},{8,12},{12,8},{1,5},{5,1},{9,13},{13,9},{2,6},{6,2},{1... | collective-permute-start | bytes 55304 | tf_op jit(solution)/shard_map/ppermute | solution.py:114
  9.6 10.0 %copy-start.6 = (f32[9,512]{1,0:T(8,128)S(1)}, f32[9,512]{1,0:T(8,128)}, u32[]{:S(2)}) copy-start(f32[9,512]{1,0:T(8,128)} %param.13) | copy-start | bytes 55300
  9.6 10.0 %copy-start.11 = (f32[512]{0:T(512)S(1)}, f32[512]{0:T(512)}, u32[]{:S(2)}) copy-start(f32[512]{0:T(512)} %param.12) | copy-start | bytes 6148
  12.5 11.0 %copy-start.4 = (f32[6,4096]{1,0:T(8,128)}, f32[6,4096]{1,0:T(8,128)S(1)}, u32[]{:S(2)}) copy-start(f32[6,4096]{1,0:T(8,128)S(1)} %reshape.1039) | copy-start | bytes 294916
  12.5 17.5 %collective-permute-start.5 = (f32[6,4096]{1,0:T(8,128)S(1)}, f32[6,4096]{1,0:T(8,128)}, u32[]{:S(2)}, u32[]{:S(2)}) collective-permute-start(f32[6,4096]{1,0:T(8,128)S(1)} %reshape.1039), channel_id=1, source_target_pairs={{0,1},{1,0},{2,3},{3,2},{4,5},{5,4},{6,7},{7,6},{8,9},{9,8},{10,11... | collective-permute-start | bytes 294920 | tf_op jit(solution)/shard_map/ppermute | solution.py:107
  12.6 17.7 %collective-permute-start.6 = (f32[6,4096]{1,0:T(8,128)S(1)}, f32[6,4096]{1,0:T(8,128)}, u32[]{:S(2)}, u32[]{:S(2)}) collective-permute-start(f32[6,4096]{1,0:T(8,128)S(1)} %reshape.1039), channel_id=1, source_target_pairs={{0,2},{1,3},{2,0},{3,1},{4,6},{5,7},{6,4},{7,5},{8,10},{9,11},{10,... | collective-permute-start | bytes 294920 | tf_op jit(solution)/shard_map/ppermute | solution.py:107
  14.1 16.1 %collective-permute-start.7 = (f32[6,4096]{1,0:T(8,128)S(1)}, f32[6,4096]{1,0:T(8,128)}, u32[]{:S(2)}, u32[]{:S(2)}) collective-permute-start(f32[6,4096]{1,0:T(8,128)S(1)} %reshape.1039), channel_id=1, source_target_pairs={{0,3},{1,2},{2,1},{3,0},{4,7},{5,6},{6,5},{7,4},{8,11},{9,10},{10,... | collective-permute-start | bytes 294920 | tf_op jit(solution)/shard_map/ppermute | solution.py:107
  14.4 5.2 %collective-permute-start.1 = (f32[9,512]{1,0:T(8,128)S(1)}, f32[9,512]{1,0:T(8,128)S(1)}, u32[]{:S(2)}, u32[]{:S(2)}) collective-permute-start(f32[9,512]{1,0:T(8,128)S(1)} %add.147), channel_id=1, source_target_pairs={{0,8},{4,12},{8,0},{12,4},{1,9},{5,13},{9,1},{13,5},{2,10},{6,14},... | collective-permute-start | bytes 55304 | tf_op jit(solution)/shard_map/ppermute | solution.py:114
  23.5 1.7 %copy-start = (f32[2,9,4096]{2,0,1:T(2,128)S(1)}, f32[2,9,4096]{2,0,1:T(2,128)}, u32[]{:S(2)}) copy-start(f32[2,9,4096]{2,0,1:T(2,128)} %param.7) | copy-start | bytes 884740
  25.8 4.5 %copy-start.5 = (f32[6,4096]{1,0:T(8,128)S(1)}, f32[6,4096]{1,0:T(8,128)}, u32[]{:S(2)}) copy-start(f32[6,4096]{1,0:T(8,128)} %copy-done.4) | copy-start | bytes 294916
  27.8 3.7 %copy-start.16 = (f32[4096]{0:T(1024)S(1)}, f32[4096]{0:T(1024)}, u32[]{:S(2)}) copy-start(f32[4096]{0:T(1024)} %param.11) | copy-start | bytes 49156
  28.4 3.7 %collective-permute-start.2 = (f32[4,4096]{1,0:T(4,128)S(1)}, f32[4,4096]{1,0:T(4,128)S(1)}, u32[]{:S(2)}, u32[]{:S(2)}) collective-permute-start(f32[4,4096]{1,0:T(4,128)S(1)} %pad_maximum_fusion.18), channel_id=1, source_target_pairs={{0,1},{1,0},{2,3},{3,2},{4,5},{5,4},{6,7},{7,6},{8,9},{9,8},{10,11... | collective-permute-start | bytes 196616 | tf_op jit(solution)/shard_map/ppermute | solution.py:107
  28.4 4.5 %collective-permute-start.3 = (f32[4,4096]{1,0:T(4,128)S(1)}, f32[4,4096]{1,0:T(4,128)S(1)}, u32[]{:S(2)}, u32[]{:S(2)}) collective-permute-start(f32[4,4096]{1,0:T(4,128)S(1)} %pad_maximum_fusion.18), channel_id=1, source_target_pairs={{0,2},{1,3},{2,0},{3,1},{4,6},{5,7},{6,4},{7,5},{8,10},{9,11},{10,... | collective-permute-start | bytes 196616 | tf_op jit(solution)/shard_map/ppermute | solution.py:107
  30.0 4.1 %collective-permute-start.4 = (f32[4,4096]{1,0:T(4,128)S(1)}, f32[4,4096]{1,0:T(4,128)S(1)}, u32[]{:S(2)}, u32[]{:S(2)}) collective-permute-start(f32[4,4096]{1,0:T(4,128)S(1)} %pad_maximum_fusion.18), channel_id=1, source_target_pairs={{0,3},{1,2},{2,1},{3,0},{4,7},{5,6},{6,5},{7,4},{8,11},{9,10},{10,... | collective-permute-start | bytes 196616 | tf_op jit(solution)/shard_map/ppermute | solution.py:107
  41.4 15.3 %copy-start.7 = (f32[9,512]{1,0:T(8,128)S(1)}, f32[9,512]{1,0:T(8,128)}, u32[]{:S(2)}) copy-start(f32[9,512]{1,0:T(8,128)} %param.13) | copy-start | bytes 55300
  41.4 15.3 %copy-start.12 = (f32[512]{0:T(512)S(1)}, f32[512]{0:T(512)}, u32[]{:S(2)}) copy-start(f32[512]{0:T(512)} %param.12) | copy-start | bytes 6148
  45.3 4.0 %collective-permute-start.8 = (f32[10,512]{1,0:T(8,128)S(1)}, f32[10,512]{1,0:T(8,128)S(1)}, u32[]{:S(2)}, u32[]{:S(2)}) collective-permute-start(f32[10,512]{1,0:T(8,128)S(1)} %pad_maximum_fusion.21), channel_id=1, source_target_pairs={{0,4},{4,0},{8,12},{12,8},{1,5},{5,1},{9,13},{13,9},{2,6},{6,2},{1... | collective-permute-start | bytes 61448 | tf_op jit(solution)/shard_map/ppermute | solution.py:114
  49.3 4.9 %collective-permute-start.9 = (f32[10,512]{1,0:T(8,128)S(1)}, f32[10,512]{1,0:T(8,128)S(1)}, u32[]{:S(2)}, u32[]{:S(2)}) collective-permute-start(f32[10,512]{1,0:T(8,128)S(1)} %fusion.136), channel_id=1, source_target_pairs={{0,8},{4,12},{8,0},{12,4},{1,9},{5,13},{9,1},{13,5},{2,10},{6,14},... | collective-permute-start | bytes 61448 | tf_op jit(solution)/shard_map/ppermute | solution.py:114
  66.0 1.9 %collective-permute-start.10 = (f32[4,4096]{1,0:T(4,128)S(1)}, f32[4,4096]{1,0:T(4,128)S(1)}, u32[]{:S(2)}, u32[]{:S(2)}) collective-permute-start(f32[4,4096]{1,0:T(4,128)S(1)} %pad_maximum_fusion.19), channel_id=1, source_target_pairs={{0,1},{1,0},{2,3},{3,2},{4,5},{5,4},{6,7},{7,6},{8,9},{9,8},{10,11... | collective-permute-start | bytes 196616 | tf_op jit(solution)/shard_map/ppermute | solution.py:107
  66.0 4.7 %collective-permute-start.11 = (f32[4,4096]{1,0:T(4,128)S(1)}, f32[4,4096]{1,0:T(4,128)S(1)}, u32[]{:S(2)}, u32[]{:S(2)}) collective-permute-start(f32[4,4096]{1,0:T(4,128)S(1)} %pad_maximum_fusion.19), channel_id=1, source_target_pairs={{0,2},{1,3},{2,0},{3,1},{4,6},{5,7},{6,4},{7,5},{8,10},{9,11},{10,... | collective-permute-start | bytes 196616 | tf_op jit(solution)/shard_map/ppermute | solution.py:107
  67.3 4.4 %collective-permute-start.12 = (f32[4,4096]{1,0:T(4,128)S(1)}, f32[4,4096]{1,0:T(4,128)S(1)}, u32[]{:S(2)}, u32[]{:S(2)}) collective-permute-start(f32[4,4096]{1,0:T(4,128)S(1)} %pad_maximum_fusion.19), channel_id=1, source_target_pairs={{0,3},{1,2},{2,1},{3,0},{4,7},{5,6},{6,5},{7,4},{8,11},{9,10},{10,... | collective-permute-start | bytes 196616 | tf_op jit(solution)/shard_map/ppermute | solution.py:107
  79.4 3.9 %copy-start.10 = (f32[4096]{0:T(1024)S(1)}, f32[4096]{0:T(1024)}, u32[]{:S(2)}) copy-start(f32[4096]{0:T(1024)} %multiply_reduce_fusion.17) | copy-start | bytes 49156
  79.4 15.3 %copy-start.9 = (f32[9,512]{1,0:T(8,128)S(1)}, f32[9,512]{1,0:T(8,128)}, u32[]{:S(2)}) copy-start(f32[9,512]{1,0:T(8,128)} %get-tuple-element.28) | copy-start | bytes 55300
  79.4 15.3 %copy-start.13 = (f32[512]{0:T(512)S(1)}, f32[512]{0:T(512)}, u32[]{:S(2)}) copy-start(f32[512]{0:T(512)} %param.12) | copy-start | bytes 6148
  83.3 4.0 %collective-permute-start.13 = (f32[10,512]{1,0:T(8,128)S(1)}, f32[10,512]{1,0:T(8,128)S(1)}, u32[]{:S(2)}, u32[]{:S(2)}) collective-permute-start(f32[10,512]{1,0:T(8,128)S(1)} %pad_maximum_fusion.22), channel_id=1, source_target_pairs={{0,4},{4,0},{8,12},{12,8},{1,5},{5,1},{9,13},{13,9},{2,6},{6,2},{1... | collective-permute-start | bytes 61448 | tf_op jit(solution)/shard_map/ppermute | solution.py:114
  87.3 4.9 %collective-permute-start.14 = (f32[10,512]{1,0:T(8,128)S(1)}, f32[10,512]{1,0:T(8,128)S(1)}, u32[]{:S(2)}, u32[]{:S(2)}) collective-permute-start(f32[10,512]{1,0:T(8,128)S(1)} %fusion.135), channel_id=1, source_target_pairs={{0,8},{4,12},{8,0},{12,4},{1,9},{5,13},{9,1},{13,5},{2,10},{6,14},... | collective-permute-start | bytes 61448 | tf_op jit(solution)/shard_map/ppermute | solution.py:114
  102.2 2.5 %copy-start.17 = (f32[512]{0:T(512)S(1)}, f32[512]{0:T(512)}, u32[]{:S(2)}) copy-start(f32[512]{0:T(512)} %get-tuple-element.16) | copy-start | bytes 6148
  102.2 2.5 %copy-start.18 = (f32[512]{0:T(512)S(1)}, f32[512]{0:T(512)}, u32[]{:S(2)}) copy-start(f32[512]{0:T(512)} %get-tuple-element.17) | copy-start | bytes 6148
  102.2 2.5 %copy-start.19 = (f32[512]{0:T(512)S(1)}, f32[512]{0:T(512)}, u32[]{:S(2)}) copy-start(f32[512]{0:T(512)} %get-tuple-element.18) | copy-start | bytes 6148
  104.8 1.9 %collective-permute-start.15 = (f32[4,4096]{1,0:T(4,128)S(1)}, f32[4,4096]{1,0:T(4,128)S(1)}, u32[]{:S(2)}, u32[]{:S(2)}) collective-permute-start(f32[4,4096]{1,0:T(4,128)S(1)} %pad_maximum_fusion.20), channel_id=1, source_target_pairs={{0,1},{1,0},{2,3},{3,2},{4,5},{5,4},{6,7},{7,6},{8,9},{9,8},{10,11... | collective-permute-start | bytes 196616 | tf_op jit(solution)/shard_map/ppermute | solution.py:107
  104.9 5.0 %collective-permute-start.16 = (f32[4,4096]{1,0:T(4,128)S(1)}, f32[4,4096]{1,0:T(4,128)S(1)}, u32[]{:S(2)}, u32[]{:S(2)}) collective-permute-start(f32[4,4096]{1,0:T(4,128)S(1)} %pad_maximum_fusion.20), channel_id=1, source_target_pairs={{0,2},{1,3},{2,0},{3,1},{4,6},{5,7},{6,4},{7,5},{8,10},{9,11},{10,... | collective-permute-start | bytes 196616 | tf_op jit(solution)/shard_map/ppermute | solution.py:107
  105.9 4.4 %collective-permute-start.17 = (f32[4,4096]{1,0:T(4,128)S(1)}, f32[4,4096]{1,0:T(4,128)S(1)}, u32[]{:S(2)}, u32[]{:S(2)}) collective-permute-start(f32[4,4096]{1,0:T(4,128)S(1)} %pad_maximum_fusion.20), channel_id=1, source_target_pairs={{0,3},{1,2},{2,1},{3,0},{4,7},{5,6},{6,5},{7,4},{8,11},{9,10},{10,... | collective-permute-start | bytes 196616 | tf_op jit(solution)/shard_map/ppermute | solution.py:107
  112.3 1.2 copy-start.3
  113.5 13.2 %copy-start.8 = (f32[9,512]{1,0:T(8,128)S(1)}, f32[9,512]{1,0:T(8,128)}, u32[]{:S(2)}) copy-start(f32[9,512]{1,0:T(8,128)} %get-tuple-element.25) | copy-start | bytes 55300
  113.5 13.2 %copy-start.14 = (f32[512]{0:T(512)S(1)}, f32[512]{0:T(512)}, u32[]{:S(2)}) copy-start(f32[512]{0:T(512)} %param.12) | copy-start | bytes 6148
  115.1 4.0 %collective-permute-start.18 = (f32[10,512]{1,0:T(8,128)S(1)}, f32[10,512]{1,0:T(8,128)S(1)}, u32[]{:S(2)}, u32[]{:S(2)}) collective-permute-start(f32[10,512]{1,0:T(8,128)S(1)} %pad_maximum_fusion.23), channel_id=1, source_target_pairs={{0,4},{4,0},{8,12},{12,8},{1,5},{5,1},{9,13},{13,9},{2,6},{6,2},{1... | collective-permute-start | bytes 61448 | tf_op jit(solution)/shard_map/ppermute | solution.py:114
  119.1 5.1 %collective-permute-start.19 = (f32[10,512]{1,0:T(8,128)S(1)}, f32[10,512]{1,0:T(8,128)S(1)}, u32[]{:S(2)}, u32[]{:S(2)}) collective-permute-start(f32[10,512]{1,0:T(8,128)S(1)} %fusion.134), channel_id=1, source_target_pairs={{0,8},{4,12},{8,0},{12,4},{1,9},{5,13},{9,1},{13,5},{2,10},{6,14},... | collective-permute-start | bytes 61448 | tf_op jit(solution)/shard_map/ppermute | solution.py:114

commit v14 on v13

--- a/solution.py
+++ b/solution.py
@@ -9,8 +9,8 @@
 F32 = jnp.float32
 
 
-def split_of(count):
-    lo = 1 << max((count.bit_length() - 1) // 2 - 2, 0)
+def split_of(count, shift):
+    lo = 1 << max((count.bit_length() - 1) // 2 - shift, 0)
     while count % lo:
         lo //= 2
     return count // lo, lo
@@ -25,9 +25,9 @@
 
 
 class Index:
-    def __init__(self, index, count):
+    def __init__(self, index, count, shift):
         self.count = count
-        self.hi, self.lo = split_of(count)
+        self.hi, self.lo = split_of(count, shift)
         high = index // self.lo
         low = index % self.lo
         hot = (lax.broadcasted_iota(jnp.int32, (self.hi, index.shape[0]), 0) == high[None, :])
@@ -123,8 +123,8 @@
 def on_device(cam_jac, point_jac, obs_cam, obs_point, point_damp, cam_damp, reduced_rhs):
     npts = point_damp.shape[0]
     ncam = reduced_rhs.shape[1]
-    by_point = Index(obs_point, npts)
-    by_cam = Index(obs_cam, ncam)
+    by_point = Index(obs_point, npts, 2)
+    by_cam = Index(obs_cam, ncam, 1)
     six_terms = allsum(by_point.segsum(normal_six(point_jac)), "cam")
     inv = point_inverse(six_terms, point_damp)
     diag_terms = by_cam.segsum(jnp.sum(cam_jac * cam_jac, axis=0))

time: 128 us -> 102 us (0.80)
  matrix products: 31.9 us -> 20.8 us
  local copies, waits for them, and re-layouts: 18.2 us -> 8.02 us
  other arithmetic: 20.1 us -> 16.4 us
    select_n x12 -> x0, local copies, waits for them, and re-layouts: 7.18 us -> none  [segsum(): jnp.where(self.low[None], part[:, None, :], jnp.zeros((), BF))]
    dot_general x8, matrix products: 17.7 us -> 10.9 us  [segsum(): lax.dot_general(self.hot3, spread, (((1,), (1,)), ((), ())), preferred_el...]
    dot_general x6, matrix products: 14.2 us -> 9.84 us  [gather(): lax.dot_general(stacked, self.hot3t, (((1,), (0,)), ((), ())), preferred_...]
    reshape x3 -> x0, local copies, waits for them, and re-layouts: 3.81 us -> none  [gather(): spread = lax.dot_general(stacked, self.hot3t, (((1,), (0,)), ((), ())), p...]
    select_n x8, other arithmetic: 3.99 us -> 1.62 us  [segsum(): jnp.where(self.low[None], part[:, None, :], jnp.zeros((), BF))]
    reduce_sum x6 -> x3, other arithmetic: 1.92 us -> 0.51 us  [gather(): return jnp.sum(jnp.where(self.low[None], spread, 0.0), axis=1)]
    reshape x20 -> x12, local copies, waits for them, and re-layouts: 3.02 us -> 2.62 us  [segsum(): out.reshape(self.hi, ncol, self.lo).transpose(1, 0, 2)]
  transfers between devices with their start and end apart: 20 -> 20, of which waited for: 13 -> 12; matrix products, arithmetic and copies ran while one was open for 13% -> 15% of each run, Pallas kernels for 0% -> 0%
where the time goes in v14:
time: 102 us
  waiting for transfers between devices  24.1 us (24%)
  starting transfers between devices  21.2 us (21%)
  matrix products  20.8 us (20%)
  other arithmetic  16.4 us (16%)
  between operations  11.3 us (11%)
  local copies, waits for them, and re-layouts  8.02 us (8%)
    ppermute x8, waiting for transfers between devices, allsum(): lax.ppermute(value, axis, [(i, i ^ step) for i in range(size)])  15.3 us
    ppermute x8, starting transfers between devices, allsum(): lax.ppermute(value, axis, [(i, i ^ step) for i in range(size)])  13.5 us
    dot_general x8, matrix products, segsum(): lax.dot_general(self.hot3, spread, (((1,), (1,)), ((), ())), preferred_el...  10.9 us
    dot_general x6, matrix products, gather(): lax.dot_general(stacked, self.hot3t, (((1,), (0,)), ((), ())), preferred_...  9.84 us
    ppermute x12, waiting for transfers between devices, allsum(): lax.ppermute(value, axis, [(i, i ^ mask) for i in range(size)])  8.72 us
    ppermute x12, starting transfers between devices, allsum(): lax.ppermute(value, axis, [(i, i ^ mask) for i in range(size)])  7.68 us
    reshape x12, local copies, waits for them, and re-layouts, segsum(): out.reshape(self.hi, ncol, self.lo).transpose(1, 0, 2)  2.62 us
  transfers between devices with their start and end apart: 20, of which 12 were waited for; matrix products, arithmetic and copies ran while one was open for 15% of the time, Pallas kernels for 0%

profile of v14, /device:TPU:0, one launch (start us, length us, event | category | flops | bytes accessed | tf_op | source)
XLA Modules:
  0.0 101.7 jit_solution(7244587929132821296)
XLA Ops:
  0.6 0.7 add_select_fusion
  1.4 1.4 %multiply_reduce_fusion.6 = f32[9,4096]{1,0:T(8,128)S(1)} fusion(f32[2,9,4096]{2,0,1:T(2,128)} %param.7), kind=kLoop, calls=%fused_computation.121 | loop fusion | flops 110592 | bytes 442368 | tf_op jit(solution)/shard_map/reduce_sum | solution.py:130
  3.2 0.6 fusion.67
  4.1 3.1 %collective-permute-start = (f32[9,512]{1,0:T(8,128)S(1)}, f32[9,512]{1,0:T(8,128)}, u32[]{:S(2)}, u32[]{:S(2)}) collective-permute-start(f32[9,512]{1,0:T(8,128)S(1)} %reshape.1029), channel_id=1, source_target_pairs={{0,4},{4,0},{8,12},{12,8},{1,5},{5,1},{9,13},{13,9},{2,6},{6,2},{1... | collective-permute-start | bytes 55304 | tf_op jit(solution)/shard_map/ppermute | solution.py:114
  7.3 0.2 multiply_reduce_fusion.23
  7.8 0.4 fusion.3
  8.2 0.3 broadcast_select_fusion.2
  8.5 2.1 %fusion.7 = f32[256,96]{0,1:T(8,128)S(1)} fusion(bf16[96,4096]{1,0:T(8,128)(2,1)S(1)} %bitcast.220, bf16[96,4096]{1,0:T(8,128)(2,1)S(1)} %bitcast.219, bf16[96,4096]{1,0:T(8,128)(2,1)S(1)} %bitcast.218, bf16[256,4096]{1,0:T(8,128)(2,1)S(1)} %fusion.3), kind=kOutput, calls=%fused_computation.13 | convolution fusion | flops 629932032 | bytes 4554752 | tf_op jit(solution)/shard_map/dot_general | solution.py:46
  10.7 0.3 copy.38
  11.0 0.4 reshape.1039
  11.4 1.6 %collective-permute-start.6 = (f32[6,4096]{1,0:T(8,128)S(1)}, f32[6,4096]{1,0:T(8,128)}, u32[]{:S(2)}, u32[]{:S(2)}) collective-permute-start(f32[6,4096]{1,0:T(8,128)S(1)} %reshape.1039), channel_id=1, source_target_pairs={{0,2},{1,3},{2,0},{3,1},{4,6},{5,7},{6,4},{7,5},{8,10},{9,11},{10,... | collective-permute-start | bytes 294920 | tf_op jit(solution)/shard_map/ppermute | solution.py:107
  13.0 0.3 collective-permute-start.7
  13.3 0.8 add.147
  14.1 2.6 %collective-permute-start.1 = (f32[9,512]{1,0:T(8,128)S(1)}, f32[9,512]{1,0:T(8,128)S(1)}, u32[]{:S(2)}, u32[]{:S(2)}) collective-permute-start(f32[9,512]{1,0:T(8,128)S(1)} %add.147), channel_id=1, source_target_pairs={{0,8},{4,12},{8,0},{12,4},{1,9},{5,13},{9,1},{13,5},{2,10},{6,14},... | collective-permute-start | bytes 55304 | tf_op jit(solution)/shard_map/ppermute | solution.py:114
  16.6 2.5 %collective-permute-done.1 = f32[9,512]{1,0:T(8,128)S(1)} collective-permute-done((f32[9,512]{1,0:T(8,128)S(1)}, f32[9,512]{1,0:T(8,128)S(1)}, u32[]{:S(2)}, u32[]{:S(2)}) %collective-permute-start.1) | collective-permute-done | bytes 18464 | tf_op jit(solution)/shard_map/ppermute | solution.py:114
  19.5 2.0 %fusion.42 = f32[9,4096]{1,0:T(8,128)S(1)} fusion(bf16[64,4096]{1,0:T(8,128)(2,1)} %copy-done.2, pred[8,4096]{1,0:T(8,128)(4,1)S(1)} %iota_compare_fusion.3, bf16[72,64]{1,0:T(8,128)(2,1)S(1)} %get-tuple-element.91, bf16[72,64]{1,0:T(8,128)(2,1)S(1)} %get-tuple-element.92, bf16[72,64]{1,0:T(8,128)(2,1)S(1)} %get-tuple-element.90), kind=kOutput, calls=%fused_computation.50 | convolution fusion | flops 118600704 | bytes 732160 | tf_op jit(solution)/shard_map/dot_general | solution.py:55
  22.1 2.0 %fusion.39 = f32[256,48]{0,1:T(8,128)S(1)} fusion(bf16[256,4096]{1,0:T(8,128)(2,1)S(1)} %fusion.3, bf16[48,4096]{1,0:T(8,128)(2,1)S(1)} %bitcast.226, bf16[48,4096]{1,0:T(8,128)(2,1)S(1)} %bitcast.225, bf16[48,4096]{1,0:T(8,128)(2,1)S(1)} %bitcast.224), kind=kOutput, calls=%fused_computation.47 | convolution fusion | flops 324403200 | bytes 3325952 | tf_op jit(solution)/shard_map/dot_general | solution.py:46
  24.3 0.2 reshape.1034
  24.8 1.6 %collective-permute-start.3 = (f32[4,4096]{1,0:T(4,128)S(1)}, f32[4,4096]{1,0:T(4,128)S(1)}, u32[]{:S(2)}, u32[]{:S(2)}) collective-permute-start(f32[4,4096]{1,0:T(4,128)S(1)} %pad_maximum_fusion.18), channel_id=1, source_target_pairs={{0,2},{1,3},{2,0},{3,1},{4,6},{5,7},{6,4},{7,5},{8,10},{9,11},{10,... | collective-permute-start | bytes 196616 | tf_op jit(solution)/shard_map/ppermute | solution.py:107
  26.6 1.0 add_add_fusion
  27.8 0.8 maximum_add_fusion
  29.2 1.2 %collective-permute-done.4 = f32[4,4096]{1,0:T(4,128)S(1)} collective-permute-done((f32[4,4096]{1,0:T(4,128)S(1)}, f32[4,4096]{1,0:T(4,128)S(1)}, u32[]{:S(2)}, u32[]{:S(2)}) %collective-permute-start.4) | collective-permute-done | bytes 65568 | tf_op jit(solution)/shard_map/ppermute | solution.py:107
  31.1 1.2 %fusion.6 = f32[48,4096]{1,0:T(8,128)S(1)} fusion(bf16[256,4096]{1,0:T(8,128)(2,1)S(1)} %fusion.3, bf16[48,256]{1,0:T(8,128)(2,1)S(1)} %get-tuple-element.82, bf16[48,256]{1,0:T(8,128)(2,1)S(1)} %get-tuple-element.83, bf16[48,256]{1,0:T(8,128)(2,1)S(1)} %get-tuple-element.81), kind=kOutput, calls=%fused_computation.12 | convolution fusion | flops 321085440 | bytes 2957312 | tf_op jit(solution)/shard_map/dot_general | solution.py:55
  32.5 0.4 multiply_reduce_fusion.4
  33.0 0.2 select_bitcast_fusion.8
  33.5 0.9 fusion.64
  35.1 3.6 %collective-permute-done.8 = f32[10,512]{1,0:T(8,128)S(1)} collective-permute-done((f32[10,512]{1,0:T(8,128)S(1)}, f32[10,512]{1,0:T(8,128)S(1)}, u32[]{:S(2)}, u32[]{:S(2)}) %collective-permute-start.8) | collective-permute-done | bytes 20512 | tf_op jit(solution)/shard_map/ppermute | solution.py:114
  38.7 2.3 %collective-permute-start.9 = (f32[10,512]{1,0:T(8,128)S(1)}, f32[10,512]{1,0:T(8,128)S(1)}, u32[]{:S(2)}, u32[]{:S(2)}) collective-permute-start(f32[10,512]{1,0:T(8,128)S(1)} %fusion.151), channel_id=1, source_target_pairs={{0,8},{4,12},{8,0},{12,4},{1,9},{5,13},{9,1},{13,5},{2,10},{6,14},... | collective-permute-start | bytes 61448 | tf_op jit(solution)/shard_map/ppermute | solution.py:114
  41.1 0.6 fusion.148
  41.7 2.0 %collective-permute-done.9 = f32[10,512]{1,0:T(8,128)S(1)} collective-permute-done((f32[10,512]{1,0:T(8,128)S(1)}, f32[10,512]{1,0:T(8,128)S(1)}, u32[]{:S(2)}, u32[]{:S(2)}) %collective-permute-start.9) | collective-permute-done | bytes 20512 | tf_op jit(solution)/shard_map/ppermute | solution.py:114
  43.6 0.7 slice_reduce_fusion.5
  46.3 0.6 multiply_reduce_fusion.22
  47.3 2.0 %fusion.41 = f32[9,4096]{1,0:T(8,128)S(1)} fusion(bf16[64,4096]{1,0:T(8,128)(2,1)} %copy-done.2, pred[8,4096]{1,0:T(8,128)(4,1)S(1)} %iota_compare_fusion.3, bf16[72,64]{1,0:T(8,128)(2,1)S(1)} %get-tuple-element.88, bf16[72,64]{1,0:T(8,128)(2,1)S(1)} %get-tuple-element.89, bf16[72,64]{1,0:T(8,128)(2,1)S(1)} %get-tuple-element.87), kind=kOutput, calls=%fused_computation.49 | convolution fusion | flops 118600704 | bytes 732160 | tf_op jit(solution)/shard_map/dot_general | solution.py:55
  49.8 2.0 %fusion.38 = f32[256,48]{0,1:T(8,128)S(1)} fusion(bf16[256,4096]{1,0:T(8,128)(2,1)S(1)} %fusion.3, bf16[48,4096]{1,0:T(8,128)(2,1)S(1)} %bitcast.229, bf16[48,4096]{1,0:T(8,128)(2,1)S(1)} %bitcast.228, bf16[48,4096]{1,0:T(8,128)(2,1)S(1)} %bitcast.227), kind=kOutput, calls=%fused_computation.46 | convolution fusion | flops 324403200 | bytes 3325952 | tf_op jit(solution)/shard_map/dot_general | solution.py:46
  52.5 1.3 %collective-permute-start.11 = (f32[4,4096]{1,0:T(4,128)S(1)}, f32[4,4096]{1,0:T(4,128)S(1)}, u32[]{:S(2)}, u32[]{:S(2)}) collective-permute-start(f32[4,4096]{1,0:T(4,128)S(1)} %pad_maximum_fusion.19), channel_id=1, source_target_pairs={{0,2},{1,3},{2,0},{3,1},{4,6},{5,7},{6,4},{7,5},{8,10},{9,11},{10,... | collective-permute-start | bytes 196616 | tf_op jit(solution)/shard_map/ppermute | solution.py:107
  53.8 0.6 collective-permute-start.12
  54.4 2.9 %collective-permute-done.11 = f32[4,4096]{1,0:T(4,128)S(1)} collective-permute-done((f32[4,4096]{1,0:T(4,128)S(1)}, f32[4,4096]{1,0:T(4,128)S(1)}, u32[]{:S(2)}, u32[]{:S(2)}) %collective-permute-start.11) | collective-permute-done | bytes 65568 | tf_op jit(solution)/shard_map/ppermute | solution.py:107
  57.2 1.0 collective-permute-done.12
  58.8 1.2 %fusion.5 = f32[48,4096]{1,0:T(8,128)S(1)} fusion(bf16[256,4096]{1,0:T(8,128)(2,1)S(1)} %fusion.3, bf16[48,256]{1,0:T(8,128)(2,1)S(1)} %get-tuple-element.79, bf16[48,256]{1,0:T(8,128)(2,1)S(1)} %get-tuple-element.80, bf16[48,256]{1,0:T(8,128)(2,1)S(1)} %get-tuple-element.78), kind=kOutput, calls=%fused_computation.11 | convolution fusion | flops 321085440 | bytes 2957312 | tf_op jit(solution)/shard_map/dot_general | solution.py:55
  60.3 0.4 multiply_reduce_fusion.2
  60.7 0.2 select_bitcast_fusion.5
  61.2 0.7 fusion.61
  62.6 3.6 %collective-permute-done.13 = f32[10,512]{1,0:T(8,128)S(1)} collective-permute-done((f32[10,512]{1,0:T(8,128)S(1)}, f32[10,512]{1,0:T(8,128)S(1)}, u32[]{:S(2)}, u32[]{:S(2)}) %collective-permute-start.13) | collective-permute-done | bytes 20512 | tf_op jit(solution)/shard_map/ppermute | solution.py:114
  66.3 2.3 %collective-permute-start.14 = (f32[10,512]{1,0:T(8,128)S(1)}, f32[10,512]{1,0:T(8,128)S(1)}, u32[]{:S(2)}, u32[]{:S(2)}) collective-permute-start(f32[10,512]{1,0:T(8,128)S(1)} %fusion.150), channel_id=1, source_target_pairs={{0,8},{4,12},{8,0},{12,4},{1,9},{5,13},{9,1},{13,5},{2,10},{6,14},... | collective-permute-start | bytes 61448 | tf_op jit(solution)/shard_map/ppermute | solution.py:114
  68.6 0.7 fusion.147
  71.2 0.6 slice_reduce_fusion.4
  73.7 0.6 multiply_reduce_fusion.20
  74.7 2.0 %fusion.40 = f32[9,4096]{1,0:T(8,128)S(1)} fusion(bf16[64,4096]{1,0:T(8,128)(2,1)} %copy-done.2, pred[8,4096]{1,0:T(8,128)(4,1)S(1)} %iota_compare_fusion.3, bf16[72,64]{1,0:T(8,128)(2,1)S(1)} %get-tuple-element.85, bf16[72,64]{1,0:T(8,128)(2,1)S(1)} %get-tuple-element.86, bf16[72,64]{1,0:T(8,128)(2,1)S(1)} %get-tuple-element.84), kind=kOutput, calls=%fused_computation.48 | convolution fusion | flops 118600704 | bytes 732160 | tf_op jit(solution)/shard_map/dot_general | solution.py:55
  77.2 2.0 %fusion.37 = f32[256,48]{0,1:T(8,128)S(1)} fusion(bf16[256,4096]{1,0:T(8,128)(2,1)S(1)} %fusion.3, bf16[48,4096]{1,0:T(8,128)(2,1)S(1)} %bitcast.232, bf16[48,4096]{1,0:T(8,128)(2,1)S(1)} %bitcast.231, bf16[48,4096]{1,0:T(8,128)(2,1)S(1)} %bitcast.230), kind=kOutput, calls=%fused_computation.45 | convolution fusion | flops 324403200 | bytes 3325952 | tf_op jit(solution)/shard_map/dot_general | solution.py:46
  79.4 0.2 reshape.1064
  79.9 1.0 collective-permute-start.16
  80.8 0.9 collective-permute-start.17
  81.7 3.2 %collective-permute-done.16 = f32[4,4096]{1,0:T(4,128)S(1)} collective-permute-done((f32[4,4096]{1,0:T(4,128)S(1)}, f32[4,4096]{1,0:T(4,128)S(1)}, u32[]{:S(2)}, u32[]{:S(2)}) %collective-permute-start.16) | collective-permute-done | bytes 65568 | tf_op jit(solution)/shard_map/ppermute | solution.py:107
  84.9 0.3 collective-permute-done.17
  85.8 1.4 %fusion.4 = f32[48,4096]{1,0:T(8,128)S(1)} fusion(bf16[256,4096]{1,0:T(8,128)(2,1)S(1)} %fusion.3, bf16[48,256]{1,0:T(8,128)(2,1)S(1)} %get-tuple-element.76, bf16[48,256]{1,0:T(8,128)(2,1)S(1)} %get-tuple-element.77, bf16[48,256]{1,0:T(8,128)(2,1)S(1)} %get-tuple-element.75), kind=kOutput, calls=%fused_computation.10 | convolution fusion | flops 321085440 | bytes 2957312 | tf_op jit(solution)/shard_map/dot_general | solution.py:55
  87.5 0.4 multiply_reduce_fusion
  88.4 0.6 fusion.58
  89.4 0.5 collective-permute-start.18
  90.1 3.3 %collective-permute-done.18 = f32[10,512]{1,0:T(8,128)S(1)} collective-permute-done((f32[10,512]{1,0:T(8,128)S(1)}, f32[10,512]{1,0:T(8,128)S(1)}, u32[]{:S(2)}, u32[]{:S(2)}) %collective-permute-start.18) | collective-permute-done | bytes 20512 | tf_op jit(solution)/shard_map/ppermute | solution.py:114
  93.4 2.3 %collective-permute-start.19 = (f32[10,512]{1,0:T(8,128)S(1)}, f32[10,512]{1,0:T(8,128)S(1)}, u32[]{:S(2)}, u32[]{:S(2)}) collective-permute-start(f32[10,512]{1,0:T(8,128)S(1)} %fusion.149), channel_id=1, source_target_pairs={{0,8},{4,12},{8,0},{12,4},{1,9},{5,13},{9,1},{13,5},{2,10},{6,14},... | collective-permute-start | bytes 61448 | tf_op jit(solution)/shard_map/ppermute | solution.py:114
  95.7 0.6 fusion.146
  98.3 0.3 collective-permute-done.19
  98.6 0.6 slice_reduce_fusion.3
  101.0 0.7 fusion.121
  (171 shorter events, 11.4 us)
Async XLA Ops:
  2.9 4.8 %copy-start.2 = (bf16[64,4096]{1,0:T(8,128)(2,1)}, bf16[64,4096]{1,0:T(8,128)(2,1)S(1)}, u32[]{:S(2)}) copy-start(bf16[64,4096]{1,0:T(8,128)(2,1)S(1)} %fusion.70) | copy-start | bytes 1572868
  3.2 4.1 %copy-start.1 = (f32[2,3,4096]{2,0,1:T(2,128)S(1)}, f32[2,3,4096]{2,0,1:T(2,128)}, u32[]{:S(2)}) copy-start(f32[2,3,4096]{2,0,1:T(2,128)} %param.8) | copy-start | bytes 294916
  3.2 4.5 %copy-start.11 = (s32[4096]{0:T(1024)S(1)}, s32[4096]{0:T(1024)}, u32[]{:S(2)}) copy-start(s32[4096]{0:T(1024)} %param.10) | copy-start | bytes 49156
  4.1 9.1 %collective-permute-start = (f32[9,512]{1,0:T(8,128)S(1)}, f32[9,512]{1,0:T(8,128)}, u32[]{:S(2)}, u32[]{:S(2)}) collective-permute-start(f32[9,512]{1,0:T(8,128)S(1)} %reshape.1029), channel_id=1, source_target_pairs={{0,4},{4,0},{8,12},{12,8},{1,5},{5,1},{9,13},{13,9},{2,6},{6,2},{1... | collective-permute-start | bytes 55304 | tf_op jit(solution)/shard_map/ppermute | solution.py:114
  8.5 10.6 %copy-start.6 = (f32[9,512]{1,0:T(8,128)S(1)}, f32[9,512]{1,0:T(8,128)}, u32[]{:S(2)}) copy-start(f32[9,512]{1,0:T(8,128)} %param.13) | copy-start | bytes 55300
  8.5 10.6 %copy-start.10 = (f32[512]{0:T(512)S(1)}, f32[512]{0:T(512)}, u32[]{:S(2)}) copy-start(f32[512]{0:T(512)} %param.12) | copy-start | bytes 6148
  11.4 15.0 %collective-permute-start.5 = (f32[6,4096]{1,0:T(8,128)S(1)}, f32[6,4096]{1,0:T(8,128)S(1)}, u32[]{:S(2)}, u32[]{:S(2)}) collective-permute-start(f32[6,4096]{1,0:T(8,128)S(1)} %reshape.1039), channel_id=1, source_target_pairs={{0,1},{1,0},{2,3},{3,2},{4,5},{5,4},{6,7},{7,6},{8,9},{9,8},{10,11... | collective-permute-start | bytes 294920 | tf_op jit(solution)/shard_map/ppermute | solution.py:107
  11.4 15.2 %collective-permute-start.6 = (f32[6,4096]{1,0:T(8,128)S(1)}, f32[6,4096]{1,0:T(8,128)}, u32[]{:S(2)}, u32[]{:S(2)}) collective-permute-start(f32[6,4096]{1,0:T(8,128)S(1)} %reshape.1039), channel_id=1, source_target_pairs={{0,2},{1,3},{2,0},{3,1},{4,6},{5,7},{6,4},{7,5},{8,10},{9,11},{10,... | collective-permute-start | bytes 294920 | tf_op jit(solution)/shard_map/ppermute | solution.py:107
  13.0 13.6 %collective-permute-start.7 = (f32[6,4096]{1,0:T(8,128)S(1)}, f32[6,4096]{1,0:T(8,128)}, u32[]{:S(2)}, u32[]{:S(2)}) collective-permute-start(f32[6,4096]{1,0:T(8,128)S(1)} %reshape.1039), channel_id=1, source_target_pairs={{0,3},{1,2},{2,1},{3,0},{4,7},{5,6},{6,5},{7,4},{8,11},{9,10},{10,... | collective-permute-start | bytes 294920 | tf_op jit(solution)/shard_map/ppermute | solution.py:107
  14.1 5.1 %collective-permute-start.1 = (f32[9,512]{1,0:T(8,128)S(1)}, f32[9,512]{1,0:T(8,128)S(1)}, u32[]{:S(2)}, u32[]{:S(2)}) collective-permute-start(f32[9,512]{1,0:T(8,128)S(1)} %add.147), channel_id=1, source_target_pairs={{0,8},{4,12},{8,0},{12,4},{1,9},{5,13},{9,1},{13,5},{2,10},{6,14},... | collective-permute-start | bytes 55304 | tf_op jit(solution)/shard_map/ppermute | solution.py:114
  19.5 2.0 %copy-start = (f32[2,9,4096]{2,0,1:T(2,128)S(1)}, f32[2,9,4096]{2,0,1:T(2,128)}, u32[]{:S(2)}) copy-start(f32[2,9,4096]{2,0,1:T(2,128)} %param.7) | copy-start | bytes 884740
  24.7 4.4 %collective-permute-start.2 = (f32[4,4096]{1,0:T(4,128)S(1)}, f32[4,4096]{1,0:T(4,128)S(1)}, u32[]{:S(2)}, u32[]{:S(2)}) collective-permute-start(f32[4,4096]{1,0:T(4,128)S(1)} %pad_maximum_fusion.18), channel_id=1, source_target_pairs={{0,1},{1,0},{2,3},{3,2},{4,5},{5,4},{6,7},{7,6},{8,9},{9,8},{10,11... | collective-permute-start | bytes 196616 | tf_op jit(solution)/shard_map/ppermute | solution.py:107
  24.8 4.5 %collective-permute-start.3 = (f32[4,4096]{1,0:T(4,128)S(1)}, f32[4,4096]{1,0:T(4,128)S(1)}, u32[]{:S(2)}, u32[]{:S(2)}) collective-permute-start(f32[4,4096]{1,0:T(4,128)S(1)} %pad_maximum_fusion.18), channel_id=1, source_target_pairs={{0,2},{1,3},{2,0},{3,1},{4,6},{5,7},{6,4},{7,5},{8,10},{9,11},{10,... | collective-permute-start | bytes 196616 | tf_op jit(solution)/shard_map/ppermute | solution.py:107
  26.4 4.1 %collective-permute-start.4 = (f32[4,4096]{1,0:T(4,128)S(1)}, f32[4,4096]{1,0:T(4,128)S(1)}, u32[]{:S(2)}, u32[]{:S(2)}) collective-permute-start(f32[4,4096]{1,0:T(4,128)S(1)} %pad_maximum_fusion.18), channel_id=1, source_target_pairs={{0,3},{1,2},{2,1},{3,0},{4,7},{5,6},{6,5},{7,4},{8,11},{9,10},{10,... | collective-permute-start | bytes 196616 | tf_op jit(solution)/shard_map/ppermute | solution.py:107
  32.4 1.0 %copy-start.3 = (bf16[64,4096]{1,0:T(8,128)(2,1)S(1)}, bf16[64,4096]{1,0:T(8,128)(2,1)}, u32[]{:S(2)}) copy-start(bf16[64,4096]{1,0:T(8,128)(2,1)} %copy-done.2) | copy-start | bytes 1572868
  33.5 12.8 %copy-start.7 = (f32[9,512]{1,0:T(8,128)S(1)}, f32[9,512]{1,0:T(8,128)}, u32[]{:S(2)}) copy-start(f32[9,512]{1,0:T(8,128)} %param.13) | copy-start | bytes 55300
  34.8 4.0 %collective-permute-start.8 = (f32[10,512]{1,0:T(8,128)S(1)}, f32[10,512]{1,0:T(8,128)S(1)}, u32[]{:S(2)}, u32[]{:S(2)}) collective-permute-start(f32[10,512]{1,0:T(8,128)S(1)} %pad_maximum_fusion.21), channel_id=1, source_target_pairs={{0,4},{4,0},{8,12},{12,8},{1,5},{5,1},{9,13},{13,9},{2,6},{6,2},{1... | collective-permute-start | bytes 61448 | tf_op jit(solution)/shard_map/ppermute | solution.py:114
  38.7 4.9 %collective-permute-start.9 = (f32[10,512]{1,0:T(8,128)S(1)}, f32[10,512]{1,0:T(8,128)S(1)}, u32[]{:S(2)}, u32[]{:S(2)}) collective-permute-start(f32[10,512]{1,0:T(8,128)S(1)} %fusion.151), channel_id=1, source_target_pairs={{0,8},{4,12},{8,0},{12,4},{1,9},{5,13},{9,1},{13,5},{2,10},{6,14},... | collective-permute-start | bytes 61448 | tf_op jit(solution)/shard_map/ppermute | solution.py:114
  52.4 1.9 %collective-permute-start.10 = (f32[4,4096]{1,0:T(4,128)S(1)}, f32[4,4096]{1,0:T(4,128)S(1)}, u32[]{:S(2)}, u32[]{:S(2)}) collective-permute-start(f32[4,4096]{1,0:T(4,128)S(1)} %pad_maximum_fusion.19), channel_id=1, source_target_pairs={{0,1},{1,0},{2,3},{3,2},{4,5},{5,4},{6,7},{7,6},{8,9},{9,8},{10,11... | collective-permute-start | bytes 196616 | tf_op jit(solution)/shard_map/ppermute | solution.py:107
  52.5 4.7 %collective-permute-start.11 = (f32[4,4096]{1,0:T(4,128)S(1)}, f32[4,4096]{1,0:T(4,128)S(1)}, u32[]{:S(2)}, u32[]{:S(2)}) collective-permute-start(f32[4,4096]{1,0:T(4,128)S(1)} %pad_maximum_fusion.19), channel_id=1, source_target_pairs={{0,2},{1,3},{2,0},{3,1},{4,6},{5,7},{6,4},{7,5},{8,10},{9,11},{10,... | collective-permute-start | bytes 196616 | tf_op jit(solution)/shard_map/ppermute | solution.py:107
  53.8 4.4 %collective-permute-start.12 = (f32[4,4096]{1,0:T(4,128)S(1)}, f32[4,4096]{1,0:T(4,128)S(1)}, u32[]{:S(2)}, u32[]{:S(2)}) collective-permute-start(f32[4,4096]{1,0:T(4,128)S(1)} %pad_maximum_fusion.19), channel_id=1, source_target_pairs={{0,3},{1,2},{2,1},{3,0},{4,7},{5,6},{6,5},{7,4},{8,11},{9,10},{10,... | collective-permute-start | bytes 196616 | tf_op jit(solution)/shard_map/ppermute | solution.py:107
  60.2 1.0 %copy-start.4 = (bf16[64,4096]{1,0:T(8,128)(2,1)S(1)}, bf16[64,4096]{1,0:T(8,128)(2,1)}, u32[]{:S(2)}) copy-start(bf16[64,4096]{1,0:T(8,128)(2,1)} %copy-done.2) | copy-start | bytes 1572868
  61.2 12.5 %copy-start.9 = (f32[9,512]{1,0:T(8,128)S(1)}, f32[9,512]{1,0:T(8,128)}, u32[]{:S(2)}) copy-start(f32[9,512]{1,0:T(8,128)} %get-tuple-element.20) | copy-start | bytes 55300
  62.3 4.0 %collective-permute-start.13 = (f32[10,512]{1,0:T(8,128)S(1)}, f32[10,512]{1,0:T(8,128)S(1)}, u32[]{:S(2)}, u32[]{:S(2)}) collective-permute-start(f32[10,512]{1,0:T(8,128)S(1)} %pad_maximum_fusion.22), channel_id=1, source_target_pairs={{0,4},{4,0},{8,12},{12,8},{1,5},{5,1},{9,13},{13,9},{2,6},{6,2},{1... | collective-permute-start | bytes 61448 | tf_op jit(solution)/shard_map/ppermute | solution.py:114
  66.3 4.9 %collective-permute-start.14 = (f32[10,512]{1,0:T(8,128)S(1)}, f32[10,512]{1,0:T(8,128)S(1)}, u32[]{:S(2)}, u32[]{:S(2)}) collective-permute-start(f32[10,512]{1,0:T(8,128)S(1)} %fusion.150), channel_id=1, source_target_pairs={{0,8},{4,12},{8,0},{12,4},{1,9},{5,13},{9,1},{13,5},{2,10},{6,14},... | collective-permute-start | bytes 61448 | tf_op jit(solution)/shard_map/ppermute | solution.py:114
  79.8 1.9 %collective-permute-start.15 = (f32[4,4096]{1,0:T(4,128)S(1)}, f32[4,4096]{1,0:T(4,128)S(1)}, u32[]{:S(2)}, u32[]{:S(2)}) collective-permute-start(f32[4,4096]{1,0:T(4,128)S(1)} %pad_maximum_fusion.20), channel_id=1, source_target_pairs={{0,1},{1,0},{2,3},{3,2},{4,5},{5,4},{6,7},{7,6},{8,9},{9,8},{10,11... | collective-permute-start | bytes 196616 | tf_op jit(solution)/shard_map/ppermute | solution.py:107
  79.9 5.0 %collective-permute-start.16 = (f32[4,4096]{1,0:T(4,128)S(1)}, f32[4,4096]{1,0:T(4,128)S(1)}, u32[]{:S(2)}, u32[]{:S(2)}) collective-permute-start(f32[4,4096]{1,0:T(4,128)S(1)} %pad_maximum_fusion.20), channel_id=1, source_target_pairs={{0,2},{1,3},{2,0},{3,1},{4,6},{5,7},{6,4},{7,5},{8,10},{9,11},{10,... | collective-permute-start | bytes 196616 | tf_op jit(solution)/shard_map/ppermute | solution.py:107
  80.8 4.4 %collective-permute-start.17 = (f32[4,4096]{1,0:T(4,128)S(1)}, f32[4,4096]{1,0:T(4,128)S(1)}, u32[]{:S(2)}, u32[]{:S(2)}) collective-permute-start(f32[4,4096]{1,0:T(4,128)S(1)} %pad_maximum_fusion.20), channel_id=1, source_target_pairs={{0,3},{1,2},{2,1},{3,0},{4,7},{5,6},{6,5},{7,4},{8,11},{9,10},{10,... | collective-permute-start | bytes 196616 | tf_op jit(solution)/shard_map/ppermute | solution.py:107
  87.4 1.0 %copy-start.5 = (bf16[64,4096]{1,0:T(8,128)(2,1)S(1)}, bf16[64,4096]{1,0:T(8,128)(2,1)}, u32[]{:S(2)}) copy-start(bf16[64,4096]{1,0:T(8,128)(2,1)} %copy-done.2) | copy-start | bytes 1572868
  88.4 12.6 %copy-start.8 = (f32[9,512]{1,0:T(8,128)S(1)}, f32[9,512]{1,0:T(8,128)}, u32[]{:S(2)}) copy-start(f32[9,512]{1,0:T(8,128)} %get-tuple-element.17) | copy-start | bytes 55300
  89.4 4.0 %collective-permute-start.18 = (f32[10,512]{1,0:T(8,128)S(1)}, f32[10,512]{1,0:T(8,128)S(1)}, u32[]{:S(2)}, u32[]{:S(2)}) collective-permute-start(f32[10,512]{1,0:T(8,128)S(1)} %pad_maximum_fusion.23), channel_id=1, source_target_pairs={{0,4},{4,0},{8,12},{12,8},{1,5},{5,1},{9,13},{13,9},{2,6},{6,2},{1... | collective-permute-start | bytes 61448 | tf_op jit(solution)/shard_map/ppermute | solution.py:114
  93.4 5.1 %collective-permute-start.19 = (f32[10,512]{1,0:T(8,128)S(1)}, f32[10,512]{1,0:T(8,128)S(1)}, u32[]{:S(2)}, u32[]{:S(2)}) collective-permute-start(f32[10,512]{1,0:T(8,128)S(1)} %fusion.149), channel_id=1, source_target_pairs={{0,8},{4,12},{8,0},{12,4},{1,9},{5,13},{9,1},{13,5},{2,10},{6,14},... | collective-permute-start | bytes 61448 | tf_op jit(solution)/shard_map/ppermute | solution.py:114

commit v15 on v14

--- a/solution.py
+++ b/solution.py
@@ -123,8 +123,8 @@
 def on_device(cam_jac, point_jac, obs_cam, obs_point, point_damp, cam_damp, reduced_rhs):
     npts = point_damp.shape[0]
     ncam = reduced_rhs.shape[1]
-    by_point = Index(obs_point, npts, 2)
-    by_cam = Index(obs_cam, ncam, 1)
+    by_point = Index(obs_point, npts, 1)
+    by_cam = Index(obs_cam, ncam, 0)
     six_terms = allsum(by_point.segsum(normal_six(point_jac)), "cam")
     inv = point_inverse(six_terms, point_damp)
     diag_terms = by_cam.segsum(jnp.sum(cam_jac * cam_jac, axis=0))

time: 102 us -> 92.7 us (0.909)
  matrix products: 20.8 us -> 12.9 us
  local copies, waits for them, and re-layouts: 8.02 us -> 5.54 us
  waiting for transfers between devices: 24.1 us -> 25.7 us
    dot_general x6, matrix products: 9.84 us -> 3.71 us  [gather(): lax.dot_general(stacked, self.hot3t, (((1,), (0,)), ((), ())), preferred_...]
    dot_general x8, matrix products: 10.9 us -> 9.2 us  [segsum(): lax.dot_general(self.hot3, spread, (((1,), (1,)), ((), ())), preferred_el...]
    ppermute x12, waiting for transfers between devices: 8.72 us -> 10.4 us  [allsum(): lax.ppermute(value, axis, [(i, i ^ mask) for i in range(size)])]
    reduce_sum x3 -> x6, other arithmetic: 0.51 us -> 2.12 us  [gather(): return jnp.sum(jnp.where(self.low[None], spread, 0.0), axis=1)]
    select_n x8, other arithmetic: 1.62 us -> 2.8 us  [segsum(): jnp.where(self.low[None], part[:, None, :], jnp.zeros((), BF))]
    reduce_sum x6, other arithmetic: 1.36 us -> 0.18 us  [lanes(): return jnp.sum(terms.reshape(-1, ncam), axis=0)]
  transfers between devices with their start and end apart: 20 -> 20, of which waited for: 12 -> 12; matrix products, arithmetic and copies ran while one was open for 15% -> 10% of each run, Pallas kernels for 0% -> 0%
where the time goes in v15:
time: 92.7 us; the launch traced here: 92.4 us
  waiting for transfers between devices  25.7 us (28%)
  starting transfers between devices  21.3 us (23%)
  other arithmetic  15.6 us (17%)
  matrix products  12.9 us (14%)
  between operations  11.4 us (12%)
  local copies, waits for them, and re-layouts  5.54 us (6%)
    ppermute x8, waiting for transfers between devices, allsum(): lax.ppermute(value, axis, [(i, i ^ step) for i in range(size)])  15.3 us
    ppermute x8, starting transfers between devices, allsum(): lax.ppermute(value, axis, [(i, i ^ step) for i in range(size)])  13.6 us
    ppermute x12, waiting for transfers between devices, allsum(): lax.ppermute(value, axis, [(i, i ^ mask) for i in range(size)])  10.4 us
    dot_general x8, matrix products, segsum(): lax.dot_general(self.hot3, spread, (((1,), (1,)), ((), ())), preferred_el...  9.2 us
    ppermute x12, starting transfers between devices, allsum(): lax.ppermute(value, axis, [(i, i ^ mask) for i in range(size)])  7.68 us
    dot_general x6, matrix products, gather(): lax.dot_general(stacked, self.hot3t, (((1,), (0,)), ((), ())), preferred_...  3.71 us
    select_n x8, other arithmetic, segsum(): jnp.where(self.low[None], part[:, None, :], jnp.zeros((), BF))  2.8 us
    reduce_sum x6, other arithmetic, gather(): return jnp.sum(jnp.where(self.low[None], spread, 0.0), axis=1)  2.12 us
  transfers between devices with their start and end apart: 20, of which 12 were waited for; matrix products, arithmetic and copies ran while one was open for 10% of the time, Pallas kernels for 0%

profile of v15, /device:TPU:0, one launch (start us, length us, event | category | flops | bytes accessed | tf_op | source)
XLA Modules:
  0.0 92.4 jit_solution(14905093494757574437)
XLA Ops:
  0.6 0.7 add_select_fusion
  1.4 1.4 %multiply_reduce_fusion.6 = f32[9,4096]{1,0:T(8,128)S(1)} fusion(f32[2,9,4096]{2,0,1:T(2,128)} %param.7), kind=kLoop, calls=%fused_computation.115 | loop fusion | flops 110592 | bytes 442368 | tf_op jit(solution)/shard_map/reduce_sum | solution.py:130
  2.9 0.4 broadcast_select_fusion.14
  3.3 1.1 %fusion.6 = f32[32,144]{0,1:T(8,128)S(1)} fusion(bf16[144,4096]{1,0:T(8,128)(2,1)S(1)} %bitcast.189, bf16[144,4096]{1,0:T(8,128)(2,1)S(1)} %bitcast.188, bf16[144,4096]{1,0:T(8,128)(2,1)S(1)} %bitcast.187, bf16[32,4096]{1,0:T(8,128)(2,1)S(1)} %fusion.52), kind=kOutput, calls=%fused_computation.6 | convolution fusion | flops 126222336 | bytes 3819520 | tf_op jit(solution)/shard_map/dot_general | solution.py:46
  4.6 3.1 %collective-permute-start = (f32[9,512]{1,0:T(8,128)S(1)}, f32[9,512]{1,0:T(8,128)S(1)}, u32[]{:S(2)}, u32[]{:S(2)}) collective-permute-start(f32[9,512]{1,0:T(8,128)S(1)} %reshape.1029), channel_id=1, source_target_pairs={{0,4},{4,0},{8,12},{12,8},{1,5},{5,1},{9,13},{13,9},{2,6},{6,2},{1... | collective-permute-start | bytes 55304 | tf_op jit(solution)/shard_map/ppermute | solution.py:114
  7.7 0.2 multiply_reduce_fusion.23
  8.5 0.4 broadcast_select_fusion.2
  9.0 1.6 %fusion = f32[128,192]{0,1:T(8,128)S(1)} fusion(bf16[192,4096]{1,0:T(8,128)(2,1)S(1)} %bitcast.179, bf16[192,4096]{1,0:T(8,128)(2,1)S(1)} %bitcast.178, bf16[192,4096]{1,0:T(8,128)(2,1)S(1)} %bitcast.177, bf16[128,4096]{1,0:T(8,128)(2,1)S(1)} %fusion.48), kind=kOutput, calls=%fused_computation | convolution fusion | flops 627572736 | bytes 5865472 | tf_op jit(solution)/shard_map/dot_general | solution.py:46
  11.0 1.6 %collective-permute-start.6 = (f32[6,4096]{1,0:T(8,128)S(1)}, f32[6,4096]{1,0:T(8,128)S(1)}, u32[]{:S(2)}, u32[]{:S(2)}) collective-permute-start(f32[6,4096]{1,0:T(8,128)S(1)} %reshape.1039), channel_id=1, source_target_pairs={{0,2},{1,3},{2,0},{3,1},{4,6},{5,7},{6,4},{7,5},{8,10},{9,11},{10,... | collective-permute-start | bytes 294920 | tf_op jit(solution)/shard_map/ppermute | solution.py:107
  12.6 0.3 collective-permute-start.7
  12.9 2.7 %collective-permute-start.1 = (f32[9,512]{1,0:T(8,128)S(1)}, f32[9,512]{1,0:T(8,128)S(1)}, u32[]{:S(2)}, u32[]{:S(2)}) collective-permute-start(f32[9,512]{1,0:T(8,128)S(1)} %add.147), channel_id=1, source_target_pairs={{0,8},{4,12},{8,0},{12,4},{1,9},{5,13},{9,1},{13,5},{2,10},{6,14},... | collective-permute-start | bytes 55304 | tf_op jit(solution)/shard_map/ppermute | solution.py:114
  15.6 2.5 %collective-permute-done.1 = f32[9,512]{1,0:T(8,128)S(1)} collective-permute-done((f32[9,512]{1,0:T(8,128)S(1)}, f32[9,512]{1,0:T(8,128)S(1)}, u32[]{:S(2)}, u32[]{:S(2)}) %collective-permute-start.1) | collective-permute-done | bytes 18464 | tf_op jit(solution)/shard_map/ppermute | solution.py:114
  18.4 0.5 fusion.55
  18.9 0.4 select_reduce_fusion.2
  20.0 1.1 %fusion.30 = f32[128,96]{0,1:T(8,128)S(1)} fusion(bf16[96,4096]{1,0:T(8,128)(2,1)S(1)} %bitcast.198, bf16[96,4096]{1,0:T(8,128)(2,1)S(1)} %bitcast.197, bf16[96,4096]{1,0:T(8,128)(2,1)S(1)} %bitcast.196, bf16[128,4096]{1,0:T(8,128)(2,1)S(1)} %fusion.48), kind=kOutput, calls=%fused_computation.32 | convolution fusion | flops 318504960 | bytes 3457024 | tf_op jit(solution)/shard_map/dot_general | solution.py:46
  21.6 1.6 %collective-permute-start.3 = (f32[4,4096]{1,0:T(4,128)S(1)}, f32[4,4096]{1,0:T(4,128)S(1)}, u32[]{:S(2)}, u32[]{:S(2)}) collective-permute-start(f32[4,4096]{1,0:T(4,128)S(1)} %pad_maximum_fusion.18), channel_id=1, source_target_pairs={{0,2},{1,3},{2,0},{3,1},{4,6},{5,7},{6,4},{7,5},{8,10},{9,11},{10,... | collective-permute-start | bytes 196616 | tf_op jit(solution)/shard_map/ppermute | solution.py:107
  23.2 0.3 collective-permute-start.4
  24.2 1.9 %collective-permute-done.3 = f32[4,4096]{1,0:T(4,128)S(1)} collective-permute-done((f32[4,4096]{1,0:T(4,128)S(1)}, f32[4,4096]{1,0:T(4,128)S(1)}, u32[]{:S(2)}, u32[]{:S(2)}) %collective-permute-start.3) | collective-permute-done | bytes 65568 | tf_op jit(solution)/shard_map/ppermute | solution.py:107
  26.1 1.2 %collective-permute-done.4 = f32[4,4096]{1,0:T(4,128)S(1)} collective-permute-done((f32[4,4096]{1,0:T(4,128)S(1)}, f32[4,4096]{1,0:T(4,128)S(1)}, u32[]{:S(2)}, u32[]{:S(2)}) %collective-permute-start.4) | collective-permute-done | bytes 65568 | tf_op jit(solution)/shard_map/ppermute | solution.py:107
  27.8 0.7 fusion.51
  28.5 0.2 select_reduce_fusion.5
  28.9 0.4 multiply_reduce_fusion.4
  29.3 0.4 broadcast_select_fusion.11
  29.8 1.1 %fusion.12 = f32[32,144]{0,1:T(8,128)S(1)} fusion(bf16[144,4096]{1,0:T(8,128)(2,1)S(1)} %bitcast.192, bf16[144,4096]{1,0:T(8,128)(2,1)S(1)} %bitcast.191, bf16[144,4096]{1,0:T(8,128)(2,1)S(1)} %bitcast.190, bf16[32,4096]{1,0:T(8,128)(2,1)S(1)} %fusion.52), kind=kOutput, calls=%fused_computation.12 | convolution fusion | flops 126222336 | bytes 3819520 | tf_op jit(solution)/shard_map/dot_general | solution.py:46
  31.7 3.6 %collective-permute-done.8 = f32[10,512]{1,0:T(8,128)S(1)} collective-permute-done((f32[10,512]{1,0:T(8,128)S(1)}, f32[10,512]{1,0:T(8,128)S(1)}, u32[]{:S(2)}, u32[]{:S(2)}) %collective-permute-start.8) | collective-permute-done | bytes 20512 | tf_op jit(solution)/shard_map/ppermute | solution.py:114
  35.3 2.3 %collective-permute-start.9 = (f32[10,512]{1,0:T(8,128)S(1)}, f32[10,512]{1,0:T(8,128)S(1)}, u32[]{:S(2)}, u32[]{:S(2)}) collective-permute-start(f32[10,512]{1,0:T(8,128)S(1)} %fusion.136), channel_id=1, source_target_pairs={{0,8},{4,12},{8,0},{12,4},{1,9},{5,13},{9,1},{13,5},{2,10},{6,14},... | collective-permute-start | bytes 61448 | tf_op jit(solution)/shard_map/ppermute | solution.py:114
  37.6 0.6 fusion.133
  38.2 2.0 %collective-permute-done.9 = f32[10,512]{1,0:T(8,128)S(1)} collective-permute-done((f32[10,512]{1,0:T(8,128)S(1)}, f32[10,512]{1,0:T(8,128)S(1)}, u32[]{:S(2)}, u32[]{:S(2)}) %collective-permute-start.9) | collective-permute-done | bytes 20512 | tf_op jit(solution)/shard_map/ppermute | solution.py:114
  40.2 0.7 slice_reduce_fusion.5
  43.2 0.5 fusion.54
  43.7 0.5 select_reduce_fusion.1
  44.8 1.1 %fusion.36 = f32[128,96]{0,1:T(8,128)S(1)} fusion(bf16[96,4096]{1,0:T(8,128)(2,1)S(1)} %bitcast.201, bf16[96,4096]{1,0:T(8,128)(2,1)S(1)} %bitcast.200, bf16[96,4096]{1,0:T(8,128)(2,1)S(1)} %bitcast.199, bf16[128,4096]{1,0:T(8,128)(2,1)S(1)} %fusion.48), kind=kOutput, calls=%fused_computation.38 | convolution fusion | flops 318504960 | bytes 3457024 | tf_op jit(solution)/shard_map/dot_general | solution.py:46
  46.4 1.3 %collective-permute-start.11 = (f32[4,4096]{1,0:T(4,128)S(1)}, f32[4,4096]{1,0:T(4,128)S(1)}, u32[]{:S(2)}, u32[]{:S(2)}) collective-permute-start(f32[4,4096]{1,0:T(4,128)S(1)} %pad_maximum_fusion.19), channel_id=1, source_target_pairs={{0,2},{1,3},{2,0},{3,1},{4,6},{5,7},{6,4},{7,5},{8,10},{9,11},{10,... | collective-permute-start | bytes 196616 | tf_op jit(solution)/shard_map/ppermute | solution.py:107
  47.7 0.6 collective-permute-start.12
  48.3 2.9 %collective-permute-done.11 = f32[4,4096]{1,0:T(4,128)S(1)} collective-permute-done((f32[4,4096]{1,0:T(4,128)S(1)}, f32[4,4096]{1,0:T(4,128)S(1)}, u32[]{:S(2)}, u32[]{:S(2)}) %collective-permute-start.11) | collective-permute-done | bytes 65568 | tf_op jit(solution)/shard_map/ppermute | solution.py:107
  51.1 1.0 %collective-permute-done.12 = f32[4,4096]{1,0:T(4,128)S(1)} collective-permute-done((f32[4,4096]{1,0:T(4,128)S(1)}, f32[4,4096]{1,0:T(4,128)S(1)}, u32[]{:S(2)}, u32[]{:S(2)}) %collective-permute-start.12) | collective-permute-done | bytes 65568 | tf_op jit(solution)/shard_map/ppermute | solution.py:107
  52.6 0.7 fusion.50
  53.3 0.3 select_reduce_fusion.4
  53.7 0.4 multiply_reduce_fusion.2
  54.1 0.4 broadcast_select_fusion.8
  54.6 1.1 %fusion.18 = f32[32,144]{0,1:T(8,128)S(1)} fusion(bf16[144,4096]{1,0:T(8,128)(2,1)S(1)} %bitcast.195, bf16[144,4096]{1,0:T(8,128)(2,1)S(1)} %bitcast.194, bf16[144,4096]{1,0:T(8,128)(2,1)S(1)} %bitcast.193, bf16[32,4096]{1,0:T(8,128)(2,1)S(1)} %fusion.52), kind=kOutput, calls=%fused_computation.18 | convolution fusion | flops 126222336 | bytes 3819520 | tf_op jit(solution)/shard_map/dot_general | solution.py:46
  56.3 3.6 %collective-permute-done.13 = f32[10,512]{1,0:T(8,128)S(1)} collective-permute-done((f32[10,512]{1,0:T(8,128)S(1)}, f32[10,512]{1,0:T(8,128)S(1)}, u32[]{:S(2)}, u32[]{:S(2)}) %collective-permute-start.13) | collective-permute-done | bytes 20512 | tf_op jit(solution)/shard_map/ppermute | solution.py:114
  59.9 2.3 %collective-permute-start.14 = (f32[10,512]{1,0:T(8,128)S(1)}, f32[10,512]{1,0:T(8,128)S(1)}, u32[]{:S(2)}, u32[]{:S(2)}) collective-permute-start(f32[10,512]{1,0:T(8,128)S(1)} %fusion.135), channel_id=1, source_target_pairs={{0,8},{4,12},{8,0},{12,4},{1,9},{5,13},{9,1},{13,5},{2,10},{6,14},... | collective-permute-start | bytes 61448 | tf_op jit(solution)/shard_map/ppermute | solution.py:114
  62.2 0.6 fusion.132
  64.8 0.6 slice_reduce_fusion.4
  67.6 0.5 fusion.53
  68.2 0.5 select_reduce_fusion
  69.2 1.1 %fusion.42 = f32[128,96]{0,1:T(8,128)S(1)} fusion(bf16[96,4096]{1,0:T(8,128)(2,1)S(1)} %bitcast.204, bf16[96,4096]{1,0:T(8,128)(2,1)S(1)} %bitcast.203, bf16[96,4096]{1,0:T(8,128)(2,1)S(1)} %bitcast.202, bf16[128,4096]{1,0:T(8,128)(2,1)S(1)} %fusion.48), kind=kOutput, calls=%fused_computation.44 | convolution fusion | flops 318504960 | bytes 3457024 | tf_op jit(solution)/shard_map/dot_general | solution.py:46
  70.9 1.0 %collective-permute-start.16 = (f32[4,4096]{1,0:T(4,128)S(1)}, f32[4,4096]{1,0:T(4,128)S(1)}, u32[]{:S(2)}, u32[]{:S(2)}) collective-permute-start(f32[4,4096]{1,0:T(4,128)S(1)} %pad_maximum_fusion.20), channel_id=1, source_target_pairs={{0,2},{1,3},{2,0},{3,1},{4,6},{5,7},{6,4},{7,5},{8,10},{9,11},{10,... | collective-permute-start | bytes 196616 | tf_op jit(solution)/shard_map/ppermute | solution.py:107
  71.8 0.9 collective-permute-start.17
  72.7 3.2 %collective-permute-done.16 = f32[4,4096]{1,0:T(4,128)S(1)} collective-permute-done((f32[4,4096]{1,0:T(4,128)S(1)}, f32[4,4096]{1,0:T(4,128)S(1)}, u32[]{:S(2)}, u32[]{:S(2)}) %collective-permute-start.16) | collective-permute-done | bytes 65568 | tf_op jit(solution)/shard_map/ppermute | solution.py:107
  75.9 0.3 collective-permute-done.17
  76.7 0.7 fusion.49
  77.5 0.2 select_reduce_fusion.3
  77.8 0.4 multiply_reduce_fusion
  78.3 0.4 broadcast_select_fusion.5
  78.7 1.1 %fusion.24 = f32[32,144]{0,1:T(8,128)S(1)} fusion(bf16[144,4096]{1,0:T(8,128)(2,1)S(1)} %bitcast.186, bf16[144,4096]{1,0:T(8,128)(2,1)S(1)} %bitcast.185, bf16[144,4096]{1,0:T(8,128)(2,1)S(1)} %bitcast.184, bf16[32,4096]{1,0:T(8,128)(2,1)S(1)} %fusion.52), kind=kOutput, calls=%fused_computation.24 | convolution fusion | flops 126222336 | bytes 3819520 | tf_op jit(solution)/shard_map/dot_general | solution.py:46
  80.1 0.5 collective-permute-start.18
  80.8 3.3 %collective-permute-done.18 = f32[10,512]{1,0:T(8,128)S(1)} collective-permute-done((f32[10,512]{1,0:T(8,128)S(1)}, f32[10,512]{1,0:T(8,128)S(1)}, u32[]{:S(2)}, u32[]{:S(2)}) %collective-permute-start.18) | collective-permute-done | bytes 20512 | tf_op jit(solution)/shard_map/ppermute | solution.py:114
  84.1 2.3 %collective-permute-start.19 = (f32[10,512]{1,0:T(8,128)S(1)}, f32[10,512]{1,0:T(8,128)S(1)}, u32[]{:S(2)}, u32[]{:S(2)}) collective-permute-start(f32[10,512]{1,0:T(8,128)S(1)} %fusion.134), channel_id=1, source_target_pairs={{0,8},{4,12},{8,0},{12,4},{1,9},{5,13},{9,1},{13,5},{2,10},{6,14},... | collective-permute-start | bytes 61448 | tf_op jit(solution)/shard_map/ppermute | solution.py:114
  86.4 0.6 fusion.131
  88.9 0.3 collective-permute-done.19
  89.2 0.6 slice_reduce_fusion.3
  91.7 0.7 fusion.106
  (162 shorter events, 9.7 us)
Async XLA Ops:
  3.3 4.4 %copy-start.1 = (f32[2,3,4096]{2,0,1:T(2,128)S(1)}, f32[2,3,4096]{2,0,1:T(2,128)}, u32[]{:S(2)}) copy-start(f32[2,3,4096]{2,0,1:T(2,128)} %param.8) | copy-start | bytes 294916
  3.3 4.9 %copy-start.4 = (s32[4096]{0:T(1024)S(1)}, s32[4096]{0:T(1024)}, u32[]{:S(2)}) copy-start(s32[4096]{0:T(1024)} %param.10) | copy-start | bytes 49156
  4.6 8.3 %collective-permute-start = (f32[9,512]{1,0:T(8,128)S(1)}, f32[9,512]{1,0:T(8,128)S(1)}, u32[]{:S(2)}, u32[]{:S(2)}) collective-permute-start(f32[9,512]{1,0:T(8,128)S(1)} %reshape.1029), channel_id=1, source_target_pairs={{0,4},{4,0},{8,12},{12,8},{1,5},{5,1},{9,13},{13,9},{2,6},{6,2},{1... | collective-permute-start | bytes 55304 | tf_op jit(solution)/shard_map/ppermute | solution.py:114
  9.0 9.1 %copy-start.2 = (f32[9,512]{1,0:T(8,128)S(1)}, f32[9,512]{1,0:T(8,128)}, u32[]{:S(2)}) copy-start(f32[9,512]{1,0:T(8,128)} %param.13) | copy-start | bytes 55300
  9.0 9.1 %copy-start.3 = (f32[512]{0:T(512)S(1)}, f32[512]{0:T(512)}, u32[]{:S(2)}) copy-start(f32[512]{0:T(512)} %param.12) | copy-start | bytes 6148
  11.0 12.2 %collective-permute-start.5 = (f32[6,4096]{1,0:T(8,128)S(1)}, f32[6,4096]{1,0:T(8,128)S(1)}, u32[]{:S(2)}, u32[]{:S(2)}) collective-permute-start(f32[6,4096]{1,0:T(8,128)S(1)} %reshape.1039), channel_id=1, source_target_pairs={{0,1},{1,0},{2,3},{3,2},{4,5},{5,4},{6,7},{7,6},{8,9},{9,8},{10,11... | collective-permute-start | bytes 294920 | tf_op jit(solution)/shard_map/ppermute | solution.py:107
  11.0 12.4 %collective-permute-start.6 = (f32[6,4096]{1,0:T(8,128)S(1)}, f32[6,4096]{1,0:T(8,128)S(1)}, u32[]{:S(2)}, u32[]{:S(2)}) collective-permute-start(f32[6,4096]{1,0:T(8,128)S(1)} %reshape.1039), channel_id=1, source_target_pairs={{0,2},{1,3},{2,0},{3,1},{4,6},{5,7},{6,4},{7,5},{8,10},{9,11},{10,... | collective-permute-start | bytes 294920 | tf_op jit(solution)/shard_map/ppermute | solution.py:107
  12.6 10.9 %collective-permute-start.7 = (f32[6,4096]{1,0:T(8,128)S(1)}, f32[6,4096]{1,0:T(8,128)S(1)}, u32[]{:S(2)}, u32[]{:S(2)}) collective-permute-start(f32[6,4096]{1,0:T(8,128)S(1)} %reshape.1039), channel_id=1, source_target_pairs={{0,3},{1,2},{2,1},{3,0},{4,7},{5,6},{6,5},{7,4},{8,11},{9,10},{10,... | collective-permute-start | bytes 294920 | tf_op jit(solution)/shard_map/ppermute | solution.py:107
  12.9 5.2 %collective-permute-start.1 = (f32[9,512]{1,0:T(8,128)S(1)}, f32[9,512]{1,0:T(8,128)S(1)}, u32[]{:S(2)}, u32[]{:S(2)}) collective-permute-start(f32[9,512]{1,0:T(8,128)S(1)} %add.147), channel_id=1, source_target_pairs={{0,8},{4,12},{8,0},{12,4},{1,9},{5,13},{9,1},{13,5},{2,10},{6,14},... | collective-permute-start | bytes 55304 | tf_op jit(solution)/shard_map/ppermute | solution.py:114
  18.3 1.0 %copy-start = (f32[2,9,4096]{2,0,1:T(2,128)S(1)}, f32[2,9,4096]{2,0,1:T(2,128)}, u32[]{:S(2)}) copy-start(f32[2,9,4096]{2,0,1:T(2,128)} %param.7) | copy-start | bytes 884740
  20.0 3.7 %copy-start.5 = (f32[4096]{0:T(1024)S(1)}, f32[4096]{0:T(1024)}, u32[]{:S(2)}) copy-start(f32[4096]{0:T(1024)} %param.11) | copy-start | bytes 49156
  21.5 2.7 %collective-permute-start.2 = (f32[4,4096]{1,0:T(4,128)S(1)}, f32[4,4096]{1,0:T(4,128)S(1)}, u32[]{:S(2)}, u32[]{:S(2)}) collective-permute-start(f32[4,4096]{1,0:T(4,128)S(1)} %pad_maximum_fusion.18), channel_id=1, source_target_pairs={{0,1},{1,0},{2,3},{3,2},{4,5},{5,4},{6,7},{7,6},{8,9},{9,8},{10,11... | collective-permute-start | bytes 196616 | tf_op jit(solution)/shard_map/ppermute | solution.py:107
  21.6 4.5 %collective-permute-start.3 = (f32[4,4096]{1,0:T(4,128)S(1)}, f32[4,4096]{1,0:T(4,128)S(1)}, u32[]{:S(2)}, u32[]{:S(2)}) collective-permute-start(f32[4,4096]{1,0:T(4,128)S(1)} %pad_maximum_fusion.18), channel_id=1, source_target_pairs={{0,2},{1,3},{2,0},{3,1},{4,6},{5,7},{6,4},{7,5},{8,10},{9,11},{10,... | collective-permute-start | bytes 196616 | tf_op jit(solution)/shard_map/ppermute | solution.py:107
  23.2 4.1 %collective-permute-start.4 = (f32[4,4096]{1,0:T(4,128)S(1)}, f32[4,4096]{1,0:T(4,128)S(1)}, u32[]{:S(2)}, u32[]{:S(2)}) collective-permute-start(f32[4,4096]{1,0:T(4,128)S(1)} %pad_maximum_fusion.18), channel_id=1, source_target_pairs={{0,3},{1,2},{2,1},{3,0},{4,7},{5,6},{6,5},{7,4},{8,11},{9,10},{10,... | collective-permute-start | bytes 196616 | tf_op jit(solution)/shard_map/ppermute | solution.py:107
  31.3 4.0 %collective-permute-start.8 = (f32[10,512]{1,0:T(8,128)S(1)}, f32[10,512]{1,0:T(8,128)S(1)}, u32[]{:S(2)}, u32[]{:S(2)}) collective-permute-start(f32[10,512]{1,0:T(8,128)S(1)} %pad_maximum_fusion.21), channel_id=1, source_target_pairs={{0,4},{4,0},{8,12},{12,8},{1,5},{5,1},{9,13},{13,9},{2,6},{6,2},{1... | collective-permute-start | bytes 61448 | tf_op jit(solution)/shard_map/ppermute | solution.py:114
  35.3 4.9 %collective-permute-start.9 = (f32[10,512]{1,0:T(8,128)S(1)}, f32[10,512]{1,0:T(8,128)S(1)}, u32[]{:S(2)}, u32[]{:S(2)}) collective-permute-start(f32[10,512]{1,0:T(8,128)S(1)} %fusion.136), channel_id=1, source_target_pairs={{0,8},{4,12},{8,0},{12,4},{1,9},{5,13},{9,1},{13,5},{2,10},{6,14},... | collective-permute-start | bytes 61448 | tf_op jit(solution)/shard_map/ppermute | solution.py:114
  46.3 1.9 %collective-permute-start.10 = (f32[4,4096]{1,0:T(4,128)S(1)}, f32[4,4096]{1,0:T(4,128)S(1)}, u32[]{:S(2)}, u32[]{:S(2)}) collective-permute-start(f32[4,4096]{1,0:T(4,128)S(1)} %pad_maximum_fusion.19), channel_id=1, source_target_pairs={{0,1},{1,0},{2,3},{3,2},{4,5},{5,4},{6,7},{7,6},{8,9},{9,8},{10,11... | collective-permute-start | bytes 196616 | tf_op jit(solution)/shard_map/ppermute | solution.py:107
  46.4 4.7 %collective-permute-start.11 = (f32[4,4096]{1,0:T(4,128)S(1)}, f32[4,4096]{1,0:T(4,128)S(1)}, u32[]{:S(2)}, u32[]{:S(2)}) collective-permute-start(f32[4,4096]{1,0:T(4,128)S(1)} %pad_maximum_fusion.19), channel_id=1, source_target_pairs={{0,2},{1,3},{2,0},{3,1},{4,6},{5,7},{6,4},{7,5},{8,10},{9,11},{10,... | collective-permute-start | bytes 196616 | tf_op jit(solution)/shard_map/ppermute | solution.py:107
  47.7 4.4 %collective-permute-start.12 = (f32[4,4096]{1,0:T(4,128)S(1)}, f32[4,4096]{1,0:T(4,128)S(1)}, u32[]{:S(2)}, u32[]{:S(2)}) collective-permute-start(f32[4,4096]{1,0:T(4,128)S(1)} %pad_maximum_fusion.19), channel_id=1, source_target_pairs={{0,3},{1,2},{2,1},{3,0},{4,7},{5,6},{6,5},{7,4},{8,11},{9,10},{10,... | collective-permute-start | bytes 196616 | tf_op jit(solution)/shard_map/ppermute | solution.py:107
  55.9 4.0 %collective-permute-start.13 = (f32[10,512]{1,0:T(8,128)S(1)}, f32[10,512]{1,0:T(8,128)S(1)}, u32[]{:S(2)}, u32[]{:S(2)}) collective-permute-start(f32[10,512]{1,0:T(8,128)S(1)} %pad_maximum_fusion.22), channel_id=1, source_target_pairs={{0,4},{4,0},{8,12},{12,8},{1,5},{5,1},{9,13},{13,9},{2,6},{6,2},{1... | collective-permute-start | bytes 61448 | tf_op jit(solution)/shard_map/ppermute | solution.py:114
  59.9 4.9 %collective-permute-start.14 = (f32[10,512]{1,0:T(8,128)S(1)}, f32[10,512]{1,0:T(8,128)S(1)}, u32[]{:S(2)}, u32[]{:S(2)}) collective-permute-start(f32[10,512]{1,0:T(8,128)S(1)} %fusion.135), channel_id=1, source_target_pairs={{0,8},{4,12},{8,0},{12,4},{1,9},{5,13},{9,1},{13,5},{2,10},{6,14},... | collective-permute-start | bytes 61448 | tf_op jit(solution)/shard_map/ppermute | solution.py:114
  70.8 1.9 %collective-permute-start.15 = (f32[4,4096]{1,0:T(4,128)S(1)}, f32[4,4096]{1,0:T(4,128)S(1)}, u32[]{:S(2)}, u32[]{:S(2)}) collective-permute-start(f32[4,4096]{1,0:T(4,128)S(1)} %pad_maximum_fusion.20), channel_id=1, source_target_pairs={{0,1},{1,0},{2,3},{3,2},{4,5},{5,4},{6,7},{7,6},{8,9},{9,8},{10,11... | collective-permute-start | bytes 196616 | tf_op jit(solution)/shard_map/ppermute | solution.py:107
  70.9 5.0 %collective-permute-start.16 = (f32[4,4096]{1,0:T(4,128)S(1)}, f32[4,4096]{1,0:T(4,128)S(1)}, u32[]{:S(2)}, u32[]{:S(2)}) collective-permute-start(f32[4,4096]{1,0:T(4,128)S(1)} %pad_maximum_fusion.20), channel_id=1, source_target_pairs={{0,2},{1,3},{2,0},{3,1},{4,6},{5,7},{6,4},{7,5},{8,10},{9,11},{10,... | collective-permute-start | bytes 196616 | tf_op jit(solution)/shard_map/ppermute | solution.py:107
  71.8 4.4 %collective-permute-start.17 = (f32[4,4096]{1,0:T(4,128)S(1)}, f32[4,4096]{1,0:T(4,128)S(1)}, u32[]{:S(2)}, u32[]{:S(2)}) collective-permute-start(f32[4,4096]{1,0:T(4,128)S(1)} %pad_maximum_fusion.20), channel_id=1, source_target_pairs={{0,3},{1,2},{2,1},{3,0},{4,7},{5,6},{6,5},{7,4},{8,11},{9,10},{10,... | collective-permute-start | bytes 196616 | tf_op jit(solution)/shard_map/ppermute | solution.py:107
  80.1 4.0 %collective-permute-start.18 = (f32[10,512]{1,0:T(8,128)S(1)}, f32[10,512]{1,0:T(8,128)S(1)}, u32[]{:S(2)}, u32[]{:S(2)}) collective-permute-start(f32[10,512]{1,0:T(8,128)S(1)} %pad_maximum_fusion.23), channel_id=1, source_target_pairs={{0,4},{4,0},{8,12},{12,8},{1,5},{5,1},{9,13},{13,9},{2,6},{6,2},{1... | collective-permute-start | bytes 61448 | tf_op jit(solution)/shard_map/ppermute | solution.py:114
  84.1 5.1 %collective-permute-start.19 = (f32[10,512]{1,0:T(8,128)S(1)}, f32[10,512]{1,0:T(8,128)S(1)}, u32[]{:S(2)}, u32[]{:S(2)}) collective-permute-start(f32[10,512]{1,0:T(8,128)S(1)} %fusion.134), channel_id=1, source_target_pairs={{0,8},{4,12},{8,0},{12,4},{1,9},{5,13},{9,1},{13,5},{2,10},{6,14},... | collective-permute-start | bytes 61448 | tf_op jit(solution)/shard_map/ppermute | solution.py:114

commit v16 on v12

--- a/solution.py
+++ b/solution.py
@@ -102,7 +102,7 @@
 
 def allsum(value, axis):
     size = SIZES[axis]
-    if size == 4 and axis == "cam":
+    if size == 4 and axis == "one_round":
         peers = [
             lax.ppermute(value, axis, [(i, i ^ mask) for i in range(size)]) for mask in (1, 2, 3)
         ]

time: 90.5 us -> 90 us (level)
  waiting for transfers between devices: 25.7 us -> 20.5 us
  starting transfers between devices: 21.3 us -> 26 us
    ppermute x8 -> x16, starting transfers between devices: 13.6 us -> 26 us  [allsum(): lax.ppermute(value, axis, [(i, i ^ step) for i in range(size)])]
    ppermute x12 -> x0, waiting for transfers between devices: 10.4 us -> none  [allsum(): lax.ppermute(value, axis, [(i, i ^ mask) for i in range(size)])]
    ppermute x12 -> x0, starting transfers between devices: 7.68 us -> none  [allsum(): lax.ppermute(value, axis, [(i, i ^ mask) for i in range(size)])]
    ppermute x8 -> x16, waiting for transfers between devices: 15.3 us -> 20.5 us  [allsum(): lax.ppermute(value, axis, [(i, i ^ step) for i in range(size)])]
  transfers between devices with their start and end apart: 20 -> 16, of which waited for: 12 -> 11; matrix products, arithmetic and copies ran while one was open for 10% -> 9% of each run, Pallas kernels for 0% -> 0%
where the time goes in v16:
time: 90 us; the launch traced here: 89.6 us
  starting transfers between devices  26 us (29%)
  waiting for transfers between devices  20.5 us (23%)
  other arithmetic  13.5 us (15%)
  matrix products  11.6 us (13%)
  between operations  11.3 us (13%)
  local copies, waits for them, and re-layouts  6.67 us (7%)
    ppermute x16, starting transfers between devices, allsum(): lax.ppermute(value, axis, [(i, i ^ step) for i in range(size)])  26 us
    ppermute x16, waiting for transfers between devices, allsum(): lax.ppermute(value, axis, [(i, i ^ step) for i in range(size)])  20.5 us
    dot_general x8, matrix products, segsum(): lax.dot_general(self.hot3, spread, (((1,), (1,)), ((), ())), preferred_el...  7.73 us
    dot_general x6, matrix products, gather(): lax.dot_general(stacked, self.hot3t, (((1,), (0,)), ((), ())), preferred_...  3.9 us
    select_n x8, other arithmetic, segsum(): jnp.where(self.low[None], part[:, None, :], jnp.zeros((), BF))  2.11 us
    reshape x12, local copies, waits for them, and re-layouts, segsum(): out.reshape(self.hi, ncol, self.lo).transpose(1, 0, 2)  1.92 us
    reduce_sum x3, other arithmetic, operate(): jnp.sum(img_all[-1:], axis=1, keepdims=True)  1.9 us
  transfers between devices with their start and end apart: 16, of which 11 were waited for; matrix products, arithmetic and copies ran while one was open for 9% of the time, Pallas kernels for 0%

profile of v16, /device:TPU:0, one launch (start us, length us, event | category | flops | bytes accessed | tf_op | source)
XLA Modules:
  0.0 89.6 jit_solution(17811791080374282664)
XLA Ops:
  0.6 0.7 add_select_fusion
  1.4 1.4 %multiply_reduce_fusion.6 = f32[9,4096]{1,0:T(8,128)S(1)} fusion(f32[2,9,4096]{2,0,1:T(2,128)} %param.7), kind=kLoop, calls=%fused_computation.122 | loop fusion | flops 110592 | bytes 442368 | tf_op jit(solution)/shard_map/reduce_sum | solution.py:130
  2.9 0.2 select_bitcast_fusion.11
  3.2 0.7 fusion.67
  4.2 3.1 %collective-permute-start = (f32[9,512]{1,0:T(8,128)S(1)}, f32[9,512]{1,0:T(8,128)S(1)}, u32[]{:S(2)}, u32[]{:S(2)}) collective-permute-start(f32[9,512]{1,0:T(8,128)S(1)} %reshape.1029), channel_id=1, source_target_pairs={{0,4},{4,0},{8,12},{12,8},{1,5},{5,1},{9,13},{13,9},{2,6},{6,2},{1... | collective-permute-start | bytes 55304 | tf_op jit(solution)/shard_map/ppermute | solution.py:114
  7.3 0.2 multiply_reduce_fusion.23
  7.9 0.4 broadcast_select_fusion.2
  8.3 0.2 fusion.27
  8.5 0.7 collective-permute-done
  9.2 3.0 %collective-permute-start.1 = (f32[9,512]{1,0:T(8,128)S(1)}, f32[9,512]{1,0:T(8,128)S(1)}, u32[]{:S(2)}, u32[]{:S(2)}) collective-permute-start(f32[9,512]{1,0:T(8,128)S(1)} %add.135), channel_id=1, source_target_pairs={{0,8},{4,12},{8,0},{12,4},{1,9},{5,13},{9,1},{13,5},{2,10},{6,14},... | collective-permute-start | bytes 55304 | tf_op jit(solution)/shard_map/ppermute | solution.py:114
  12.2 1.6 %fusion = f32[128,192]{0,1:T(8,128)S(1)} fusion(bf16[192,4096]{1,0:T(8,128)(2,1)S(1)} %bitcast.207, bf16[192,4096]{1,0:T(8,128)(2,1)S(1)} %bitcast.206, bf16[192,4096]{1,0:T(8,128)(2,1)S(1)} %bitcast.205, bf16[128,4096]{1,0:T(8,128)(2,1)S(1)} %fusion.27), kind=kOutput, calls=%fused_computation | convolution fusion | flops 627572736 | bytes 5865472 | tf_op jit(solution)/shard_map/dot_general | solution.py:46
  14.7 0.6 fusion.57
  15.3 0.4 copy-done
  16.0 0.2 broadcast_select_fusion.11
  16.3 1.1 %fusion.9 = f32[128,96]{0,1:T(8,128)S(1)} fusion(bf16[96,4096]{1,0:T(8,128)(2,1)S(1)} %bitcast.217, bf16[96,4096]{1,0:T(8,128)(2,1)S(1)} %bitcast.216, bf16[96,4096]{1,0:T(8,128)(2,1)S(1)} %bitcast.215, bf16[128,4096]{1,0:T(8,128)(2,1)S(1)} %fusion.27), kind=kOutput, calls=%fused_computation.14 | convolution fusion | flops 318504960 | bytes 3457024 | tf_op jit(solution)/shard_map/dot_general | solution.py:46
  17.8 0.5 collective-permute-start.2
  18.4 1.6 %collective-permute-start.5 = (f32[6,4096]{1,0:T(8,128)S(1)}, f32[6,4096]{1,0:T(8,128)S(1)}, u32[]{:S(2)}, u32[]{:S(2)}) collective-permute-start(f32[6,4096]{1,0:T(8,128)S(1)} %add.141), channel_id=1, source_target_pairs={{0,2},{1,3},{2,0},{3,1},{4,6},{5,7},{6,4},{7,5},{8,10},{9,11},{10,... | collective-permute-start | bytes 294920 | tf_op jit(solution)/shard_map/ppermute | solution.py:114
  20.0 0.9 %collective-permute-start.3 = (f32[4,4096]{1,0:T(4,128)S(1)}, f32[4,4096]{1,0:T(4,128)S(1)}, u32[]{:S(2)}, u32[]{:S(2)}) collective-permute-start(f32[4,4096]{1,0:T(4,128)S(1)} %fusion.154), channel_id=1, source_target_pairs={{0,2},{1,3},{2,0},{3,1},{4,6},{5,7},{6,4},{7,5},{8,10},{9,11},{10,... | collective-permute-start | bytes 196616 | tf_op jit(solution)/shard_map/ppermute | solution.py:114
  20.9 4.4 %collective-permute-done.3 = f32[4,4096]{1,0:T(4,128)S(1)} collective-permute-done((f32[4,4096]{1,0:T(4,128)S(1)}, f32[4,4096]{1,0:T(4,128)S(1)}, u32[]{:S(2)}, u32[]{:S(2)}) %collective-permute-start.3) | collective-permute-done | bytes 65568 | tf_op jit(solution)/shard_map/ppermute | solution.py:114
  26.6 0.7 fusion.54
  27.3 0.2 select_reduce_fusion.2
  27.7 0.4 multiply_reduce_fusion.4
  28.1 0.2 select_bitcast_fusion.8
  28.4 0.7 fusion.64
  29.5 1.8 %collective-permute-start.6 = (f32[10,512]{1,0:T(8,128)S(1)}, f32[10,512]{1,0:T(8,128)S(1)}, u32[]{:S(2)}, u32[]{:S(2)}) collective-permute-start(f32[10,512]{1,0:T(8,128)S(1)} %pad_maximum_fusion.21), channel_id=1, source_target_pairs={{0,4},{4,0},{8,12},{12,8},{1,5},{5,1},{9,13},{13,9},{2,6},{6,2},{1... | collective-permute-start | bytes 61448 | tf_op jit(solution)/shard_map/ppermute | solution.py:114
  31.5 2.0 %collective-permute-done.6 = f32[10,512]{1,0:T(8,128)S(1)} collective-permute-done((f32[10,512]{1,0:T(8,128)S(1)}, f32[10,512]{1,0:T(8,128)S(1)}, u32[]{:S(2)}, u32[]{:S(2)}) %collective-permute-start.6) | collective-permute-done | bytes 20512 | tf_op jit(solution)/shard_map/ppermute | solution.py:114
  33.5 2.8 %collective-permute-start.7 = (f32[10,512]{1,0:T(8,128)S(1)}, f32[10,512]{1,0:T(8,128)S(1)}, u32[]{:S(2)}, u32[]{:S(2)}) collective-permute-start(f32[10,512]{1,0:T(8,128)S(1)} %fusion.153), channel_id=1, source_target_pairs={{0,8},{4,12},{8,0},{12,4},{1,9},{5,13},{9,1},{13,5},{2,10},{6,14},... | collective-permute-start | bytes 61448 | tf_op jit(solution)/shard_map/ppermute | solution.py:114
  36.3 0.6 fusion.148
  36.9 1.5 %collective-permute-done.7 = f32[10,512]{1,0:T(8,128)S(1)} collective-permute-done((f32[10,512]{1,0:T(8,128)S(1)}, f32[10,512]{1,0:T(8,128)S(1)}, u32[]{:S(2)}, u32[]{:S(2)}) %collective-permute-start.7) | collective-permute-done | bytes 20512 | tf_op jit(solution)/shard_map/ppermute | solution.py:114
  38.4 0.7 slice_reduce_fusion.5
  41.5 0.6 fusion.56
  42.2 0.3 multiply_reduce_fusion.13
  42.6 0.2 broadcast_select_fusion.8
  42.8 1.1 %fusion.15 = f32[128,96]{0,1:T(8,128)S(1)} fusion(bf16[96,4096]{1,0:T(8,128)(2,1)S(1)} %bitcast.220, bf16[96,4096]{1,0:T(8,128)(2,1)S(1)} %bitcast.219, bf16[96,4096]{1,0:T(8,128)(2,1)S(1)} %bitcast.218, bf16[128,4096]{1,0:T(8,128)(2,1)S(1)} %fusion.27), kind=kOutput, calls=%fused_computation.20 | convolution fusion | flops 318504960 | bytes 3457024 | tf_op jit(solution)/shard_map/dot_general | solution.py:46
  44.5 1.2 %collective-permute-done.8 = f32[4,4096]{1,0:T(4,128)S(1)} collective-permute-done((f32[4,4096]{1,0:T(4,128)S(1)}, f32[4,4096]{1,0:T(4,128)S(1)}, u32[]{:S(2)}, u32[]{:S(2)}) %collective-permute-start.8) | collective-permute-done | bytes 65568 | tf_op jit(solution)/shard_map/ppermute | solution.py:114
  45.8 1.7 %collective-permute-start.9 = (f32[4,4096]{1,0:T(4,128)S(1)}, f32[4,4096]{1,0:T(4,128)S(1)}, u32[]{:S(2)}, u32[]{:S(2)}) collective-permute-start(f32[4,4096]{1,0:T(4,128)S(1)} %fusion.152), channel_id=1, source_target_pairs={{0,2},{1,3},{2,0},{3,1},{4,6},{5,7},{6,4},{7,5},{8,10},{9,11},{10,... | collective-permute-start | bytes 196616 | tf_op jit(solution)/shard_map/ppermute | solution.py:114
  47.5 2.6 %collective-permute-done.9 = f32[4,4096]{1,0:T(4,128)S(1)} collective-permute-done((f32[4,4096]{1,0:T(4,128)S(1)}, f32[4,4096]{1,0:T(4,128)S(1)}, u32[]{:S(2)}, u32[]{:S(2)}) %collective-permute-start.9) | collective-permute-done | bytes 65568 | tf_op jit(solution)/shard_map/ppermute | solution.py:114
  50.6 0.7 fusion.53
  51.3 0.2 select_reduce_fusion.1
  51.6 0.4 multiply_reduce_fusion.2
  52.1 0.2 select_bitcast_fusion.5
  52.3 0.7 fusion.61
  53.5 1.8 %collective-permute-start.10 = (f32[10,512]{1,0:T(8,128)S(1)}, f32[10,512]{1,0:T(8,128)S(1)}, u32[]{:S(2)}, u32[]{:S(2)}) collective-permute-start(f32[10,512]{1,0:T(8,128)S(1)} %pad_maximum_fusion.22), channel_id=1, source_target_pairs={{0,4},{4,0},{8,12},{12,8},{1,5},{5,1},{9,13},{13,9},{2,6},{6,2},{1... | collective-permute-start | bytes 61448 | tf_op jit(solution)/shard_map/ppermute | solution.py:114
  55.4 2.0 %collective-permute-done.10 = f32[10,512]{1,0:T(8,128)S(1)} collective-permute-done((f32[10,512]{1,0:T(8,128)S(1)}, f32[10,512]{1,0:T(8,128)S(1)}, u32[]{:S(2)}, u32[]{:S(2)}) %collective-permute-start.10) | collective-permute-done | bytes 20512 | tf_op jit(solution)/shard_map/ppermute | solution.py:114
  57.5 2.8 %collective-permute-start.11 = (f32[10,512]{1,0:T(8,128)S(1)}, f32[10,512]{1,0:T(8,128)S(1)}, u32[]{:S(2)}, u32[]{:S(2)}) collective-permute-start(f32[10,512]{1,0:T(8,128)S(1)} %fusion.151), channel_id=1, source_target_pairs={{0,8},{4,12},{8,0},{12,4},{1,9},{5,13},{9,1},{13,5},{2,10},{6,14},... | collective-permute-start | bytes 61448 | tf_op jit(solution)/shard_map/ppermute | solution.py:114
  60.3 0.6 fusion.147
  62.9 0.6 slice_reduce_fusion.4
  65.8 0.6 fusion.55
  66.8 0.2 broadcast_select_fusion.5
  67.0 1.1 %fusion.21 = f32[128,96]{0,1:T(8,128)S(1)} fusion(bf16[96,4096]{1,0:T(8,128)(2,1)S(1)} %bitcast.223, bf16[96,4096]{1,0:T(8,128)(2,1)S(1)} %bitcast.222, bf16[96,4096]{1,0:T(8,128)(2,1)S(1)} %bitcast.221, bf16[128,4096]{1,0:T(8,128)(2,1)S(1)} %fusion.27), kind=kOutput, calls=%fused_computation.26 | convolution fusion | flops 318504960 | bytes 3457024 | tf_op jit(solution)/shard_map/dot_general | solution.py:46
  68.6 1.2 %collective-permute-done.12 = f32[4,4096]{1,0:T(4,128)S(1)} collective-permute-done((f32[4,4096]{1,0:T(4,128)S(1)}, f32[4,4096]{1,0:T(4,128)S(1)}, u32[]{:S(2)}, u32[]{:S(2)}) %collective-permute-start.12) | collective-permute-done | bytes 65568 | tf_op jit(solution)/shard_map/ppermute | solution.py:114
  69.9 1.6 %collective-permute-start.13 = (f32[4,4096]{1,0:T(4,128)S(1)}, f32[4,4096]{1,0:T(4,128)S(1)}, u32[]{:S(2)}, u32[]{:S(2)}) collective-permute-start(f32[4,4096]{1,0:T(4,128)S(1)} %fusion.150), channel_id=1, source_target_pairs={{0,2},{1,3},{2,0},{3,1},{4,6},{5,7},{6,4},{7,5},{8,10},{9,11},{10,... | collective-permute-start | bytes 196616 | tf_op jit(solution)/shard_map/ppermute | solution.py:114
  71.5 2.8 %collective-permute-done.13 = f32[4,4096]{1,0:T(4,128)S(1)} collective-permute-done((f32[4,4096]{1,0:T(4,128)S(1)}, f32[4,4096]{1,0:T(4,128)S(1)}, u32[]{:S(2)}, u32[]{:S(2)}) %collective-permute-start.13) | collective-permute-done | bytes 65568 | tf_op jit(solution)/shard_map/ppermute | solution.py:114
  74.7 0.7 fusion.52
  75.4 0.3 select_reduce_fusion
  75.8 0.4 multiply_reduce_fusion
  76.3 0.2 select_bitcast_fusion.2
  76.5 0.7 fusion.58
  77.6 1.9 %collective-permute-start.14 = (f32[10,512]{1,0:T(8,128)S(1)}, f32[10,512]{1,0:T(8,128)S(1)}, u32[]{:S(2)}, u32[]{:S(2)}) collective-permute-start(f32[10,512]{1,0:T(8,128)S(1)} %pad_maximum_fusion.23), channel_id=1, source_target_pairs={{0,4},{4,0},{8,12},{12,8},{1,5},{5,1},{9,13},{13,9},{2,6},{6,2},{1... | collective-permute-start | bytes 61448 | tf_op jit(solution)/shard_map/ppermute | solution.py:114
  79.6 1.9 %collective-permute-done.14 = f32[10,512]{1,0:T(8,128)S(1)} collective-permute-done((f32[10,512]{1,0:T(8,128)S(1)}, f32[10,512]{1,0:T(8,128)S(1)}, u32[]{:S(2)}, u32[]{:S(2)}) %collective-permute-start.14) | collective-permute-done | bytes 20512 | tf_op jit(solution)/shard_map/ppermute | solution.py:114
  81.6 2.3 %collective-permute-start.15 = (f32[10,512]{1,0:T(8,128)S(1)}, f32[10,512]{1,0:T(8,128)S(1)}, u32[]{:S(2)}, u32[]{:S(2)}) collective-permute-start(f32[10,512]{1,0:T(8,128)S(1)} %fusion.149), channel_id=1, source_target_pairs={{0,8},{4,12},{8,0},{12,4},{1,9},{5,13},{9,1},{13,5},{2,10},{6,14},... | collective-permute-start | bytes 61448 | tf_op jit(solution)/shard_map/ppermute | solution.py:114
  83.8 0.6 fusion.146
  86.4 0.6 slice_reduce_fusion.3
  89.0 0.7 fusion.121
  (155 shorter events, 8.9 us)
Async XLA Ops:
  3.2 4.1 %copy-start.1 = (f32[2,3,4096]{2,0,1:T(2,128)S(1)}, f32[2,3,4096]{2,0,1:T(2,128)}, u32[]{:S(2)}) copy-start(f32[2,3,4096]{2,0,1:T(2,128)} %param.8) | copy-start | bytes 294916
  3.2 4.6 %copy-start.4 = (s32[4096]{0:T(1024)S(1)}, s32[4096]{0:T(1024)}, u32[]{:S(2)}) copy-start(s32[4096]{0:T(1024)} %param.10) | copy-start | bytes 49156
  4.2 5.0 %collective-permute-start = (f32[9,512]{1,0:T(8,128)S(1)}, f32[9,512]{1,0:T(8,128)S(1)}, u32[]{:S(2)}, u32[]{:S(2)}) collective-permute-start(f32[9,512]{1,0:T(8,128)S(1)} %reshape.1029), channel_id=1, source_target_pairs={{0,4},{4,0},{8,12},{12,8},{1,5},{5,1},{9,13},{13,9},{2,6},{6,2},{1... | collective-permute-start | bytes 55304 | tf_op jit(solution)/shard_map/ppermute | solution.py:114
  9.2 5.1 %collective-permute-start.1 = (f32[9,512]{1,0:T(8,128)S(1)}, f32[9,512]{1,0:T(8,128)S(1)}, u32[]{:S(2)}, u32[]{:S(2)}) collective-permute-start(f32[9,512]{1,0:T(8,128)S(1)} %add.135), channel_id=1, source_target_pairs={{0,8},{4,12},{8,0},{12,4},{1,9},{5,13},{9,1},{13,5},{2,10},{6,14},... | collective-permute-start | bytes 55304 | tf_op jit(solution)/shard_map/ppermute | solution.py:114
  12.2 2.1 %copy-start.2 = (f32[9,512]{1,0:T(8,128)S(1)}, f32[9,512]{1,0:T(8,128)}, u32[]{:S(2)}) copy-start(f32[9,512]{1,0:T(8,128)} %param.13) | copy-start | bytes 55300
  12.2 2.1 %copy-start.3 = (f32[512]{0:T(512)S(1)}, f32[512]{0:T(512)}, u32[]{:S(2)}) copy-start(f32[512]{0:T(512)} %param.12) | copy-start | bytes 6148
  14.2 4.2 %collective-permute-start.4 = (f32[6,4096]{1,0:T(8,128)S(1)}, f32[6,4096]{1,0:T(8,128)S(1)}, u32[]{:S(2)}, u32[]{:S(2)}) collective-permute-start(f32[6,4096]{1,0:T(8,128)S(1)} %reshape.1039), channel_id=1, source_target_pairs={{0,1},{1,0},{2,3},{3,2},{4,5},{5,4},{6,7},{7,6},{8,9},{9,8},{10,11... | collective-permute-start | bytes 294920 | tf_op jit(solution)/shard_map/ppermute | solution.py:114
  14.7 1.0 %copy-start = (f32[2,9,4096]{2,0,1:T(2,128)S(1)}, f32[2,9,4096]{2,0,1:T(2,128)}, u32[]{:S(2)}) copy-start(f32[2,9,4096]{2,0,1:T(2,128)} %param.7) | copy-start | bytes 884740
  17.4 8.1 %copy-start.5 = (f32[4096]{0:T(1024)S(1)}, f32[4096]{0:T(1024)}, u32[]{:S(2)}) copy-start(f32[4096]{0:T(1024)} %param.11) | copy-start | bytes 49156
  17.8 2.1 %collective-permute-start.2 = (f32[4,4096]{1,0:T(4,128)S(1)}, f32[4,4096]{1,0:T(4,128)S(1)}, u32[]{:S(2)}, u32[]{:S(2)}) collective-permute-start(f32[4,4096]{1,0:T(4,128)S(1)} %pad_maximum_fusion.18), channel_id=1, source_target_pairs={{0,1},{1,0},{2,3},{3,2},{4,5},{5,4},{6,7},{7,6},{8,9},{9,8},{10,11... | collective-permute-start | bytes 196616 | tf_op jit(solution)/shard_map/ppermute | solution.py:114
  18.4 6.9 %collective-permute-start.5 = (f32[6,4096]{1,0:T(8,128)S(1)}, f32[6,4096]{1,0:T(8,128)S(1)}, u32[]{:S(2)}, u32[]{:S(2)}) collective-permute-start(f32[6,4096]{1,0:T(8,128)S(1)} %add.141), channel_id=1, source_target_pairs={{0,2},{1,3},{2,0},{3,1},{4,6},{5,7},{6,4},{7,5},{8,10},{9,11},{10,... | collective-permute-start | bytes 294920 | tf_op jit(solution)/shard_map/ppermute | solution.py:114
  20.0 5.3 %collective-permute-start.3 = (f32[4,4096]{1,0:T(4,128)S(1)}, f32[4,4096]{1,0:T(4,128)S(1)}, u32[]{:S(2)}, u32[]{:S(2)}) collective-permute-start(f32[4,4096]{1,0:T(4,128)S(1)} %fusion.154), channel_id=1, source_target_pairs={{0,2},{1,3},{2,0},{3,1},{4,6},{5,7},{6,4},{7,5},{8,10},{9,11},{10,... | collective-permute-start | bytes 196616 | tf_op jit(solution)/shard_map/ppermute | solution.py:114
  29.5 4.0 %collective-permute-start.6 = (f32[10,512]{1,0:T(8,128)S(1)}, f32[10,512]{1,0:T(8,128)S(1)}, u32[]{:S(2)}, u32[]{:S(2)}) collective-permute-start(f32[10,512]{1,0:T(8,128)S(1)} %pad_maximum_fusion.21), channel_id=1, source_target_pairs={{0,4},{4,0},{8,12},{12,8},{1,5},{5,1},{9,13},{13,9},{2,6},{6,2},{1... | collective-permute-start | bytes 61448 | tf_op jit(solution)/shard_map/ppermute | solution.py:114
  33.5 4.9 %collective-permute-start.7 = (f32[10,512]{1,0:T(8,128)S(1)}, f32[10,512]{1,0:T(8,128)S(1)}, u32[]{:S(2)}, u32[]{:S(2)}) collective-permute-start(f32[10,512]{1,0:T(8,128)S(1)} %fusion.153), channel_id=1, source_target_pairs={{0,8},{4,12},{8,0},{12,4},{1,9},{5,13},{9,1},{13,5},{2,10},{6,14},... | collective-permute-start | bytes 61448 | tf_op jit(solution)/shard_map/ppermute | solution.py:114
  44.4 1.3 %collective-permute-start.8 = (f32[4,4096]{1,0:T(4,128)S(1)}, f32[4,4096]{1,0:T(4,128)S(1)}, u32[]{:S(2)}, u32[]{:S(2)}) collective-permute-start(f32[4,4096]{1,0:T(4,128)S(1)} %pad_maximum_fusion.19), channel_id=1, source_target_pairs={{0,1},{1,0},{2,3},{3,2},{4,5},{5,4},{6,7},{7,6},{8,9},{9,8},{10,11... | collective-permute-start | bytes 196616 | tf_op jit(solution)/shard_map/ppermute | solution.py:114
  45.8 4.3 %collective-permute-start.9 = (f32[4,4096]{1,0:T(4,128)S(1)}, f32[4,4096]{1,0:T(4,128)S(1)}, u32[]{:S(2)}, u32[]{:S(2)}) collective-permute-start(f32[4,4096]{1,0:T(4,128)S(1)} %fusion.152), channel_id=1, source_target_pairs={{0,2},{1,3},{2,0},{3,1},{4,6},{5,7},{6,4},{7,5},{8,10},{9,11},{10,... | collective-permute-start | bytes 196616 | tf_op jit(solution)/shard_map/ppermute | solution.py:114
  53.5 4.0 %collective-permute-start.10 = (f32[10,512]{1,0:T(8,128)S(1)}, f32[10,512]{1,0:T(8,128)S(1)}, u32[]{:S(2)}, u32[]{:S(2)}) collective-permute-start(f32[10,512]{1,0:T(8,128)S(1)} %pad_maximum_fusion.22), channel_id=1, source_target_pairs={{0,4},{4,0},{8,12},{12,8},{1,5},{5,1},{9,13},{13,9},{2,6},{6,2},{1... | collective-permute-start | bytes 61448 | tf_op jit(solution)/shard_map/ppermute | solution.py:114
  57.5 5.4 %collective-permute-start.11 = (f32[10,512]{1,0:T(8,128)S(1)}, f32[10,512]{1,0:T(8,128)S(1)}, u32[]{:S(2)}, u32[]{:S(2)}) collective-permute-start(f32[10,512]{1,0:T(8,128)S(1)} %fusion.151), channel_id=1, source_target_pairs={{0,8},{4,12},{8,0},{12,4},{1,9},{5,13},{9,1},{13,5},{2,10},{6,14},... | collective-permute-start | bytes 61448 | tf_op jit(solution)/shard_map/ppermute | solution.py:114
  68.5 1.3 %collective-permute-start.12 = (f32[4,4096]{1,0:T(4,128)S(1)}, f32[4,4096]{1,0:T(4,128)S(1)}, u32[]{:S(2)}, u32[]{:S(2)}) collective-permute-start(f32[4,4096]{1,0:T(4,128)S(1)} %pad_maximum_fusion.20), channel_id=1, source_target_pairs={{0,1},{1,0},{2,3},{3,2},{4,5},{5,4},{6,7},{7,6},{8,9},{9,8},{10,11... | collective-permute-start | bytes 196616 | tf_op jit(solution)/shard_map/ppermute | solution.py:114
  69.9 4.3 %collective-permute-start.13 = (f32[4,4096]{1,0:T(4,128)S(1)}, f32[4,4096]{1,0:T(4,128)S(1)}, u32[]{:S(2)}, u32[]{:S(2)}) collective-permute-start(f32[4,4096]{1,0:T(4,128)S(1)} %fusion.150), channel_id=1, source_target_pairs={{0,2},{1,3},{2,0},{3,1},{4,6},{5,7},{6,4},{7,5},{8,10},{9,11},{10,... | collective-permute-start | bytes 196616 | tf_op jit(solution)/shard_map/ppermute | solution.py:114
  77.6 4.0 %collective-permute-start.14 = (f32[10,512]{1,0:T(8,128)S(1)}, f32[10,512]{1,0:T(8,128)S(1)}, u32[]{:S(2)}, u32[]{:S(2)}) collective-permute-start(f32[10,512]{1,0:T(8,128)S(1)} %pad_maximum_fusion.23), channel_id=1, source_target_pairs={{0,4},{4,0},{8,12},{12,8},{1,5},{5,1},{9,13},{13,9},{2,6},{6,2},{1... | collective-permute-start | bytes 61448 | tf_op jit(solution)/shard_map/ppermute | solution.py:114
  81.6 4.9 %collective-permute-start.15 = (f32[10,512]{1,0:T(8,128)S(1)}, f32[10,512]{1,0:T(8,128)S(1)}, u32[]{:S(2)}, u32[]{:S(2)}) collective-permute-start(f32[10,512]{1,0:T(8,128)S(1)} %fusion.149), channel_id=1, source_target_pairs={{0,8},{4,12},{8,0},{12,4},{1,9},{5,13},{9,1},{13,5},{2,10},{6,14},... | collective-permute-start | bytes 61448 | tf_op jit(solution)/shard_map/ppermute | solution.py:114

commit v17 on v16

--- a/solution.py
+++ b/solution.py
@@ -148,13 +148,12 @@
         u = u_all[:3]
         got = jnp.sum(u_all[3:].reshape(-1)[: count * ncam].reshape(count, ncam), axis=1, keepdims=True)
         w = jnp.sum(inv * u[None, :, :], axis=1)
-        pt_terms = jnp.sum(u * w, axis=0).reshape(-1, ncam)
-        pt_row = u_all[3:].reshape(-1)[(count - 1) * ncam : count * ncam] - jnp.sum(pt_terms, axis=0)
+        pt_row = jnp.broadcast_to(got[count - 1] - jnp.sum(u * w), (ncam,))
         z = y - jnp.sum(point_jac * by_point.gather(w)[None], axis=1)
         img_part = by_cam.segsum(jnp.sum(cam_jac * z[:, None, :], axis=0))
         img_all = allsum(jnp.concatenate([img_part, pt_row[None]], axis=0), "pts")
         image = cam_damp[None, :] * vec + img_all[:-1]
-        energy = got[count - 2 : count - 1] + jnp.sum(img_all[-1:], axis=1, keepdims=True)
+        energy = got[count - 2] + img_all[-1:]
         return image, got, energy
 
     solution = jnp.zeros_like(reduced_rhs)

time: 90 us -> 106 us (1.18)
  other arithmetic: 13.5 us -> 23.8 us
  waiting for transfers between devices: 20.5 us -> 25.5 us
  matrix products: 11.6 us -> 14.9 us
  starting transfers between devices: 26 us -> 23.3 us
  between operations: 11.3 us -> 9.08 us
  local copies, waits for them, and re-layouts: 6.67 us -> 8.56 us
    div x0 -> x3, other arithmetic: none -> 5.08 us  [the longest x2 3.82 us: on_device(): alpha = new_rz / curv]
    ppermute x16, waiting for transfers between devices: 20.5 us -> 25.5 us  [allsum(): lax.ppermute(value, axis, [(i, i ^ step) for i in range(size)])]
    ppermute x16, starting transfers between devices: 26 us -> 23.3 us  [allsum(): lax.ppermute(value, axis, [(i, i ^ step) for i in range(size)])]
    reduce_sum x6, other arithmetic: 0.19 us -> 2.53 us  [lanes(): return jnp.sum(terms.reshape(-1, ncam), axis=0)]
    dot_general x8, matrix products: 7.73 us -> 9.45 us  [segsum(): lax.dot_general(self.hot3, spread, (((1,), (1,)), ((), ())), preferred_el...]
    select_n x8, other arithmetic: 2.11 us -> 3.78 us  [segsum(): jnp.where(self.low[None], part[:, None, :], jnp.zeros((), BF))]
    dot_general x6, matrix products: 3.9 us -> 5.46 us  [gather(): lax.dot_general(stacked, self.hot3t, (((1,), (0,)), ((), ())), preferred_...]
  transfers between devices with their start and end apart: 16 -> 16, of which waited for: 11 -> 13; matrix products, arithmetic and copies ran while one was open for 9% -> 8% of each run, Pallas kernels for 0% -> 0%
where the time goes in v17:
time: 106 us; the launch traced here: 105 us
  waiting for transfers between devices  25.5 us (24%)
  other arithmetic  23.8 us (22%)
  starting transfers between devices  23.3 us (22%)
  matrix products  14.9 us (14%)
  between operations  9.08 us (9%)
  local copies, waits for them, and re-layouts  8.56 us (8%)
    ppermute x16, waiting for transfers between devices, allsum(): lax.ppermute(value, axis, [(i, i ^ step) for i in range(size)])  25.5 us
    ppermute x16, starting transfers between devices, allsum(): lax.ppermute(value, axis, [(i, i ^ step) for i in range(size)])  23.3 us
    dot_general x8, matrix products, segsum(): lax.dot_general(self.hot3, spread, (((1,), (1,)), ((), ())), preferred_el...  9.45 us
    dot_general x6, matrix products, gather(): lax.dot_general(stacked, self.hot3t, (((1,), (0,)), ((), ())), preferred_...  5.46 us
    div x2, other arithmetic, on_device(): alpha = new_rz / curv  3.82 us
    select_n x8, other arithmetic, segsum(): jnp.where(self.low[None], part[:, None, :], jnp.zeros((), BF))  3.78 us
    reduce_sum x6, other arithmetic, lanes(): return jnp.sum(terms.reshape(-1, ncam), axis=0)  2.53 us
  transfers between devices with their start and end apart: 16, of which 13 were waited for; matrix products, arithmetic and copies ran while one was open for 8% of the time, Pallas kernels for 0%

profile of v17, /device:TPU:0, one launch (start us, length us, event | category | flops | bytes accessed | tf_op | source)
XLA Modules:
  0.0 105.2 jit_solution(10347949580878608642)
XLA Ops:
  0.6 0.7 add_select_fusion
  1.4 1.4 %multiply_reduce_fusion.6 = f32[9,4096]{1,0:T(8,128)S(1)} fusion(f32[2,9,4096]{2,0,1:T(2,128)} %param.7), kind=kLoop, calls=%fused_computation.122 | loop fusion | flops 110592 | bytes 442368 | tf_op jit(solution)/shard_map/reduce_sum | solution.py:130
  3.2 0.5 copy-done.2
  3.7 0.7 fusion.67
  4.7 3.1 %collective-permute-start = (f32[9,512]{1,0:T(8,128)S(1)}, f32[9,512]{1,0:T(8,128)S(1)}, u32[]{:S(2)}, u32[]{:S(2)}) collective-permute-start(f32[9,512]{1,0:T(8,128)S(1)} %reshape.1052), channel_id=1, source_target_pairs={{0,4},{4,0},{8,12},{12,8},{1,5},{5,1},{9,13},{13,9},{2,6},{6,2},{1... | collective-permute-start | bytes 55304 | tf_op jit(solution)/shard_map/ppermute | solution.py:114
  8.4 2.1 %broadcast_select_fusion.2 = (bf16[6,32,4096]{2,1,0:T(8,128)(2,1)S(1)}, bf16[6,32,4096]{2,1,0:T(8,128)(2,1)}, bf16[6,32,4096]{2,1,0:T(8,128)(2,1)}) fusion(pred[32,4096]{1,0:T(8,128)(4,1)S(1)} %iota_compare_fusion.2, bf16[6,4096]{1,0:T(8,128)(2,1)S(1)} %get-tuple-element.62, bf16[6,4096]{1,0:T(8,128)(2,1)S(1)} %get-tuple-element.64, ...), kind=kLoop, calls=%fused_computation.65 | loop fusion | flops 2359296 | bytes 4997120 | tf_op jit(solution)/shard_map/jit(_where)/select_n | solution.py:42
  10.6 2.7 %collective-permute-start.1 = (f32[9,512]{1,0:T(8,128)S(1)}, f32[9,512]{1,0:T(8,128)S(1)}, u32[]{:S(2)}, u32[]{:S(2)}) collective-permute-start(f32[9,512]{1,0:T(8,128)S(1)} %add.176), channel_id=1, source_target_pairs={{0,8},{4,12},{8,0},{12,4},{1,9},{5,13},{9,1},{13,5},{2,10},{6,14},... | collective-permute-start | bytes 55304 | tf_op jit(solution)/shard_map/ppermute | solution.py:114
  13.4 2.0 %collective-permute-done.1 = f32[9,512]{1,0:T(8,128)S(1)} collective-permute-done((f32[9,512]{1,0:T(8,128)S(1)}, f32[9,512]{1,0:T(8,128)S(1)}, u32[]{:S(2)}, u32[]{:S(2)}) %collective-permute-start.1) | collective-permute-done | bytes 18464 | tf_op jit(solution)/shard_map/ppermute | solution.py:114
  15.8 2.1 %fusion.57 = f32[9,4096]{1,0:T(8,128)S(1)} fusion(bf16[64,4096]{1,0:T(8,128)(2,1)} %copy-done.2, pred[8,4096]{1,0:T(8,128)(4,1)S(1)} %iota_compare_fusion.3, bf16[72,64]{1,0:T(8,128)(2,1)S(1)} %get-tuple-element.95, bf16[72,64]{1,0:T(8,128)(2,1)S(1)} %get-tuple-element.96, bf16[72,64]{1,0:T(8,128)(2,1)S(1)} %get-tuple-element.94), kind=kOutput, calls=%fused_computation.71 | convolution fusion | flops 118600704 | bytes 732160 | tf_op jit(solution)/shard_map/dot_general | solution.py:55
  18.3 0.6 mul.584
  19.2 1.1 %fusion.9 = f32[128,96]{0,1:T(8,128)S(1)} fusion(bf16[96,4096]{1,0:T(8,128)(2,1)S(1)} %bitcast.217, bf16[96,4096]{1,0:T(8,128)(2,1)S(1)} %bitcast.216, bf16[96,4096]{1,0:T(8,128)(2,1)S(1)} %bitcast.215, bf16[128,4096]{1,0:T(8,128)(2,1)S(1)} %fusion.27), kind=kOutput, calls=%fused_computation.14 | convolution fusion | flops 318504960 | bytes 3457024 | tf_op jit(solution)/shard_map/dot_general | solution.py:46
  20.6 0.8 mul.585
  21.6 3.3 %fusion = f32[128,192]{0,1:T(8,128)S(1)} fusion(bf16[192,4096]{1,0:T(8,128)(2,1)} %bitcast.207, bf16[192,4096]{1,0:T(8,128)(2,1)} %bitcast.206, bf16[192,4096]{1,0:T(8,128)(2,1)S(1)} %bitcast.205, bf16[128,4096]{1,0:T(8,128)(2,1)S(1)} %fusion.27), kind=kOutput, calls=%fused_computation | convolution fusion | flops 627572736 | bytes 5865472 | tf_op jit(solution)/shard_map/dot_general | solution.py:46
  25.3 0.6 collective-permute-start.4
  25.8 0.9 fusion.155
  26.7 1.6 %collective-permute-start.3 = (f32[4,4096]{1,0:T(4,128)S(1)}, f32[4,4096]{1,0:T(4,128)S(1)}, u32[]{:S(2)}, u32[]{:S(2)}) collective-permute-start(f32[4,4096]{1,0:T(4,128)S(1)} %fusion.155), channel_id=1, source_target_pairs={{0,2},{1,3},{2,0},{3,1},{4,6},{5,7},{6,4},{7,5},{8,10},{9,11},{10,... | collective-permute-start | bytes 196616 | tf_op jit(solution)/shard_map/ppermute | solution.py:114
  28.3 0.6 collective-permute-start.5
  28.9 2.5 %collective-permute-done.3 = f32[4,4096]{1,0:T(4,128)S(1)} collective-permute-done((f32[4,4096]{1,0:T(4,128)S(1)}, f32[4,4096]{1,0:T(4,128)S(1)}, u32[]{:S(2)}, u32[]{:S(2)}) %collective-permute-start.3) | collective-permute-done | bytes 65568 | tf_op jit(solution)/shard_map/ppermute | solution.py:114
  31.5 0.7 fusion.152
  32.2 1.6 %collective-permute-done.5 = f32[6,4096]{1,0:T(8,128)S(1)} collective-permute-done((f32[6,4096]{1,0:T(8,128)S(1)}, f32[6,4096]{1,0:T(8,128)S(1)}, u32[]{:S(2)}, u32[]{:S(2)}) %collective-permute-start.5) | collective-permute-done | bytes 98336 | tf_op jit(solution)/shard_map/ppermute | solution.py:114
  34.8 0.6 multiply_reduce_fusion.18
  35.6 0.7 fusion.54
  36.4 0.3 select_reduce_fusion.2
  36.7 0.4 multiply_reduce_fusion.4
  37.4 0.7 copy-done.3
  38.2 0.7 fusion.64
  40.6 1.2 %collective-permute-start.6 = (f32[10,512]{1,0:T(8,128)S(1)}, f32[10,512]{1,0:T(8,128)S(1)}, u32[]{:S(2)}, u32[]{:S(2)}) collective-permute-start(f32[10,512]{1,0:T(8,128)S(1)} %concatenate.98), channel_id=1, source_target_pairs={{0,4},{4,0},{8,12},{12,8},{1,5},{5,1},{9,13},{13,9},{2,6},{6,2},{1... | collective-permute-start | bytes 61448 | tf_op jit(solution)/shard_map/ppermute | solution.py:114
  41.8 2.8 %collective-permute-done.6 = f32[10,512]{1,0:T(8,128)S(1)} collective-permute-done((f32[10,512]{1,0:T(8,128)S(1)}, f32[10,512]{1,0:T(8,128)S(1)}, u32[]{:S(2)}, u32[]{:S(2)}) %collective-permute-start.6) | collective-permute-done | bytes 20512 | tf_op jit(solution)/shard_map/ppermute | solution.py:114
  44.5 2.7 %collective-permute-start.7 = (f32[10,512]{1,0:T(8,128)S(1)}, f32[10,512]{1,0:T(8,128)S(1)}, u32[]{:S(2)}, u32[]{:S(2)}) collective-permute-start(f32[10,512]{1,0:T(8,128)S(1)} %pad_add_fusion.2), channel_id=1, source_target_pairs={{0,8},{4,12},{8,0},{12,4},{1,9},{5,13},{9,1},{13,5},{2,10},{6,14},... | collective-permute-start | bytes 61448 | tf_op jit(solution)/shard_map/ppermute | solution.py:114
  47.2 2.2 %collective-permute-done.7 = f32[10,512]{1,0:T(8,128)S(1)} collective-permute-done((f32[10,512]{1,0:T(8,128)S(1)}, f32[10,512]{1,0:T(8,128)S(1)}, u32[]{:S(2)}, u32[]{:S(2)}) %collective-permute-start.7) | collective-permute-done | bytes 20512 | tf_op jit(solution)/shard_map/ppermute | solution.py:114
  49.4 1.3 %broadcast_divide_fusion.1 = f32[1,512]{1,0:T(1,128)S(1)} fusion(f32[]{:T(128)} %bitcast.17, f32[10,512]{1,0:T(8,128)S(1)} %add.190, f32[]{:T(128)} %bitcast.18), kind=kLoop, calls=%fused_computation.301 | loop fusion | flops 1024 | bytes 4104 | tf_op jit(solution)/shard_map/div | solution.py:165
  50.7 1.2 %multiply_reduce_fusion.22 = (f32[512]{0:T(512)S(1)}, f32[512]{0:T(512)S(1)}, f32[512]{0:T(512)}, f32[9,512]{1,0:T(8,128)S(1)}, f32[9,512]{1,0:T(8,128)S(1)}, /*index=5*/f32[9,512]{1,0:T(8,128)}) fusion(f32[512]{0:T(512)S(1)} %copy-done.9, f32[9,512]{1,0:T(8,128)S(1)} %get-tuple-element.26, f32[9,512]{1,0:T(8,128)S(1)} %copy-done.6, f32[512]{0:T(512)S(1)} %bitcast.255, ...), kind=kLoop, calls=%fused_computation.249 | loop fusion | flops 53760 | bytes 139264 | tf_op jit(solution)/shard_map/reduce_sum | solution.py:139
  52.3 0.6 fusion.56
  53.0 0.3 multiply_reduce_fusion.13
  53.7 1.1 %fusion.15 = f32[128,96]{0,1:T(8,128)S(1)} fusion(bf16[96,4096]{1,0:T(8,128)(2,1)S(1)} %bitcast.220, bf16[96,4096]{1,0:T(8,128)(2,1)S(1)} %bitcast.219, bf16[96,4096]{1,0:T(8,128)(2,1)S(1)} %bitcast.218, bf16[128,4096]{1,0:T(8,128)(2,1)S(1)} %fusion.27), kind=kOutput, calls=%fused_computation.20 | convolution fusion | flops 318504960 | bytes 3457024 | tf_op jit(solution)/shard_map/dot_general | solution.py:46
  55.3 1.2 %collective-permute-done.8 = f32[4,4096]{1,0:T(4,128)S(1)} collective-permute-done((f32[4,4096]{1,0:T(4,128)S(1)}, f32[4,4096]{1,0:T(4,128)S(1)}, u32[]{:S(2)}, u32[]{:S(2)}) %collective-permute-start.8) | collective-permute-done | bytes 65568 | tf_op jit(solution)/shard_map/ppermute | solution.py:114
  56.6 1.3 %collective-permute-start.9 = (f32[4,4096]{1,0:T(4,128)S(1)}, f32[4,4096]{1,0:T(4,128)S(1)}, u32[]{:S(2)}, u32[]{:S(2)}) collective-permute-start(f32[4,4096]{1,0:T(4,128)S(1)} %fusion.154), channel_id=1, source_target_pairs={{0,2},{1,3},{2,0},{3,1},{4,6},{5,7},{6,4},{7,5},{8,10},{9,11},{10,... | collective-permute-start | bytes 196616 | tf_op jit(solution)/shard_map/ppermute | solution.py:114
  57.9 3.0 %collective-permute-done.9 = f32[4,4096]{1,0:T(4,128)S(1)} collective-permute-done((f32[4,4096]{1,0:T(4,128)S(1)}, f32[4,4096]{1,0:T(4,128)S(1)}, u32[]{:S(2)}, u32[]{:S(2)}) %collective-permute-start.9) | collective-permute-done | bytes 65568 | tf_op jit(solution)/shard_map/ppermute | solution.py:114
  61.1 0.6 multiply_reduce_fusion.17
  62.0 0.6 fusion.151
  62.8 0.7 fusion.53
  63.9 0.4 multiply_reduce_fusion.2
  64.6 0.7 fusion.61
  66.9 1.2 %collective-permute-start.10 = (f32[10,512]{1,0:T(8,128)S(1)}, f32[10,512]{1,0:T(8,128)S(1)}, u32[]{:S(2)}, u32[]{:S(2)}) collective-permute-start(f32[10,512]{1,0:T(8,128)S(1)} %concatenate.104), channel_id=1, source_target_pairs={{0,4},{4,0},{8,12},{12,8},{1,5},{5,1},{9,13},{13,9},{2,6},{6,2},{1... | collective-permute-start | bytes 61448 | tf_op jit(solution)/shard_map/ppermute | solution.py:114
  68.1 2.8 %collective-permute-done.10 = f32[10,512]{1,0:T(8,128)S(1)} collective-permute-done((f32[10,512]{1,0:T(8,128)S(1)}, f32[10,512]{1,0:T(8,128)S(1)}, u32[]{:S(2)}, u32[]{:S(2)}) %collective-permute-start.10) | collective-permute-done | bytes 20512 | tf_op jit(solution)/shard_map/ppermute | solution.py:114
  70.9 2.8 %collective-permute-start.11 = (f32[10,512]{1,0:T(8,128)S(1)}, f32[10,512]{1,0:T(8,128)S(1)}, u32[]{:S(2)}, u32[]{:S(2)}) collective-permute-start(f32[10,512]{1,0:T(8,128)S(1)} %pad_add_fusion.1), channel_id=1, source_target_pairs={{0,8},{4,12},{8,0},{12,4},{1,9},{5,13},{9,1},{13,5},{2,10},{6,14},... | collective-permute-start | bytes 61448 | tf_op jit(solution)/shard_map/ppermute | solution.py:114
  75.8 2.5 %broadcast_divide_fusion = (f32[1,512]{1,0:T(1,128)S(1)}, f32[1,512]{1,0:T(1,128)}) fusion(f32[]{:T(128)} %bitcast.70, f32[10,512]{1,0:T(8,128)S(1)} %add.190, f32[]{:T(128)} %bitcast.18, f32[]{:T(128)} %bitcast.83, f32[]{:T(128)} %bitcast.82, f32[10,512]{1,0:T(8,128)S(1)} %add.198, f32[]{:T(128)} %bitcast.71), kind=kLoop, calls=%fused_computation.300 | loop fusion | flops 3584 | bytes 8212 | tf_op jit(solution)/shard_map/div | solution.py:176
  78.3 1.2 %multiply_reduce_fusion.20 = (f32[512]{0:T(512)S(1)}, f32[512]{0:T(512)}, f32[512]{0:T(512)}, f32[9,512]{1,0:T(8,128)S(1)}, f32[9,512]{1,0:T(8,128)}) fusion(f32[9,512]{1,0:T(8,128)S(1)} %get-tuple-element.21, f32[512]{0:T(512)S(1)} %bitcast.257, f32[512]{0:T(512)S(1)} %copy-done.9, f32[9,512]{1,0:T(8,128)S(1)} %get-tuple-element.26, ...), kind=kLoop, calls=%fused_computation.246 | loop fusion | flops 62976 | bytes 139268 | tf_op jit(solution)/shard_map/reduce_sum | solution.py:139
  79.9 0.6 fusion.55
  81.1 1.1 %fusion.21 = f32[128,96]{0,1:T(8,128)S(1)} fusion(bf16[96,4096]{1,0:T(8,128)(2,1)S(1)} %bitcast.223, bf16[96,4096]{1,0:T(8,128)(2,1)S(1)} %bitcast.222, bf16[96,4096]{1,0:T(8,128)(2,1)S(1)} %bitcast.221, bf16[128,4096]{1,0:T(8,128)(2,1)S(1)} %fusion.27), kind=kOutput, calls=%fused_computation.26 | convolution fusion | flops 318504960 | bytes 3457024 | tf_op jit(solution)/shard_map/dot_general | solution.py:46
  82.8 1.2 %collective-permute-done.12 = f32[4,4096]{1,0:T(4,128)S(1)} collective-permute-done((f32[4,4096]{1,0:T(4,128)S(1)}, f32[4,4096]{1,0:T(4,128)S(1)}, u32[]{:S(2)}, u32[]{:S(2)}) %collective-permute-start.12) | collective-permute-done | bytes 65568 | tf_op jit(solution)/shard_map/ppermute | solution.py:114
  84.0 1.3 %collective-permute-start.13 = (f32[4,4096]{1,0:T(4,128)S(1)}, f32[4,4096]{1,0:T(4,128)S(1)}, u32[]{:S(2)}, u32[]{:S(2)}) collective-permute-start(f32[4,4096]{1,0:T(4,128)S(1)} %fusion.153), channel_id=1, source_target_pairs={{0,2},{1,3},{2,0},{3,1},{4,6},{5,7},{6,4},{7,5},{8,10},{9,11},{10,... | collective-permute-start | bytes 196616 | tf_op jit(solution)/shard_map/ppermute | solution.py:114
  85.4 3.0 %collective-permute-done.13 = f32[4,4096]{1,0:T(4,128)S(1)} collective-permute-done((f32[4,4096]{1,0:T(4,128)S(1)}, f32[4,4096]{1,0:T(4,128)S(1)}, u32[]{:S(2)}, u32[]{:S(2)}) %collective-permute-start.13) | collective-permute-done | bytes 65568 | tf_op jit(solution)/shard_map/ppermute | solution.py:114
  88.6 0.6 multiply_reduce_fusion.16
  89.5 0.7 fusion.150
  90.3 0.7 fusion.52
  91.0 0.3 select_reduce_fusion
  91.3 0.4 multiply_reduce_fusion
  92.1 0.7 fusion.58
  94.3 1.2 %collective-permute-start.14 = (f32[10,512]{1,0:T(8,128)S(1)}, f32[10,512]{1,0:T(8,128)S(1)}, u32[]{:S(2)}, u32[]{:S(2)}) collective-permute-start(f32[10,512]{1,0:T(8,128)S(1)} %concatenate.110), channel_id=1, source_target_pairs={{0,4},{4,0},{8,12},{12,8},{1,5},{5,1},{9,13},{13,9},{2,6},{6,2},{1... | collective-permute-start | bytes 61448 | tf_op jit(solution)/shard_map/ppermute | solution.py:114
  95.5 2.8 %collective-permute-done.14 = f32[10,512]{1,0:T(8,128)S(1)} collective-permute-done((f32[10,512]{1,0:T(8,128)S(1)}, f32[10,512]{1,0:T(8,128)S(1)}, u32[]{:S(2)}, u32[]{:S(2)}) %collective-permute-start.14) | collective-permute-done | bytes 20512 | tf_op jit(solution)/shard_map/ppermute | solution.py:114
  98.3 2.9 %collective-permute-start.15 = (f32[10,512]{1,0:T(8,128)S(1)}, f32[10,512]{1,0:T(8,128)S(1)}, u32[]{:S(2)}, u32[]{:S(2)}) collective-permute-start(f32[10,512]{1,0:T(8,128)S(1)} %pad_add_fusion), channel_id=1, source_target_pairs={{0,8},{4,12},{8,0},{12,4},{1,9},{5,13},{9,1},{13,5},{2,10},{6,14},... | collective-permute-start | bytes 61448 | tf_op jit(solution)/shard_map/ppermute | solution.py:114
  103.2 1.3 %fusion.129 = f32[1,512]{1,0:T(1,128)S(1)} fusion(f32[1,512]{1,0:T(1,128)S(1)} %copy-done.15, f32[10,512]{1,0:T(8,128)S(1)} %add.213, f32[]{:T(128)} %bitcast.111, f32[]{:T(128)} %bitcast.110, f32[]{:T(128)} %bitcast.99, f32[]{:T(128)} %bitcast.98), kind=kLoop, calls=%fused_computation.298 | loop fusion | flops 3072 | bytes 6160 | tf_op jit(solution)/shard_map/div | solution.py:176
  104.5 0.7 fusion.121
  (166 shorter events, 11.1 us)
Async XLA Ops:
  2.9 0.8 copy-start.2
  3.7 4.2 %copy-start.1 = (f32[2,3,4096]{2,0,1:T(2,128)S(1)}, f32[2,3,4096]{2,0,1:T(2,128)}, u32[]{:S(2)}) copy-start(f32[2,3,4096]{2,0,1:T(2,128)} %param.8) | copy-start | bytes 294916
  3.7 4.6 %copy-start.10 = (s32[4096]{0:T(1024)S(1)}, s32[4096]{0:T(1024)}, u32[]{:S(2)}) copy-start(s32[4096]{0:T(1024)} %param.10) | copy-start | bytes 49156
  4.7 5.8 %collective-permute-start = (f32[9,512]{1,0:T(8,128)S(1)}, f32[9,512]{1,0:T(8,128)S(1)}, u32[]{:S(2)}, u32[]{:S(2)}) collective-permute-start(f32[9,512]{1,0:T(8,128)S(1)} %reshape.1052), channel_id=1, source_target_pairs={{0,4},{4,0},{8,12},{12,8},{1,5},{5,1},{9,13},{13,9},{2,6},{6,2},{1... | collective-permute-start | bytes 55304 | tf_op jit(solution)/shard_map/ppermute | solution.py:114
  8.4 7.0 %copy-start.5 = (f32[9,512]{1,0:T(8,128)S(1)}, f32[9,512]{1,0:T(8,128)}, u32[]{:S(2)}) copy-start(f32[9,512]{1,0:T(8,128)} %param.13) | copy-start | bytes 55300
  8.4 7.0 %copy-start.8 = (f32[512]{0:T(512)S(1)}, f32[512]{0:T(512)}, u32[]{:S(2)}) copy-start(f32[512]{0:T(512)} %param.12) | copy-start | bytes 6148
  10.6 4.9 %collective-permute-start.1 = (f32[9,512]{1,0:T(8,128)S(1)}, f32[9,512]{1,0:T(8,128)S(1)}, u32[]{:S(2)}, u32[]{:S(2)}) collective-permute-start(f32[9,512]{1,0:T(8,128)S(1)} %add.176), channel_id=1, source_target_pairs={{0,8},{4,12},{8,0},{12,4},{1,9},{5,13},{9,1},{13,5},{2,10},{6,14},... | collective-permute-start | bytes 55304 | tf_op jit(solution)/shard_map/ppermute | solution.py:114
  15.8 2.1 %copy-start = (f32[2,9,4096]{2,0,1:T(2,128)S(1)}, f32[2,9,4096]{2,0,1:T(2,128)}, u32[]{:S(2)}) copy-start(f32[2,9,4096]{2,0,1:T(2,128)} %param.7) | copy-start | bytes 884740
  21.5 4.3 %collective-permute-start.2 = (f32[4,4096]{1,0:T(4,128)S(1)}, f32[4,4096]{1,0:T(4,128)}, u32[]{:S(2)}, u32[]{:S(2)}) collective-permute-start(f32[4,4096]{1,0:T(4,128)S(1)} %pad_maximum_fusion.18), channel_id=1, source_target_pairs={{0,1},{1,0},{2,3},{3,2},{4,5},{5,4},{6,7},{7,6},{8,9},{9,8},{10,11... | collective-permute-start | bytes 196616 | tf_op jit(solution)/shard_map/ppermute | solution.py:114
  24.9 9.2 %copy-start.11 = (f32[4096]{0:T(1024)S(1)}, f32[4096]{0:T(1024)}, u32[]{:S(2)}) copy-start(f32[4096]{0:T(1024)} %param.11) | copy-start | bytes 49156
  25.3 3.0 %collective-permute-start.4 = (f32[6,4096]{1,0:T(8,128)S(1)}, f32[6,4096]{1,0:T(8,128)S(1)}, u32[]{:S(2)}, u32[]{:S(2)}) collective-permute-start(f32[6,4096]{1,0:T(8,128)S(1)} %reshape.1062), channel_id=1, source_target_pairs={{0,1},{1,0},{2,3},{3,2},{4,5},{5,4},{6,7},{7,6},{8,9},{9,8},{10,11... | collective-permute-start | bytes 294920 | tf_op jit(solution)/shard_map/ppermute | solution.py:114
  26.7 4.7 %collective-permute-start.3 = (f32[4,4096]{1,0:T(4,128)S(1)}, f32[4,4096]{1,0:T(4,128)S(1)}, u32[]{:S(2)}, u32[]{:S(2)}) collective-permute-start(f32[4,4096]{1,0:T(4,128)S(1)} %fusion.155), channel_id=1, source_target_pairs={{0,2},{1,3},{2,0},{3,1},{4,6},{5,7},{6,4},{7,5},{8,10},{9,11},{10,... | collective-permute-start | bytes 196616 | tf_op jit(solution)/shard_map/ppermute | solution.py:114
  28.3 5.5 %collective-permute-start.5 = (f32[6,4096]{1,0:T(8,128)S(1)}, f32[6,4096]{1,0:T(8,128)S(1)}, u32[]{:S(2)}, u32[]{:S(2)}) collective-permute-start(f32[6,4096]{1,0:T(8,128)S(1)} %add.184), channel_id=1, source_target_pairs={{0,2},{1,3},{2,0},{3,1},{4,6},{5,7},{6,4},{7,5},{8,10},{9,11},{10,... | collective-permute-start | bytes 294920 | tf_op jit(solution)/shard_map/ppermute | solution.py:114
  37.1 1.0 copy-start.3
  38.2 12.5 %copy-start.6 = (f32[9,512]{1,0:T(8,128)S(1)}, f32[9,512]{1,0:T(8,128)}, u32[]{:S(2)}) copy-start(f32[9,512]{1,0:T(8,128)} %param.13) | copy-start | bytes 55300
  38.2 12.5 %copy-start.9 = (f32[512]{0:T(512)S(1)}, f32[512]{0:T(512)}, u32[]{:S(2)}) copy-start(f32[512]{0:T(512)} %param.12) | copy-start | bytes 6148
  40.6 4.0 %collective-permute-start.6 = (f32[10,512]{1,0:T(8,128)S(1)}, f32[10,512]{1,0:T(8,128)S(1)}, u32[]{:S(2)}, u32[]{:S(2)}) collective-permute-start(f32[10,512]{1,0:T(8,128)S(1)} %concatenate.98), channel_id=1, source_target_pairs={{0,4},{4,0},{8,12},{12,8},{1,5},{5,1},{9,13},{13,9},{2,6},{6,2},{1... | collective-permute-start | bytes 61448 | tf_op jit(solution)/shard_map/ppermute | solution.py:114
  44.5 4.9 %collective-permute-start.7 = (f32[10,512]{1,0:T(8,128)S(1)}, f32[10,512]{1,0:T(8,128)S(1)}, u32[]{:S(2)}, u32[]{:S(2)}) collective-permute-start(f32[10,512]{1,0:T(8,128)S(1)} %pad_add_fusion.2), channel_id=1, source_target_pairs={{0,8},{4,12},{8,0},{12,4},{1,9},{5,13},{9,1},{13,5},{2,10},{6,14},... | collective-permute-start | bytes 61448 | tf_op jit(solution)/shard_map/ppermute | solution.py:114
  53.6 1.5 %copy-start.14 = (f32[512]{0:T(512)S(1)}, f32[512]{0:T(512)}, u32[]{:S(2)}) copy-start(f32[512]{0:T(512)} %get-tuple-element.13) | copy-start | bytes 6148
  55.2 1.3 %collective-permute-start.8 = (f32[4,4096]{1,0:T(4,128)S(1)}, f32[4,4096]{1,0:T(4,128)S(1)}, u32[]{:S(2)}, u32[]{:S(2)}) collective-permute-start(f32[4,4096]{1,0:T(4,128)S(1)} %pad_maximum_fusion.19), channel_id=1, source_target_pairs={{0,1},{1,0},{2,3},{3,2},{4,5},{5,4},{6,7},{7,6},{8,9},{9,8},{10,11... | collective-permute-start | bytes 196616 | tf_op jit(solution)/shard_map/ppermute | solution.py:114
  56.6 4.3 %collective-permute-start.9 = (f32[4,4096]{1,0:T(4,128)S(1)}, f32[4,4096]{1,0:T(4,128)S(1)}, u32[]{:S(2)}, u32[]{:S(2)}) collective-permute-start(f32[4,4096]{1,0:T(4,128)S(1)} %fusion.154), channel_id=1, source_target_pairs={{0,2},{1,3},{2,0},{3,1},{4,6},{5,7},{6,4},{7,5},{8,10},{9,11},{10,... | collective-permute-start | bytes 196616 | tf_op jit(solution)/shard_map/ppermute | solution.py:114
  64.6 13.7 %copy-start.7 = (f32[9,512]{1,0:T(8,128)S(1)}, f32[9,512]{1,0:T(8,128)}, u32[]{:S(2)}) copy-start(f32[9,512]{1,0:T(8,128)} %get-tuple-element.22) | copy-start | bytes 55300
  66.9 4.0 %collective-permute-start.10 = (f32[10,512]{1,0:T(8,128)S(1)}, f32[10,512]{1,0:T(8,128)S(1)}, u32[]{:S(2)}, u32[]{:S(2)}) collective-permute-start(f32[10,512]{1,0:T(8,128)S(1)} %concatenate.104), channel_id=1, source_target_pairs={{0,4},{4,0},{8,12},{12,8},{1,5},{5,1},{9,13},{13,9},{2,6},{6,2},{1... | collective-permute-start | bytes 61448 | tf_op jit(solution)/shard_map/ppermute | solution.py:114
  70.9 4.9 %collective-permute-start.11 = (f32[10,512]{1,0:T(8,128)S(1)}, f32[10,512]{1,0:T(8,128)S(1)}, u32[]{:S(2)}, u32[]{:S(2)}) collective-permute-start(f32[10,512]{1,0:T(8,128)S(1)} %pad_add_fusion.1), channel_id=1, source_target_pairs={{0,8},{4,12},{8,0},{12,4},{1,9},{5,13},{9,1},{13,5},{2,10},{6,14},... | collective-permute-start | bytes 61448 | tf_op jit(solution)/shard_map/ppermute | solution.py:114
  81.1 1.5 %copy-start.12 = (f32[512]{0:T(512)S(1)}, f32[512]{0:T(512)}, u32[]{:S(2)}) copy-start(f32[512]{0:T(512)} %get-tuple-element.9) | copy-start | bytes 6148
  81.1 1.5 %copy-start.13 = (f32[512]{0:T(512)S(1)}, f32[512]{0:T(512)}, u32[]{:S(2)}) copy-start(f32[512]{0:T(512)} %get-tuple-element.10) | copy-start | bytes 6148
  82.7 1.3 %collective-permute-start.12 = (f32[4,4096]{1,0:T(4,128)S(1)}, f32[4,4096]{1,0:T(4,128)S(1)}, u32[]{:S(2)}, u32[]{:S(2)}) collective-permute-start(f32[4,4096]{1,0:T(4,128)S(1)} %pad_maximum_fusion.20), channel_id=1, source_target_pairs={{0,1},{1,0},{2,3},{3,2},{4,5},{5,4},{6,7},{7,6},{8,9},{9,8},{10,11... | collective-permute-start | bytes 196616 | tf_op jit(solution)/shard_map/ppermute | solution.py:114
  84.0 4.3 %collective-permute-start.13 = (f32[4,4096]{1,0:T(4,128)S(1)}, f32[4,4096]{1,0:T(4,128)S(1)}, u32[]{:S(2)}, u32[]{:S(2)}) collective-permute-start(f32[4,4096]{1,0:T(4,128)S(1)} %fusion.153), channel_id=1, source_target_pairs={{0,2},{1,3},{2,0},{3,1},{4,6},{5,7},{6,4},{7,5},{8,10},{9,11},{10,... | collective-permute-start | bytes 196616 | tf_op jit(solution)/shard_map/ppermute | solution.py:114
  92.1 11.1 %copy-start.15 = (f32[1,512]{1,0:T(1,128)S(1)}, f32[1,512]{1,0:T(1,128)}, u32[]{:S(2)}) copy-start(f32[1,512]{1,0:T(1,128)} %get-tuple-element.19) | copy-start | bytes 6148
  92.1 12.4 %copy-start.4 = (f32[9,512]{1,0:T(8,128)S(1)}, f32[9,512]{1,0:T(8,128)}, u32[]{:S(2)}) copy-start(f32[9,512]{1,0:T(8,128)} %get-tuple-element.17) | copy-start | bytes 55300
  94.3 4.0 %collective-permute-start.14 = (f32[10,512]{1,0:T(8,128)S(1)}, f32[10,512]{1,0:T(8,128)S(1)}, u32[]{:S(2)}, u32[]{:S(2)}) collective-permute-start(f32[10,512]{1,0:T(8,128)S(1)} %concatenate.110), channel_id=1, source_target_pairs={{0,4},{4,0},{8,12},{12,8},{1,5},{5,1},{9,13},{13,9},{2,6},{6,2},{1... | collective-permute-start | bytes 61448 | tf_op jit(solution)/shard_map/ppermute | solution.py:114
  98.3 4.9 %collective-permute-start.15 = (f32[10,512]{1,0:T(8,128)S(1)}, f32[10,512]{1,0:T(8,128)S(1)}, u32[]{:S(2)}, u32[]{:S(2)}) collective-permute-start(f32[10,512]{1,0:T(8,128)S(1)} %pad_add_fusion), channel_id=1, source_target_pairs={{0,8},{4,12},{8,0},{12,4},{1,9},{5,13},{9,1},{13,5},{2,10},{6,14},... | collective-permute-start | bytes 61448 | tf_op jit(solution)/shard_map/ppermute | solution.py:114

commit v18 on v16

--- a/solution.py
+++ b/solution.py
@@ -102,7 +102,7 @@
 
 def allsum(value, axis):
     size = SIZES[axis]
-    if size == 4 and axis == "one_round":
+    if size == 4 and axis == "pts":
         peers = [
             lax.ppermute(value, axis, [(i, i ^ mask) for i in range(size)]) for mask in (1, 2, 3)
         ]

time: 90 us -> 103 us (1.14)
  local copies, waits for them, and re-layouts: 6.67 us -> 12.7 us
  other arithmetic: 13.5 us -> 19.4 us
  matrix products: 11.6 us -> 15.6 us
  starting transfers between devices: 26 us -> 24.6 us
  waiting for transfers between devices: 20.5 us -> 19.2 us
    ppermute x16 -> x8, starting transfers between devices: 26 us -> 5.54 us  [allsum(): lax.ppermute(value, axis, [(i, i ^ step) for i in range(size)])]
    ppermute x0 -> x12, starting transfers between devices: none -> 19 us  [allsum(): lax.ppermute(value, axis, [(i, i ^ mask) for i in range(size)])]
    ppermute x16 -> x8, waiting for transfers between devices: 20.5 us -> 12.8 us  [allsum(): lax.ppermute(value, axis, [(i, i ^ step) for i in range(size)])]
    ppermute x0 -> x12, waiting for transfers between devices: none -> 6.39 us  [allsum(): lax.ppermute(value, axis, [(i, i ^ mask) for i in range(size)])]
    reduce_sum x6, other arithmetic: 0.19 us -> 2.73 us  [lanes(): return jnp.sum(terms.reshape(-1, ncam), axis=0)]
    unnamed x14 -> x34, local copies, waits for them, and re-layouts: 0.4 us -> 2.78 us
    dot_general x8, matrix products: 7.73 us -> 9.95 us  [segsum(): lax.dot_general(self.hot3, spread, (((1,), (1,)), ((), ())), preferred_el...]
    dot_general x6, matrix products: 3.9 us -> 5.62 us  [gather(): lax.dot_general(stacked, self.hot3t, (((1,), (0,)), ((), ())), preferred_...]
  transfers between devices with their start and end apart: 16 -> 20, of which waited for: 11 -> 10; matrix products, arithmetic and copies ran while one was open for 9% -> 11% of each run, Pallas kernels for 0% -> 0%
where the time goes in v18:
time: 103 us
  starting transfers between devices  24.6 us (24%)
  other arithmetic  19.4 us (19%)
  waiting for transfers between devices  19.2 us (19%)
  matrix products  15.6 us (15%)
  local copies, waits for them, and re-layouts  12.7 us (12%)
  between operations  11.2 us (11%)
    ppermute x12, starting transfers between devices, allsum(): lax.ppermute(value, axis, [(i, i ^ mask) for i in range(size)])  19 us
    ppermute x8, waiting for transfers between devices, allsum(): lax.ppermute(value, axis, [(i, i ^ step) for i in range(size)])  12.8 us
    dot_general x8, matrix products, segsum(): lax.dot_general(self.hot3, spread, (((1,), (1,)), ((), ())), preferred_el...  9.95 us
    ppermute x12, waiting for transfers between devices, allsum(): lax.ppermute(value, axis, [(i, i ^ mask) for i in range(size)])  6.39 us
    dot_general x6, matrix products, gather(): lax.dot_general(stacked, self.hot3t, (((1,), (0,)), ((), ())), preferred_...  5.62 us
    ppermute x8, starting transfers between devices, allsum(): lax.ppermute(value, axis, [(i, i ^ step) for i in range(size)])  5.54 us
    select_n x8, other arithmetic, segsum(): jnp.where(self.low[None], part[:, None, :], jnp.zeros((), BF))  3.77 us
    unnamed x34, local copies, waits for them, and re-layouts  2.78 us
  transfers between devices with their start and end apart: 20, of which 10 were waited for; matrix products, arithmetic and copies ran while one was open for 11% of the time, Pallas kernels for 0%

profile of v18, /device:TPU:0, one launch (start us, length us, event | category | flops | bytes accessed | tf_op | source)
XLA Modules:
  0.0 102.6 jit_solution(14586998884542397678)
XLA Ops:
  0.6 0.7 add_select_fusion
  1.4 1.4 %multiply_reduce_fusion.6 = f32[9,4096]{1,0:T(8,128)S(1)} fusion(f32[2,9,4096]{2,0,1:T(2,128)} %param.7), kind=kLoop, calls=%fused_computation.122 | loop fusion | flops 110592 | bytes 442368 | tf_op jit(solution)/shard_map/reduce_sum | solution.py:130
  3.2 0.5 copy-done.2
  3.7 0.7 fusion.67
  4.7 3.1 %collective-permute-start = (f32[9,512]{1,0:T(8,128)S(1)}, f32[9,512]{1,0:T(8,128)S(1)}, u32[]{:S(2)}, u32[]{:S(2)}) collective-permute-start(f32[9,512]{1,0:T(8,128)S(1)} %reshape.1029), channel_id=1, source_target_pairs={{0,4},{4,0},{8,12},{12,8},{1,5},{5,1},{9,13},{13,9},{2,6},{6,2},{1... | collective-permute-start | bytes 55304 | tf_op jit(solution)/shard_map/ppermute | solution.py:107
  7.9 2.6 %collective-permute-start.1 = (f32[9,512]{1,0:T(8,128)S(1)}, f32[9,512]{1,0:T(8,128)S(1)}, u32[]{:S(2)}, u32[]{:S(2)}) collective-permute-start(f32[9,512]{1,0:T(8,128)S(1)} %reshape.1029), channel_id=1, source_target_pairs={{0,8},{4,12},{8,0},{12,4},{1,9},{5,13},{9,1},{13,5},{2,10},{6,14},... | collective-permute-start | bytes 55304 | tf_op jit(solution)/shard_map/ppermute | solution.py:107
  11.0 2.1 %broadcast_select_fusion.2 = (bf16[6,32,4096]{2,1,0:T(8,128)(2,1)S(1)}, bf16[6,32,4096]{2,1,0:T(8,128)(2,1)}, bf16[6,32,4096]{2,1,0:T(8,128)(2,1)}) fusion(pred[32,4096]{1,0:T(8,128)(4,1)S(1)} %iota_compare_fusion.2, bf16[6,4096]{1,0:T(8,128)(2,1)S(1)} %get-tuple-element.60, bf16[6,4096]{1,0:T(8,128)(2,1)S(1)} %get-tuple-element.62, ...), kind=kLoop, calls=%fused_computation.65 | loop fusion | flops 2359296 | bytes 4997120 | tf_op jit(solution)/shard_map/jit(_where)/select_n | solution.py:42
  13.4 2.8 %collective-permute-done.2 = f32[9,512]{1,0:T(8,128)S(1)} collective-permute-done((f32[9,512]{1,0:T(8,128)S(1)}, f32[9,512]{1,0:T(8,128)S(1)}, u32[]{:S(2)}, u32[]{:S(2)}) %collective-permute-start.2) | collective-permute-done | bytes 18464 | tf_op jit(solution)/shard_map/ppermute | solution.py:107
  16.6 2.1 %fusion.57 = f32[9,4096]{1,0:T(8,128)S(1)} fusion(bf16[64,4096]{1,0:T(8,128)(2,1)} %copy-done.2, pred[8,4096]{1,0:T(8,128)(4,1)S(1)} %iota_compare_fusion.3, bf16[72,64]{1,0:T(8,128)(2,1)S(1)} %get-tuple-element.91, bf16[72,64]{1,0:T(8,128)(2,1)S(1)} %get-tuple-element.92, bf16[72,64]{1,0:T(8,128)(2,1)S(1)} %get-tuple-element.90), kind=kOutput, calls=%fused_computation.71 | convolution fusion | flops 118600704 | bytes 732160 | tf_op jit(solution)/shard_map/dot_general | solution.py:55
  19.0 0.6 mul.572
  19.9 1.1 %fusion.9 = f32[128,96]{0,1:T(8,128)S(1)} fusion(bf16[96,4096]{1,0:T(8,128)(2,1)S(1)} %bitcast.217, bf16[96,4096]{1,0:T(8,128)(2,1)S(1)} %bitcast.216, bf16[96,4096]{1,0:T(8,128)(2,1)S(1)} %bitcast.215, bf16[128,4096]{1,0:T(8,128)(2,1)S(1)} %fusion.27), kind=kOutput, calls=%fused_computation.14 | convolution fusion | flops 318504960 | bytes 3457024 | tf_op jit(solution)/shard_map/dot_general | solution.py:46
  21.3 0.8 mul.573
  22.3 3.3 %fusion = f32[128,192]{0,1:T(8,128)S(1)} fusion(bf16[192,4096]{1,0:T(8,128)(2,1)} %bitcast.207, bf16[192,4096]{1,0:T(8,128)(2,1)} %bitcast.206, bf16[192,4096]{1,0:T(8,128)(2,1)S(1)} %bitcast.205, bf16[128,4096]{1,0:T(8,128)(2,1)S(1)} %fusion.27), kind=kOutput, calls=%fused_computation | convolution fusion | flops 627572736 | bytes 5865472 | tf_op jit(solution)/shard_map/dot_general | solution.py:46
  26.0 0.6 collective-permute-start.5
  26.5 0.9 fusion.151
  27.4 1.6 %collective-permute-start.4 = (f32[4,4096]{1,0:T(4,128)S(1)}, f32[4,4096]{1,0:T(4,128)S(1)}, u32[]{:S(2)}, u32[]{:S(2)}) collective-permute-start(f32[4,4096]{1,0:T(4,128)S(1)} %fusion.151), channel_id=1, source_target_pairs={{0,2},{1,3},{2,0},{3,1},{4,6},{5,7},{6,4},{7,5},{8,10},{9,11},{10,... | collective-permute-start | bytes 196616 | tf_op jit(solution)/shard_map/ppermute | solution.py:114
  29.0 0.6 collective-permute-start.6
  29.6 2.5 %collective-permute-done.4 = f32[4,4096]{1,0:T(4,128)S(1)} collective-permute-done((f32[4,4096]{1,0:T(4,128)S(1)}, f32[4,4096]{1,0:T(4,128)S(1)}, u32[]{:S(2)}, u32[]{:S(2)}) %collective-permute-start.4) | collective-permute-done | bytes 65568 | tf_op jit(solution)/shard_map/ppermute | solution.py:114
  32.2 0.6 reduce_sum.472
  32.8 1.8 %collective-permute-done.6 = f32[6,4096]{1,0:T(8,128)S(1)} collective-permute-done((f32[6,4096]{1,0:T(8,128)S(1)}, f32[6,4096]{1,0:T(8,128)S(1)}, u32[]{:S(2)}, u32[]{:S(2)}) %collective-permute-start.6) | collective-permute-done | bytes 98336 | tf_op jit(solution)/shard_map/ppermute | solution.py:114
  35.8 0.7 fusion.54
  36.5 0.2 select_reduce_fusion.2
  36.9 0.4 multiply_reduce_fusion.4
  37.6 0.7 copy-done.3
  38.3 0.7 fusion.64
  39.5 1.6 %collective-permute-start.8 = (f32[10,512]{1,0:T(8,128)S(1)}, f32[10,512]{1,0:T(8,128)S(1)}, u32[]{:S(2)}, u32[]{:S(2)}) collective-permute-start(f32[10,512]{1,0:T(8,128)S(1)} %pad_maximum_fusion.21), channel_id=1, source_target_pairs={{0,8},{4,12},{8,0},{12,4},{1,9},{5,13},{9,1},{13,5},{2,10},{6,14},... | collective-permute-start | bytes 61448 | tf_op jit(solution)/shard_map/ppermute | solution.py:107
  41.1 2.7 %collective-permute-start.9 = (f32[10,512]{1,0:T(8,128)S(1)}, f32[10,512]{1,0:T(8,128)S(1)}, u32[]{:S(2)}, u32[]{:S(2)}) collective-permute-start(f32[10,512]{1,0:T(8,128)S(1)} %pad_maximum_fusion.21), channel_id=1, source_target_pairs={{0,12},{4,8},{8,4},{12,0},{1,13},{5,9},{9,5},{13,1},{2,14},{6,10},... | collective-permute-start | bytes 61448 | tf_op jit(solution)/shard_map/ppermute | solution.py:107
  43.9 1.3 %fusion.148 = (f32[1]{0:T(128)}, f32[1]{0:T(128)}) fusion(f32[3]{0:T(128)} %reduce_sum.472), kind=kLoop, calls=%fused_computation.324 | loop fusion | bytes 16 | tf_op jit(solution)/shard_map/slice | solution.py:157
  45.2 1.7 %collective-permute-done.9 = f32[10,512]{1,0:T(8,128)S(1)} collective-permute-done((f32[10,512]{1,0:T(8,128)S(1)}, f32[10,512]{1,0:T(8,128)S(1)}, u32[]{:S(2)}, u32[]{:S(2)}) %collective-permute-start.9) | collective-permute-done | bytes 20512 | tf_op jit(solution)/shard_map/ppermute | solution.py:107
  46.9 0.6 slice_reduce_fusion.5
  49.4 1.3 %multiply_reduce_fusion.22 = (f32[512]{0:T(512)S(1)}, f32[512]{0:T(512)S(1)}, f32[512]{0:T(512)S(1)}, f32[9,512]{1,0:T(8,128)S(1)}, f32[9,512]{1,0:T(8,128)S(1)}, /*index=5*/f32[9,512]{1,0:T(8,128)}) fusion(f32[512]{0:T(512)} %param.12, f32[9,512]{1,0:T(8,128)S(1)} %get-tuple-element.24, f32[9,512]{1,0:T(8,128)S(1)} %copy-done.9, f32[]{:T(128)} %bitcast.56, ...), kind=kLoop, calls=%fused_computation.254 | loop fusion | flops 53760 | bytes 137220 | tf_op jit(solution)/shard_map/reduce_sum | solution.py:139
  51.1 0.8 fusion.56
  52.4 1.1 %fusion.15 = f32[128,96]{0,1:T(8,128)S(1)} fusion(bf16[96,4096]{1,0:T(8,128)(2,1)S(1)} %bitcast.220, bf16[96,4096]{1,0:T(8,128)(2,1)S(1)} %bitcast.219, bf16[96,4096]{1,0:T(8,128)(2,1)S(1)} %bitcast.218, bf16[128,4096]{1,0:T(8,128)(2,1)S(1)} %fusion.27), kind=kOutput, calls=%fused_computation.20 | convolution fusion | flops 318504960 | bytes 3457024 | tf_op jit(solution)/shard_map/dot_general | solution.py:46
  54.1 1.2 %collective-permute-done.10 = f32[4,4096]{1,0:T(4,128)S(1)} collective-permute-done((f32[4,4096]{1,0:T(4,128)S(1)}, f32[4,4096]{1,0:T(4,128)S(1)}, u32[]{:S(2)}, u32[]{:S(2)}) %collective-permute-start.10) | collective-permute-done | bytes 65568 | tf_op jit(solution)/shard_map/ppermute | solution.py:114
  55.4 1.3 %collective-permute-start.11 = (f32[4,4096]{1,0:T(4,128)S(1)}, f32[4,4096]{1,0:T(4,128)S(1)}, u32[]{:S(2)}, u32[]{:S(2)}) collective-permute-start(f32[4,4096]{1,0:T(4,128)S(1)} %fusion.150), channel_id=1, source_target_pairs={{0,2},{1,3},{2,0},{3,1},{4,6},{5,7},{6,4},{7,5},{8,10},{9,11},{10,... | collective-permute-start | bytes 196616 | tf_op jit(solution)/shard_map/ppermute | solution.py:114
  56.7 3.0 %collective-permute-done.11 = f32[4,4096]{1,0:T(4,128)S(1)} collective-permute-done((f32[4,4096]{1,0:T(4,128)S(1)}, f32[4,4096]{1,0:T(4,128)S(1)}, u32[]{:S(2)}, u32[]{:S(2)}) %collective-permute-start.11) | collective-permute-done | bytes 65568 | tf_op jit(solution)/shard_map/ppermute | solution.py:114
  59.7 0.6 slice_reduce_fusion.1
  60.8 0.7 fusion.53
  61.9 0.4 multiply_reduce_fusion.2
  62.6 0.7 copy-done.5
  63.3 1.3 %fusion.61 = f32[9,64,8]{1,2,0:T(8,128)} fusion(bf16[72,4096]{1,0:T(8,128)(2,1)S(1)} %get-tuple-element.100, bf16[72,4096]{1,0:T(8,128)(2,1)S(1)} %get-tuple-element.99, bf16[72,4096]{1,0:T(8,128)(2,1)S(1)} %get-tuple-element.98, bf16[64,4096]{1,0:T(8,128)(2,1)S(1)} %copy-done.5), kind=kOutput, calls=%fused_computation.73 | convolution fusion | flops 123273216 | bytes 2312192 | tf_op jit(solution)/shard_map/dot_general | solution.py:46
  64.6 1.0 copy.46
  65.9 3.3 %collective-permute-start.13 = (f32[10,512]{1,0:T(8,128)S(1)}, f32[10,512]{1,0:T(8,128)S(1)}, u32[]{:S(2)}, u32[]{:S(2)}) collective-permute-start(f32[10,512]{1,0:T(8,128)S(1)} %pad_maximum_fusion.22), channel_id=1, source_target_pairs={{0,8},{4,12},{8,0},{12,4},{1,9},{5,13},{9,1},{13,5},{2,10},{6,14},... | collective-permute-start | bytes 61448 | tf_op jit(solution)/shard_map/ppermute | solution.py:107
  69.2 1.1 %collective-permute-start.14 = (f32[10,512]{1,0:T(8,128)S(1)}, f32[10,512]{1,0:T(8,128)S(1)}, u32[]{:S(2)}, u32[]{:S(2)}) collective-permute-start(f32[10,512]{1,0:T(8,128)S(1)} %pad_maximum_fusion.22), channel_id=1, source_target_pairs={{0,12},{4,8},{8,4},{12,0},{1,13},{5,9},{9,5},{13,1},{2,14},{6,10},... | collective-permute-start | bytes 61448 | tf_op jit(solution)/shard_map/ppermute | solution.py:107
  70.3 0.7 reshape.1053
  71.1 0.6 fusion.147
  73.7 1.2 %collective-permute-done.14 = f32[10,512]{1,0:T(8,128)S(1)} collective-permute-done((f32[10,512]{1,0:T(8,128)S(1)}, f32[10,512]{1,0:T(8,128)S(1)}, u32[]{:S(2)}, u32[]{:S(2)}) %collective-permute-start.14) | collective-permute-done | bytes 20512 | tf_op jit(solution)/shard_map/ppermute | solution.py:107
  75.0 0.6 slice_reduce_fusion.4
  77.4 1.3 %multiply_reduce_fusion.20 = (f32[512]{0:T(512)S(1)}, f32[512]{0:T(512)S(1)}, f32[512]{0:T(512)S(1)}, f32[9,512]{1,0:T(8,128)S(1)}, f32[9,512]{1,0:T(8,128)}) fusion(f32[9,512]{1,0:T(8,128)S(1)} %get-tuple-element.19, f32[]{:T(128)} %bitcast.83, f32[512]{0:T(512)} %param.12, f32[9,512]{1,0:T(8,128)S(1)} %get-tuple-element.24, f32[9,512]{1,0:T(8,128)S(1)} %copy-done.11, ...), kind=kLoop, calls=%fused_computation.250 | loop fusion | flops 62976 | bytes 137224 | tf_op jit(solution)/shard_map/reduce_sum | solution.py:139
  79.1 0.6 fusion.55
  80.3 1.1 %fusion.21 = f32[128,96]{0,1:T(8,128)S(1)} fusion(bf16[96,4096]{1,0:T(8,128)(2,1)S(1)} %bitcast.223, bf16[96,4096]{1,0:T(8,128)(2,1)S(1)} %bitcast.222, bf16[96,4096]{1,0:T(8,128)(2,1)S(1)} %bitcast.221, bf16[128,4096]{1,0:T(8,128)(2,1)S(1)} %fusion.27), kind=kOutput, calls=%fused_computation.26 | convolution fusion | flops 318504960 | bytes 3457024 | tf_op jit(solution)/shard_map/dot_general | solution.py:46
  81.9 1.2 %collective-permute-done.15 = f32[4,4096]{1,0:T(4,128)S(1)} collective-permute-done((f32[4,4096]{1,0:T(4,128)S(1)}, f32[4,4096]{1,0:T(4,128)S(1)}, u32[]{:S(2)}, u32[]{:S(2)}) %collective-permute-start.15) | collective-permute-done | bytes 65568 | tf_op jit(solution)/shard_map/ppermute | solution.py:114
  83.2 1.3 %collective-permute-start.16 = (f32[4,4096]{1,0:T(4,128)S(1)}, f32[4,4096]{1,0:T(4,128)S(1)}, u32[]{:S(2)}, u32[]{:S(2)}) collective-permute-start(f32[4,4096]{1,0:T(4,128)S(1)} %fusion.149), channel_id=1, source_target_pairs={{0,2},{1,3},{2,0},{3,1},{4,6},{5,7},{6,4},{7,5},{8,10},{9,11},{10,... | collective-permute-start | bytes 196616 | tf_op jit(solution)/shard_map/ppermute | solution.py:114
  84.5 3.0 %collective-permute-done.16 = f32[4,4096]{1,0:T(4,128)S(1)} collective-permute-done((f32[4,4096]{1,0:T(4,128)S(1)}, f32[4,4096]{1,0:T(4,128)S(1)}, u32[]{:S(2)}, u32[]{:S(2)}) %collective-permute-start.16) | collective-permute-done | bytes 65568 | tf_op jit(solution)/shard_map/ppermute | solution.py:114
  88.1 0.7 fusion.52
  89.1 0.4 multiply_reduce_fusion
  89.9 0.7 copy-done.7
  90.6 0.6 fusion.58
  91.7 2.1 %collective-permute-start.18 = (f32[10,512]{1,0:T(8,128)S(1)}, f32[10,512]{1,0:T(8,128)S(1)}, u32[]{:S(2)}, u32[]{:S(2)}) collective-permute-start(f32[10,512]{1,0:T(8,128)S(1)} %pad_maximum_fusion.23), channel_id=1, source_target_pairs={{0,8},{4,12},{8,0},{12,4},{1,9},{5,13},{9,1},{13,5},{2,10},{6,14},... | collective-permute-start | bytes 61448 | tf_op jit(solution)/shard_map/ppermute | solution.py:107
  93.8 2.3 %collective-permute-start.19 = (f32[10,512]{1,0:T(8,128)S(1)}, f32[10,512]{1,0:T(8,128)S(1)}, u32[]{:S(2)}, u32[]{:S(2)}) collective-permute-start(f32[10,512]{1,0:T(8,128)S(1)} %pad_maximum_fusion.23), channel_id=1, source_target_pairs={{0,12},{4,8},{8,4},{12,0},{1,13},{5,9},{9,5},{13,1},{2,14},{6,10},... | collective-permute-start | bytes 61448 | tf_op jit(solution)/shard_map/ppermute | solution.py:107
  96.2 0.6 fusion.146
  98.8 0.7 collective-permute-done.19
  99.5 0.6 slice_reduce_fusion.3
  102.0 0.7 fusion.121
  (179 shorter events, 11.4 us)
Async XLA Ops:
  2.9 0.8 copy-start.2
  3.7 6.7 %copy-start.1 = (f32[2,3,4096]{2,0,1:T(2,128)S(1)}, f32[2,3,4096]{2,0,1:T(2,128)}, u32[]{:S(2)}) copy-start(f32[2,3,4096]{2,0,1:T(2,128)} %param.8) | copy-start | bytes 294916
  3.7 7.2 %copy-start.14 = (s32[4096]{0:T(1024)S(1)}, s32[4096]{0:T(1024)}, u32[]{:S(2)}) copy-start(s32[4096]{0:T(1024)} %param.10) | copy-start | bytes 49156
  4.7 8.6 %collective-permute-start = (f32[9,512]{1,0:T(8,128)S(1)}, f32[9,512]{1,0:T(8,128)S(1)}, u32[]{:S(2)}, u32[]{:S(2)}) collective-permute-start(f32[9,512]{1,0:T(8,128)S(1)} %reshape.1029), channel_id=1, source_target_pairs={{0,4},{4,0},{8,12},{12,8},{1,5},{5,1},{9,13},{13,9},{2,6},{6,2},{1... | collective-permute-start | bytes 55304 | tf_op jit(solution)/shard_map/ppermute | solution.py:107
  7.9 5.5 %collective-permute-start.1 = (f32[9,512]{1,0:T(8,128)S(1)}, f32[9,512]{1,0:T(8,128)S(1)}, u32[]{:S(2)}, u32[]{:S(2)}) collective-permute-start(f32[9,512]{1,0:T(8,128)S(1)} %reshape.1029), channel_id=1, source_target_pairs={{0,8},{4,12},{8,0},{12,4},{1,9},{5,13},{9,1},{13,5},{2,10},{6,14},... | collective-permute-start | bytes 55304 | tf_op jit(solution)/shard_map/ppermute | solution.py:107
  10.4 5.7 %collective-permute-start.2 = (f32[9,512]{1,0:T(8,128)S(1)}, f32[9,512]{1,0:T(8,128)S(1)}, u32[]{:S(2)}, u32[]{:S(2)}) collective-permute-start(f32[9,512]{1,0:T(8,128)S(1)} %reshape.1029), channel_id=1, source_target_pairs={{0,12},{4,8},{8,4},{12,0},{1,13},{5,9},{9,5},{13,1},{2,14},{6,10},... | collective-permute-start | bytes 55304 | tf_op jit(solution)/shard_map/ppermute | solution.py:107
  11.0 5.2 %copy-start.8 = (f32[9,512]{1,0:T(8,128)S(1)}, f32[9,512]{1,0:T(8,128)}, u32[]{:S(2)}) copy-start(f32[9,512]{1,0:T(8,128)} %param.13) | copy-start | bytes 55300
  11.0 5.1 %copy-start.12 = (f32[512]{0:T(512)S(1)}, f32[512]{0:T(512)}, u32[]{:S(2)}) copy-start(f32[512]{0:T(512)} %param.12) | copy-start | bytes 6148
  16.6 2.1 %copy-start = (f32[2,9,4096]{2,0,1:T(2,128)S(1)}, f32[2,9,4096]{2,0,1:T(2,128)}, u32[]{:S(2)}) copy-start(f32[2,9,4096]{2,0,1:T(2,128)} %param.7) | copy-start | bytes 884740
  22.2 4.3 %collective-permute-start.3 = (f32[4,4096]{1,0:T(4,128)S(1)}, f32[4,4096]{1,0:T(4,128)}, u32[]{:S(2)}, u32[]{:S(2)}) collective-permute-start(f32[4,4096]{1,0:T(4,128)S(1)} %pad_maximum_fusion.18), channel_id=1, source_target_pairs={{0,1},{1,0},{2,3},{3,2},{4,5},{5,4},{6,7},{7,6},{8,9},{9,8},{10,11... | collective-permute-start | bytes 196616 | tf_op jit(solution)/shard_map/ppermute | solution.py:114
  25.6 9.2 %copy-start.15 = (f32[4096]{0:T(1024)S(1)}, f32[4096]{0:T(1024)}, u32[]{:S(2)}) copy-start(f32[4096]{0:T(1024)} %param.11) | copy-start | bytes 49156
  26.0 3.0 %collective-permute-start.5 = (f32[6,4096]{1,0:T(8,128)S(1)}, f32[6,4096]{1,0:T(8,128)S(1)}, u32[]{:S(2)}, u32[]{:S(2)}) collective-permute-start(f32[6,4096]{1,0:T(8,128)S(1)} %reshape.1039), channel_id=1, source_target_pairs={{0,1},{1,0},{2,3},{3,2},{4,5},{5,4},{6,7},{7,6},{8,9},{9,8},{10,11... | collective-permute-start | bytes 294920 | tf_op jit(solution)/shard_map/ppermute | solution.py:114
  27.4 4.7 %collective-permute-start.4 = (f32[4,4096]{1,0:T(4,128)S(1)}, f32[4,4096]{1,0:T(4,128)S(1)}, u32[]{:S(2)}, u32[]{:S(2)}) collective-permute-start(f32[4,4096]{1,0:T(4,128)S(1)} %fusion.151), channel_id=1, source_target_pairs={{0,2},{1,3},{2,0},{3,1},{4,6},{5,7},{6,4},{7,5},{8,10},{9,11},{10,... | collective-permute-start | bytes 196616 | tf_op jit(solution)/shard_map/ppermute | solution.py:114
  29.0 5.6 %collective-permute-start.6 = (f32[6,4096]{1,0:T(8,128)S(1)}, f32[6,4096]{1,0:T(8,128)S(1)}, u32[]{:S(2)}, u32[]{:S(2)}) collective-permute-start(f32[6,4096]{1,0:T(8,128)S(1)} %add.154), channel_id=1, source_target_pairs={{0,2},{1,3},{2,0},{3,1},{4,6},{5,7},{6,4},{7,5},{8,10},{9,11},{10,... | collective-permute-start | bytes 294920 | tf_op jit(solution)/shard_map/ppermute | solution.py:114
  37.3 1.0 %copy-start.3 = (bf16[64,4096]{1,0:T(8,128)(2,1)S(1)}, bf16[64,4096]{1,0:T(8,128)(2,1)}, u32[]{:S(2)}) copy-start(bf16[64,4096]{1,0:T(8,128)(2,1)} %copy-done.2) | copy-start | bytes 1572868
  38.3 11.1 %copy-start.9 = (f32[9,512]{1,0:T(8,128)S(1)}, f32[9,512]{1,0:T(8,128)}, u32[]{:S(2)}) copy-start(f32[9,512]{1,0:T(8,128)} %param.13) | copy-start | bytes 55300
  39.0 12.0 %copy-start.4 = (bf16[64,4096]{1,0:T(8,128)(2,1)S(1)}, bf16[64,4096]{1,0:T(8,128)(2,1)}, u32[]{:S(2)}) copy-start(bf16[64,4096]{1,0:T(8,128)(2,1)} %copy-done.2) | copy-start | bytes 1572868
  39.4 5.8 %collective-permute-start.7 = (f32[10,512]{1,0:T(8,128)S(1)}, f32[10,512]{1,0:T(8,128)S(1)}, u32[]{:S(2)}, u32[]{:S(2)}) collective-permute-start(f32[10,512]{1,0:T(8,128)S(1)} %pad_maximum_fusion.21), channel_id=1, source_target_pairs={{0,4},{4,0},{8,12},{12,8},{1,5},{5,1},{9,13},{13,9},{2,6},{6,2},{1... | collective-permute-start | bytes 61448 | tf_op jit(solution)/shard_map/ppermute | solution.py:107
  39.5 5.7 %collective-permute-start.8 = (f32[10,512]{1,0:T(8,128)S(1)}, f32[10,512]{1,0:T(8,128)S(1)}, u32[]{:S(2)}, u32[]{:S(2)}) collective-permute-start(f32[10,512]{1,0:T(8,128)S(1)} %pad_maximum_fusion.21), channel_id=1, source_target_pairs={{0,8},{4,12},{8,0},{12,4},{1,9},{5,13},{9,1},{13,5},{2,10},{6,14},... | collective-permute-start | bytes 61448 | tf_op jit(solution)/shard_map/ppermute | solution.py:107
  41.1 5.7 %collective-permute-start.9 = (f32[10,512]{1,0:T(8,128)S(1)}, f32[10,512]{1,0:T(8,128)S(1)}, u32[]{:S(2)}, u32[]{:S(2)}) collective-permute-start(f32[10,512]{1,0:T(8,128)S(1)} %pad_maximum_fusion.21), channel_id=1, source_target_pairs={{0,12},{4,8},{8,4},{12,0},{1,13},{5,9},{9,5},{13,1},{2,14},{6,10},... | collective-permute-start | bytes 61448 | tf_op jit(solution)/shard_map/ppermute | solution.py:107
  54.0 1.3 %collective-permute-start.10 = (f32[4,4096]{1,0:T(4,128)S(1)}, f32[4,4096]{1,0:T(4,128)S(1)}, u32[]{:S(2)}, u32[]{:S(2)}) collective-permute-start(f32[4,4096]{1,0:T(4,128)S(1)} %pad_maximum_fusion.19), channel_id=1, source_target_pairs={{0,1},{1,0},{2,3},{3,2},{4,5},{5,4},{6,7},{7,6},{8,9},{9,8},{10,11... | collective-permute-start | bytes 196616 | tf_op jit(solution)/shard_map/ppermute | solution.py:114
  55.4 4.3 %collective-permute-start.11 = (f32[4,4096]{1,0:T(4,128)S(1)}, f32[4,4096]{1,0:T(4,128)S(1)}, u32[]{:S(2)}, u32[]{:S(2)}) collective-permute-start(f32[4,4096]{1,0:T(4,128)S(1)} %fusion.150), channel_id=1, source_target_pairs={{0,2},{1,3},{2,0},{3,1},{4,6},{5,7},{6,4},{7,5},{8,10},{9,11},{10,... | collective-permute-start | bytes 196616 | tf_op jit(solution)/shard_map/ppermute | solution.py:114
  62.3 1.0 %copy-start.5 = (bf16[64,4096]{1,0:T(8,128)(2,1)S(1)}, bf16[64,4096]{1,0:T(8,128)(2,1)}, u32[]{:S(2)}) copy-start(bf16[64,4096]{1,0:T(8,128)(2,1)} %copy-done.2) | copy-start | bytes 1572868
  63.3 14.1 %copy-start.11 = (f32[9,512]{1,0:T(8,128)S(1)}, f32[9,512]{1,0:T(8,128)}, u32[]{:S(2)}) copy-start(f32[9,512]{1,0:T(8,128)} %get-tuple-element.20) | copy-start | bytes 55300
  64.6 14.5 %copy-start.6 = (bf16[64,4096]{1,0:T(8,128)(2,1)S(1)}, bf16[64,4096]{1,0:T(8,128)(2,1)}, u32[]{:S(2)}) copy-start(bf16[64,4096]{1,0:T(8,128)(2,1)} %copy-done.2) | copy-start | bytes 1572868
  65.9 7.8 %collective-permute-start.12 = (f32[10,512]{1,0:T(8,128)S(1)}, f32[10,512]{1,0:T(8,128)S(1)}, u32[]{:S(2)}, u32[]{:S(2)}) collective-permute-start(f32[10,512]{1,0:T(8,128)S(1)} %pad_maximum_fusion.22), channel_id=1, source_target_pairs={{0,4},{4,0},{8,12},{12,8},{1,5},{5,1},{9,13},{13,9},{2,6},{6,2},{1... | collective-permute-start | bytes 61448 | tf_op jit(solution)/shard_map/ppermute | solution.py:107
  65.9 7.8 %collective-permute-start.13 = (f32[10,512]{1,0:T(8,128)S(1)}, f32[10,512]{1,0:T(8,128)S(1)}, u32[]{:S(2)}, u32[]{:S(2)}) collective-permute-start(f32[10,512]{1,0:T(8,128)S(1)} %pad_maximum_fusion.22), channel_id=1, source_target_pairs={{0,8},{4,12},{8,0},{12,4},{1,9},{5,13},{9,1},{13,5},{2,10},{6,14},... | collective-permute-start | bytes 61448 | tf_op jit(solution)/shard_map/ppermute | solution.py:107
  69.2 5.7 %collective-permute-start.14 = (f32[10,512]{1,0:T(8,128)S(1)}, f32[10,512]{1,0:T(8,128)S(1)}, u32[]{:S(2)}, u32[]{:S(2)}) collective-permute-start(f32[10,512]{1,0:T(8,128)S(1)} %pad_maximum_fusion.22), channel_id=1, source_target_pairs={{0,12},{4,8},{8,4},{12,0},{1,13},{5,9},{9,5},{13,1},{2,14},{6,10},... | collective-permute-start | bytes 61448 | tf_op jit(solution)/shard_map/ppermute | solution.py:107
  81.9 1.3 %collective-permute-start.15 = (f32[4,4096]{1,0:T(4,128)S(1)}, f32[4,4096]{1,0:T(4,128)S(1)}, u32[]{:S(2)}, u32[]{:S(2)}) collective-permute-start(f32[4,4096]{1,0:T(4,128)S(1)} %pad_maximum_fusion.20), channel_id=1, source_target_pairs={{0,1},{1,0},{2,3},{3,2},{4,5},{5,4},{6,7},{7,6},{8,9},{9,8},{10,11... | collective-permute-start | bytes 196616 | tf_op jit(solution)/shard_map/ppermute | solution.py:114
  83.2 4.3 %collective-permute-start.16 = (f32[4,4096]{1,0:T(4,128)S(1)}, f32[4,4096]{1,0:T(4,128)S(1)}, u32[]{:S(2)}, u32[]{:S(2)}) collective-permute-start(f32[4,4096]{1,0:T(4,128)S(1)} %fusion.149), channel_id=1, source_target_pairs={{0,2},{1,3},{2,0},{3,1},{4,6},{5,7},{6,4},{7,5},{8,10},{9,11},{10,... | collective-permute-start | bytes 196616 | tf_op jit(solution)/shard_map/ppermute | solution.py:114
  89.5 1.0 %copy-start.7 = (bf16[64,4096]{1,0:T(8,128)(2,1)S(1)}, bf16[64,4096]{1,0:T(8,128)(2,1)}, u32[]{:S(2)}) copy-start(bf16[64,4096]{1,0:T(8,128)(2,1)} %copy-done.2) | copy-start | bytes 1572868
  90.6 11.4 %copy-start.10 = (f32[9,512]{1,0:T(8,128)S(1)}, f32[9,512]{1,0:T(8,128)}, u32[]{:S(2)}) copy-start(f32[9,512]{1,0:T(8,128)} %get-tuple-element.17) | copy-start | bytes 55300
  90.6 11.4 %copy-start.13 = (f32[512]{0:T(512)S(1)}, f32[512]{0:T(512)}, u32[]{:S(2)}) copy-start(f32[512]{0:T(512)} %param.12) | copy-start | bytes 6148
  91.6 7.1 %collective-permute-start.17 = (f32[10,512]{1,0:T(8,128)S(1)}, f32[10,512]{1,0:T(8,128)S(1)}, u32[]{:S(2)}, u32[]{:S(2)}) collective-permute-start(f32[10,512]{1,0:T(8,128)S(1)} %pad_maximum_fusion.23), channel_id=1, source_target_pairs={{0,4},{4,0},{8,12},{12,8},{1,5},{5,1},{9,13},{13,9},{2,6},{6,2},{1... | collective-permute-start | bytes 61448 | tf_op jit(solution)/shard_map/ppermute | solution.py:107
  91.7 7.1 %collective-permute-start.18 = (f32[10,512]{1,0:T(8,128)S(1)}, f32[10,512]{1,0:T(8,128)S(1)}, u32[]{:S(2)}, u32[]{:S(2)}) collective-permute-start(f32[10,512]{1,0:T(8,128)S(1)} %pad_maximum_fusion.23), channel_id=1, source_target_pairs={{0,8},{4,12},{8,0},{12,4},{1,9},{5,13},{9,1},{13,5},{2,10},{6,14},... | collective-permute-start | bytes 61448 | tf_op jit(solution)/shard_map/ppermute | solution.py:107
  93.8 5.7 %collective-permute-start.19 = (f32[10,512]{1,0:T(8,128)S(1)}, f32[10,512]{1,0:T(8,128)S(1)}, u32[]{:S(2)}, u32[]{:S(2)}) collective-permute-start(f32[10,512]{1,0:T(8,128)S(1)} %pad_maximum_fusion.23), channel_id=1, source_target_pairs={{0,12},{4,8},{8,4},{12,0},{1,13},{5,9},{9,5},{13,1},{2,14},{6,10},... | collective-permute-start | bytes 61448 | tf_op jit(solution)/shard_map/ppermute | solution.py:107

commit v19 on v16

--- a/solution.py
+++ b/solution.py
@@ -42,11 +42,12 @@
             jnp.where(self.low[None], part[:, None, :], jnp.zeros((), BF)).reshape(ncol * self.lo, -1)
             for part in pieces(terms)
         ]
-        spread = jnp.concatenate(parts, axis=1)
+        spread = jnp.concatenate(parts, axis=0)
         out = lax.dot_general(
-            self.hot3, spread, (((1,), (1,)), ((), ())), preferred_element_type=F32
-        )
-        return out.reshape(self.hi, ncol, self.lo).transpose(1, 0, 2).reshape(ncol, self.count)
+            self.hot, spread, (((1,), (1,)), ((), ())), preferred_element_type=F32
+        ).reshape(self.hi, 3, ncol, self.lo)
+        out = (out[:, 0] + out[:, 1]) + out[:, 2]
+        return out.transpose(1, 0, 2).reshape(ncol, self.count)
 
     def gather(self, table):
         ncol = table.shape[0]

time: 90 us -> 91.8 us (1.020)
  waiting for transfers between devices: 20.5 us -> 28.1 us
  starting transfers between devices: 26 us -> 19.7 us
  local copies, waits for them, and re-layouts: 6.67 us -> 7.99 us
  matrix products: 11.6 us -> 10.6 us
    ppermute x16, waiting for transfers between devices: 20.5 us -> 28.1 us  [allsum(): lax.ppermute(value, axis, [(i, i ^ step) for i in range(size)])]
    ppermute x16, starting transfers between devices: 26 us -> 19.7 us  [allsum(): lax.ppermute(value, axis, [(i, i ^ step) for i in range(size)])]
    unnamed x14 -> x26, local copies, waits for them, and re-layouts: 0.4 us -> 2.06 us
    dot_general x8, matrix products: 7.73 us -> 6.53 us  [segsum(): lax.dot_general(self.hot, spread, (((1,), (1,)), ((), ())), preferred_ele...]
    reshape x12 -> x8, local copies, waits for them, and re-layouts: 1.92 us -> 1.35 us  [segsum(): return out.transpose(1, 0, 2).reshape(ncol, self.count)]
  transfers between devices with their start and end apart: 16 -> 16, of which waited for: 11 -> 10; matrix products, arithmetic and copies ran while one was open for 9% -> 10% of each run, Pallas kernels for 0% -> 0%
where the time goes in v19:
time: 91.8 us; the launch traced here: 91.4 us
  waiting for transfers between devices  28.1 us (31%)
  starting transfers between devices  19.7 us (21%)
  other arithmetic  13.6 us (15%)
  between operations  11.5 us (13%)
  matrix products  10.6 us (12%)
  local copies, waits for them, and re-layouts  7.99 us (9%)
    ppermute x16, waiting for transfers between devices, allsum(): lax.ppermute(value, axis, [(i, i ^ step) for i in range(size)])  28.1 us
    ppermute x16, starting transfers between devices, allsum(): lax.ppermute(value, axis, [(i, i ^ step) for i in range(size)])  19.7 us
    dot_general x8, matrix products, segsum(): lax.dot_general(self.hot, spread, (((1,), (1,)), ((), ())), preferred_ele...  6.53 us
    dot_general x6, matrix products, gather(): lax.dot_general(stacked, self.hot3t, (((1,), (0,)), ((), ())), preferred_...  4.05 us
    select_n x8, other arithmetic, segsum(): jnp.where(self.low[None], part[:, None, :], jnp.zeros((), BF))  2.1 us
    unnamed x26, local copies, waits for them, and re-layouts  2.06 us
    reduce_sum x3, other arithmetic, operate(): jnp.sum(img_all[-1:], axis=1, keepdims=True)  1.89 us
  transfers between devices with their start and end apart: 16, of which 10 were waited for; matrix products, arithmetic and copies ran while one was open for 10% of the time, Pallas kernels for 0%

profile of v19, /device:TPU:0, one launch (start us, length us, event | category | flops | bytes accessed | tf_op | source)
XLA Modules:
  0.0 91.4 jit_solution(12804722689841609496)
XLA Ops:
  0.6 0.7 add_select_fusion
  1.4 1.4 %multiply_reduce_fusion.6 = f32[9,4096]{1,0:T(8,128)S(1)} fusion(f32[2,9,4096]{2,0,1:T(2,128)} %param.7), kind=kLoop, calls=%fused_computation.120 | loop fusion | flops 110592 | bytes 442368 | tf_op jit(solution)/shard_map/reduce_sum | solution.py:131
  2.8 0.2 select_bitcast_fusion.11
  3.1 0.6 fusion.27
  3.9 0.2 reshape.1045
  4.1 3.1 %collective-permute-start = (f32[9,512]{1,0:T(8,128)S(1)}, f32[9,512]{1,0:T(8,128)S(1)}, u32[]{:S(2)}, u32[]{:S(2)}) collective-permute-start(f32[9,512]{1,0:T(8,128)S(1)} %reshape.1045), channel_id=1, source_target_pairs={{0,4},{4,0},{8,12},{12,8},{1,5},{5,1},{9,13},{13,9},{2,6},{6,2},{1... | collective-permute-start | bytes 55304 | tf_op jit(solution)/shard_map/ppermute | solution.py:115
  7.2 0.2 multiply_reduce_fusion.23
  7.8 0.4 broadcast_select_fusion.2
  8.2 1.4 %fusion = f32[128,576]{0,1:T(8,128)S(1)} fusion(bf16[192,4096]{1,0:T(8,128)(2,1)S(1)} %bitcast.223, bf16[192,4096]{1,0:T(8,128)(2,1)S(1)} %bitcast.222, bf16[192,4096]{1,0:T(8,128)(2,1)S(1)} %bitcast.221, s32[4096]{0:T(1024)S(1)} %get-tuple-element.119), kind=kOutput, calls=%fused_computation.1 | convolution fusion | flops 618659840 | bytes 5029888 | tf_op jit(solution)/shard_map/dot_general | solution.py:46
  10.3 0.2 reshape.1055
  10.6 2.7 %collective-permute-start.1 = (f32[9,512]{1,0:T(8,128)S(1)}, f32[9,512]{1,0:T(8,128)S(1)}, u32[]{:S(2)}, u32[]{:S(2)}) collective-permute-start(f32[9,512]{1,0:T(8,128)S(1)} %add.218), channel_id=1, source_target_pairs={{0,8},{4,12},{8,0},{12,4},{1,9},{5,13},{9,1},{13,5},{2,10},{6,14},... | collective-permute-start | bytes 55304 | tf_op jit(solution)/shard_map/ppermute | solution.py:115
  13.4 2.5 %collective-permute-done.1 = f32[9,512]{1,0:T(8,128)S(1)} collective-permute-done((f32[9,512]{1,0:T(8,128)S(1)}, f32[9,512]{1,0:T(8,128)S(1)}, u32[]{:S(2)}, u32[]{:S(2)}) %collective-permute-start.1) | collective-permute-done | bytes 18464 | tf_op jit(solution)/shard_map/ppermute | solution.py:115
  16.2 0.6 fusion.53
  16.9 0.3 copy-done
  17.6 0.2 broadcast_select_fusion.11
  17.8 0.8 fusion.9
  19.5 0.3 iota_compare_fusion
  19.8 1.6 %collective-permute-start.5 = (f32[6,4096]{1,0:T(8,128)S(1)}, f32[6,4096]{1,0:T(8,128)S(1)}, u32[]{:S(2)}, u32[]{:S(2)}) collective-permute-start(f32[6,4096]{1,0:T(8,128)S(1)} %add.230), channel_id=1, source_target_pairs={{0,2},{1,3},{2,0},{3,1},{4,6},{5,7},{6,4},{7,5},{8,10},{9,11},{10,... | collective-permute-start | bytes 294920 | tf_op jit(solution)/shard_map/ppermute | solution.py:115
  21.5 0.9 %collective-permute-start.3 = (f32[4,4096]{1,0:T(4,128)S(1)}, f32[4,4096]{1,0:T(4,128)S(1)}, u32[]{:S(2)}, u32[]{:S(2)}) collective-permute-start(f32[4,4096]{1,0:T(4,128)S(1)} %fusion.156), channel_id=1, source_target_pairs={{0,2},{1,3},{2,0},{3,1},{4,6},{5,7},{6,4},{7,5},{8,10},{9,11},{10,... | collective-permute-start | bytes 196616 | tf_op jit(solution)/shard_map/ppermute | solution.py:115
  22.4 4.8 %collective-permute-done.3 = f32[4,4096]{1,0:T(4,128)S(1)} collective-permute-done((f32[4,4096]{1,0:T(4,128)S(1)}, f32[4,4096]{1,0:T(4,128)S(1)}, u32[]{:S(2)}, u32[]{:S(2)}) %collective-permute-start.3) | collective-permute-done | bytes 65568 | tf_op jit(solution)/shard_map/ppermute | solution.py:115
  28.5 0.7 fusion.67
  29.2 0.2 select_reduce_fusion.2
  29.6 0.4 multiply_reduce_fusion.4
  30.0 0.2 select_bitcast_fusion.8
  30.3 0.7 fusion.33
  31.1 0.2 reshape.1060
  31.7 3.7 %collective-permute-done.6 = f32[10,512]{1,0:T(8,128)S(1)} collective-permute-done((f32[10,512]{1,0:T(8,128)S(1)}, f32[10,512]{1,0:T(8,128)S(1)}, u32[]{:S(2)}, u32[]{:S(2)}) %collective-permute-start.6) | collective-permute-done | bytes 20512 | tf_op jit(solution)/shard_map/ppermute | solution.py:115
  35.3 2.3 %collective-permute-start.7 = (f32[10,512]{1,0:T(8,128)S(1)}, f32[10,512]{1,0:T(8,128)S(1)}, u32[]{:S(2)}, u32[]{:S(2)}) collective-permute-start(f32[10,512]{1,0:T(8,128)S(1)} %fusion.155), channel_id=1, source_target_pairs={{0,8},{4,12},{8,0},{12,4},{1,9},{5,13},{9,1},{13,5},{2,10},{6,14},... | collective-permute-start | bytes 61448 | tf_op jit(solution)/shard_map/ppermute | solution.py:115
  37.6 0.6 fusion.150
  38.2 2.0 %collective-permute-done.7 = f32[10,512]{1,0:T(8,128)S(1)} collective-permute-done((f32[10,512]{1,0:T(8,128)S(1)}, f32[10,512]{1,0:T(8,128)S(1)}, u32[]{:S(2)}, u32[]{:S(2)}) %collective-permute-start.7) | collective-permute-done | bytes 20512 | tf_op jit(solution)/shard_map/ppermute | solution.py:115
  40.2 0.7 slice_reduce_fusion.5
  42.9 0.3 reshape.1062
  43.5 0.6 fusion.52
  44.5 0.2 broadcast_select_fusion.8
  44.7 0.8 fusion.15
  46.4 1.2 %collective-permute-done.8 = f32[4,4096]{1,0:T(4,128)S(1)} collective-permute-done((f32[4,4096]{1,0:T(4,128)S(1)}, f32[4,4096]{1,0:T(4,128)S(1)}, u32[]{:S(2)}, u32[]{:S(2)}) %collective-permute-start.8) | collective-permute-done | bytes 65568 | tf_op jit(solution)/shard_map/ppermute | solution.py:115
  47.7 1.6 %collective-permute-start.9 = (f32[4,4096]{1,0:T(4,128)S(1)}, f32[4,4096]{1,0:T(4,128)S(1)}, u32[]{:S(2)}, u32[]{:S(2)}) collective-permute-start(f32[4,4096]{1,0:T(4,128)S(1)} %fusion.154), channel_id=1, source_target_pairs={{0,2},{1,3},{2,0},{3,1},{4,6},{5,7},{6,4},{7,5},{8,10},{9,11},{10,... | collective-permute-start | bytes 196616 | tf_op jit(solution)/shard_map/ppermute | solution.py:115
  49.3 2.7 %collective-permute-done.9 = f32[4,4096]{1,0:T(4,128)S(1)} collective-permute-done((f32[4,4096]{1,0:T(4,128)S(1)}, f32[4,4096]{1,0:T(4,128)S(1)}, u32[]{:S(2)}, u32[]{:S(2)}) %collective-permute-start.9) | collective-permute-done | bytes 65568 | tf_op jit(solution)/shard_map/ppermute | solution.py:115
  52.5 0.7 fusion.73
  53.2 0.2 select_reduce_fusion.1
  53.6 0.4 multiply_reduce_fusion.2
  54.0 0.2 select_bitcast_fusion.5
  54.3 0.7 fusion.39
  55.7 3.7 %collective-permute-done.10 = f32[10,512]{1,0:T(8,128)S(1)} collective-permute-done((f32[10,512]{1,0:T(8,128)S(1)}, f32[10,512]{1,0:T(8,128)S(1)}, u32[]{:S(2)}, u32[]{:S(2)}) %collective-permute-start.10) | collective-permute-done | bytes 20512 | tf_op jit(solution)/shard_map/ppermute | solution.py:115
  59.3 2.5 %collective-permute-start.11 = (f32[10,512]{1,0:T(8,128)S(1)}, f32[10,512]{1,0:T(8,128)S(1)}, u32[]{:S(2)}, u32[]{:S(2)}) collective-permute-start(f32[10,512]{1,0:T(8,128)S(1)} %fusion.153), channel_id=1, source_target_pairs={{0,8},{4,12},{8,0},{12,4},{1,9},{5,13},{9,1},{13,5},{2,10},{6,14},... | collective-permute-start | bytes 61448 | tf_op jit(solution)/shard_map/ppermute | solution.py:115
  61.8 0.6 fusion.149
  64.4 0.6 slice_reduce_fusion.4
  67.3 0.6 fusion.51
  68.3 0.2 broadcast_select_fusion.5
  68.6 0.8 fusion.21
  70.2 1.2 %collective-permute-done.12 = f32[4,4096]{1,0:T(4,128)S(1)} collective-permute-done((f32[4,4096]{1,0:T(4,128)S(1)}, f32[4,4096]{1,0:T(4,128)S(1)}, u32[]{:S(2)}, u32[]{:S(2)}) %collective-permute-start.12) | collective-permute-done | bytes 65568 | tf_op jit(solution)/shard_map/ppermute | solution.py:115
  71.5 1.6 %collective-permute-start.13 = (f32[4,4096]{1,0:T(4,128)S(1)}, f32[4,4096]{1,0:T(4,128)S(1)}, u32[]{:S(2)}, u32[]{:S(2)}) collective-permute-start(f32[4,4096]{1,0:T(4,128)S(1)} %fusion.152), channel_id=1, source_target_pairs={{0,2},{1,3},{2,0},{3,1},{4,6},{5,7},{6,4},{7,5},{8,10},{9,11},{10,... | collective-permute-start | bytes 196616 | tf_op jit(solution)/shard_map/ppermute | solution.py:115
  73.1 2.7 %collective-permute-done.13 = f32[4,4096]{1,0:T(4,128)S(1)} collective-permute-done((f32[4,4096]{1,0:T(4,128)S(1)}, f32[4,4096]{1,0:T(4,128)S(1)}, u32[]{:S(2)}, u32[]{:S(2)}) %collective-permute-start.13) | collective-permute-done | bytes 65568 | tf_op jit(solution)/shard_map/ppermute | solution.py:115
  76.3 0.7 fusion.79
  77.1 0.2 select_reduce_fusion
  77.4 0.4 multiply_reduce_fusion
  77.9 0.2 select_bitcast_fusion.2
  78.1 0.6 fusion.45
  79.2 0.3 collective-permute-start.14
  79.7 3.5 %collective-permute-done.14 = f32[10,512]{1,0:T(8,128)S(1)} collective-permute-done((f32[10,512]{1,0:T(8,128)S(1)}, f32[10,512]{1,0:T(8,128)S(1)}, u32[]{:S(2)}, u32[]{:S(2)}) %collective-permute-start.14) | collective-permute-done | bytes 20512 | tf_op jit(solution)/shard_map/ppermute | solution.py:115
  83.2 2.5 %collective-permute-start.15 = (f32[10,512]{1,0:T(8,128)S(1)}, f32[10,512]{1,0:T(8,128)S(1)}, u32[]{:S(2)}, u32[]{:S(2)}) collective-permute-start(f32[10,512]{1,0:T(8,128)S(1)} %fusion.151), channel_id=1, source_target_pairs={{0,8},{4,12},{8,0},{12,4},{1,9},{5,13},{9,1},{13,5},{2,10},{6,14},... | collective-permute-start | bytes 61448 | tf_op jit(solution)/shard_map/ppermute | solution.py:115
  85.7 0.6 fusion.148
  88.2 0.6 slice_reduce_fusion.3
  90.7 0.7 fusion.119
  (175 shorter events, 10.0 us)
Async XLA Ops:
  3.1 4.1 %copy-start.1 = (f32[2,3,4096]{2,0,1:T(2,128)S(1)}, f32[2,3,4096]{2,0,1:T(2,128)}, u32[]{:S(2)}) copy-start(f32[2,3,4096]{2,0,1:T(2,128)} %param.8) | copy-start | bytes 294916
  3.7 3.9 %copy-start.4 = (s32[4096]{0:T(1024)S(1)}, s32[4096]{0:T(1024)}, u32[]{:S(2)}) copy-start(s32[4096]{0:T(1024)} %param.10) | copy-start | bytes 49156
  4.1 6.5 %collective-permute-start = (f32[9,512]{1,0:T(8,128)S(1)}, f32[9,512]{1,0:T(8,128)S(1)}, u32[]{:S(2)}, u32[]{:S(2)}) collective-permute-start(f32[9,512]{1,0:T(8,128)S(1)} %reshape.1045), channel_id=1, source_target_pairs={{0,4},{4,0},{8,12},{12,8},{1,5},{5,1},{9,13},{13,9},{2,6},{6,2},{1... | collective-permute-start | bytes 55304 | tf_op jit(solution)/shard_map/ppermute | solution.py:115
  10.0 5.8 %copy-start.2 = (f32[9,512]{1,0:T(8,128)S(1)}, f32[9,512]{1,0:T(8,128)}, u32[]{:S(2)}) copy-start(f32[9,512]{1,0:T(8,128)} %param.13) | copy-start | bytes 55300
  10.0 5.8 %copy-start.3 = (f32[512]{0:T(512)S(1)}, f32[512]{0:T(512)}, u32[]{:S(2)}) copy-start(f32[512]{0:T(512)} %param.12) | copy-start | bytes 6148
  10.5 9.3 %collective-permute-start.4 = (f32[6,4096]{1,0:T(8,128)S(1)}, f32[6,4096]{1,0:T(8,128)S(1)}, u32[]{:S(2)}, u32[]{:S(2)}) collective-permute-start(f32[6,4096]{1,0:T(8,128)S(1)} %reshape.1055), channel_id=1, source_target_pairs={{0,1},{1,0},{2,3},{3,2},{4,5},{5,4},{6,7},{7,6},{8,9},{9,8},{10,11... | collective-permute-start | bytes 294920 | tf_op jit(solution)/shard_map/ppermute | solution.py:115
  10.6 5.3 %collective-permute-start.1 = (f32[9,512]{1,0:T(8,128)S(1)}, f32[9,512]{1,0:T(8,128)S(1)}, u32[]{:S(2)}, u32[]{:S(2)}) collective-permute-start(f32[9,512]{1,0:T(8,128)S(1)} %add.218), channel_id=1, source_target_pairs={{0,8},{4,12},{8,0},{12,4},{1,9},{5,13},{9,1},{13,5},{2,10},{6,14},... | collective-permute-start | bytes 55304 | tf_op jit(solution)/shard_map/ppermute | solution.py:115
  16.2 1.0 %copy-start = (f32[2,9,4096]{2,0,1:T(2,128)S(1)}, f32[2,9,4096]{2,0,1:T(2,128)}, u32[]{:S(2)}) copy-start(f32[2,9,4096]{2,0,1:T(2,128)} %param.7) | copy-start | bytes 884740
  19.1 8.3 %copy-start.5 = (f32[4096]{0:T(1024)S(1)}, f32[4096]{0:T(1024)}, u32[]{:S(2)}) copy-start(f32[4096]{0:T(1024)} %param.11) | copy-start | bytes 49156
  19.4 2.0 %collective-permute-start.2 = (f32[4,4096]{1,0:T(4,128)S(1)}, f32[4,4096]{1,0:T(4,128)S(1)}, u32[]{:S(2)}, u32[]{:S(2)}) collective-permute-start(f32[4,4096]{1,0:T(4,128)S(1)} %pad_maximum_fusion), channel_id=1, source_target_pairs={{0,1},{1,0},{2,3},{3,2},{4,5},{5,4},{6,7},{7,6},{8,9},{9,8},{10,11... | collective-permute-start | bytes 196616 | tf_op jit(solution)/shard_map/ppermute | solution.py:115
  19.8 7.4 %collective-permute-start.5 = (f32[6,4096]{1,0:T(8,128)S(1)}, f32[6,4096]{1,0:T(8,128)S(1)}, u32[]{:S(2)}, u32[]{:S(2)}) collective-permute-start(f32[6,4096]{1,0:T(8,128)S(1)} %add.230), channel_id=1, source_target_pairs={{0,2},{1,3},{2,0},{3,1},{4,6},{5,7},{6,4},{7,5},{8,10},{9,11},{10,... | collective-permute-start | bytes 294920 | tf_op jit(solution)/shard_map/ppermute | solution.py:115
  21.5 5.7 %collective-permute-start.3 = (f32[4,4096]{1,0:T(4,128)S(1)}, f32[4,4096]{1,0:T(4,128)S(1)}, u32[]{:S(2)}, u32[]{:S(2)}) collective-permute-start(f32[4,4096]{1,0:T(4,128)S(1)} %fusion.156), channel_id=1, source_target_pairs={{0,2},{1,3},{2,0},{3,1},{4,6},{5,7},{6,4},{7,5},{8,10},{9,11},{10,... | collective-permute-start | bytes 196616 | tf_op jit(solution)/shard_map/ppermute | solution.py:115
  31.3 4.0 %collective-permute-start.6 = (f32[10,512]{1,0:T(8,128)S(1)}, f32[10,512]{1,0:T(8,128)S(1)}, u32[]{:S(2)}, u32[]{:S(2)}) collective-permute-start(f32[10,512]{1,0:T(8,128)S(1)} %pad_maximum_fusion.3), channel_id=1, source_target_pairs={{0,4},{4,0},{8,12},{12,8},{1,5},{5,1},{9,13},{13,9},{2,6},{6,2},{1... | collective-permute-start | bytes 61448 | tf_op jit(solution)/shard_map/ppermute | solution.py:115
  35.3 4.9 %collective-permute-start.7 = (f32[10,512]{1,0:T(8,128)S(1)}, f32[10,512]{1,0:T(8,128)S(1)}, u32[]{:S(2)}, u32[]{:S(2)}) collective-permute-start(f32[10,512]{1,0:T(8,128)S(1)} %fusion.155), channel_id=1, source_target_pairs={{0,8},{4,12},{8,0},{12,4},{1,9},{5,13},{9,1},{13,5},{2,10},{6,14},... | collective-permute-start | bytes 61448 | tf_op jit(solution)/shard_map/ppermute | solution.py:115
  46.3 1.3 %collective-permute-start.8 = (f32[4,4096]{1,0:T(4,128)S(1)}, f32[4,4096]{1,0:T(4,128)S(1)}, u32[]{:S(2)}, u32[]{:S(2)}) collective-permute-start(f32[4,4096]{1,0:T(4,128)S(1)} %pad_maximum_fusion.1), channel_id=1, source_target_pairs={{0,1},{1,0},{2,3},{3,2},{4,5},{5,4},{6,7},{7,6},{8,9},{9,8},{10,11... | collective-permute-start | bytes 196616 | tf_op jit(solution)/shard_map/ppermute | solution.py:115
  47.7 4.3 %collective-permute-start.9 = (f32[4,4096]{1,0:T(4,128)S(1)}, f32[4,4096]{1,0:T(4,128)S(1)}, u32[]{:S(2)}, u32[]{:S(2)}) collective-permute-start(f32[4,4096]{1,0:T(4,128)S(1)} %fusion.154), channel_id=1, source_target_pairs={{0,2},{1,3},{2,0},{3,1},{4,6},{5,7},{6,4},{7,5},{8,10},{9,11},{10,... | collective-permute-start | bytes 196616 | tf_op jit(solution)/shard_map/ppermute | solution.py:115
  55.3 4.0 %collective-permute-start.10 = (f32[10,512]{1,0:T(8,128)S(1)}, f32[10,512]{1,0:T(8,128)S(1)}, u32[]{:S(2)}, u32[]{:S(2)}) collective-permute-start(f32[10,512]{1,0:T(8,128)S(1)} %pad_maximum_fusion.4), channel_id=1, source_target_pairs={{0,4},{4,0},{8,12},{12,8},{1,5},{5,1},{9,13},{13,9},{2,6},{6,2},{1... | collective-permute-start | bytes 61448 | tf_op jit(solution)/shard_map/ppermute | solution.py:115
  59.3 5.1 %collective-permute-start.11 = (f32[10,512]{1,0:T(8,128)S(1)}, f32[10,512]{1,0:T(8,128)S(1)}, u32[]{:S(2)}, u32[]{:S(2)}) collective-permute-start(f32[10,512]{1,0:T(8,128)S(1)} %fusion.153), channel_id=1, source_target_pairs={{0,8},{4,12},{8,0},{12,4},{1,9},{5,13},{9,1},{13,5},{2,10},{6,14},... | collective-permute-start | bytes 61448 | tf_op jit(solution)/shard_map/ppermute | solution.py:115
  70.1 1.3 %collective-permute-start.12 = (f32[4,4096]{1,0:T(4,128)S(1)}, f32[4,4096]{1,0:T(4,128)S(1)}, u32[]{:S(2)}, u32[]{:S(2)}) collective-permute-start(f32[4,4096]{1,0:T(4,128)S(1)} %pad_maximum_fusion.2), channel_id=1, source_target_pairs={{0,1},{1,0},{2,3},{3,2},{4,5},{5,4},{6,7},{7,6},{8,9},{9,8},{10,11... | collective-permute-start | bytes 196616 | tf_op jit(solution)/shard_map/ppermute | solution.py:115
  71.5 4.3 %collective-permute-start.13 = (f32[4,4096]{1,0:T(4,128)S(1)}, f32[4,4096]{1,0:T(4,128)S(1)}, u32[]{:S(2)}, u32[]{:S(2)}) collective-permute-start(f32[4,4096]{1,0:T(4,128)S(1)} %fusion.152), channel_id=1, source_target_pairs={{0,2},{1,3},{2,0},{3,1},{4,6},{5,7},{6,4},{7,5},{8,10},{9,11},{10,... | collective-permute-start | bytes 196616 | tf_op jit(solution)/shard_map/ppermute | solution.py:115
  79.2 4.0 %collective-permute-start.14 = (f32[10,512]{1,0:T(8,128)S(1)}, f32[10,512]{1,0:T(8,128)S(1)}, u32[]{:S(2)}, u32[]{:S(2)}) collective-permute-start(f32[10,512]{1,0:T(8,128)S(1)} %pad_maximum_fusion.5), channel_id=1, source_target_pairs={{0,4},{4,0},{8,12},{12,8},{1,5},{5,1},{9,13},{13,9},{2,6},{6,2},{1... | collective-permute-start | bytes 61448 | tf_op jit(solution)/shard_map/ppermute | solution.py:115
  83.2 5.0 %collective-permute-start.15 = (f32[10,512]{1,0:T(8,128)S(1)}, f32[10,512]{1,0:T(8,128)S(1)}, u32[]{:S(2)}, u32[]{:S(2)}) collective-permute-start(f32[10,512]{1,0:T(8,128)S(1)} %fusion.151), channel_id=1, source_target_pairs={{0,8},{4,12},{8,0},{12,4},{1,9},{5,13},{9,1},{13,5},{2,10},{6,14},... | collective-permute-start | bytes 61448 | tf_op jit(solution)/shard_map/ppermute | solution.py:115

commit v20 on v16

--- a/solution.py
+++ b/solution.py
@@ -109,10 +109,10 @@
         return (value + peers[0]) + (peers[1] + peers[2])
     if size & (size - 1):
         return lax.psum(value, axis)
-    step = 1
-    while step < size:
+    step = size // 2 if axis == "pts" else 1
+    while 0 < step < size:
         value = value + lax.ppermute(value, axis, [(i, i ^ step) for i in range(size)])
-        step *= 2
+        step = step // 2 if axis == "pts" else step * 2
     return value
 
 

time: 90 us -> 89.9 us (level)
  starting transfers between devices: 26 us -> 24.4 us
  waiting for transfers between devices: 20.5 us -> 22 us
    ppermute x16, starting transfers between devices: 26 us -> 24.4 us  [allsum(): lax.ppermute(value, axis, [(i, i ^ step) for i in range(size)])]
    ppermute x16, waiting for transfers between devices: 20.5 us -> 22 us  [allsum(): lax.ppermute(value, axis, [(i, i ^ step) for i in range(size)])]
  transfers between devices with their start and end apart: 16 -> 16, of which waited for: 11 -> 12; matrix products, arithmetic and copies ran while one was open for 9% -> 10% of each run, Pallas kernels for 0% -> 0%
where the time goes in v20:
time: 89.9 us; the launch traced here: 89.5 us
  starting transfers between devices  24.4 us (27%)
  waiting for transfers between devices  22 us (24%)
  other arithmetic  13.5 us (15%)
  matrix products  11.6 us (13%)
  between operations  11.3 us (13%)
  local copies, waits for them, and re-layouts  6.67 us (7%)
    ppermute x16, starting transfers between devices, allsum(): lax.ppermute(value, axis, [(i, i ^ step) for i in range(size)])  24.4 us
    ppermute x16, waiting for transfers between devices, allsum(): lax.ppermute(value, axis, [(i, i ^ step) for i in range(size)])  22 us
    dot_general x8, matrix products, segsum(): lax.dot_general(self.hot3, spread, (((1,), (1,)), ((), ())), preferred_el...  7.74 us
    dot_general x6, matrix products, gather(): lax.dot_general(stacked, self.hot3t, (((1,), (0,)), ((), ())), preferred_...  3.9 us
    select_n x8, other arithmetic, segsum(): jnp.where(self.low[None], part[:, None, :], jnp.zeros((), BF))  2.11 us
    reshape x12, local copies, waits for them, and re-layouts, segsum(): out.reshape(self.hi, ncol, self.lo).transpose(1, 0, 2)  1.92 us
    reduce_sum x3, other arithmetic, operate(): jnp.sum(img_all[-1:], axis=1, keepdims=True)  1.9 us
  transfers between devices with their start and end apart: 16, of which 12 were waited for; matrix products, arithmetic and copies ran while one was open for 10% of the time, Pallas kernels for 0%

profile of v20, /device:TPU:0, one launch (start us, length us, event | category | flops | bytes accessed | tf_op | source)
XLA Modules:
  0.0 89.5 jit_solution(7408186316291483071)
XLA Ops:
  0.6 0.7 add_select_fusion
  1.4 1.4 %multiply_reduce_fusion.6 = f32[9,4096]{1,0:T(8,128)S(1)} fusion(f32[2,9,4096]{2,0,1:T(2,128)} %param.7), kind=kLoop, calls=%fused_computation.122 | loop fusion | flops 110592 | bytes 442368 | tf_op jit(solution)/shard_map/reduce_sum | solution.py:130
  2.9 0.2 select_bitcast_fusion.11
  3.2 0.7 fusion.67
  4.2 4.1 %collective-permute-start = (f32[9,512]{1,0:T(8,128)S(1)}, f32[9,512]{1,0:T(8,128)S(1)}, u32[]{:S(2)}, u32[]{:S(2)}) collective-permute-start(f32[9,512]{1,0:T(8,128)S(1)} %reshape.1029), channel_id=1, source_target_pairs={{0,8},{4,12},{8,0},{12,4},{1,9},{5,13},{9,1},{13,5},{2,10},{6,14},... | collective-permute-start | bytes 55304 | tf_op jit(solution)/shard_map/ppermute | solution.py:114
  8.3 0.2 multiply_reduce_fusion.23
  8.9 0.4 broadcast_select_fusion.2
  9.6 1.0 %collective-permute-done = f32[9,512]{1,0:T(8,128)S(1)} collective-permute-done((f32[9,512]{1,0:T(8,128)S(1)}, f32[9,512]{1,0:T(8,128)S(1)}, u32[]{:S(2)}, u32[]{:S(2)}) %collective-permute-start) | collective-permute-done | bytes 18464 | tf_op jit(solution)/shard_map/ppermute | solution.py:114
  10.6 1.6 %collective-permute-start.1 = (f32[9,512]{1,0:T(8,128)S(1)}, f32[9,512]{1,0:T(8,128)S(1)}, u32[]{:S(2)}, u32[]{:S(2)}) collective-permute-start(f32[9,512]{1,0:T(8,128)S(1)} %add.135), channel_id=1, source_target_pairs={{0,4},{4,0},{8,12},{12,8},{1,5},{5,1},{9,13},{13,9},{2,6},{6,2},{1... | collective-permute-start | bytes 55304 | tf_op jit(solution)/shard_map/ppermute | solution.py:114
  12.1 1.6 %fusion = f32[128,192]{0,1:T(8,128)S(1)} fusion(bf16[192,4096]{1,0:T(8,128)(2,1)S(1)} %bitcast.207, bf16[192,4096]{1,0:T(8,128)(2,1)S(1)} %bitcast.206, bf16[192,4096]{1,0:T(8,128)(2,1)S(1)} %bitcast.205, bf16[128,4096]{1,0:T(8,128)(2,1)S(1)} %fusion.27), kind=kOutput, calls=%fused_computation | convolution fusion | flops 627572736 | bytes 5865472 | tf_op jit(solution)/shard_map/dot_general | solution.py:46
  14.2 0.3 collective-permute-done.1
  14.9 0.6 fusion.57
  15.5 0.4 copy-done
  16.2 0.2 broadcast_select_fusion.11
  16.5 1.1 %fusion.9 = f32[128,96]{0,1:T(8,128)S(1)} fusion(bf16[96,4096]{1,0:T(8,128)(2,1)S(1)} %bitcast.217, bf16[96,4096]{1,0:T(8,128)(2,1)S(1)} %bitcast.216, bf16[96,4096]{1,0:T(8,128)(2,1)S(1)} %bitcast.215, bf16[128,4096]{1,0:T(8,128)(2,1)S(1)} %fusion.27), kind=kOutput, calls=%fused_computation.14 | convolution fusion | flops 318504960 | bytes 3457024 | tf_op jit(solution)/shard_map/dot_general | solution.py:46
  18.0 0.3 collective-permute-start.2
  18.3 1.6 %collective-permute-start.5 = (f32[6,4096]{1,0:T(8,128)S(1)}, f32[6,4096]{1,0:T(8,128)S(1)}, u32[]{:S(2)}, u32[]{:S(2)}) collective-permute-start(f32[6,4096]{1,0:T(8,128)S(1)} %add.141), channel_id=1, source_target_pairs={{0,2},{1,3},{2,0},{3,1},{4,6},{5,7},{6,4},{7,5},{8,10},{9,11},{10,... | collective-permute-start | bytes 294920 | tf_op jit(solution)/shard_map/ppermute | solution.py:114
  19.9 1.2 %collective-permute-start.3 = (f32[4,4096]{1,0:T(4,128)S(1)}, f32[4,4096]{1,0:T(4,128)S(1)}, u32[]{:S(2)}, u32[]{:S(2)}) collective-permute-start(f32[4,4096]{1,0:T(4,128)S(1)} %fusion.154), channel_id=1, source_target_pairs={{0,2},{1,3},{2,0},{3,1},{4,6},{5,7},{6,4},{7,5},{8,10},{9,11},{10,... | collective-permute-start | bytes 196616 | tf_op jit(solution)/shard_map/ppermute | solution.py:114
  21.2 4.3 %collective-permute-done.3 = f32[4,4096]{1,0:T(4,128)S(1)} collective-permute-done((f32[4,4096]{1,0:T(4,128)S(1)}, f32[4,4096]{1,0:T(4,128)S(1)}, u32[]{:S(2)}, u32[]{:S(2)}) %collective-permute-start.3) | collective-permute-done | bytes 65568 | tf_op jit(solution)/shard_map/ppermute | solution.py:114
  26.8 0.7 fusion.54
  27.5 0.2 select_reduce_fusion.2
  27.8 0.4 multiply_reduce_fusion.4
  28.3 0.2 select_bitcast_fusion.8
  28.5 0.7 fusion.64
  29.7 2.6 %collective-permute-start.6 = (f32[10,512]{1,0:T(8,128)S(1)}, f32[10,512]{1,0:T(8,128)S(1)}, u32[]{:S(2)}, u32[]{:S(2)}) collective-permute-start(f32[10,512]{1,0:T(8,128)S(1)} %pad_maximum_fusion.21), channel_id=1, source_target_pairs={{0,8},{4,12},{8,0},{12,4},{1,9},{5,13},{9,1},{13,5},{2,10},{6,14},... | collective-permute-start | bytes 61448 | tf_op jit(solution)/shard_map/ppermute | solution.py:114
  32.5 2.3 %collective-permute-done.6 = f32[10,512]{1,0:T(8,128)S(1)} collective-permute-done((f32[10,512]{1,0:T(8,128)S(1)}, f32[10,512]{1,0:T(8,128)S(1)}, u32[]{:S(2)}, u32[]{:S(2)}) %collective-permute-start.6) | collective-permute-done | bytes 20512 | tf_op jit(solution)/shard_map/ppermute | solution.py:114
  34.8 1.4 %collective-permute-start.7 = (f32[10,512]{1,0:T(8,128)S(1)}, f32[10,512]{1,0:T(8,128)S(1)}, u32[]{:S(2)}, u32[]{:S(2)}) collective-permute-start(f32[10,512]{1,0:T(8,128)S(1)} %fusion.153), channel_id=1, source_target_pairs={{0,4},{4,0},{8,12},{12,8},{1,5},{5,1},{9,13},{13,9},{2,6},{6,2},{1... | collective-permute-start | bytes 61448 | tf_op jit(solution)/shard_map/ppermute | solution.py:114
  36.2 0.6 fusion.148
  36.8 2.0 %collective-permute-done.7 = f32[10,512]{1,0:T(8,128)S(1)} collective-permute-done((f32[10,512]{1,0:T(8,128)S(1)}, f32[10,512]{1,0:T(8,128)S(1)}, u32[]{:S(2)}, u32[]{:S(2)}) %collective-permute-start.7) | collective-permute-done | bytes 20512 | tf_op jit(solution)/shard_map/ppermute | solution.py:114
  38.7 0.7 slice_reduce_fusion.5
  41.8 0.6 fusion.56
  42.6 0.3 multiply_reduce_fusion.13
  43.0 0.2 broadcast_select_fusion.8
  43.2 1.1 %fusion.15 = f32[128,96]{0,1:T(8,128)S(1)} fusion(bf16[96,4096]{1,0:T(8,128)(2,1)S(1)} %bitcast.220, bf16[96,4096]{1,0:T(8,128)(2,1)S(1)} %bitcast.219, bf16[96,4096]{1,0:T(8,128)(2,1)S(1)} %bitcast.218, bf16[128,4096]{1,0:T(8,128)(2,1)S(1)} %fusion.27), kind=kOutput, calls=%fused_computation.20 | convolution fusion | flops 318504960 | bytes 3457024 | tf_op jit(solution)/shard_map/dot_general | solution.py:46
  44.8 1.2 %collective-permute-done.8 = f32[4,4096]{1,0:T(4,128)S(1)} collective-permute-done((f32[4,4096]{1,0:T(4,128)S(1)}, f32[4,4096]{1,0:T(4,128)S(1)}, u32[]{:S(2)}, u32[]{:S(2)}) %collective-permute-start.8) | collective-permute-done | bytes 65568 | tf_op jit(solution)/shard_map/ppermute | solution.py:114
  46.1 1.6 %collective-permute-start.9 = (f32[4,4096]{1,0:T(4,128)S(1)}, f32[4,4096]{1,0:T(4,128)S(1)}, u32[]{:S(2)}, u32[]{:S(2)}) collective-permute-start(f32[4,4096]{1,0:T(4,128)S(1)} %fusion.152), channel_id=1, source_target_pairs={{0,2},{1,3},{2,0},{3,1},{4,6},{5,7},{6,4},{7,5},{8,10},{9,11},{10,... | collective-permute-start | bytes 196616 | tf_op jit(solution)/shard_map/ppermute | solution.py:114
  47.7 2.8 %collective-permute-done.9 = f32[4,4096]{1,0:T(4,128)S(1)} collective-permute-done((f32[4,4096]{1,0:T(4,128)S(1)}, f32[4,4096]{1,0:T(4,128)S(1)}, u32[]{:S(2)}, u32[]{:S(2)}) %collective-permute-start.9) | collective-permute-done | bytes 65568 | tf_op jit(solution)/shard_map/ppermute | solution.py:114
  50.9 0.7 fusion.53
  51.6 0.2 select_reduce_fusion.1
  52.0 0.4 multiply_reduce_fusion.2
  52.5 0.2 select_bitcast_fusion.5
  52.7 0.7 fusion.61
  53.8 2.5 %collective-permute-start.10 = (f32[10,512]{1,0:T(8,128)S(1)}, f32[10,512]{1,0:T(8,128)S(1)}, u32[]{:S(2)}, u32[]{:S(2)}) collective-permute-start(f32[10,512]{1,0:T(8,128)S(1)} %pad_maximum_fusion.22), channel_id=1, source_target_pairs={{0,8},{4,12},{8,0},{12,4},{1,9},{5,13},{9,1},{13,5},{2,10},{6,14},... | collective-permute-start | bytes 61448 | tf_op jit(solution)/shard_map/ppermute | solution.py:114
  56.5 2.3 %collective-permute-done.10 = f32[10,512]{1,0:T(8,128)S(1)} collective-permute-done((f32[10,512]{1,0:T(8,128)S(1)}, f32[10,512]{1,0:T(8,128)S(1)}, u32[]{:S(2)}, u32[]{:S(2)}) %collective-permute-start.10) | collective-permute-done | bytes 20512 | tf_op jit(solution)/shard_map/ppermute | solution.py:114
  58.7 1.4 %collective-permute-start.11 = (f32[10,512]{1,0:T(8,128)S(1)}, f32[10,512]{1,0:T(8,128)S(1)}, u32[]{:S(2)}, u32[]{:S(2)}) collective-permute-start(f32[10,512]{1,0:T(8,128)S(1)} %fusion.151), channel_id=1, source_target_pairs={{0,4},{4,0},{8,12},{12,8},{1,5},{5,1},{9,13},{13,9},{2,6},{6,2},{1... | collective-permute-start | bytes 61448 | tf_op jit(solution)/shard_map/ppermute | solution.py:114
  60.2 0.6 fusion.147
  62.7 0.6 slice_reduce_fusion.4
  65.7 0.6 fusion.55
  66.6 0.2 broadcast_select_fusion.5
  66.9 1.1 %fusion.21 = f32[128,96]{0,1:T(8,128)S(1)} fusion(bf16[96,4096]{1,0:T(8,128)(2,1)S(1)} %bitcast.223, bf16[96,4096]{1,0:T(8,128)(2,1)S(1)} %bitcast.222, bf16[96,4096]{1,0:T(8,128)(2,1)S(1)} %bitcast.221, bf16[128,4096]{1,0:T(8,128)(2,1)S(1)} %fusion.27), kind=kOutput, calls=%fused_computation.26 | convolution fusion | flops 318504960 | bytes 3457024 | tf_op jit(solution)/shard_map/dot_general | solution.py:46
  68.5 1.2 %collective-permute-done.12 = f32[4,4096]{1,0:T(4,128)S(1)} collective-permute-done((f32[4,4096]{1,0:T(4,128)S(1)}, f32[4,4096]{1,0:T(4,128)S(1)}, u32[]{:S(2)}, u32[]{:S(2)}) %collective-permute-start.12) | collective-permute-done | bytes 65568 | tf_op jit(solution)/shard_map/ppermute | solution.py:114
  69.8 1.6 %collective-permute-start.13 = (f32[4,4096]{1,0:T(4,128)S(1)}, f32[4,4096]{1,0:T(4,128)S(1)}, u32[]{:S(2)}, u32[]{:S(2)}) collective-permute-start(f32[4,4096]{1,0:T(4,128)S(1)} %fusion.150), channel_id=1, source_target_pairs={{0,2},{1,3},{2,0},{3,1},{4,6},{5,7},{6,4},{7,5},{8,10},{9,11},{10,... | collective-permute-start | bytes 196616 | tf_op jit(solution)/shard_map/ppermute | solution.py:114
  71.3 2.8 %collective-permute-done.13 = f32[4,4096]{1,0:T(4,128)S(1)} collective-permute-done((f32[4,4096]{1,0:T(4,128)S(1)}, f32[4,4096]{1,0:T(4,128)S(1)}, u32[]{:S(2)}, u32[]{:S(2)}) %collective-permute-start.13) | collective-permute-done | bytes 65568 | tf_op jit(solution)/shard_map/ppermute | solution.py:114
  74.6 0.7 fusion.52
  75.3 0.2 select_reduce_fusion
  75.7 0.4 multiply_reduce_fusion
  76.1 0.2 select_bitcast_fusion.2
  76.4 0.7 fusion.58
  77.4 2.9 %collective-permute-start.14 = (f32[10,512]{1,0:T(8,128)S(1)}, f32[10,512]{1,0:T(8,128)S(1)}, u32[]{:S(2)}, u32[]{:S(2)}) collective-permute-start(f32[10,512]{1,0:T(8,128)S(1)} %pad_maximum_fusion.23), channel_id=1, source_target_pairs={{0,8},{4,12},{8,0},{12,4},{1,9},{5,13},{9,1},{13,5},{2,10},{6,14},... | collective-permute-start | bytes 61448 | tf_op jit(solution)/shard_map/ppermute | solution.py:114
  80.5 1.8 %collective-permute-done.14 = f32[10,512]{1,0:T(8,128)S(1)} collective-permute-done((f32[10,512]{1,0:T(8,128)S(1)}, f32[10,512]{1,0:T(8,128)S(1)}, u32[]{:S(2)}, u32[]{:S(2)}) %collective-permute-start.14) | collective-permute-done | bytes 20512 | tf_op jit(solution)/shard_map/ppermute | solution.py:114
  82.3 1.4 %collective-permute-start.15 = (f32[10,512]{1,0:T(8,128)S(1)}, f32[10,512]{1,0:T(8,128)S(1)}, u32[]{:S(2)}, u32[]{:S(2)}) collective-permute-start(f32[10,512]{1,0:T(8,128)S(1)} %fusion.149), channel_id=1, source_target_pairs={{0,4},{4,0},{8,12},{12,8},{1,5},{5,1},{9,13},{13,9},{2,6},{6,2},{1... | collective-permute-start | bytes 61448 | tf_op jit(solution)/shard_map/ppermute | solution.py:114
  83.7 0.6 fusion.146
  86.3 0.6 slice_reduce_fusion.3
  88.8 0.7 fusion.121
  (155 shorter events, 9.1 us)
Async XLA Ops:
  3.2 5.2 %copy-start.1 = (f32[2,3,4096]{2,0,1:T(2,128)S(1)}, f32[2,3,4096]{2,0,1:T(2,128)}, u32[]{:S(2)}) copy-start(f32[2,3,4096]{2,0,1:T(2,128)} %param.8) | copy-start | bytes 294916
  3.2 5.6 %copy-start.4 = (s32[4096]{0:T(1024)S(1)}, s32[4096]{0:T(1024)}, u32[]{:S(2)}) copy-start(s32[4096]{0:T(1024)} %param.10) | copy-start | bytes 49156
  4.2 6.4 %collective-permute-start = (f32[9,512]{1,0:T(8,128)S(1)}, f32[9,512]{1,0:T(8,128)S(1)}, u32[]{:S(2)}, u32[]{:S(2)}) collective-permute-start(f32[9,512]{1,0:T(8,128)S(1)} %reshape.1029), channel_id=1, source_target_pairs={{0,8},{4,12},{8,0},{12,4},{1,9},{5,13},{9,1},{13,5},{2,10},{6,14},... | collective-permute-start | bytes 55304 | tf_op jit(solution)/shard_map/ppermute | solution.py:114
  10.6 3.9 %collective-permute-start.1 = (f32[9,512]{1,0:T(8,128)S(1)}, f32[9,512]{1,0:T(8,128)S(1)}, u32[]{:S(2)}, u32[]{:S(2)}) collective-permute-start(f32[9,512]{1,0:T(8,128)S(1)} %add.135), channel_id=1, source_target_pairs={{0,4},{4,0},{8,12},{12,8},{1,5},{5,1},{9,13},{13,9},{2,6},{6,2},{1... | collective-permute-start | bytes 55304 | tf_op jit(solution)/shard_map/ppermute | solution.py:114
  12.1 2.4 %copy-start.2 = (f32[9,512]{1,0:T(8,128)S(1)}, f32[9,512]{1,0:T(8,128)}, u32[]{:S(2)}) copy-start(f32[9,512]{1,0:T(8,128)} %param.13) | copy-start | bytes 55300
  12.1 2.4 %copy-start.3 = (f32[512]{0:T(512)S(1)}, f32[512]{0:T(512)}, u32[]{:S(2)}) copy-start(f32[512]{0:T(512)} %param.12) | copy-start | bytes 6148
  14.1 4.2 %collective-permute-start.4 = (f32[6,4096]{1,0:T(8,128)S(1)}, f32[6,4096]{1,0:T(8,128)S(1)}, u32[]{:S(2)}, u32[]{:S(2)}) collective-permute-start(f32[6,4096]{1,0:T(8,128)S(1)} %reshape.1039), channel_id=1, source_target_pairs={{0,1},{1,0},{2,3},{3,2},{4,5},{5,4},{6,7},{7,6},{8,9},{9,8},{10,11... | collective-permute-start | bytes 294920 | tf_op jit(solution)/shard_map/ppermute | solution.py:114
  14.9 1.0 %copy-start = (f32[2,9,4096]{2,0,1:T(2,128)S(1)}, f32[2,9,4096]{2,0,1:T(2,128)}, u32[]{:S(2)}) copy-start(f32[2,9,4096]{2,0,1:T(2,128)} %param.7) | copy-start | bytes 884740
  17.6 8.1 %copy-start.5 = (f32[4096]{0:T(1024)S(1)}, f32[4096]{0:T(1024)}, u32[]{:S(2)}) copy-start(f32[4096]{0:T(1024)} %param.11) | copy-start | bytes 49156
  18.0 1.9 %collective-permute-start.2 = (f32[4,4096]{1,0:T(4,128)S(1)}, f32[4,4096]{1,0:T(4,128)S(1)}, u32[]{:S(2)}, u32[]{:S(2)}) collective-permute-start(f32[4,4096]{1,0:T(4,128)S(1)} %pad_maximum_fusion.18), channel_id=1, source_target_pairs={{0,1},{1,0},{2,3},{3,2},{4,5},{5,4},{6,7},{7,6},{8,9},{9,8},{10,11... | collective-permute-start | bytes 196616 | tf_op jit(solution)/shard_map/ppermute | solution.py:114
  18.3 7.2 %collective-permute-start.5 = (f32[6,4096]{1,0:T(8,128)S(1)}, f32[6,4096]{1,0:T(8,128)S(1)}, u32[]{:S(2)}, u32[]{:S(2)}) collective-permute-start(f32[6,4096]{1,0:T(8,128)S(1)} %add.141), channel_id=1, source_target_pairs={{0,2},{1,3},{2,0},{3,1},{4,6},{5,7},{6,4},{7,5},{8,10},{9,11},{10,... | collective-permute-start | bytes 294920 | tf_op jit(solution)/shard_map/ppermute | solution.py:114
  19.9 5.5 %collective-permute-start.3 = (f32[4,4096]{1,0:T(4,128)S(1)}, f32[4,4096]{1,0:T(4,128)S(1)}, u32[]{:S(2)}, u32[]{:S(2)}) collective-permute-start(f32[4,4096]{1,0:T(4,128)S(1)} %fusion.154), channel_id=1, source_target_pairs={{0,2},{1,3},{2,0},{3,1},{4,6},{5,7},{6,4},{7,5},{8,10},{9,11},{10,... | collective-permute-start | bytes 196616 | tf_op jit(solution)/shard_map/ppermute | solution.py:114
  29.7 5.1 %collective-permute-start.6 = (f32[10,512]{1,0:T(8,128)S(1)}, f32[10,512]{1,0:T(8,128)S(1)}, u32[]{:S(2)}, u32[]{:S(2)}) collective-permute-start(f32[10,512]{1,0:T(8,128)S(1)} %pad_maximum_fusion.21), channel_id=1, source_target_pairs={{0,8},{4,12},{8,0},{12,4},{1,9},{5,13},{9,1},{13,5},{2,10},{6,14},... | collective-permute-start | bytes 61448 | tf_op jit(solution)/shard_map/ppermute | solution.py:114
  34.8 4.0 %collective-permute-start.7 = (f32[10,512]{1,0:T(8,128)S(1)}, f32[10,512]{1,0:T(8,128)S(1)}, u32[]{:S(2)}, u32[]{:S(2)}) collective-permute-start(f32[10,512]{1,0:T(8,128)S(1)} %fusion.153), channel_id=1, source_target_pairs={{0,4},{4,0},{8,12},{12,8},{1,5},{5,1},{9,13},{13,9},{2,6},{6,2},{1... | collective-permute-start | bytes 61448 | tf_op jit(solution)/shard_map/ppermute | solution.py:114
  44.8 1.3 %collective-permute-start.8 = (f32[4,4096]{1,0:T(4,128)S(1)}, f32[4,4096]{1,0:T(4,128)S(1)}, u32[]{:S(2)}, u32[]{:S(2)}) collective-permute-start(f32[4,4096]{1,0:T(4,128)S(1)} %pad_maximum_fusion.19), channel_id=1, source_target_pairs={{0,1},{1,0},{2,3},{3,2},{4,5},{5,4},{6,7},{7,6},{8,9},{9,8},{10,11... | collective-permute-start | bytes 196616 | tf_op jit(solution)/shard_map/ppermute | solution.py:114
  46.1 4.3 %collective-permute-start.9 = (f32[4,4096]{1,0:T(4,128)S(1)}, f32[4,4096]{1,0:T(4,128)S(1)}, u32[]{:S(2)}, u32[]{:S(2)}) collective-permute-start(f32[4,4096]{1,0:T(4,128)S(1)} %fusion.152), channel_id=1, source_target_pairs={{0,2},{1,3},{2,0},{3,1},{4,6},{5,7},{6,4},{7,5},{8,10},{9,11},{10,... | collective-permute-start | bytes 196616 | tf_op jit(solution)/shard_map/ppermute | solution.py:114
  53.8 4.9 %collective-permute-start.10 = (f32[10,512]{1,0:T(8,128)S(1)}, f32[10,512]{1,0:T(8,128)S(1)}, u32[]{:S(2)}, u32[]{:S(2)}) collective-permute-start(f32[10,512]{1,0:T(8,128)S(1)} %pad_maximum_fusion.22), channel_id=1, source_target_pairs={{0,8},{4,12},{8,0},{12,4},{1,9},{5,13},{9,1},{13,5},{2,10},{6,14},... | collective-permute-start | bytes 61448 | tf_op jit(solution)/shard_map/ppermute | solution.py:114
  58.7 4.0 %collective-permute-start.11 = (f32[10,512]{1,0:T(8,128)S(1)}, f32[10,512]{1,0:T(8,128)S(1)}, u32[]{:S(2)}, u32[]{:S(2)}) collective-permute-start(f32[10,512]{1,0:T(8,128)S(1)} %fusion.151), channel_id=1, source_target_pairs={{0,4},{4,0},{8,12},{12,8},{1,5},{5,1},{9,13},{13,9},{2,6},{6,2},{1... | collective-permute-start | bytes 61448 | tf_op jit(solution)/shard_map/ppermute | solution.py:114
  68.4 1.3 %collective-permute-start.12 = (f32[4,4096]{1,0:T(4,128)S(1)}, f32[4,4096]{1,0:T(4,128)S(1)}, u32[]{:S(2)}, u32[]{:S(2)}) collective-permute-start(f32[4,4096]{1,0:T(4,128)S(1)} %pad_maximum_fusion.20), channel_id=1, source_target_pairs={{0,1},{1,0},{2,3},{3,2},{4,5},{5,4},{6,7},{7,6},{8,9},{9,8},{10,11... | collective-permute-start | bytes 196616 | tf_op jit(solution)/shard_map/ppermute | solution.py:114
  69.8 4.3 %collective-permute-start.13 = (f32[4,4096]{1,0:T(4,128)S(1)}, f32[4,4096]{1,0:T(4,128)S(1)}, u32[]{:S(2)}, u32[]{:S(2)}) collective-permute-start(f32[4,4096]{1,0:T(4,128)S(1)} %fusion.150), channel_id=1, source_target_pairs={{0,2},{1,3},{2,0},{3,1},{4,6},{5,7},{6,4},{7,5},{8,10},{9,11},{10,... | collective-permute-start | bytes 196616 | tf_op jit(solution)/shard_map/ppermute | solution.py:114
  77.4 4.9 %collective-permute-start.14 = (f32[10,512]{1,0:T(8,128)S(1)}, f32[10,512]{1,0:T(8,128)S(1)}, u32[]{:S(2)}, u32[]{:S(2)}) collective-permute-start(f32[10,512]{1,0:T(8,128)S(1)} %pad_maximum_fusion.23), channel_id=1, source_target_pairs={{0,8},{4,12},{8,0},{12,4},{1,9},{5,13},{9,1},{13,5},{2,10},{6,14},... | collective-permute-start | bytes 61448 | tf_op jit(solution)/shard_map/ppermute | solution.py:114
  82.3 4.0 %collective-permute-start.15 = (f32[10,512]{1,0:T(8,128)S(1)}, f32[10,512]{1,0:T(8,128)S(1)}, u32[]{:S(2)}, u32[]{:S(2)}) collective-permute-start(f32[10,512]{1,0:T(8,128)S(1)} %fusion.149), channel_id=1, source_target_pairs={{0,4},{4,0},{8,12},{12,8},{1,5},{5,1},{9,13},{13,9},{2,6},{6,2},{1... | collective-permute-start | bytes 61448 | tf_op jit(solution)/shard_map/ppermute | solution.py:114

commit v21 on v20

--- a/solution.py
+++ b/solution.py
@@ -109,10 +109,10 @@
         return (value + peers[0]) + (peers[1] + peers[2])
     if size & (size - 1):
         return lax.psum(value, axis)
-    step = size // 2 if axis == "pts" else 1
+    step = size // 2 if axis == "cam" else 1
     while 0 < step < size:
         value = value + lax.ppermute(value, axis, [(i, i ^ step) for i in range(size)])
-        step = step // 2 if axis == "pts" else step * 2
+        step = step // 2 if axis == "cam" else step * 2
     return value
 
 

time: 89.9 us -> 89.1 us (level)
  starting transfers between devices: 24.4 us -> 18.9 us
  waiting for transfers between devices: 22 us -> 26.8 us
    ppermute x16, starting transfers between devices: 24.4 us -> 18.9 us  [allsum(): lax.ppermute(value, axis, [(i, i ^ step) for i in range(size)])]
    ppermute x16, waiting for transfers between devices: 22 us -> 26.8 us  [allsum(): lax.ppermute(value, axis, [(i, i ^ step) for i in range(size)])]
  transfers between devices with their start and end apart: 16 -> 16, of which waited for: 12 -> 13; matrix products, arithmetic and copies ran while one was open for 10% -> 10% of each run, Pallas kernels for 0% -> 0%
where the time goes in v21:
time: 89.1 us; the launch traced here: 88.8 us
  waiting for transfers between devices  26.8 us (30%)
  starting transfers between devices  18.9 us (21%)
  other arithmetic  13.5 us (15%)
  matrix products  11.6 us (13%)
  between operations  11.3 us (13%)
  local copies, waits for them, and re-layouts  6.67 us (7%)
    ppermute x16, waiting for transfers between devices, allsum(): lax.ppermute(value, axis, [(i, i ^ step) for i in range(size)])  26.8 us
    ppermute x16, starting transfers between devices, allsum(): lax.ppermute(value, axis, [(i, i ^ step) for i in range(size)])  18.9 us
    dot_general x8, matrix products, segsum(): lax.dot_general(self.hot3, spread, (((1,), (1,)), ((), ())), preferred_el...  7.73 us
    dot_general x6, matrix products, gather(): lax.dot_general(stacked, self.hot3t, (((1,), (0,)), ((), ())), preferred_...  3.89 us
    select_n x8, other arithmetic, segsum(): jnp.where(self.low[None], part[:, None, :], jnp.zeros((), BF))  2.11 us
    reshape x12, local copies, waits for them, and re-layouts, segsum(): out.reshape(self.hi, ncol, self.lo).transpose(1, 0, 2)  1.92 us
    reduce_sum x3, other arithmetic, operate(): jnp.sum(img_all[-1:], axis=1, keepdims=True)  1.9 us
  transfers between devices with their start and end apart: 16, of which 13 were waited for; matrix products, arithmetic and copies ran while one was open for 10% of the time, Pallas kernels for 0%

profile of v21, /device:TPU:0, one launch (start us, length us, event | category | flops | bytes accessed | tf_op | source)
XLA Modules:
  0.0 88.8 jit_solution(15273405227041746875)
XLA Ops:
  0.6 0.7 add_select_fusion
  1.4 1.4 %multiply_reduce_fusion.6 = f32[9,4096]{1,0:T(8,128)S(1)} fusion(f32[2,9,4096]{2,0,1:T(2,128)} %param.7), kind=kLoop, calls=%fused_computation.122 | loop fusion | flops 110592 | bytes 442368 | tf_op jit(solution)/shard_map/reduce_sum | solution.py:130
  2.9 0.2 select_bitcast_fusion.11
  3.2 0.7 fusion.67
  4.2 3.1 %collective-permute-start = (f32[9,512]{1,0:T(8,128)S(1)}, f32[9,512]{1,0:T(8,128)S(1)}, u32[]{:S(2)}, u32[]{:S(2)}) collective-permute-start(f32[9,512]{1,0:T(8,128)S(1)} %reshape.1029), channel_id=1, source_target_pairs={{0,4},{4,0},{8,12},{12,8},{1,5},{5,1},{9,13},{13,9},{2,6},{6,2},{1... | collective-permute-start | bytes 55304 | tf_op jit(solution)/shard_map/ppermute | solution.py:114
  7.3 0.2 multiply_reduce_fusion.23
  7.9 0.4 broadcast_select_fusion.2
  8.5 0.7 collective-permute-done
  9.2 3.0 %collective-permute-start.1 = (f32[9,512]{1,0:T(8,128)S(1)}, f32[9,512]{1,0:T(8,128)S(1)}, u32[]{:S(2)}, u32[]{:S(2)}) collective-permute-start(f32[9,512]{1,0:T(8,128)S(1)} %add.135), channel_id=1, source_target_pairs={{0,8},{4,12},{8,0},{12,4},{1,9},{5,13},{9,1},{13,5},{2,10},{6,14},... | collective-permute-start | bytes 55304 | tf_op jit(solution)/shard_map/ppermute | solution.py:114
  12.2 1.6 %fusion = f32[128,192]{0,1:T(8,128)S(1)} fusion(bf16[192,4096]{1,0:T(8,128)(2,1)S(1)} %bitcast.207, bf16[192,4096]{1,0:T(8,128)(2,1)S(1)} %bitcast.206, bf16[192,4096]{1,0:T(8,128)(2,1)S(1)} %bitcast.205, bf16[128,4096]{1,0:T(8,128)(2,1)S(1)} %fusion.27), kind=kOutput, calls=%fused_computation | convolution fusion | flops 627572736 | bytes 5865472 | tf_op jit(solution)/shard_map/dot_general | solution.py:46
  14.2 1.6 %collective-permute-start.4 = (f32[6,4096]{1,0:T(8,128)S(1)}, f32[6,4096]{1,0:T(8,128)S(1)}, u32[]{:S(2)}, u32[]{:S(2)}) collective-permute-start(f32[6,4096]{1,0:T(8,128)S(1)} %reshape.1039), channel_id=1, source_target_pairs={{0,2},{1,3},{2,0},{3,1},{4,6},{5,7},{6,4},{7,5},{8,10},{9,11},{10,... | collective-permute-start | bytes 294920 | tf_op jit(solution)/shard_map/ppermute | solution.py:114
  16.2 0.6 fusion.57
  16.8 0.4 copy-done
  17.5 0.2 broadcast_select_fusion.11
  17.7 1.1 %fusion.9 = f32[128,96]{0,1:T(8,128)S(1)} fusion(bf16[96,4096]{1,0:T(8,128)(2,1)S(1)} %bitcast.217, bf16[96,4096]{1,0:T(8,128)(2,1)S(1)} %bitcast.216, bf16[96,4096]{1,0:T(8,128)(2,1)S(1)} %bitcast.215, bf16[128,4096]{1,0:T(8,128)(2,1)S(1)} %fusion.27), kind=kOutput, calls=%fused_computation.14 | convolution fusion | flops 318504960 | bytes 3457024 | tf_op jit(solution)/shard_map/dot_general | solution.py:46
  19.3 0.6 collective-permute-start.2
  20.0 3.6 %collective-permute-done.2 = f32[4,4096]{1,0:T(4,128)S(1)} collective-permute-done((f32[4,4096]{1,0:T(4,128)S(1)}, f32[4,4096]{1,0:T(4,128)S(1)}, u32[]{:S(2)}, u32[]{:S(2)}) %collective-permute-start.2) | collective-permute-done | bytes 65568 | tf_op jit(solution)/shard_map/ppermute | solution.py:114
  23.8 1.2 %collective-permute-done.3 = f32[4,4096]{1,0:T(4,128)S(1)} collective-permute-done((f32[4,4096]{1,0:T(4,128)S(1)}, f32[4,4096]{1,0:T(4,128)S(1)}, u32[]{:S(2)}, u32[]{:S(2)}) %collective-permute-start.3) | collective-permute-done | bytes 65568 | tf_op jit(solution)/shard_map/ppermute | solution.py:114
  26.3 0.7 fusion.54
  27.0 0.2 select_reduce_fusion.2
  27.3 0.4 multiply_reduce_fusion.4
  27.8 0.2 select_bitcast_fusion.8
  28.1 0.7 fusion.64
  29.2 1.6 %collective-permute-start.6 = (f32[10,512]{1,0:T(8,128)S(1)}, f32[10,512]{1,0:T(8,128)S(1)}, u32[]{:S(2)}, u32[]{:S(2)}) collective-permute-start(f32[10,512]{1,0:T(8,128)S(1)} %pad_maximum_fusion.21), channel_id=1, source_target_pairs={{0,4},{4,0},{8,12},{12,8},{1,5},{5,1},{9,13},{13,9},{2,6},{6,2},{1... | collective-permute-start | bytes 61448 | tf_op jit(solution)/shard_map/ppermute | solution.py:114
  31.0 2.2 %collective-permute-done.6 = f32[10,512]{1,0:T(8,128)S(1)} collective-permute-done((f32[10,512]{1,0:T(8,128)S(1)}, f32[10,512]{1,0:T(8,128)S(1)}, u32[]{:S(2)}, u32[]{:S(2)}) %collective-permute-start.6) | collective-permute-done | bytes 20512 | tf_op jit(solution)/shard_map/ppermute | solution.py:114
  33.2 1.4 %collective-permute-start.7 = (f32[10,512]{1,0:T(8,128)S(1)}, f32[10,512]{1,0:T(8,128)S(1)}, u32[]{:S(2)}, u32[]{:S(2)}) collective-permute-start(f32[10,512]{1,0:T(8,128)S(1)} %fusion.153), channel_id=1, source_target_pairs={{0,8},{4,12},{8,0},{12,4},{1,9},{5,13},{9,1},{13,5},{2,10},{6,14},... | collective-permute-start | bytes 61448 | tf_op jit(solution)/shard_map/ppermute | solution.py:114
  34.5 0.6 fusion.148
  35.1 2.9 %collective-permute-done.7 = f32[10,512]{1,0:T(8,128)S(1)} collective-permute-done((f32[10,512]{1,0:T(8,128)S(1)}, f32[10,512]{1,0:T(8,128)S(1)}, u32[]{:S(2)}, u32[]{:S(2)}) %collective-permute-start.7) | collective-permute-done | bytes 20512 | tf_op jit(solution)/shard_map/ppermute | solution.py:114
  38.1 0.7 slice_reduce_fusion.5
  41.1 0.6 fusion.56
  41.9 0.3 multiply_reduce_fusion.13
  42.3 0.2 broadcast_select_fusion.8
  42.5 1.1 %fusion.15 = f32[128,96]{0,1:T(8,128)S(1)} fusion(bf16[96,4096]{1,0:T(8,128)(2,1)S(1)} %bitcast.220, bf16[96,4096]{1,0:T(8,128)(2,1)S(1)} %bitcast.219, bf16[96,4096]{1,0:T(8,128)(2,1)S(1)} %bitcast.218, bf16[128,4096]{1,0:T(8,128)(2,1)S(1)} %fusion.27), kind=kOutput, calls=%fused_computation.20 | convolution fusion | flops 318504960 | bytes 3457024 | tf_op jit(solution)/shard_map/dot_general | solution.py:46
  44.1 0.6 collective-permute-start.8
  44.7 3.7 %collective-permute-done.8 = f32[4,4096]{1,0:T(4,128)S(1)} collective-permute-done((f32[4,4096]{1,0:T(4,128)S(1)}, f32[4,4096]{1,0:T(4,128)S(1)}, u32[]{:S(2)}, u32[]{:S(2)}) %collective-permute-start.8) | collective-permute-done | bytes 65568 | tf_op jit(solution)/shard_map/ppermute | solution.py:114
  48.5 1.2 %collective-permute-done.9 = f32[4,4096]{1,0:T(4,128)S(1)} collective-permute-done((f32[4,4096]{1,0:T(4,128)S(1)}, f32[4,4096]{1,0:T(4,128)S(1)}, u32[]{:S(2)}, u32[]{:S(2)}) %collective-permute-start.9) | collective-permute-done | bytes 65568 | tf_op jit(solution)/shard_map/ppermute | solution.py:114
  50.2 0.7 fusion.53
  51.0 0.2 select_reduce_fusion.1
  51.3 0.4 multiply_reduce_fusion.2
  51.8 0.2 select_bitcast_fusion.5
  52.0 0.7 fusion.61
  53.1 1.6 %collective-permute-start.10 = (f32[10,512]{1,0:T(8,128)S(1)}, f32[10,512]{1,0:T(8,128)S(1)}, u32[]{:S(2)}, u32[]{:S(2)}) collective-permute-start(f32[10,512]{1,0:T(8,128)S(1)} %pad_maximum_fusion.22), channel_id=1, source_target_pairs={{0,4},{4,0},{8,12},{12,8},{1,5},{5,1},{9,13},{13,9},{2,6},{6,2},{1... | collective-permute-start | bytes 61448 | tf_op jit(solution)/shard_map/ppermute | solution.py:114
  55.0 2.2 %collective-permute-done.10 = f32[10,512]{1,0:T(8,128)S(1)} collective-permute-done((f32[10,512]{1,0:T(8,128)S(1)}, f32[10,512]{1,0:T(8,128)S(1)}, u32[]{:S(2)}, u32[]{:S(2)}) %collective-permute-start.10) | collective-permute-done | bytes 20512 | tf_op jit(solution)/shard_map/ppermute | solution.py:114
  57.1 1.4 %collective-permute-start.11 = (f32[10,512]{1,0:T(8,128)S(1)}, f32[10,512]{1,0:T(8,128)S(1)}, u32[]{:S(2)}, u32[]{:S(2)}) collective-permute-start(f32[10,512]{1,0:T(8,128)S(1)} %fusion.151), channel_id=1, source_target_pairs={{0,8},{4,12},{8,0},{12,4},{1,9},{5,13},{9,1},{13,5},{2,10},{6,14},... | collective-permute-start | bytes 61448 | tf_op jit(solution)/shard_map/ppermute | solution.py:114
  58.5 0.6 fusion.147
  61.1 0.9 %collective-permute-done.11 = f32[10,512]{1,0:T(8,128)S(1)} collective-permute-done((f32[10,512]{1,0:T(8,128)S(1)}, f32[10,512]{1,0:T(8,128)S(1)}, u32[]{:S(2)}, u32[]{:S(2)}) %collective-permute-start.11) | collective-permute-done | bytes 20512 | tf_op jit(solution)/shard_map/ppermute | solution.py:114
  62.0 0.6 slice_reduce_fusion.4
  64.9 0.6 fusion.55
  66.1 1.1 %fusion.21 = f32[128,96]{0,1:T(8,128)S(1)} fusion(bf16[96,4096]{1,0:T(8,128)(2,1)S(1)} %bitcast.223, bf16[96,4096]{1,0:T(8,128)(2,1)S(1)} %bitcast.222, bf16[96,4096]{1,0:T(8,128)(2,1)S(1)} %bitcast.221, bf16[128,4096]{1,0:T(8,128)(2,1)S(1)} %fusion.27), kind=kOutput, calls=%fused_computation.26 | convolution fusion | flops 318504960 | bytes 3457024 | tf_op jit(solution)/shard_map/dot_general | solution.py:46
  67.7 0.6 collective-permute-start.12
  68.3 3.7 %collective-permute-done.12 = f32[4,4096]{1,0:T(4,128)S(1)} collective-permute-done((f32[4,4096]{1,0:T(4,128)S(1)}, f32[4,4096]{1,0:T(4,128)S(1)}, u32[]{:S(2)}, u32[]{:S(2)}) %collective-permute-start.12) | collective-permute-done | bytes 65568 | tf_op jit(solution)/shard_map/ppermute | solution.py:114
  72.1 1.2 %collective-permute-done.13 = f32[4,4096]{1,0:T(4,128)S(1)} collective-permute-done((f32[4,4096]{1,0:T(4,128)S(1)}, f32[4,4096]{1,0:T(4,128)S(1)}, u32[]{:S(2)}, u32[]{:S(2)}) %collective-permute-start.13) | collective-permute-done | bytes 65568 | tf_op jit(solution)/shard_map/ppermute | solution.py:114
  73.9 0.7 fusion.52
  74.6 0.2 select_reduce_fusion
  74.9 0.4 multiply_reduce_fusion
  75.4 0.2 select_bitcast_fusion.2
  75.6 0.7 fusion.58
  76.7 1.6 %collective-permute-start.14 = (f32[10,512]{1,0:T(8,128)S(1)}, f32[10,512]{1,0:T(8,128)S(1)}, u32[]{:S(2)}, u32[]{:S(2)}) collective-permute-start(f32[10,512]{1,0:T(8,128)S(1)} %pad_maximum_fusion.23), channel_id=1, source_target_pairs={{0,4},{4,0},{8,12},{12,8},{1,5},{5,1},{9,13},{13,9},{2,6},{6,2},{1... | collective-permute-start | bytes 61448 | tf_op jit(solution)/shard_map/ppermute | solution.py:114
  78.5 2.2 %collective-permute-done.14 = f32[10,512]{1,0:T(8,128)S(1)} collective-permute-done((f32[10,512]{1,0:T(8,128)S(1)}, f32[10,512]{1,0:T(8,128)S(1)}, u32[]{:S(2)}, u32[]{:S(2)}) %collective-permute-start.14) | collective-permute-done | bytes 20512 | tf_op jit(solution)/shard_map/ppermute | solution.py:114
  80.7 1.4 %collective-permute-start.15 = (f32[10,512]{1,0:T(8,128)S(1)}, f32[10,512]{1,0:T(8,128)S(1)}, u32[]{:S(2)}, u32[]{:S(2)}) collective-permute-start(f32[10,512]{1,0:T(8,128)S(1)} %fusion.149), channel_id=1, source_target_pairs={{0,8},{4,12},{8,0},{12,4},{1,9},{5,13},{9,1},{13,5},{2,10},{6,14},... | collective-permute-start | bytes 61448 | tf_op jit(solution)/shard_map/ppermute | solution.py:114
  82.1 0.6 fusion.146
  84.6 1.0 %collective-permute-done.15 = f32[10,512]{1,0:T(8,128)S(1)} collective-permute-done((f32[10,512]{1,0:T(8,128)S(1)}, f32[10,512]{1,0:T(8,128)S(1)}, u32[]{:S(2)}, u32[]{:S(2)}) %collective-permute-start.15) | collective-permute-done | bytes 20512 | tf_op jit(solution)/shard_map/ppermute | solution.py:114
  85.6 0.6 slice_reduce_fusion.3
  88.1 0.7 fusion.121
  (155 shorter events, 9.3 us)
Async XLA Ops:
  3.2 4.1 %copy-start.1 = (f32[2,3,4096]{2,0,1:T(2,128)S(1)}, f32[2,3,4096]{2,0,1:T(2,128)}, u32[]{:S(2)}) copy-start(f32[2,3,4096]{2,0,1:T(2,128)} %param.8) | copy-start | bytes 294916
  3.2 4.6 %copy-start.4 = (s32[4096]{0:T(1024)S(1)}, s32[4096]{0:T(1024)}, u32[]{:S(2)}) copy-start(s32[4096]{0:T(1024)} %param.10) | copy-start | bytes 49156
  4.2 5.0 %collective-permute-start = (f32[9,512]{1,0:T(8,128)S(1)}, f32[9,512]{1,0:T(8,128)S(1)}, u32[]{:S(2)}, u32[]{:S(2)}) collective-permute-start(f32[9,512]{1,0:T(8,128)S(1)} %reshape.1029), channel_id=1, source_target_pairs={{0,4},{4,0},{8,12},{12,8},{1,5},{5,1},{9,13},{13,9},{2,6},{6,2},{1... | collective-permute-start | bytes 55304 | tf_op jit(solution)/shard_map/ppermute | solution.py:114
  9.2 6.6 %collective-permute-start.1 = (f32[9,512]{1,0:T(8,128)S(1)}, f32[9,512]{1,0:T(8,128)S(1)}, u32[]{:S(2)}, u32[]{:S(2)}) collective-permute-start(f32[9,512]{1,0:T(8,128)S(1)} %add.135), channel_id=1, source_target_pairs={{0,8},{4,12},{8,0},{12,4},{1,9},{5,13},{9,1},{13,5},{2,10},{6,14},... | collective-permute-start | bytes 55304 | tf_op jit(solution)/shard_map/ppermute | solution.py:114
  12.2 3.5 %copy-start.2 = (f32[9,512]{1,0:T(8,128)S(1)}, f32[9,512]{1,0:T(8,128)}, u32[]{:S(2)}) copy-start(f32[9,512]{1,0:T(8,128)} %param.13) | copy-start | bytes 55300
  12.2 3.5 %copy-start.3 = (f32[512]{0:T(512)S(1)}, f32[512]{0:T(512)}, u32[]{:S(2)}) copy-start(f32[512]{0:T(512)} %param.12) | copy-start | bytes 6148
  14.2 5.7 %collective-permute-start.4 = (f32[6,4096]{1,0:T(8,128)S(1)}, f32[6,4096]{1,0:T(8,128)S(1)}, u32[]{:S(2)}, u32[]{:S(2)}) collective-permute-start(f32[6,4096]{1,0:T(8,128)S(1)} %reshape.1039), channel_id=1, source_target_pairs={{0,2},{1,3},{2,0},{3,1},{4,6},{5,7},{6,4},{7,5},{8,10},{9,11},{10,... | collective-permute-start | bytes 294920 | tf_op jit(solution)/shard_map/ppermute | solution.py:114
  16.2 1.0 %copy-start = (f32[2,9,4096]{2,0,1:T(2,128)S(1)}, f32[2,9,4096]{2,0,1:T(2,128)}, u32[]{:S(2)}) copy-start(f32[2,9,4096]{2,0,1:T(2,128)} %param.7) | copy-start | bytes 884740
  18.9 6.4 %copy-start.5 = (f32[4096]{0:T(1024)S(1)}, f32[4096]{0:T(1024)}, u32[]{:S(2)}) copy-start(f32[4096]{0:T(1024)} %param.11) | copy-start | bytes 49156
  19.3 4.3 %collective-permute-start.2 = (f32[4,4096]{1,0:T(4,128)S(1)}, f32[4,4096]{1,0:T(4,128)S(1)}, u32[]{:S(2)}, u32[]{:S(2)}) collective-permute-start(f32[4,4096]{1,0:T(4,128)S(1)} %pad_maximum_fusion.18), channel_id=1, source_target_pairs={{0,2},{1,3},{2,0},{3,1},{4,6},{5,7},{6,4},{7,5},{8,10},{9,11},{10,... | collective-permute-start | bytes 196616 | tf_op jit(solution)/shard_map/ppermute | solution.py:114
  19.9 5.1 %collective-permute-start.5 = (f32[6,4096]{1,0:T(8,128)S(1)}, f32[6,4096]{1,0:T(8,128)S(1)}, u32[]{:S(2)}, u32[]{:S(2)}) collective-permute-start(f32[6,4096]{1,0:T(8,128)S(1)} %add.141), channel_id=1, source_target_pairs={{0,1},{1,0},{2,3},{3,2},{4,5},{5,4},{6,7},{7,6},{8,9},{9,8},{10,11... | collective-permute-start | bytes 294920 | tf_op jit(solution)/shard_map/ppermute | solution.py:114
  23.7 1.3 %collective-permute-start.3 = (f32[4,4096]{1,0:T(4,128)S(1)}, f32[4,4096]{1,0:T(4,128)S(1)}, u32[]{:S(2)}, u32[]{:S(2)}) collective-permute-start(f32[4,4096]{1,0:T(4,128)S(1)} %fusion.154), channel_id=1, source_target_pairs={{0,1},{1,0},{2,3},{3,2},{4,5},{5,4},{6,7},{7,6},{8,9},{9,8},{10,11... | collective-permute-start | bytes 196616 | tf_op jit(solution)/shard_map/ppermute | solution.py:114
  29.2 4.0 %collective-permute-start.6 = (f32[10,512]{1,0:T(8,128)S(1)}, f32[10,512]{1,0:T(8,128)S(1)}, u32[]{:S(2)}, u32[]{:S(2)}) collective-permute-start(f32[10,512]{1,0:T(8,128)S(1)} %pad_maximum_fusion.21), channel_id=1, source_target_pairs={{0,4},{4,0},{8,12},{12,8},{1,5},{5,1},{9,13},{13,9},{2,6},{6,2},{1... | collective-permute-start | bytes 61448 | tf_op jit(solution)/shard_map/ppermute | solution.py:114
  33.2 4.9 %collective-permute-start.7 = (f32[10,512]{1,0:T(8,128)S(1)}, f32[10,512]{1,0:T(8,128)S(1)}, u32[]{:S(2)}, u32[]{:S(2)}) collective-permute-start(f32[10,512]{1,0:T(8,128)S(1)} %fusion.153), channel_id=1, source_target_pairs={{0,8},{4,12},{8,0},{12,4},{1,9},{5,13},{9,1},{13,5},{2,10},{6,14},... | collective-permute-start | bytes 61448 | tf_op jit(solution)/shard_map/ppermute | solution.py:114
  44.1 4.3 %collective-permute-start.8 = (f32[4,4096]{1,0:T(4,128)S(1)}, f32[4,4096]{1,0:T(4,128)S(1)}, u32[]{:S(2)}, u32[]{:S(2)}) collective-permute-start(f32[4,4096]{1,0:T(4,128)S(1)} %pad_maximum_fusion.19), channel_id=1, source_target_pairs={{0,2},{1,3},{2,0},{3,1},{4,6},{5,7},{6,4},{7,5},{8,10},{9,11},{10,... | collective-permute-start | bytes 196616 | tf_op jit(solution)/shard_map/ppermute | solution.py:114
  48.4 1.3 %collective-permute-start.9 = (f32[4,4096]{1,0:T(4,128)S(1)}, f32[4,4096]{1,0:T(4,128)S(1)}, u32[]{:S(2)}, u32[]{:S(2)}) collective-permute-start(f32[4,4096]{1,0:T(4,128)S(1)} %fusion.152), channel_id=1, source_target_pairs={{0,1},{1,0},{2,3},{3,2},{4,5},{5,4},{6,7},{7,6},{8,9},{9,8},{10,11... | collective-permute-start | bytes 196616 | tf_op jit(solution)/shard_map/ppermute | solution.py:114
  53.1 4.0 %collective-permute-start.10 = (f32[10,512]{1,0:T(8,128)S(1)}, f32[10,512]{1,0:T(8,128)S(1)}, u32[]{:S(2)}, u32[]{:S(2)}) collective-permute-start(f32[10,512]{1,0:T(8,128)S(1)} %pad_maximum_fusion.22), channel_id=1, source_target_pairs={{0,4},{4,0},{8,12},{12,8},{1,5},{5,1},{9,13},{13,9},{2,6},{6,2},{1... | collective-permute-start | bytes 61448 | tf_op jit(solution)/shard_map/ppermute | solution.py:114
  57.1 4.9 %collective-permute-start.11 = (f32[10,512]{1,0:T(8,128)S(1)}, f32[10,512]{1,0:T(8,128)S(1)}, u32[]{:S(2)}, u32[]{:S(2)}) collective-permute-start(f32[10,512]{1,0:T(8,128)S(1)} %fusion.151), channel_id=1, source_target_pairs={{0,8},{4,12},{8,0},{12,4},{1,9},{5,13},{9,1},{13,5},{2,10},{6,14},... | collective-permute-start | bytes 61448 | tf_op jit(solution)/shard_map/ppermute | solution.py:114
  67.7 4.3 %collective-permute-start.12 = (f32[4,4096]{1,0:T(4,128)S(1)}, f32[4,4096]{1,0:T(4,128)S(1)}, u32[]{:S(2)}, u32[]{:S(2)}) collective-permute-start(f32[4,4096]{1,0:T(4,128)S(1)} %pad_maximum_fusion.20), channel_id=1, source_target_pairs={{0,2},{1,3},{2,0},{3,1},{4,6},{5,7},{6,4},{7,5},{8,10},{9,11},{10,... | collective-permute-start | bytes 196616 | tf_op jit(solution)/shard_map/ppermute | solution.py:114
  72.1 1.3 %collective-permute-start.13 = (f32[4,4096]{1,0:T(4,128)S(1)}, f32[4,4096]{1,0:T(4,128)S(1)}, u32[]{:S(2)}, u32[]{:S(2)}) collective-permute-start(f32[4,4096]{1,0:T(4,128)S(1)} %fusion.150), channel_id=1, source_target_pairs={{0,1},{1,0},{2,3},{3,2},{4,5},{5,4},{6,7},{7,6},{8,9},{9,8},{10,11... | collective-permute-start | bytes 196616 | tf_op jit(solution)/shard_map/ppermute | solution.py:114
  76.7 4.0 %collective-permute-start.14 = (f32[10,512]{1,0:T(8,128)S(1)}, f32[10,512]{1,0:T(8,128)S(1)}, u32[]{:S(2)}, u32[]{:S(2)}) collective-permute-start(f32[10,512]{1,0:T(8,128)S(1)} %pad_maximum_fusion.23), channel_id=1, source_target_pairs={{0,4},{4,0},{8,12},{12,8},{1,5},{5,1},{9,13},{13,9},{2,6},{6,2},{1... | collective-permute-start | bytes 61448 | tf_op jit(solution)/shard_map/ppermute | solution.py:114
  80.7 4.9 %collective-permute-start.15 = (f32[10,512]{1,0:T(8,128)S(1)}, f32[10,512]{1,0:T(8,128)S(1)}, u32[]{:S(2)}, u32[]{:S(2)}) collective-permute-start(f32[10,512]{1,0:T(8,128)S(1)} %fusion.149), channel_id=1, source_target_pairs={{0,8},{4,12},{8,0},{12,4},{1,9},{5,13},{9,1},{13,5},{2,10},{6,14},... | collective-permute-start | bytes 61448 | tf_op jit(solution)/shard_map/ppermute | solution.py:114

commit v22 on v21

--- a/solution.py
+++ b/solution.py
@@ -109,10 +109,10 @@
         return (value + peers[0]) + (peers[1] + peers[2])
     if size & (size - 1):
         return lax.psum(value, axis)
-    step = size // 2 if axis == "cam" else 1
+    step = size // 2
     while 0 < step < size:
         value = value + lax.ppermute(value, axis, [(i, i ^ step) for i in range(size)])
-        step = step // 2 if axis == "cam" else step * 2
+        step = step // 2
     return value
 
 

time: 89.1 us -> 89.9 us (level)
  no operation moved by 1% of the time
where the time goes in v22:
time: 89.9 us; the launch traced here: 89.5 us
  waiting for transfers between devices  27.6 us (31%)
  starting transfers between devices  18.8 us (21%)
  other arithmetic  13.5 us (15%)
  matrix products  11.6 us (13%)
  between operations  11.3 us (13%)
  local copies, waits for them, and re-layouts  6.67 us (7%)
    ppermute x16, waiting for transfers between devices, allsum(): lax.ppermute(value, axis, [(i, i ^ step) for i in range(size)])  27.6 us
    ppermute x16, starting transfers between devices, allsum(): lax.ppermute(value, axis, [(i, i ^ step) for i in range(size)])  18.8 us
    dot_general x8, matrix products, segsum(): lax.dot_general(self.hot3, spread, (((1,), (1,)), ((), ())), preferred_el...  7.73 us
    dot_general x6, matrix products, gather(): lax.dot_general(stacked, self.hot3t, (((1,), (0,)), ((), ())), preferred_...  3.9 us
    select_n x8, other arithmetic, segsum(): jnp.where(self.low[None], part[:, None, :], jnp.zeros((), BF))  2.11 us
    reshape x12, local copies, waits for them, and re-layouts, segsum(): out.reshape(self.hi, ncol, self.lo).transpose(1, 0, 2)  1.92 us
    reduce_sum x3, other arithmetic, operate(): jnp.sum(img_all[-1:], axis=1, keepdims=True)  1.9 us
  transfers between devices with their start and end apart: 16, of which 13 were waited for; matrix products, arithmetic and copies ran while one was open for 10% of the time, Pallas kernels for 0%

profile of v22, /device:TPU:0, one launch (start us, length us, event | category | flops | bytes accessed | tf_op | source)
XLA Modules:
  0.0 89.5 jit_solution(12095765556869519475)
XLA Ops:
  0.6 0.7 add_select_fusion
  1.4 1.4 %multiply_reduce_fusion.6 = f32[9,4096]{1,0:T(8,128)S(1)} fusion(f32[2,9,4096]{2,0,1:T(2,128)} %param.7), kind=kLoop, calls=%fused_computation.122 | loop fusion | flops 110592 | bytes 442368 | tf_op jit(solution)/shard_map/reduce_sum | solution.py:130
  2.9 0.2 select_bitcast_fusion.11
  3.2 0.7 fusion.67
  4.2 4.1 %collective-permute-start = (f32[9,512]{1,0:T(8,128)S(1)}, f32[9,512]{1,0:T(8,128)S(1)}, u32[]{:S(2)}, u32[]{:S(2)}) collective-permute-start(f32[9,512]{1,0:T(8,128)S(1)} %reshape.1029), channel_id=1, source_target_pairs={{0,8},{4,12},{8,0},{12,4},{1,9},{5,13},{9,1},{13,5},{2,10},{6,14},... | collective-permute-start | bytes 55304 | tf_op jit(solution)/shard_map/ppermute | solution.py:114
  8.3 0.2 multiply_reduce_fusion.23
  8.9 0.4 broadcast_select_fusion.2
  9.6 1.0 %collective-permute-done = f32[9,512]{1,0:T(8,128)S(1)} collective-permute-done((f32[9,512]{1,0:T(8,128)S(1)}, f32[9,512]{1,0:T(8,128)S(1)}, u32[]{:S(2)}, u32[]{:S(2)}) %collective-permute-start) | collective-permute-done | bytes 18464 | tf_op jit(solution)/shard_map/ppermute | solution.py:114
  10.6 1.6 %collective-permute-start.1 = (f32[9,512]{1,0:T(8,128)S(1)}, f32[9,512]{1,0:T(8,128)S(1)}, u32[]{:S(2)}, u32[]{:S(2)}) collective-permute-start(f32[9,512]{1,0:T(8,128)S(1)} %add.135), channel_id=1, source_target_pairs={{0,4},{4,0},{8,12},{12,8},{1,5},{5,1},{9,13},{13,9},{2,6},{6,2},{1... | collective-permute-start | bytes 55304 | tf_op jit(solution)/shard_map/ppermute | solution.py:114
  12.1 1.6 %fusion = f32[128,192]{0,1:T(8,128)S(1)} fusion(bf16[192,4096]{1,0:T(8,128)(2,1)S(1)} %bitcast.207, bf16[192,4096]{1,0:T(8,128)(2,1)S(1)} %bitcast.206, bf16[192,4096]{1,0:T(8,128)(2,1)S(1)} %bitcast.205, bf16[128,4096]{1,0:T(8,128)(2,1)S(1)} %fusion.27), kind=kOutput, calls=%fused_computation | convolution fusion | flops 627572736 | bytes 5865472 | tf_op jit(solution)/shard_map/dot_general | solution.py:46
  14.1 1.6 %collective-permute-start.4 = (f32[6,4096]{1,0:T(8,128)S(1)}, f32[6,4096]{1,0:T(8,128)S(1)}, u32[]{:S(2)}, u32[]{:S(2)}) collective-permute-start(f32[6,4096]{1,0:T(8,128)S(1)} %reshape.1039), channel_id=1, source_target_pairs={{0,2},{1,3},{2,0},{3,1},{4,6},{5,7},{6,4},{7,5},{8,10},{9,11},{10,... | collective-permute-start | bytes 294920 | tf_op jit(solution)/shard_map/ppermute | solution.py:114
  16.1 0.6 fusion.57
  16.6 0.4 copy-done
  17.4 0.2 broadcast_select_fusion.11
  17.6 1.1 %fusion.9 = f32[128,96]{0,1:T(8,128)S(1)} fusion(bf16[96,4096]{1,0:T(8,128)(2,1)S(1)} %bitcast.217, bf16[96,4096]{1,0:T(8,128)(2,1)S(1)} %bitcast.216, bf16[96,4096]{1,0:T(8,128)(2,1)S(1)} %bitcast.215, bf16[128,4096]{1,0:T(8,128)(2,1)S(1)} %fusion.27), kind=kOutput, calls=%fused_computation.14 | convolution fusion | flops 318504960 | bytes 3457024 | tf_op jit(solution)/shard_map/dot_general | solution.py:46
  19.2 0.6 collective-permute-start.2
  19.9 3.6 %collective-permute-done.2 = f32[4,4096]{1,0:T(4,128)S(1)} collective-permute-done((f32[4,4096]{1,0:T(4,128)S(1)}, f32[4,4096]{1,0:T(4,128)S(1)}, u32[]{:S(2)}, u32[]{:S(2)}) %collective-permute-start.2) | collective-permute-done | bytes 65568 | tf_op jit(solution)/shard_map/ppermute | solution.py:114
  23.7 1.2 %collective-permute-done.3 = f32[4,4096]{1,0:T(4,128)S(1)} collective-permute-done((f32[4,4096]{1,0:T(4,128)S(1)}, f32[4,4096]{1,0:T(4,128)S(1)}, u32[]{:S(2)}, u32[]{:S(2)}) %collective-permute-start.3) | collective-permute-done | bytes 65568 | tf_op jit(solution)/shard_map/ppermute | solution.py:114
  26.2 0.7 fusion.54
  26.9 0.2 select_reduce_fusion.2
  27.2 0.4 multiply_reduce_fusion.4
  27.7 0.2 select_bitcast_fusion.8
  27.9 0.7 fusion.64
  29.1 2.9 %collective-permute-start.6 = (f32[10,512]{1,0:T(8,128)S(1)}, f32[10,512]{1,0:T(8,128)S(1)}, u32[]{:S(2)}, u32[]{:S(2)}) collective-permute-start(f32[10,512]{1,0:T(8,128)S(1)} %pad_maximum_fusion.21), channel_id=1, source_target_pairs={{0,8},{4,12},{8,0},{12,4},{1,9},{5,13},{9,1},{13,5},{2,10},{6,14},... | collective-permute-start | bytes 61448 | tf_op jit(solution)/shard_map/ppermute | solution.py:114
  32.1 2.2 %collective-permute-done.6 = f32[10,512]{1,0:T(8,128)S(1)} collective-permute-done((f32[10,512]{1,0:T(8,128)S(1)}, f32[10,512]{1,0:T(8,128)S(1)}, u32[]{:S(2)}, u32[]{:S(2)}) %collective-permute-start.6) | collective-permute-done | bytes 20512 | tf_op jit(solution)/shard_map/ppermute | solution.py:114
  34.3 0.4 collective-permute-start.7
  34.7 0.6 fusion.148
  35.3 3.0 %collective-permute-done.7 = f32[10,512]{1,0:T(8,128)S(1)} collective-permute-done((f32[10,512]{1,0:T(8,128)S(1)}, f32[10,512]{1,0:T(8,128)S(1)}, u32[]{:S(2)}, u32[]{:S(2)}) %collective-permute-start.7) | collective-permute-done | bytes 20512 | tf_op jit(solution)/shard_map/ppermute | solution.py:114
  38.3 0.7 slice_reduce_fusion.5
  41.4 0.6 fusion.56
  42.1 0.3 multiply_reduce_fusion.13
  42.5 0.2 broadcast_select_fusion.8
  42.8 1.1 %fusion.15 = f32[128,96]{0,1:T(8,128)S(1)} fusion(bf16[96,4096]{1,0:T(8,128)(2,1)S(1)} %bitcast.220, bf16[96,4096]{1,0:T(8,128)(2,1)S(1)} %bitcast.219, bf16[96,4096]{1,0:T(8,128)(2,1)S(1)} %bitcast.218, bf16[128,4096]{1,0:T(8,128)(2,1)S(1)} %fusion.27), kind=kOutput, calls=%fused_computation.20 | convolution fusion | flops 318504960 | bytes 3457024 | tf_op jit(solution)/shard_map/dot_general | solution.py:46
  44.3 0.6 collective-permute-start.8
  44.9 3.7 %collective-permute-done.8 = f32[4,4096]{1,0:T(4,128)S(1)} collective-permute-done((f32[4,4096]{1,0:T(4,128)S(1)}, f32[4,4096]{1,0:T(4,128)S(1)}, u32[]{:S(2)}, u32[]{:S(2)}) %collective-permute-start.8) | collective-permute-done | bytes 65568 | tf_op jit(solution)/shard_map/ppermute | solution.py:114
  48.8 1.2 %collective-permute-done.9 = f32[4,4096]{1,0:T(4,128)S(1)} collective-permute-done((f32[4,4096]{1,0:T(4,128)S(1)}, f32[4,4096]{1,0:T(4,128)S(1)}, u32[]{:S(2)}, u32[]{:S(2)}) %collective-permute-start.9) | collective-permute-done | bytes 65568 | tf_op jit(solution)/shard_map/ppermute | solution.py:114
  50.5 0.7 fusion.53
  51.2 0.2 select_reduce_fusion.1
  51.6 0.4 multiply_reduce_fusion.2
  52.0 0.2 select_bitcast_fusion.5
  52.3 0.7 fusion.61
  53.4 2.5 %collective-permute-start.10 = (f32[10,512]{1,0:T(8,128)S(1)}, f32[10,512]{1,0:T(8,128)S(1)}, u32[]{:S(2)}, u32[]{:S(2)}) collective-permute-start(f32[10,512]{1,0:T(8,128)S(1)} %pad_maximum_fusion.22), channel_id=1, source_target_pairs={{0,8},{4,12},{8,0},{12,4},{1,9},{5,13},{9,1},{13,5},{2,10},{6,14},... | collective-permute-start | bytes 61448 | tf_op jit(solution)/shard_map/ppermute | solution.py:114
  56.1 2.3 %collective-permute-done.10 = f32[10,512]{1,0:T(8,128)S(1)} collective-permute-done((f32[10,512]{1,0:T(8,128)S(1)}, f32[10,512]{1,0:T(8,128)S(1)}, u32[]{:S(2)}, u32[]{:S(2)}) %collective-permute-start.10) | collective-permute-done | bytes 20512 | tf_op jit(solution)/shard_map/ppermute | solution.py:114
  58.4 0.3 collective-permute-start.11
  58.7 0.6 fusion.147
  61.3 1.1 %collective-permute-done.11 = f32[10,512]{1,0:T(8,128)S(1)} collective-permute-done((f32[10,512]{1,0:T(8,128)S(1)}, f32[10,512]{1,0:T(8,128)S(1)}, u32[]{:S(2)}, u32[]{:S(2)}) %collective-permute-start.11) | collective-permute-done | bytes 20512 | tf_op jit(solution)/shard_map/ppermute | solution.py:114
  62.4 0.6 slice_reduce_fusion.4
  65.3 0.6 fusion.55
  66.5 1.1 %fusion.21 = f32[128,96]{0,1:T(8,128)S(1)} fusion(bf16[96,4096]{1,0:T(8,128)(2,1)S(1)} %bitcast.223, bf16[96,4096]{1,0:T(8,128)(2,1)S(1)} %bitcast.222, bf16[96,4096]{1,0:T(8,128)(2,1)S(1)} %bitcast.221, bf16[128,4096]{1,0:T(8,128)(2,1)S(1)} %fusion.27), kind=kOutput, calls=%fused_computation.26 | convolution fusion | flops 318504960 | bytes 3457024 | tf_op jit(solution)/shard_map/dot_general | solution.py:46
  68.1 1.2 %collective-permute-start.12 = (f32[4,4096]{1,0:T(4,128)S(1)}, f32[4,4096]{1,0:T(4,128)S(1)}, u32[]{:S(2)}, u32[]{:S(2)}) collective-permute-start(f32[4,4096]{1,0:T(4,128)S(1)} %pad_maximum_fusion.20), channel_id=1, source_target_pairs={{0,2},{1,3},{2,0},{3,1},{4,6},{5,7},{6,4},{7,5},{8,10},{9,11},{10,... | collective-permute-start | bytes 196616 | tf_op jit(solution)/shard_map/ppermute | solution.py:114
  69.2 3.2 %collective-permute-done.12 = f32[4,4096]{1,0:T(4,128)S(1)} collective-permute-done((f32[4,4096]{1,0:T(4,128)S(1)}, f32[4,4096]{1,0:T(4,128)S(1)}, u32[]{:S(2)}, u32[]{:S(2)}) %collective-permute-start.12) | collective-permute-done | bytes 65568 | tf_op jit(solution)/shard_map/ppermute | solution.py:114
  72.5 1.2 %collective-permute-done.13 = f32[4,4096]{1,0:T(4,128)S(1)} collective-permute-done((f32[4,4096]{1,0:T(4,128)S(1)}, f32[4,4096]{1,0:T(4,128)S(1)}, u32[]{:S(2)}, u32[]{:S(2)}) %collective-permute-start.13) | collective-permute-done | bytes 65568 | tf_op jit(solution)/shard_map/ppermute | solution.py:114
  74.2 0.7 fusion.52
  75.0 0.3 select_reduce_fusion
  75.3 0.4 multiply_reduce_fusion
  75.8 0.2 select_bitcast_fusion.2
  76.0 0.7 fusion.58
  77.1 2.4 %collective-permute-start.14 = (f32[10,512]{1,0:T(8,128)S(1)}, f32[10,512]{1,0:T(8,128)S(1)}, u32[]{:S(2)}, u32[]{:S(2)}) collective-permute-start(f32[10,512]{1,0:T(8,128)S(1)} %pad_maximum_fusion.23), channel_id=1, source_target_pairs={{0,8},{4,12},{8,0},{12,4},{1,9},{5,13},{9,1},{13,5},{2,10},{6,14},... | collective-permute-start | bytes 61448 | tf_op jit(solution)/shard_map/ppermute | solution.py:114
  79.6 2.7 %collective-permute-done.14 = f32[10,512]{1,0:T(8,128)S(1)} collective-permute-done((f32[10,512]{1,0:T(8,128)S(1)}, f32[10,512]{1,0:T(8,128)S(1)}, u32[]{:S(2)}, u32[]{:S(2)}) %collective-permute-start.14) | collective-permute-done | bytes 20512 | tf_op jit(solution)/shard_map/ppermute | solution.py:114
  82.3 0.4 collective-permute-start.15
  82.7 0.6 fusion.146
  85.3 1.1 %collective-permute-done.15 = f32[10,512]{1,0:T(8,128)S(1)} collective-permute-done((f32[10,512]{1,0:T(8,128)S(1)}, f32[10,512]{1,0:T(8,128)S(1)}, u32[]{:S(2)}, u32[]{:S(2)}) %collective-permute-start.15) | collective-permute-done | bytes 20512 | tf_op jit(solution)/shard_map/ppermute | solution.py:114
  86.3 0.6 slice_reduce_fusion.3
  88.8 0.7 fusion.121
  (155 shorter events, 9.3 us)
Async XLA Ops:
  3.2 5.2 %copy-start.1 = (f32[2,3,4096]{2,0,1:T(2,128)S(1)}, f32[2,3,4096]{2,0,1:T(2,128)}, u32[]{:S(2)}) copy-start(f32[2,3,4096]{2,0,1:T(2,128)} %param.8) | copy-start | bytes 294916
  3.2 5.6 %copy-start.4 = (s32[4096]{0:T(1024)S(1)}, s32[4096]{0:T(1024)}, u32[]{:S(2)}) copy-start(s32[4096]{0:T(1024)} %param.10) | copy-start | bytes 49156
  4.2 6.4 %collective-permute-start = (f32[9,512]{1,0:T(8,128)S(1)}, f32[9,512]{1,0:T(8,128)S(1)}, u32[]{:S(2)}, u32[]{:S(2)}) collective-permute-start(f32[9,512]{1,0:T(8,128)S(1)} %reshape.1029), channel_id=1, source_target_pairs={{0,8},{4,12},{8,0},{12,4},{1,9},{5,13},{9,1},{13,5},{2,10},{6,14},... | collective-permute-start | bytes 55304 | tf_op jit(solution)/shard_map/ppermute | solution.py:114
  10.6 5.1 %collective-permute-start.1 = (f32[9,512]{1,0:T(8,128)S(1)}, f32[9,512]{1,0:T(8,128)S(1)}, u32[]{:S(2)}, u32[]{:S(2)}) collective-permute-start(f32[9,512]{1,0:T(8,128)S(1)} %add.135), channel_id=1, source_target_pairs={{0,4},{4,0},{8,12},{12,8},{1,5},{5,1},{9,13},{13,9},{2,6},{6,2},{1... | collective-permute-start | bytes 55304 | tf_op jit(solution)/shard_map/ppermute | solution.py:114
  12.1 3.5 %copy-start.2 = (f32[9,512]{1,0:T(8,128)S(1)}, f32[9,512]{1,0:T(8,128)}, u32[]{:S(2)}) copy-start(f32[9,512]{1,0:T(8,128)} %param.13) | copy-start | bytes 55300
  12.1 3.5 %copy-start.3 = (f32[512]{0:T(512)S(1)}, f32[512]{0:T(512)}, u32[]{:S(2)}) copy-start(f32[512]{0:T(512)} %param.12) | copy-start | bytes 6148
  14.1 5.7 %collective-permute-start.4 = (f32[6,4096]{1,0:T(8,128)S(1)}, f32[6,4096]{1,0:T(8,128)S(1)}, u32[]{:S(2)}, u32[]{:S(2)}) collective-permute-start(f32[6,4096]{1,0:T(8,128)S(1)} %reshape.1039), channel_id=1, source_target_pairs={{0,2},{1,3},{2,0},{3,1},{4,6},{5,7},{6,4},{7,5},{8,10},{9,11},{10,... | collective-permute-start | bytes 294920 | tf_op jit(solution)/shard_map/ppermute | solution.py:114
  16.0 1.0 %copy-start = (f32[2,9,4096]{2,0,1:T(2,128)S(1)}, f32[2,9,4096]{2,0,1:T(2,128)}, u32[]{:S(2)}) copy-start(f32[2,9,4096]{2,0,1:T(2,128)} %param.7) | copy-start | bytes 884740
  18.8 6.4 %copy-start.5 = (f32[4096]{0:T(1024)S(1)}, f32[4096]{0:T(1024)}, u32[]{:S(2)}) copy-start(f32[4096]{0:T(1024)} %param.11) | copy-start | bytes 49156
  19.2 4.3 %collective-permute-start.2 = (f32[4,4096]{1,0:T(4,128)S(1)}, f32[4,4096]{1,0:T(4,128)S(1)}, u32[]{:S(2)}, u32[]{:S(2)}) collective-permute-start(f32[4,4096]{1,0:T(4,128)S(1)} %pad_maximum_fusion.18), channel_id=1, source_target_pairs={{0,2},{1,3},{2,0},{3,1},{4,6},{5,7},{6,4},{7,5},{8,10},{9,11},{10,... | collective-permute-start | bytes 196616 | tf_op jit(solution)/shard_map/ppermute | solution.py:114
  19.8 5.1 %collective-permute-start.5 = (f32[6,4096]{1,0:T(8,128)S(1)}, f32[6,4096]{1,0:T(8,128)S(1)}, u32[]{:S(2)}, u32[]{:S(2)}) collective-permute-start(f32[6,4096]{1,0:T(8,128)S(1)} %add.141), channel_id=1, source_target_pairs={{0,1},{1,0},{2,3},{3,2},{4,5},{5,4},{6,7},{7,6},{8,9},{9,8},{10,11... | collective-permute-start | bytes 294920 | tf_op jit(solution)/shard_map/ppermute | solution.py:114
  23.6 1.3 %collective-permute-start.3 = (f32[4,4096]{1,0:T(4,128)S(1)}, f32[4,4096]{1,0:T(4,128)S(1)}, u32[]{:S(2)}, u32[]{:S(2)}) collective-permute-start(f32[4,4096]{1,0:T(4,128)S(1)} %fusion.154), channel_id=1, source_target_pairs={{0,1},{1,0},{2,3},{3,2},{4,5},{5,4},{6,7},{7,6},{8,9},{9,8},{10,11... | collective-permute-start | bytes 196616 | tf_op jit(solution)/shard_map/ppermute | solution.py:114
  29.1 5.2 %collective-permute-start.6 = (f32[10,512]{1,0:T(8,128)S(1)}, f32[10,512]{1,0:T(8,128)S(1)}, u32[]{:S(2)}, u32[]{:S(2)}) collective-permute-start(f32[10,512]{1,0:T(8,128)S(1)} %pad_maximum_fusion.21), channel_id=1, source_target_pairs={{0,8},{4,12},{8,0},{12,4},{1,9},{5,13},{9,1},{13,5},{2,10},{6,14},... | collective-permute-start | bytes 61448 | tf_op jit(solution)/shard_map/ppermute | solution.py:114
  34.3 4.0 %collective-permute-start.7 = (f32[10,512]{1,0:T(8,128)S(1)}, f32[10,512]{1,0:T(8,128)S(1)}, u32[]{:S(2)}, u32[]{:S(2)}) collective-permute-start(f32[10,512]{1,0:T(8,128)S(1)} %fusion.153), channel_id=1, source_target_pairs={{0,4},{4,0},{8,12},{12,8},{1,5},{5,1},{9,13},{13,9},{2,6},{6,2},{1... | collective-permute-start | bytes 61448 | tf_op jit(solution)/shard_map/ppermute | solution.py:114
  44.3 4.3 %collective-permute-start.8 = (f32[4,4096]{1,0:T(4,128)S(1)}, f32[4,4096]{1,0:T(4,128)S(1)}, u32[]{:S(2)}, u32[]{:S(2)}) collective-permute-start(f32[4,4096]{1,0:T(4,128)S(1)} %pad_maximum_fusion.19), channel_id=1, source_target_pairs={{0,2},{1,3},{2,0},{3,1},{4,6},{5,7},{6,4},{7,5},{8,10},{9,11},{10,... | collective-permute-start | bytes 196616 | tf_op jit(solution)/shard_map/ppermute | solution.py:114
  48.7 1.3 %collective-permute-start.9 = (f32[4,4096]{1,0:T(4,128)S(1)}, f32[4,4096]{1,0:T(4,128)S(1)}, u32[]{:S(2)}, u32[]{:S(2)}) collective-permute-start(f32[4,4096]{1,0:T(4,128)S(1)} %fusion.152), channel_id=1, source_target_pairs={{0,1},{1,0},{2,3},{3,2},{4,5},{5,4},{6,7},{7,6},{8,9},{9,8},{10,11... | collective-permute-start | bytes 196616 | tf_op jit(solution)/shard_map/ppermute | solution.py:114
  53.4 5.0 %collective-permute-start.10 = (f32[10,512]{1,0:T(8,128)S(1)}, f32[10,512]{1,0:T(8,128)S(1)}, u32[]{:S(2)}, u32[]{:S(2)}) collective-permute-start(f32[10,512]{1,0:T(8,128)S(1)} %pad_maximum_fusion.22), channel_id=1, source_target_pairs={{0,8},{4,12},{8,0},{12,4},{1,9},{5,13},{9,1},{13,5},{2,10},{6,14},... | collective-permute-start | bytes 61448 | tf_op jit(solution)/shard_map/ppermute | solution.py:114
  58.4 4.0 %collective-permute-start.11 = (f32[10,512]{1,0:T(8,128)S(1)}, f32[10,512]{1,0:T(8,128)S(1)}, u32[]{:S(2)}, u32[]{:S(2)}) collective-permute-start(f32[10,512]{1,0:T(8,128)S(1)} %fusion.151), channel_id=1, source_target_pairs={{0,4},{4,0},{8,12},{12,8},{1,5},{5,1},{9,13},{13,9},{2,6},{6,2},{1... | collective-permute-start | bytes 61448 | tf_op jit(solution)/shard_map/ppermute | solution.py:114
  68.1 4.3 %collective-permute-start.12 = (f32[4,4096]{1,0:T(4,128)S(1)}, f32[4,4096]{1,0:T(4,128)S(1)}, u32[]{:S(2)}, u32[]{:S(2)}) collective-permute-start(f32[4,4096]{1,0:T(4,128)S(1)} %pad_maximum_fusion.20), channel_id=1, source_target_pairs={{0,2},{1,3},{2,0},{3,1},{4,6},{5,7},{6,4},{7,5},{8,10},{9,11},{10,... | collective-permute-start | bytes 196616 | tf_op jit(solution)/shard_map/ppermute | solution.py:114
  72.4 1.3 %collective-permute-start.13 = (f32[4,4096]{1,0:T(4,128)S(1)}, f32[4,4096]{1,0:T(4,128)S(1)}, u32[]{:S(2)}, u32[]{:S(2)}) collective-permute-start(f32[4,4096]{1,0:T(4,128)S(1)} %fusion.150), channel_id=1, source_target_pairs={{0,1},{1,0},{2,3},{3,2},{4,5},{5,4},{6,7},{7,6},{8,9},{9,8},{10,11... | collective-permute-start | bytes 196616 | tf_op jit(solution)/shard_map/ppermute | solution.py:114
  77.1 5.2 %collective-permute-start.14 = (f32[10,512]{1,0:T(8,128)S(1)}, f32[10,512]{1,0:T(8,128)S(1)}, u32[]{:S(2)}, u32[]{:S(2)}) collective-permute-start(f32[10,512]{1,0:T(8,128)S(1)} %pad_maximum_fusion.23), channel_id=1, source_target_pairs={{0,8},{4,12},{8,0},{12,4},{1,9},{5,13},{9,1},{13,5},{2,10},{6,14},... | collective-permute-start | bytes 61448 | tf_op jit(solution)/shard_map/ppermute | solution.py:114
  82.3 4.0 %collective-permute-start.15 = (f32[10,512]{1,0:T(8,128)S(1)}, f32[10,512]{1,0:T(8,128)S(1)}, u32[]{:S(2)}, u32[]{:S(2)}) collective-permute-start(f32[10,512]{1,0:T(8,128)S(1)} %fusion.149), channel_id=1, source_target_pairs={{0,4},{4,0},{8,12},{12,8},{1,5},{5,1},{9,13},{13,9},{2,6},{6,2},{1... | collective-permute-start | bytes 61448 | tf_op jit(solution)/shard_map/ppermute | solution.py:114
